TPU v7x, 32 devices: a whole 2x2x4 slice. The times are simulated.
32 devices in a mesh: dp: 2 (over core), ctx: 4 (over z), expert: 4 (over y, x).
Axes of the slice: x: 2, y: 2, z: 4, core: 2. Of those that a mesh axis runs over, the one named last changes fastest.
Arguments:
- x_in: bfloat16 [4, 64, 8192], P('dp', 'ctx', 'expert'), may hold values from -6 to 6
- z_in: bfloat16 [4, 64, 8192], P('dp', 'ctx', 'expert'), may hold values from -6 to 6
- b_in: bfloat16 [4, 64, 128], P('dp', 'ctx'), may hold values from -0.5 to 0.5
- c_in: bfloat16 [4, 64, 128], P('dp', 'ctx'), may hold values from -0.75 to 0.75
- decay_log: float32 [4, 64, 128], P('dp', 'ctx', 'expert'), may hold values from -2 to 0, as said below
- skip: float32 [128], P('expert'), may hold values from 0.5 to 1.5
- out_weight: bfloat16 [8192, 4096], P('expert', 'ctx'), may hold values from -1 to 1
- moe_gain: float32 [4096], replicated, may hold values from 0.5 to 1.5
- gate_up: bfloat16 [4, 2, 7168, 4096], P('expert', None, ('dp', 'ctx')), may hold values from -0.09375 to 0.09375
- expert_ids: int32 [4, 64, 2], P('dp', ('ctx', 'expert')), may hold values from 0 to 3, as said below
- slot_ids: int32 [4, 64, 2], P('dp', ('ctx', 'expert')), may hold values from 0 to 7, as said below
Outputs:
- mamba_out: bfloat16 [4, 64, 4096], P('dp', ('ctx', 'expert'))
- expert_hidden: bfloat16 [4, 7168, 256], P('expert', ('dp', 'ctx'))
Inputs may be any that keep to these rules, and one draw needn't show every extreme that they name: `decay_log`: its values are negative. `expert_ids`: each token names two different experts. In the rows of one device (streams s with the same s // 2, positions t with the same t // 4) one expert, the same for all devices, is named by exactly 8 rows, and no expert by more than 8 rows. `slot_ids`: in the rows of one device the pairs (expert, slot) are all different.
All inputs are finite; a program needn't handle non-finite values.
Results may differ from a plain program's by a relative error of at most 0.0085.
Values may be sent and summed in bfloat16 or wider, within the bound.
No kernel may reach another device: no remote copies, remote signals or barrier semaphores. Data moves between devices by JAX's collectives and lax.ppermute only.
A program may use at most 128 MiB of HBM per device.

v0:
```python
import jax
import jax.numpy as jnp
from jax import lax
from jax.sharding import PartitionSpec as P

P_SIZE = 64


def carried_in(value, axis, join, neutral):
    count, mine = (lax.axis_size(axis), lax.axis_index(axis))
    pieces = jax.tree.map(lambda part: lax.all_gather(part, axis), value)
    running = jax.tree.map(
        lambda part, zero: jnp.full_like(part, 0) + jnp.asarray(zero, part.dtype), value, neutral
    )

    def step(position, running):
        longer = join(running, jax.tree.map(lambda part: part[position], pieces))
        return jax.tree.map(lambda new, old: jnp.where(position < mine, new, old), longer, running)

    return lax.fori_loop(0, count - 1, step, running)


def local(
    x_in, z_in, b_in, c_in, decay_log, skip, out_weight, moe_gain, gate_up, expert_ids, slot_ids
):
    highest = lax.Precision.HIGHEST
    seq_count, block_len, width_in = x_in.shape
    head_count = skip.shape[0]
    model_width = moe_gain.shape[0]
    per_block = expert_ids.shape[1]
    pick_count = expert_ids.shape[2]
    row_count = seq_count * per_block
    x_float = x_in.astype(jnp.float32).reshape(seq_count, block_len, head_count, P_SIZE)
    b_float = b_in.astype(jnp.float32)
    c_float = c_in.astype(jnp.float32)
    cum_decay = jnp.cumsum(decay_log, axis=1)
    scores = jnp.einsum("stn,sun->stu", c_float, b_float, precision=highest)
    causal = (jnp.arange(block_len)[:, None] >= jnp.arange(block_len)[None, :])[None, :, :, None]
    spans = cum_decay[:, :, None, :] - cum_decay[:, None, :, :]
    kernel = jnp.where(causal, jnp.exp(jnp.where(causal, spans, 0.0)), 0.0) * scores[:, :, :, None]
    inside = jnp.einsum("stuh,suhp->sthp", kernel, x_float, precision=highest)
    final_decay = cum_decay[:, -1, :]
    tails = jnp.exp(final_decay[:, None, :] - cum_decay)
    local_state = jnp.einsum("suh,suhp,sun->shpn", tails, x_float, b_float, precision=highest)

    def compose(earlier, following):
        return (
            earlier[0] * following[0],
            following[0][:, :, None, None] * earlier[1] + following[1],
        )

    carried = carried_in(
        (jnp.exp(final_decay), local_state),
        "ctx",
        compose,
        (jnp.ones_like(final_decay), jnp.zeros_like(local_state)),
    )
    incoming = carried[1]
    outside = jnp.exp(cum_decay)[:, :, :, None] * jnp.einsum(
        "stn,shpn->sthp", c_float, incoming, precision=highest
    )
    ssd = inside + outside + skip[None, None, :, None] * x_float
    gated = (
        ssd.reshape(seq_count, block_len, width_in) * jax.nn.silu(z_in.astype(jnp.float32))
    ).astype(jnp.bfloat16)
    partial_value = jnp.einsum(
        "stk,kd->std",
        lax.all_gather(gated, "ctx", axis=1, tiled=True),
        out_weight,
        preferred_element_type=jnp.float32,
    )
    ctx_count = lax.axis_size("ctx")
    group_count = lax.axis_size("expert")
    grouped = partial_value.reshape(
        seq_count, ctx_count, group_count, per_block, out_weight.shape[1]
    )
    reduced = lax.psum_scatter(grouped, "expert", scatter_dimension=2, tiled=True).astype(
        jnp.bfloat16
    )
    swapped = lax.all_to_all(reduced, "ctx", split_axis=1, concat_axis=4, tiled=True)
    mamba_out = swapped.reshape(seq_count, per_block, model_width)
    flat = mamba_out.reshape(row_count, model_width).astype(jnp.float32)
    scale = lax.rsqrt(jnp.mean(flat * flat, axis=1, keepdims=True) + 1e-05)
    normed = (flat * scale * moe_gain[None, :]).astype(jnp.bfloat16)
    expert_count = lax.axis_size("expert")
    capacity = max(2, 4 * row_count // expert_count)
    chosen_experts = expert_ids.reshape(row_count, pick_count)
    placed = slot_ids.reshape(row_count, pick_count)
    match_expert = chosen_experts[:, :, None, None] == jnp.arange(expert_count)[None, None, :, None]
    match_slot = placed[:, :, None, None] == jnp.arange(capacity)[None, None, None, :]
    selector = (match_expert & match_slot).astype(jnp.bfloat16)
    outgoing = jnp.einsum(
        "rkec,rd->ecd", selector, normed, preferred_element_type=jnp.float32
    ).astype(jnp.bfloat16)
    arrived = lax.all_to_all(outgoing, "expert", split_axis=0, concat_axis=0, tiled=True)
    weights_local = gate_up[0]
    piece = lax.all_gather(arrived[None], ("dp", "ctx"), axis=0, tiled=True)
    slot_rows = piece.reshape(-1, piece.shape[3])
    both = jnp.einsum("gfd,qd->gfq", weights_local, slot_rows, preferred_element_type=jnp.float32)
    hidden = (jax.nn.silu(both[0]) * both[1]).astype(jnp.bfloat16)
    expert_hidden = hidden[None]
    return (mamba_out, expert_hidden)


def solution(mesh):
    in_specs = (
        P("dp", "ctx", "expert"),
        P("dp", "ctx", "expert"),
        P("dp", "ctx", None),
        P("dp", "ctx", None),
        P("dp", "ctx", "expert"),
        P("expert"),
        P("expert", "ctx"),
        P(),
        P("expert", None, ("dp", "ctx"), None),
        P("dp", ("ctx", "expert"), None),
        P("dp", ("ctx", "expert"), None),
    )
    out_specs = (P("dp", ("ctx", "expert"), None), P("expert", ("dp", "ctx"), None))
    return jax.shard_map(local, mesh=mesh, in_specs=in_specs, out_specs=out_specs, check_vma=False)
```

profile of v0, /device:TPU:0, one launch (start us, length us, event | category | flops | bytes accessed | tf_op | source)
XLA Modules:
  0.0 281.5 jit_solution(16585877219669629236)
XLA Ops:
  7.2 0.8 reduce_window_sum.11
  8.1 1.2 reshape.92
  9.3 3.3 %fusion.15 = f32[2,32,64,128]{3,2,1,0:T(8,128)} fusion(f32[2,16,32]{1,2,0:T(8,128)S(1)} %copy.70, bf16[2,16,32,64]{3,2,1,0:T(8,128)(2,1)S(1)} %reshape.92, bf16[2,16,128]{2,1,0:T(8,128)(2,1)S(1)} %copy-done), kind=kOutput, calls=%fused_computation.19 | convolution fusion | flops 100794368 | bytes 2240512 | tf_op jit(solution)/shard_map/suh,suhp,sun->shpn/dot_general | solution.py:44
  13.0 0.7 dynamic-slice
  13.7 12.6 %all-gather = f32[8,1,32]{2,1,0:T(1,128)S(1)} all-gather(f32[2,1,32]{2,1,0:T(1,128)S(1)} %get-tuple-element.138), channel_id=2, replica_groups=mesh['dp'=2,'ctx'=4,'expert'=4] {'ctx'}, dimensions={0}, use_global_device_ids=true | all-gather | bytes 1280 | tf_op jit(solution)/shard_map/all_gather | solution.py:11
  26.6 138.6 %all-gather.6.cloned.1.call-done = f32[8,32,64,128]{3,2,1,0:T(8,128)} async-done(((f32[2,32,64,128]{3,2,1,0:T(8,128)}), f32[8,32,64,128]{3,2,1,0:T(8,128)}) %all-gather.6.cloned.1.call-update) | async-done | bytes 8388624 | tf_op jit(solution)/shard_map/all_gather | solution.py:11
  165.2 6.3 %while.14 = (s32[]{:T(128)}, f32[2,32,64,128]{3,2,1,0:T(8,128)S(1)}, s32[]{:T(128)}, f32[4,2,32]{2,1,0:T(2,128)S(1)}, f32[4,2,32,64,128]{4,3,2,1,0:T(8,128)}, /*index=5*/s32[]{:T(128)}, s32[]{:T(128)}) while((s32[]{:T(128)}, f32[2,32,64,128]{3,2,1,0:T(8,128)S(1)}, s32[]{:T(128)}, f32[4,2,32]{2,1,0:T(2,128)S(1)}, ...), condition=%wide.region_2.3_spmd.clone, body=%wide.region_1.2_spmd.clone.sunk | while | flops 2097156 | bytes 6292329 | solution.py:20
  165.2 2.1 fusion.50
  167.3 2.1 fusion.50
  169.4 2.1 fusion.50
  171.5 2.6 fusion.11
  174.1 0.7 fusion.13
  175.3 16.1 %all_gather.19 = bf16[2,64,2048]{2,1,0:T(8,128)(2,1)S(1)} all-gather(bf16[2,16,2048]{2,1,0:T(8,128)(2,1)S(1)} %fusion.30), channel_id=1, replica_groups=mesh['dp'=2,'ctx'=4,'expert'=4] {'ctx'}, dimensions={1}, use_global_device_ids=true | all-gather | bytes 655360 | tf_op jit(solution)/shard_map/all_gather | solution.py:68
  191.4 2.9 %fusion.3 = f32[2,64,1024]{2,1,0:T(8,128)S(1)} fusion(bf16[2,64,2048]{2,1,0:T(8,128)(2,1)S(1)} %all_gather.19, bf16[2048,1024]{1,0:T(8,128)(2,1)} %param.19), kind=kOutput, calls=%fused_computation.6 | convolution fusion | flops 536870912 | bytes 5242880 | tf_op jit(solution)/shard_map/stk,kd->std/dot_general | solution.py:66
  194.5 23.9 %all-reduce.2 = bf16[2,4,4,4,1024]{4,3,2,1,0:T(4,128)(2,1)S(1)} all-reduce(f32[2,4,4,4,1024]{4,3,2,1,0:T(4,128)S(1)} %reshape.94), channel_id=5, replica_groups=mesh['dp'=2,'ctx'=4,'expert'=4] {'expert'}, use_global_device_ids=true, to_apply=%region_3.4.clone | all-reduce | flops 131072 | bytes 786432
  218.4 0.7 dynamic-slice_convert_fusion
  219.1 0.7 copy.73
  219.8 3.3 %all-to-all-start = ((bf16[2,4,1,4,1024]{4,3,2,0,1:T(4,128)(2,1)}), bf16[2,4,1,4,1024]{4,3,2,0,1:T(4,128)(2,1)S(1)}, u32[]{:S(2)}, u32[]{:S(2)}) async-start(bf16[2,4,1,4,1024]{4,3,2,0,1:T(4,128)(2,1)} %copy.73), calls=%async_computation | async-start | bytes 131072 | tf_op jit(solution)/shard_map/all_to_all | solution.py:80
  223.2 5.6 %all-to-all-done = bf16[2,4,1,4,1024]{4,3,2,0,1:T(4,128)(2,1)S(1)} async-done(((bf16[2,4,1,4,1024]{4,3,2,0,1:T(4,128)(2,1)}), bf16[2,4,1,4,1024]{4,3,2,0,1:T(4,128)(2,1)S(1)}, u32[]{:S(2)}, u32[]{:S(2)}) %all-to-all-start) | async-done | bytes 65568 | tf_op jit(solution)/shard_map/all_to_all | solution.py:80
  229.5 9.1 %all_to_all.20 = bf16[4,8,4096]{2,1,0:T(8,128)(2,1)} all-to-all(bf16[4,8,4096]{2,1,0:T(8,128)(2,1)S(1)} %convolution_convert_fusion), channel_id=1, replica_groups=mesh['dp'=2,'ctx'=4,'expert'=4] {'expert'}, dimensions={0} | all-to-all | bytes 524288 | tf_op jit(solution)/shard_map/all_to_all | solution.py:95
  238.7 0.7 reshape.95
  239.4 25.6 %all-gather.8.cloned.1.call-done = bf16[32,8,4096]{2,1,0:T(8,128)(2,1)} async-done(((bf16[4,8,4096]{2,1,0:T(8,128)(2,1)}), bf16[32,8,4096]{2,1,0:T(8,128)(2,1)}) %all-gather.8.cloned.1.call-update) | async-done | bytes 2097168 | tf_op jit(solution)/shard_map/all_gather | solution.py:97
  265.0 8.4 %fusion.6 = f32[2,896,256]{1,2,0:T(8,128)S(1)} fusion(bf16[1,2,896,4096]{3,2,1,0:T(8,128)(2,1)} %param.21, bf16[32,8,4096]{2,1,0:T(8,128)(2,1)} %all-gather.8.cloned.1.call-done), kind=kOutput, calls=%fused_computation.9 | convolution fusion | flops 3758096384 | bytes 18612224 | tf_op jit(solution)/shard_map/gfd,qd->gfq/dot_general | solution.py:99
  273.7 1.0 copy.79
  (51 shorter events, 2.5 us)
Async XLA Ops:
  7.2 2.1 copy-start
  7.2 158.0 %all-gather.6.cloned.1.call-start = ((), (), s32[]{:S(2)}) async-start(), calls=%async_computation.2 | async-start | bytes 10485760 | tf_op jit(solution)/shard_map/all_gather | solution.py:11
  9.3 3.6 %copy-start.4 = (s32[2,4,2]{1,2,0:T(2,128)S(1)}, s32[2,4,2]{1,2,0:T(2,128)}, u32[]{:S(2)}) copy-start(s32[2,4,2]{1,2,0:T(2,128)} %param.23) | copy-start | bytes 196
  9.3 3.7 %copy-start.5 = (s32[2,4,2]{1,2,0:T(2,128)S(1)}, s32[2,4,2]{1,2,0:T(2,128)}, u32[]{:S(2)}) copy-start(s32[2,4,2]{1,2,0:T(2,128)} %param.22) | copy-start | bytes 196
  9.3 3.7 %copy-start.7 = (u32[32]{0:T(128)S(1)}, u32[32]{0:T(128)}, u32[]{:S(2)}) copy-start(u32[32]{0:T(128)} %constant.50) | copy-start | bytes 388
  9.3 17.1 %copy-start.2 = (bf16[2,16,128]{2,1,0:T(8,128)(2,1)S(1)}, bf16[2,16,128]{2,1,0:T(8,128)(2,1)}, u32[]{:S(2)}) copy-start(bf16[2,16,128]{2,1,0:T(8,128)(2,1)} %param.16) | copy-start | bytes 24580
  171.5 2.6 copy-start.6
  174.1 1.1 copy-start.1
  194.3 34.9 %copy-start.3 = (f32[4096]{0:T(1024)S(1)}, f32[4096]{0:T(1024)}, u32[]{:S(2)}) copy-start(f32[4096]{0:T(1024)} %param.20) | copy-start | bytes 49156
  219.8 9.0 %all-to-all-start = ((bf16[2,4,1,4,1024]{4,3,2,0,1:T(4,128)(2,1)}), bf16[2,4,1,4,1024]{4,3,2,0,1:T(4,128)(2,1)S(1)}, u32[]{:S(2)}, u32[]{:S(2)}) async-start(bf16[2,4,1,4,1024]{4,3,2,0,1:T(4,128)(2,1)} %copy.73), calls=%async_computation | async-start | bytes 131072 | tf_op jit(solution)/shard_map/all_to_all | solution.py:80
  223.1 41.9 %all-gather.8.cloned.1.call-start = ((), (), s32[]{:S(2)}) async-start(), calls=%async_computation.3 | async-start | bytes 2359296 | tf_op jit(solution)/shard_map/all_gather | solution.py:97
Sparse Core Ops, SparseCore 0:
  12.8 152.3 all-gather.5
  238.7 26.1 all-gather.7
where the time goes:
time: 282 us; the launch traced here: 281 us
  waiting for transfers between devices  170 us (60%)
  blocking collectives  61.8 us (22%)
  matrix products  18.4 us (7%)
  between operations  14.3 us (5%)
  other arithmetic  7.66 us (3%)
  local copies, waits for them, and re-layouts  6.17 us (2%)
  starting transfers between devices  3.37 us (1%)
    all_gather x1, waiting for transfers between devices, carried_in(): pieces = jax.tree.map(lambda part: lax.all_gather(part, axis), value)  139 us
    all_gather x1, waiting for transfers between devices, local(): piece = lax.all_gather(arrived[None], ('dp', 'ctx'), axis=0, tiled=True)  25.6 us
    unnamed x1, blocking collectives  23.9 us
    all_gather x1, blocking collectives, local(): lax.all_gather(gated, 'ctx', axis=1, tiled=True)  16.1 us
    all_gather x1, blocking collectives, carried_in(): pieces = jax.tree.map(lambda part: lax.all_gather(part, axis), value)  12.6 us
    all_to_all x1, blocking collectives, local(): lax.all_to_all(outgoing, 'expert', split_axis=0, concat_axis=0, tiled=True)  9.09 us
    dot_general x1, matrix products, local(): jnp.einsum('gfd,qd->gfq', weights_local, slot_rows, preferred_element_typ...  8.43 us
    select_n x3, other arithmetic, step(): jnp.where(position < mine, new, old)  6.23 us
  transfers between devices with their start and end apart: 3, of which 3 were waited for; matrix products, arithmetic and copies ran while one was open for 1% of the time, Pallas kernels for 0%

commit v1 on v0

v1 whole, which is shorter than its diff:
```python
import jax
import jax.numpy as jnp
from jax import lax
from jax.sharding import PartitionSpec as P

P_SIZE = 64
ALL_AXES = ("dp", "ctx", "expert")


def mixer(x_in, b_in, c_in, decay_log, skip):
    highest = lax.Precision.HIGHEST
    seq_count, total_len, width_in = x_in.shape
    head_count = skip.shape[0]
    state_size = b_in.shape[2]
    chunk = total_len if total_len <= 128 else 64
    chunks = total_len // chunk
    x_float = x_in.astype(jnp.float32).reshape(seq_count, chunks, chunk, head_count, P_SIZE)
    b_float = b_in.astype(jnp.float32).reshape(seq_count, chunks, chunk, state_size)
    c_float = c_in.astype(jnp.float32).reshape(seq_count, chunks, chunk, state_size)
    cum_decay = jnp.cumsum(decay_log.reshape(seq_count, chunks, chunk, head_count), axis=2)
    scores = jnp.einsum("sktn,skun->sktu", c_float, b_float, precision=highest)
    causal = (jnp.arange(chunk)[:, None] >= jnp.arange(chunk)[None, :])[None, None, :, :, None]
    spans = cum_decay[:, :, :, None, :] - cum_decay[:, :, None, :, :]
    kernel = jnp.where(causal, jnp.exp(jnp.where(causal, spans, 0.0)), 0.0) * scores[..., None]
    ssd = jnp.einsum("sktuh,skuhp->skthp", kernel, x_float, precision=highest)
    if chunks > 1:
        final_decay = cum_decay[:, :, -1, :]
        tails = jnp.exp(final_decay[:, :, None, :] - cum_decay)
        states = jnp.einsum("skuh,skuhp,skun->skhpn", tails, x_float, b_float, precision=highest)

        def step(carry, inputs):
            decay_k, state_k = inputs
            return decay_k[:, :, None, None] * carry + state_k, carry

        _, incoming = lax.scan(
            step,
            jnp.zeros_like(states[:, 0]),
            (jnp.moveaxis(jnp.exp(final_decay), 1, 0), jnp.moveaxis(states, 1, 0)),
        )
        incoming = jnp.moveaxis(incoming, 0, 1)
        ssd = ssd + jnp.exp(cum_decay)[..., None] * jnp.einsum(
            "sktn,skhpn->skthp", c_float, incoming, precision=highest
        )
    ssd = ssd + skip[None, None, None, :, None] * x_float
    return ssd.reshape(seq_count, total_len, width_in)


def expert_ffn(gate_up, slot_rows):
    both = jnp.einsum("gfd,qd->gfq", gate_up[0], slot_rows, preferred_element_type=jnp.float32)
    return (jax.nn.silu(both[0]) * both[1]).astype(jnp.bfloat16)


def dispatch_routed(partial_value, moe_gain, gate_up, expert_ids, slot_ids, capacity):
    seq_count = partial_value.shape[0]
    model_width = moe_gain.shape[0]
    per_block = expert_ids.shape[1]
    pick_count = expert_ids.shape[2]
    row_count = seq_count * per_block
    ctx_count = lax.axis_size("ctx")
    group_count = lax.axis_size("expert")
    grouped = partial_value.reshape(
        seq_count, ctx_count, group_count, per_block, partial_value.shape[2]
    )
    reduced = lax.psum_scatter(grouped, "expert", scatter_dimension=2, tiled=True).astype(
        jnp.bfloat16
    )
    swapped = lax.all_to_all(reduced, "ctx", split_axis=1, concat_axis=4, tiled=True)
    mamba_out = swapped.reshape(seq_count, per_block, model_width)
    flat = mamba_out.reshape(row_count, model_width).astype(jnp.float32)
    scale = lax.rsqrt(jnp.mean(flat * flat, axis=1, keepdims=True) + 1e-05)
    normed = (flat * scale * moe_gain[None, :]).astype(jnp.bfloat16)
    chosen = expert_ids.reshape(row_count, pick_count)
    placed = slot_ids.reshape(row_count, pick_count)
    match_expert = chosen[:, :, None, None] == jnp.arange(group_count)[None, None, :, None]
    match_slot = placed[:, :, None, None] == jnp.arange(capacity)[None, None, None, :]
    selector = (match_expert & match_slot).astype(jnp.bfloat16)
    outgoing = jnp.einsum(
        "rkec,rd->ecd", selector, normed, preferred_element_type=jnp.float32
    ).astype(jnp.bfloat16)
    arrived = lax.all_to_all(outgoing, "expert", split_axis=0, concat_axis=0, tiled=True)
    piece = lax.all_gather(arrived[None], ("dp", "ctx"), axis=0, tiled=True)
    slot_rows = piece.reshape(-1, piece.shape[3])
    return (mamba_out, expert_ffn(gate_up, slot_rows)[None])


def local(
    x_in, z_in, b_in, c_in, decay_log, skip, out_weight, moe_gain, gate_up, expert_ids, slot_ids
):
    seq_count, block_len, width_in = x_in.shape
    state_size = b_in.shape[2]
    model_width = moe_gain.shape[0]
    col_width = out_weight.shape[1]
    per_block = expert_ids.shape[1]
    pick_count = expert_ids.shape[2]
    dp_count = lax.axis_size("dp")
    ctx_count = lax.axis_size("ctx")
    group_count = lax.axis_size("expert")
    device_count = dp_count * ctx_count * group_count
    row_count = seq_count * per_block
    capacity = max(2, 4 * row_count // group_count)

    packed = jnp.concatenate([x_in, z_in, b_in, c_in], axis=2)
    packed = lax.all_gather(packed, "ctx", axis=1, tiled=True)
    decay_all = lax.all_gather(decay_log, "ctx", axis=1, tiled=True)
    route = jnp.stack([expert_ids, slot_ids], axis=-1)
    routes = lax.all_gather(route[None], ALL_AXES, axis=0, tiled=True)

    x_all = packed[:, :, :width_in]
    z_all = packed[:, :, width_in : 2 * width_in]
    b_all = packed[:, :, 2 * width_in : 2 * width_in + state_size]
    c_all = packed[:, :, 2 * width_in + state_size :]
    ssd = mixer(x_all, b_all, c_all, decay_all, skip)
    gated = (ssd * jax.nn.silu(z_all.astype(jnp.float32))).astype(jnp.bfloat16)
    partial_value = jnp.einsum(
        "stk,kd->std", gated, out_weight, preferred_element_type=jnp.float32
    )
    if device_count * row_count * model_width * 2 > (8 << 20):
        return dispatch_routed(partial_value, moe_gain, gate_up, expert_ids, slot_ids, capacity)
    grouped = partial_value.reshape(seq_count, ctx_count, group_count, per_block, col_width)
    grouped = jnp.moveaxis(grouped, 2, 0)
    reduced = lax.psum_scatter(grouped, "expert", scatter_dimension=0, tiled=True)
    reduced = reduced.astype(jnp.bfloat16)
    gathered = lax.all_gather(reduced, ALL_AXES, axis=0, tiled=True)
    gathered = gathered.reshape(
        dp_count, ctx_count, group_count, seq_count, ctx_count, per_block, col_width
    )
    tokens = jnp.transpose(gathered, (0, 4, 2, 3, 5, 1, 6)).reshape(
        device_count, row_count, model_width
    )
    me = (lax.axis_index("dp") * ctx_count + lax.axis_index("ctx")) * group_count + lax.axis_index(
        "expert"
    )
    mamba_out = lax.dynamic_index_in_dim(tokens, me, axis=0, keepdims=False).reshape(
        seq_count, per_block, model_width
    )
    flat = tokens.reshape(device_count * row_count, model_width).astype(jnp.float32)
    scale = lax.rsqrt(jnp.mean(flat * flat, axis=1, keepdims=True) + 1e-05)
    normed = (flat * scale * moe_gain[None, :]).astype(jnp.bfloat16)

    chosen = routes[..., 0].reshape(device_count, row_count, pick_count)
    placed = routes[..., 1].reshape(device_count, row_count, pick_count)
    target = jnp.arange(device_count)[:, None, None] * capacity + placed
    mine = chosen == lax.axis_index("expert")
    slot_count = device_count * capacity
    hit = mine[..., None] & (target[..., None] == jnp.arange(slot_count))
    selector = jnp.any(hit, axis=2).reshape(device_count * row_count, slot_count)
    dispatched = jnp.einsum(
        "rq,rd->qd", selector.astype(jnp.bfloat16), normed, preferred_element_type=jnp.float32
    ).astype(jnp.bfloat16)
    hidden = expert_ffn(gate_up, dispatched)
    return (mamba_out, hidden[None])


def solution(mesh):
    in_specs = (
        P("dp", "ctx", "expert"),
        P("dp", "ctx", "expert"),
        P("dp", "ctx", None),
        P("dp", "ctx", None),
        P("dp", "ctx", "expert"),
        P("expert"),
        P("expert", "ctx"),
        P(),
        P("expert", None, ("dp", "ctx"), None),
        P("dp", ("ctx", "expert"), None),
        P("dp", ("ctx", "expert"), None),
    )
    out_specs = (P("dp", ("ctx", "expert"), None), P("expert", ("dp", "ctx"), None))
    return jax.shard_map(local, mesh=mesh, in_specs=in_specs, out_specs=out_specs, check_vma=False)
```

time: 282 us -> 190 us (0.67)
  waiting for transfers between devices: 170 us -> 16.5 us
  blocking collectives: 61.8 us -> 107 us
  local copies, waits for them, and re-layouts: 6.17 us -> 24 us
  starting transfers between devices: 3.37 us -> 0.08 us
    all_gather x2, waiting for transfers between devices: 164 us -> 16.5 us  [the longest x1 16.5 us: local(): packed = lax.all_gather(packed, 'ctx', axis=1, tiled=True)]
    all_gather x2, blocking collectives: 28.8 us -> 79.7 us  [the longest x1 64.4 us: local(): routes = lax.all_gather(route[None], ALL_AXES, axis=0, tiled=True)]
    all_to_all x1 -> x0, blocking collectives: 9.09 us -> none  [local(): lax.all_to_all(outgoing, 'expert', split_axis=0, concat_axis=0, tiled=True)]
    select_n x3 -> x0, other arithmetic: 6.23 us -> none  [step(): jnp.where(position < mine, new, old)]
    reshape x4 -> x6, local copies, waits for them, and re-layouts: 2.2 us -> 8.3 us  [the longest x1 4.59 us: local(): jnp.transpose(gathered, (0, 4, 2, 3, 5, 1, 6))]
    transpose x0 -> x1, local copies, waits for them, and re-layouts: none -> 5.78 us  [local(): jnp.transpose(gathered, (0, 4, 2, 3, 5, 1, 6))]
    all_to_all x1 -> x0, waiting for transfers between devices: 5.57 us -> none  [local(): lax.all_to_all(reduced, 'ctx', split_axis=1, concat_axis=4, tiled=True)]
    unnamed x1, blocking collectives: 23.9 us -> 27.4 us
  transfers between devices with their start and end apart: 3 -> 2, of which waited for: 3 -> 1; matrix products, arithmetic and copies ran while one was open for 1% -> 1% of each run, Pallas kernels for 0% -> 0%
where the time goes in v1:
time: 190 us; the launch traced here: 188 us
  blocking collectives  107 us (56%)
  local copies, waits for them, and re-layouts  24 us (13%)
  matrix products  17.2 us (9%)
  waiting for transfers between devices  16.5 us (9%)
  between operations  14.3 us (8%)
  other arithmetic  8.9 us (5%)
    all_gather x1, blocking collectives, local(): routes = lax.all_gather(route[None], ALL_AXES, axis=0, tiled=True)  64.4 us
    unnamed x1, blocking collectives  27.4 us
    all_gather x1, waiting for transfers between devices, local(): packed = lax.all_gather(packed, 'ctx', axis=1, tiled=True)  16.5 us
    all_gather x1, blocking collectives, local(): decay_all = lax.all_gather(decay_log, 'ctx', axis=1, tiled=True)  15.2 us
    dot_general x1, matrix products, expert_ffn(): jnp.einsum('gfd,qd->gfq', gate_up[0], slot_rows, preferred_element_type=j...  9.9 us
    transpose x1, local copies, waits for them, and re-layouts, local(): jnp.transpose(gathered, (0, 4, 2, 3, 5, 1, 6))  5.78 us
    reshape x1, local copies, waits for them, and re-layouts, local(): jnp.transpose(gathered, (0, 4, 2, 3, 5, 1, 6))  4.59 us
  transfers between devices with their start and end apart: 2, of which 1 were waited for; matrix products, arithmetic and copies ran while one was open for 1% of the time, Pallas kernels for 0%

profile of v1, /device:TPU:0, one launch (start us, length us, event | category | flops | bytes accessed | tf_op | source)
XLA Modules:
  0.0 188.1 jit_solution(6318419469247914936)
XLA Ops:
  7.2 1.7 pad_maximum_fusion
  9.0 15.2 %all_gather.13 = f32[2,64,32]{2,1,0:T(8,128)S(1)} all-gather(f32[2,16,32]{2,1,0:T(8,128)} %param.15), channel_id=1, replica_groups=mesh['dp'=2,'ctx'=4,'expert'=4] {'ctx'}, dimensions={1}, use_global_device_ids=true | all-gather | bytes 20480 | tf_op jit(solution)/shard_map/all_gather | solution.py:104
  24.4 1.2 dynamic-slice
  25.7 16.5 %all-gather.4.cloned.1.call-done = bf16[2,64,4352]{2,1,0:T(8,128)(2,1)} async-done(((bf16[2,16,4352]{2,1,0:T(8,128)(2,1)}), bf16[2,64,4352]{2,1,0:T(8,128)(2,1)}) %all-gather.4.cloned.1.call-update) | async-done | bytes 1114128 | tf_op jit(solution)/shard_map/all_gather | solution.py:103
  42.2 2.0 %fusion.42 = (bf16[2,64,2048]{2,1,0:T(8,128)(2,1)}, f32[2,64,2048]{2,1,0:T(8,128)S(1)}) fusion(bf16[2,64,4352]{2,1,0:T(8,128)(2,1)} %all-gather.4.cloned.1.call-done), kind=kLoop, calls=%fused_computation.55 | loop fusion | flops 262144 | bytes 2097152 | tf_op jit(solution)/shard_map/slice | solution.py:108
  44.8 1.5 copy.81
  46.3 0.9 fusion.37
  47.2 3.4 %bitcast_add_fusion = f32[2,1,64,32,64]{2,4,3,0,1:T(8,128)} fusion(f32[2,1,64,32,64]{2,4,3,0,1:T(8,128)S(1)} %bitcast.50, bf16[2,64,32,64]{1,3,2,0:T(8,128)(2,1)S(1)} %bitcast.54, f32[32]{0:T(128)S(1)} %copy-done.5, f32[2,64,64]{2,1,0:T(8,128)S(1)} %fusion.37, f32[2,64,32]{1,2,0:T(8,128)S(1)} %copy.68, pred[64,64]{1,0:T(8,128)(4,1)S(1)} %iota_compare_fusion.1), kind=kOutput, calls=%fused_computation.11 | convolution fusion | flops 202899456 | bytes 2674816 | tf_op jit(solution)/shard_map/sktuh,skuhp->skthp/dot_general | solution.py:25
  50.6 2.3 %copy.83 = f32[2,64,2048]{2,1,0:T(8,128)S(1)} copy(f32[2,64,2048]{1,2,0:T(8,128)} %bitcast.51) | data formatting | bytes 2097152 | tf_op jit(solution)/shard_map/reshape | solution.py:45
  52.9 3.0 %fusion.6 = f32[2,64,1024]{2,1,0:T(8,128)S(1)} fusion(bf16[2048,1024]{1,0:T(8,128)(2,1)} %param.17, f32[2,64,2048]{2,1,0:T(8,128)S(1)} %copy.83, bf16[2,64,4352]{2,1,0:T(8,128)(2,1)S(1)} %copy-done.1), kind=kOutput, calls=%fused_computation.9 | convolution fusion | flops 538705920 | bytes 6291456 | tf_op jit(solution)/shard_map/stk,kd->std/dot_general | solution.py:114
  56.2 27.4 %all-reduce.2 = bf16[4,2,4,4,1024]{4,3,2,1,0:T(4,128)(2,1)S(1)} all-reduce(f32[4,2,4,4,1024]{4,3,2,1,0:T(4,128)S(1)} %bitcast.53), channel_id=3, replica_groups=mesh['dp'=2,'ctx'=4,'expert'=4] {'expert'}, use_global_device_ids=true, to_apply=%region_1.2.clone | all-reduce | flops 131072 | bytes 786432
  83.6 1.2 dynamic-slice_convert_fusion
  84.9 64.4 %all-gather = s32[64,4,2,2]{1,2,0,3:T(2,128)S(1)} all-gather(s32[2,4,2,2]{1,2,0,3:T(2,128)S(1)} %pad_add_fusion), channel_id=2, replica_groups=mesh['dp'=2,'ctx'=4,'expert'=4] {'dp','ctx','expert'}, dimensions={0}, use_global_device_ids=true | all-gather | bytes 4224 | tf_op jit(solution)/shard_map/all_gather | solution.py:106
  150.1 5.8 %copy.74 = bf16[2,4,4,2,4,4,1024]{6,5,4,3,2,1,0:T(4,128)(2,1)} copy(bf16[2,4,4,2,4,4,1024]{6,4,1,3,2,5,0:T(4,128)(2,1)} %bitcast.47) | data formatting | bytes 4194304 | tf_op jit(solution)/shard_map/transpose | solution.py:127
  155.8 1.2 fusion.3
  157.0 4.6 %reshape.136 = bf16[32,8,4096]{2,1,0:T(8,128)(2,1)} reshape(bf16[2,4,4,2,4,4,1024]{6,5,4,3,2,1,0:T(4,128)(2,1)} %copy.74) | data formatting | bytes 4194304 | tf_op jit(solution)/shard_map/reshape | solution.py:127
  161.6 0.8 constant_dynamic-slice_fusion
  162.4 0.7 reshape.137
  163.1 1.9 %fusion.5 = bf16[2,4,4,2,4,4,1024]{6,4,1,3,2,5,0:T(4,128)(2,1)S(1)} fusion(f32[4,1024]{1,0:T(4,128)S(1)} %mul.97, f32[2,4,4,2,4]{4,1,3,2,0:T(4,128)S(1)} %add_rsqrt_fusion, bf16[32,2,4,4,1024]{4,3,2,1,0:T(4,128)(2,1)S(1)} %copy-done), kind=kLoop, calls=%fused_computation.8 | loop fusion | flops 4194304 | bytes 4211712 | tf_op jit(solution)/shard_map/convert_element_type | solution.py:138
  165.1 2.7 %copy.79 = bf16[2,4,4,2,4,4,1024]{6,5,4,3,2,1,0:T(4,128)(2,1)S(1)} copy(bf16[2,4,4,2,4,4,1024]{6,4,1,3,2,5,0:T(4,128)(2,1)S(1)} %fusion.5) | data formatting | bytes 4194304 | tf_op jit(solution)/shard_map/convert_element_type | solution.py:138
  167.8 0.9 copy.86
  168.6 9.9 %fusion.16 = f32[2,896,256]{1,2,0:T(8,128)} fusion(bf16[1,2,896,4096]{3,2,1,0:T(8,128)(2,1)} %param.19, bf16[256,4096]{1,0:T(8,128)(2,1)S(1)} %bitcast.52, pred[32,8,256]{2,1,0:T(8,128)(4,1)S(1)} %fusion.34), kind=kOutput, calls=%fused_computation.18 | convolution fusion | flops 4296015872 | bytes 18677760 | tf_op jit(solution)/shard_map/gfd,qd->gfq/dot_general | solution.py:49
  178.5 1.7 fusion.29
  180.3 1.0 copy.80
  (35 shorter events, 1.8 us)
Async XLA Ops:
  7.2 35.0 %all-gather.4.cloned.1.call-start = ((), (), s32[]{:S(2)}) async-start(), calls=%async_computation | async-start | bytes 1392640 | tf_op jit(solution)/shard_map/all_gather | solution.py:103
  9.0 141.1 %all-gather.6.cloned.1.call-start = ((), (), s32[]{:S(2)}) async-start(), calls=%async_computation.1 | async-start | bytes 2162688 | tf_op jit(solution)/shard_map/all_gather | solution.py:123
  44.2 3.0 %copy-start.5 = (f32[32]{0:T(128)S(1)}, f32[32]{0:T(128)}, u32[]{:S(2)}) copy-start(f32[32]{0:T(128)} %param.16) | copy-start | bytes 388
  50.6 2.3 %copy-start.1 = (bf16[2,64,4352]{2,1,0:T(8,128)(2,1)S(1)}, bf16[2,64,4352]{2,1,0:T(8,128)(2,1)}, u32[]{:S(2)}) copy-start(bf16[2,64,4352]{2,1,0:T(8,128)(2,1)} %all-gather.4.cloned.1.call-done) | copy-start | bytes 3342340
  55.9 28.9 %copy-start.2 = (f32[4096]{0:T(1024)S(1)}, f32[4096]{0:T(1024)}, u32[]{:S(2)}) copy-start(f32[4096]{0:T(1024)} %param.18) | copy-start | bytes 49156
  55.9 28.9 %copy-start.3 = (s32[2,4,2]{1,2,0:T(2,128)S(1)}, s32[2,4,2]{1,2,0:T(2,128)}, u32[]{:S(2)}) copy-start(s32[2,4,2]{1,2,0:T(2,128)} %param.21) | copy-start | bytes 196
  55.9 28.9 %copy-start.4 = (s32[2,4,2]{1,2,0:T(2,128)S(1)}, s32[2,4,2]{1,2,0:T(2,128)}, u32[]{:S(2)}) copy-start(s32[2,4,2]{1,2,0:T(2,128)} %param.20) | copy-start | bytes 196
  150.0 5.8 %copy-start = (bf16[32,2,4,4,1024]{4,3,2,1,0:T(4,128)(2,1)S(1)}, bf16[32,2,4,4,1024]{4,3,2,1,0:T(4,128)(2,1)}, u32[]{:S(2)}) copy-start(bf16[32,2,4,4,1024]{4,3,2,1,0:T(4,128)(2,1)} %all-gather.6.cloned.1.call-done) | copy-start | bytes 6291460
Sparse Core Ops, SparseCore 0:
  10.1 32.0 all-gather.3
  85.0 54.1 all-gather.5

commit v2 on v1

--- a/solution.py
+++ b/solution.py
@@ -105,6 +105,7 @@
     route = jnp.stack([expert_ids, slot_ids], axis=-1)
     routes = lax.all_gather(route[None], ALL_AXES, axis=0, tiled=True)
 
+    packed, decay_all, routes = lax.optimization_barrier((packed, decay_all, routes))
     x_all = packed[:, :, :width_in]
     z_all = packed[:, :, width_in : 2 * width_in]
     b_all = packed[:, :, 2 * width_in : 2 * width_in + state_size]
@@ -116,15 +117,12 @@
     )
     if device_count * row_count * model_width * 2 > (8 << 20):
         return dispatch_routed(partial_value, moe_gain, gate_up, expert_ids, slot_ids, capacity)
-    grouped = partial_value.reshape(seq_count, ctx_count, group_count, per_block, col_width)
-    grouped = jnp.moveaxis(grouped, 2, 0)
-    reduced = lax.psum_scatter(grouped, "expert", scatter_dimension=0, tiled=True)
-    reduced = reduced.astype(jnp.bfloat16)
-    gathered = lax.all_gather(reduced, ALL_AXES, axis=0, tiled=True)
+    summed = lax.psum(partial_value, "expert").astype(jnp.bfloat16)
+    gathered = lax.all_gather(summed[None], ("dp", "ctx"), axis=0, tiled=True)
     gathered = gathered.reshape(
-        dp_count, ctx_count, group_count, seq_count, ctx_count, per_block, col_width
+        dp_count, ctx_count, seq_count, ctx_count, group_count, per_block, col_width
     )
-    tokens = jnp.transpose(gathered, (0, 4, 2, 3, 5, 1, 6)).reshape(
+    tokens = jnp.transpose(gathered, (0, 3, 4, 2, 5, 1, 6)).reshape(
         device_count, row_count, model_width
     )
     me = (lax.axis_index("dp") * ctx_count + lax.axis_index("ctx")) * group_count + lax.axis_index(

time: 190 us -> 198 us (1.042)
  waiting for transfers between devices: 16.5 us -> 26.3 us
  local copies, waits for them, and re-layouts: 24 us -> 19.4 us
  blocking collectives: 107 us -> 109 us
    unnamed x1 -> x0, blocking collectives: 27.4 us -> none
    all_gather x1, waiting for transfers between devices: 0.02 us -> 26.2 us  [local(): gathered = lax.all_gather(summed[None], ('dp', 'ctx'), axis=0, tiled=True)]
    psum x0 -> x1, blocking collectives: none -> 23.6 us  [local(): summed = lax.psum(partial_value, 'expert').astype(jnp.bfloat16)]
    all_gather x1, waiting for transfers between devices: 16.5 us -> 0.02 us  [local(): packed = lax.all_gather(packed, 'ctx', axis=1, tiled=True)]
    all_gather x1, blocking collectives: 64.4 us -> 71.7 us  [local(): routes = lax.all_gather(route[None], ALL_AXES, axis=0, tiled=True)]
    reshape x3, local copies, waits for them, and re-layouts: 4.77 us -> 11.4 us  [the longest x2 6.91 us: local(): gathered.reshape(dp_count, ctx_count, seq_count, ctx_count, group_count,...]
    transpose x1 -> x0, local copies, waits for them, and re-layouts: 5.78 us -> none  [local(): jnp.transpose(gathered, (0, 4, 2, 3, 5, 1, 6))]
    convert_element_type x2 -> x0, local copies, waits for them, and re-layouts: 3.91 us -> none  [the longest x1 2.7 us: local(): normed = (flat * scale * moe_gain[None, :]).astype(jnp.bfloat16)]
where the time goes in v2:
time: 198 us
  blocking collectives  109 us (55%)
  waiting for transfers between devices  26.3 us (13%)
  local copies, waits for them, and re-layouts  19.4 us (10%)
  matrix products  18.6 us (9%)
  between operations  14.2 us (7%)
  other arithmetic  10.5 us (5%)
    all_gather x1, blocking collectives, local(): routes = lax.all_gather(route[None], ALL_AXES, axis=0, tiled=True)  71.7 us
    all_gather x1, waiting for transfers between devices, local(): gathered = lax.all_gather(summed[None], ('dp', 'ctx'), axis=0, tiled=True)  26.2 us
    psum x1, blocking collectives, local(): summed = lax.psum(partial_value, 'expert').astype(jnp.bfloat16)  23.6 us
    all_gather x1, blocking collectives, local(): decay_all = lax.all_gather(decay_log, 'ctx', axis=1, tiled=True)  13.3 us
    dot_general x1, matrix products, expert_ffn(): jnp.einsum('gfd,qd->gfq', gate_up[0], slot_rows, preferred_element_type=j...  9.91 us
    reshape x2, local copies, waits for them, and re-layouts, local(): gathered.reshape(dp_count, ctx_count, seq_count, ctx_count, group_count,...  6.91 us
    dot_general x1, matrix products, mixer(): ssd = jnp.einsum('sktuh,skuhp->skthp', kernel, x_float, precision=highest)  4.79 us
    reshape x1, local copies, waits for them, and re-layouts, local(): jnp.transpose(gathered, (0, 3, 4, 2, 5, 1, 6))  4.48 us
  transfers between devices with their start and end apart: 2, of which 1 were waited for; matrix products, arithmetic and copies ran while one was open for 1% of the time, Pallas kernels for 0%

profile of v2, /device:TPU:0, one launch (start us, length us, event | category | flops | bytes accessed | tf_op | source)
XLA Modules:
  0.0 197.7 jit_solution(9487829076397545816)
XLA Ops:
  7.2 1.7 pad_maximum_fusion
  9.0 0.7 pad_add_fusion
  9.7 71.7 %all-gather = s32[64,4,2,2]{1,2,0,3:T(2,128)S(1)} all-gather(s32[2,4,2,2]{1,2,0,3:T(2,128)S(1)} %pad_add_fusion), channel_id=2, replica_groups=mesh['dp'=2,'ctx'=4,'expert'=4] {'dp','ctx','expert'}, dimensions={0}, use_global_device_ids=true | all-gather | bytes 4224 | tf_op jit(solution)/shard_map/all_gather | solution.py:106
  81.4 13.3 %all_gather.13 = f32[2,64,32]{2,1,0:T(8,128)S(1)} all-gather(f32[2,16,32]{2,1,0:T(8,128)} %param.15), channel_id=1, replica_groups=mesh['dp'=2,'ctx'=4,'expert'=4] {'ctx'}, dimensions={1}, use_global_device_ids=true | all-gather | bytes 20480 | tf_op jit(solution)/shard_map/all_gather | solution.py:104
  94.8 0.9 fusion.37
  95.7 1.2 fusion.42
  97.1 1.3 copy.52
  98.4 0.6 copy.53
  99.0 4.8 %bitcast_add_fusion = f32[2,1,64,32,64]{2,4,3,0,1:T(8,128)} fusion(f32[2,1,64,32,64]{2,4,3,0,1:T(8,128)S(1)} %bitcast.46, bf16[2,64,32,64]{1,3,2,0:T(8,128)(2,1)} %bitcast.49, f32[32]{0:T(128)S(1)} %copy-done.2, f32[2,64,64]{2,1,0:T(8,128)S(1)} %fusion.37, f32[2,64,32]{1,2,0:T(8,128)S(1)} %copy.41, pred[64,64]{1,0:T(8,128)(4,1)S(1)} %iota_compare_fusion.1), kind=kOutput, calls=%fused_computation.11 | convolution fusion | flops 202899456 | bytes 2674816 | tf_op jit(solution)/shard_map/sktuh,skuhp->skthp/dot_general | solution.py:25
  103.8 2.3 %copy.54 = f32[2,64,2048]{2,1,0:T(8,128)S(1)} copy(f32[2,64,2048]{1,2,0:T(8,128)} %bitcast.47) | data formatting | bytes 2097152 | tf_op jit(solution)/shard_map/reshape | solution.py:45
  106.1 3.0 %fusion.6 = f32[2,64,1024]{2,1,0:T(8,128)S(1)} fusion(bf16[2048,1024]{1,0:T(8,128)(2,1)} %param.17, f32[2,64,2048]{2,1,0:T(8,128)S(1)} %copy.54, bf16[2,64,4352]{2,1,0:T(8,128)(2,1)S(1)} %copy-done), kind=kOutput, calls=%fused_computation.9 | convolution fusion | flops 538705920 | bytes 6291456 | tf_op jit(solution)/shard_map/stk,kd->std/dot_general | solution.py:115
  109.1 23.6 %all-reduce.1 = bf16[2,64,1024]{2,1,0:T(8,128)(2,1)} all-reduce(f32[2,64,1024]{2,1,0:T(8,128)S(1)} %fusion.6), channel_id=1, replica_groups=mesh['dp'=2,'ctx'=4,'expert'=4] {'expert'}, use_global_device_ids=true, to_apply=%region_1.2 | all-reduce | flops 131072 | bytes 786432 | tf_op jit(solution)/shard_map/psum | solution.py:120
  133.4 26.2 %all-gather.7.cloned.1.call-done = bf16[16,64,1024]{2,1,0:T(8,128)(2,1)} async-done(((bf16[2,64,1024]{2,1,0:T(8,128)(2,1)}), bf16[16,64,1024]{2,1,0:T(8,128)(2,1)}) %all-gather.7.cloned.1.call-update) | async-done | bytes 2097168 | tf_op jit(solution)/shard_map/all_gather | solution.py:121
  159.6 2.7 %reshape.131 = bf16[2,4,2,4,4,4,1024]{6,5,4,3,2,1,0:T(4,128)(2,1)S(1)} reshape(bf16[16,64,1024]{2,1,0:T(8,128)(2,1)} %all-gather.7.cloned.1.call-done) | data formatting | bytes 4194304 | tf_op jit(solution)/shard_map/reshape | solution.py:122
  162.4 2.1 %fusion.3 = f32[2,4,4,2,4]{4,3,2,1,0:T(2,128)S(1)} fusion(bf16[2,4,2,4,4,4,1024]{6,5,4,3,2,1,0:T(4,128)(2,1)S(1)} %reshape.131), kind=kLoop, calls=%fused_computation.6 | loop fusion | flops 3145472 | bytes 2098176 | tf_op jit(solution)/shard_map/reduce_sum | solution.py:135
  164.5 4.2 %copy.61 = bf16[2,4,2,4,4,4,1024]{6,1,5,2,4,3,0:T(4,128)(2,1)} copy(bf16[2,4,2,4,4,4,1024]{6,5,4,3,2,1,0:T(4,128)(2,1)S(1)} %reshape.131) | data formatting | bytes 4194304 | tf_op jit(solution)/shard_map/reshape | solution.py:122
  168.7 4.5 %reshape.132 = bf16[32,8,4096]{2,1,0:T(8,128)(2,1)} reshape(bf16[2,4,4,2,4,4,1024]{6,5,4,3,2,1,0:T(4,128)(2,1)} %bitcast.45) | data formatting | bytes 4194304 | tf_op jit(solution)/shard_map/reshape | solution.py:125
  173.2 0.8 constant_dynamic-slice_fusion
  174.1 0.7 reshape.133
  174.7 2.6 %fusion.5 = bf16[2,4,4,2,4,4,1024]{6,5,4,3,2,1,0:T(4,128)(2,1)S(1)} fusion(f32[4,1024]{1,0:T(4,128)S(1)} %mul.97, f32[2,4,4,2,4]{4,3,2,1,0:T(2,128)S(1)} %add_rsqrt_fusion, bf16[2,4,2,4,4,4,1024]{6,5,4,3,2,1,0:T(4,128)(2,1)S(1)} %reshape.131), kind=kLoop, calls=%fused_computation.8 | loop fusion | flops 4194304 | bytes 4211712 | tf_op jit(solution)/shard_map/convert_element_type | solution.py:136
  177.4 0.9 copy.55
  178.2 9.9 %fusion.16 = f32[2,896,256]{1,2,0:T(8,128)} fusion(bf16[1,2,896,4096]{3,2,1,0:T(8,128)(2,1)} %param.19, bf16[256,4096]{1,0:T(8,128)(2,1)S(1)} %bitcast.48, pred[32,8,256]{2,1,0:T(8,128)(4,1)S(1)} %fusion.34), kind=kOutput, calls=%fused_computation.19 | convolution fusion | flops 4296015872 | bytes 18677760 | tf_op jit(solution)/shard_map/gfd,qd->gfq/dot_general | solution.py:49
  188.2 1.7 fusion.29
  189.9 1.0 copy.51
  (24 shorter events, 0.9 us)
Async XLA Ops:
  7.2 87.6 %all-gather.5.cloned.1.call-start = ((), (), s32[]{:S(2)}) async-start(), calls=%async_computation | async-start | bytes 1392640 | tf_op jit(solution)/shard_map/all_gather | solution.py:103
  9.0 150.7 %all-gather.7.cloned.1.call-start = ((), (), s32[]{:S(2)}) async-start(), calls=%async_computation.1 | async-start | bytes 2359296 | tf_op jit(solution)/shard_map/all_gather | solution.py:121
  97.1 1.9 copy-start.2
  103.8 2.3 %copy-start = (bf16[2,64,4352]{2,1,0:T(8,128)(2,1)S(1)}, bf16[2,64,4352]{2,1,0:T(8,128)(2,1)}, u32[]{:S(2)}) copy-start(bf16[2,64,4352]{2,1,0:T(8,128)(2,1)} %all-gather.5.cloned.1.call-done) | copy-start | bytes 3342340
  106.1 26.7 %copy-start.1 = (f32[4096]{0:T(1024)S(1)}, f32[4096]{0:T(1024)}, u32[]{:S(2)}) copy-start(f32[4096]{0:T(1024)} %param.18) | copy-start | bytes 49156
Sparse Core Ops, SparseCore 0:
  10.1 32.3 all-gather.4
  132.9 26.6 all-gather.6

commit v3 on v2

--- a/solution.py
+++ b/solution.py
@@ -102,10 +102,8 @@
     packed = jnp.concatenate([x_in, z_in, b_in, c_in], axis=2)
     packed = lax.all_gather(packed, "ctx", axis=1, tiled=True)
     decay_all = lax.all_gather(decay_log, "ctx", axis=1, tiled=True)
-    route = jnp.stack([expert_ids, slot_ids], axis=-1)
-    routes = lax.all_gather(route[None], ALL_AXES, axis=0, tiled=True)
+    packed, decay_all = lax.optimization_barrier((packed, decay_all))
 
-    packed, decay_all, routes = lax.optimization_barrier((packed, decay_all, routes))
     x_all = packed[:, :, :width_in]
     z_all = packed[:, :, width_in : 2 * width_in]
     b_all = packed[:, :, 2 * width_in : 2 * width_in + state_size]
@@ -117,31 +115,51 @@
     )
     if device_count * row_count * model_width * 2 > (8 << 20):
         return dispatch_routed(partial_value, moe_gain, gate_up, expert_ids, slot_ids, capacity)
-    summed = lax.psum(partial_value, "expert").astype(jnp.bfloat16)
+    total_len = partial_value.shape[1]
+    route = jnp.stack([expert_ids, slot_ids], axis=-1).astype(jnp.float32).reshape(-1)
+    route_len = route.shape[0]
+    extra_rows = -(-(group_count * route_len) // col_width)
+    route_row = jnp.zeros((extra_rows * col_width,), jnp.float32)
+    route_row = lax.dynamic_update_slice(route_row, route, (lax.axis_index("expert") * route_len,))
+    extended = jnp.concatenate(
+        [partial_value.reshape(seq_count * total_len, col_width), route_row.reshape(extra_rows, col_width)],
+        axis=0,
+    )
+    summed = lax.psum(extended, "expert").astype(jnp.bfloat16)
     gathered = lax.all_gather(summed[None], ("dp", "ctx"), axis=0, tiled=True)
-    gathered = gathered.reshape(
-        dp_count, ctx_count, seq_count, ctx_count, group_count, per_block, col_width
+    gathered = gathered.reshape(dp_count, ctx_count, seq_count * total_len + extra_rows, col_width)
+    routes = gathered[:, :, seq_count * total_len :, :].reshape(dp_count, ctx_count, -1)
+    routes = routes[:, :, : group_count * route_len].astype(jnp.int32)
+    routes = routes.reshape(dp_count, ctx_count, group_count, seq_count, per_block, pick_count, 2)
+    routes = jnp.transpose(routes, (0, 3, 1, 2, 4, 5, 6))
+    tokens = gathered[:, :, : seq_count * total_len, :].reshape(
+        dp_count, ctx_count, seq_count, total_len, col_width
     )
-    tokens = jnp.transpose(gathered, (0, 3, 4, 2, 5, 1, 6)).reshape(
-        device_count, row_count, model_width
+    tokens = jnp.transpose(tokens, (0, 2, 3, 1, 4))
+    tok_blocks = tokens.reshape(dp_count, seq_count, ctx_count * group_count, per_block, model_width)
+    mine_block = lax.axis_index("ctx") * group_count + lax.axis_index("expert")
+    mamba_out = lax.dynamic_index_in_dim(
+        lax.dynamic_index_in_dim(tok_blocks, lax.axis_index("dp"), axis=0, keepdims=False),
+        mine_block,
+        axis=1,
+        keepdims=False,
     )
-    me = (lax.axis_index("dp") * ctx_count + lax.axis_index("ctx")) * group_count + lax.axis_index(
-        "expert"
-    )
-    mamba_out = lax.dynamic_index_in_dim(tokens, me, axis=0, keepdims=False).reshape(
-        seq_count, per_block, model_width
-    )
-    flat = tokens.reshape(device_count * row_count, model_width).astype(jnp.float32)
+    token_count = dp_count * seq_count * total_len
+    flat = tokens.reshape(token_count, model_width).astype(jnp.float32)
     scale = lax.rsqrt(jnp.mean(flat * flat, axis=1, keepdims=True) + 1e-05)
     normed = (flat * scale * moe_gain[None, :]).astype(jnp.bfloat16)
 
-    chosen = routes[..., 0].reshape(device_count, row_count, pick_count)
-    placed = routes[..., 1].reshape(device_count, row_count, pick_count)
-    target = jnp.arange(device_count)[:, None, None] * capacity + placed
-    mine = chosen == lax.axis_index("expert")
+    group = (
+        (jnp.arange(dp_count)[:, None, None, None, None] * ctx_count
+         + jnp.arange(ctx_count)[None, None, :, None, None]) * group_count
+        + jnp.arange(group_count)[None, None, None, :, None]
+    )
+    group = jnp.broadcast_to(group, (dp_count, seq_count, ctx_count, group_count, per_block))
+    target = group.reshape(token_count, 1) * capacity + routes[..., 1].reshape(token_count, pick_count)
+    mine = routes[..., 0].reshape(token_count, pick_count) == lax.axis_index("expert")
     slot_count = device_count * capacity
     hit = mine[..., None] & (target[..., None] == jnp.arange(slot_count))
-    selector = jnp.any(hit, axis=2).reshape(device_count * row_count, slot_count)
+    selector = jnp.any(hit, axis=1)
     dispatched = jnp.einsum(
         "rq,rd->qd", selector.astype(jnp.bfloat16), normed, preferred_element_type=jnp.float32
     ).astype(jnp.bfloat16)

time: 198 us -> 149 us (0.75)
  blocking collectives: 109 us -> 43.9 us
  waiting for transfers between devices: 26.3 us -> 44.5 us
  other arithmetic: 10.5 us -> 5.85 us
    all_gather x1 -> x0, blocking collectives: 71.7 us -> none  [local(): routes = lax.all_gather(route[None], ALL_AXES, axis=0, tiled=True)]
    all_gather x1, waiting for transfers between devices: 0.02 us -> 16.6 us  [local(): packed = lax.all_gather(packed, 'ctx', axis=1, tiled=True)]
    reshape x4 -> x1, local copies, waits for them, and re-layouts: 12.1 us -> 2.84 us  [local(): tokens.reshape(dp_count, seq_count, ctx_count * group_count, per_block, m...]
    slice x1 -> x5, local copies, waits for them, and re-layouts: 0.01 us -> 7.24 us  [the longest x2 6.29 us: local(): gathered[:, :, :seq_count * total_len, :]]
    psum x1, blocking collectives: 23.6 us -> 28.7 us  [local(): summed = lax.psum(extended, 'expert').astype(jnp.bfloat16)]
    unnamed x8 -> x9, local copies, waits for them, and re-layouts: 1.86 us -> 3.89 us
  transfers between devices with their start and end apart: 2 -> 2, of which waited for: 1 -> 2; matrix products, arithmetic and copies ran while one was open for 1% -> 1% of each run, Pallas kernels for 0% -> 0%
where the time goes in v3:
time: 149 us
  waiting for transfers between devices  44.5 us (30%)
  blocking collectives  43.9 us (29%)
  local copies, waits for them, and re-layouts  21.3 us (14%)
  matrix products  19 us (13%)
  between operations  14.3 us (10%)
  other arithmetic  5.85 us (4%)
    psum x1, blocking collectives, local(): summed = lax.psum(extended, 'expert').astype(jnp.bfloat16)  28.7 us
    all_gather x1, waiting for transfers between devices, local(): gathered = lax.all_gather(summed[None], ('dp', 'ctx'), axis=0, tiled=True)  27.9 us
    all_gather x1, waiting for transfers between devices, local(): packed = lax.all_gather(packed, 'ctx', axis=1, tiled=True)  16.6 us
    all_gather x1, blocking collectives, local(): decay_all = lax.all_gather(decay_log, 'ctx', axis=1, tiled=True)  15.2 us
    dot_general x1, matrix products, expert_ffn(): jnp.einsum('gfd,qd->gfq', gate_up[0], slot_rows, preferred_element_type=j...  10.3 us
    slice x2, local copies, waits for them, and re-layouts, local(): gathered[:, :, :seq_count * total_len, :]  6.29 us
    dot_general x1, matrix products, mixer(): ssd = jnp.einsum('sktuh,skuhp->skthp', kernel, x_float, precision=highest)  4.8 us
    unnamed x9, local copies, waits for them, and re-layouts  3.89 us
  transfers between devices with their start and end apart: 2, of which 2 were waited for; matrix products, arithmetic and copies ran while one was open for 1% of the time, Pallas kernels for 0%

profile of v3, /device:TPU:0, one launch (start us, length us, event | category | flops | bytes accessed | tf_op | source)
XLA Modules:
  0.0 148.9 jit_solution(13019308692588653984)
XLA Ops:
  7.2 1.7 %pad_maximum_fusion.1 = bf16[2,16,4352]{2,1,0:T(8,128)(2,1)} fusion(bf16[2,16,128]{2,1,0:T(8,128)(2,1)} %param.14, bf16[2,16,128]{2,1,0:T(8,128)(2,1)} %param.13, bf16[2,16,2048]{2,1,0:T(8,128)(2,1)} %param.12, bf16[2,16,2048]{2,1,0:T(8,128)(2,1)} %param.11), kind=kLoop, calls=%fused_computation.38 | loop fusion | flops 1114112 | bytes 557056 | tf_op jit(solution)/shard_map/concatenate | solution.py:102
  9.0 0.7 add_convert_fusion
  10.1 15.2 %all_gather.10 = f32[2,64,32]{2,1,0:T(8,128)S(1)} all-gather(f32[2,16,32]{2,1,0:T(8,128)} %param.15), channel_id=1, replica_groups=mesh['dp'=2,'ctx'=4,'expert'=4] {'ctx'}, dimensions={1}, use_global_device_ids=true | all-gather | bytes 20480 | tf_op jit(solution)/shard_map/all_gather | solution.py:104
  25.3 16.6 %all-gather.5.cloned.1.call-done = bf16[2,64,4352]{2,1,0:T(8,128)(2,1)} async-done(((bf16[2,16,4352]{2,1,0:T(8,128)(2,1)}), bf16[2,64,4352]{2,1,0:T(8,128)(2,1)}) %all-gather.5.cloned.1.call-update) | async-done | bytes 1114128 | tf_op jit(solution)/shard_map/all_gather | solution.py:103
  41.9 0.9 fusion.36
  42.8 1.2 fusion.41
  44.2 1.3 copy.73
  45.5 0.6 copy.74
  46.2 4.8 %bitcast_add_fusion = f32[2,1,64,32,64]{2,4,3,0,1:T(8,128)} fusion(f32[2,1,64,32,64]{2,4,3,0,1:T(8,128)S(1)} %bitcast.55, bf16[2,64,32,64]{1,3,2,0:T(8,128)(2,1)} %bitcast.60, f32[32]{0:T(128)S(1)} %copy-done.2, f32[2,64,64]{2,1,0:T(8,128)S(1)} %fusion.36, f32[2,64,32]{1,2,0:T(8,128)S(1)} %copy.60, pred[64,64]{1,0:T(8,128)(4,1)S(1)} %iota_compare_fusion.1), kind=kOutput, calls=%fused_computation.8 | convolution fusion | flops 202899456 | bytes 2674816 | tf_op jit(solution)/shard_map/sktuh,skuhp->skthp/dot_general | solution.py:25
  51.0 2.3 %copy.75 = f32[2,64,2048]{2,1,0:T(8,128)S(1)} copy(f32[2,64,2048]{1,2,0:T(8,128)} %bitcast.56) | data formatting | bytes 2097152 | tf_op jit(solution)/shard_map/reshape | solution.py:45
  53.2 3.0 %fusion.3 = f32[2,64,1024]{2,1,0:T(8,128)S(1)} fusion(bf16[2048,1024]{1,0:T(8,128)(2,1)} %param.17, f32[2,64,2048]{2,1,0:T(8,128)S(1)} %copy.75, bf16[2,64,4352]{2,1,0:T(8,128)(2,1)S(1)} %copy-done), kind=kOutput, calls=%fused_computation.4 | convolution fusion | flops 538705920 | bytes 6291456 | tf_op jit(solution)/shard_map/stk,kd->std/dot_general | solution.py:113
  56.3 28.7 %all-reduce.1 = bf16[129,1024]{1,0:T(8,128)(2,1)} all-reduce(f32[129,1024]{1,0:T(8,128)S(1)} %pad_maximum_fusion), channel_id=1, replica_groups=mesh['dp'=2,'ctx'=4,'expert'=4] {'expert'}, use_global_device_ids=true, to_apply=%region_1.2 | all-reduce | flops 132096 | bytes 792576 | tf_op jit(solution)/shard_map/psum | solution.py:128
  85.4 27.9 %all-gather.7.cloned.1.call-done = bf16[8,129,1024]{2,1,0:T(8,128)(2,1)} async-done(((bf16[1,129,1024]{2,1,0:T(8,128)(2,1)}), bf16[8,129,1024]{2,1,0:T(8,128)(2,1)}) %all-gather.7.cloned.1.call-update) | async-done | bytes 2113552 | tf_op jit(solution)/shard_map/all_gather | solution.py:129
  113.2 0.9 slice.45
  114.2 3.1 %slice.44 = bf16[2,4,128,1024]{3,2,1,0:T(8,128)(2,1)} slice(bf16[2,4,129,1024]{3,2,1,0:T(8,128)(2,1)} %bitcast.58), slice={[0:2], [0:4], [0:128], [0:1024]} | slice | bytes 4194304 | tf_op jit(solution)/shard_map/slice | solution.py:135
  117.4 0.5 copy.69
  118.0 3.2 %copy.66 = bf16[2,4,128,1024]{3,1,2,0:T(4,128)(2,1)S(1)} copy(bf16[2,4,128,1024]{3,2,1,0:T(8,128)(2,1)} %slice.44) | data formatting | bytes 4194304 | tf_op jit(solution)/shard_map/slice | solution.py:135
  121.2 1.4 multiply_reduce_fusion
  122.6 2.8 %reshape.214 = bf16[2,2,16,4,4096]{4,3,2,1,0:T(4,128)(2,1)} reshape(bf16[2,2,64,4,1024]{4,3,2,1,0:T(4,128)(2,1)S(1)} %bitcast.52) | data formatting | bytes 4194304 | tf_op jit(solution)/shard_map/reshape | solution.py:139
  125.9 2.9 %copy.77 = f32[32,8,4,1024]{3,1,2,0:T(8,128)} copy(bf16[32,8,4,1024]{3,2,1,0:T(4,128)(2,1)S(1)} %bitcast.53) | data formatting | bytes 6291456
  129.0 10.3 %fusion.17 = f32[2,896,256]{1,2,0:T(8,128)S(1)} fusion(bf16[1,2,896,4096]{3,2,1,0:T(8,128)(2,1)} %param.19, pred[256,256]{1,0:T(8,128)(4,1)S(1)} %fusion.35, f32[256,4096]{1,0:T(8,128)} %bitcast.54, f32[4096]{0:T(1024)S(1)} %copy-done.1, f32[256]{0:T(256)S(1)} %rsqrt.12), kind=kOutput, calls=%fused_computation.17 | convolution fusion | flops 4299161600 | bytes 20792320 | tf_op jit(solution)/shard_map/gfd,qd->gfq/dot_general | solution.py:49
  139.3 0.3 fusion.30
  139.5 1.0 copy.72
  140.5 1.5 %dynamic-slice_bitcast_fusion = bf16[2,4,4096]{2,1,0:T(4,128)(2,1)} fusion(bf16[2,2,16,4,4096]{4,3,2,1,0:T(4,128)(2,1)} %reshape.214, s32[]{:T(128)S(6)} %select_n.32, s32[]{:T(128)S(6)} %select_n.34), kind=kLoop, calls=%fused_computation.41 | loop fusion | bytes 131080 | tf_op jit(solution)/shard_map/jit(dynamic_index_in_dim)/squeeze | solution.py:141
  (36 shorter events, 1.8 us)
Async XLA Ops:
  7.2 34.8 %all-gather.5.cloned.1.call-start = ((), (), s32[]{:S(2)}) async-start(), calls=%async_computation | async-start | bytes 1392640 | tf_op jit(solution)/shard_map/all_gather | solution.py:103
  9.0 104.3 %all-gather.7.cloned.1.call-start = ((), (), s32[]{:S(2)}) async-start(), calls=%async_computation.1 | async-start | bytes 2506752 | tf_op jit(solution)/shard_map/all_gather | solution.py:129
  44.2 1.9 %copy-start.2 = (f32[32]{0:T(128)S(1)}, f32[32]{0:T(128)}, u32[]{:S(2)}) copy-start(f32[32]{0:T(128)} %param.16) | copy-start | bytes 388
  51.0 2.3 %copy-start = (bf16[2,64,4352]{2,1,0:T(8,128)(2,1)S(1)}, bf16[2,64,4352]{2,1,0:T(8,128)(2,1)}, u32[]{:S(2)}) copy-start(bf16[2,64,4352]{2,1,0:T(8,128)(2,1)} %all-gather.5.cloned.1.call-done) | copy-start | bytes 3342340
  125.8 3.1 %copy-start.1 = (f32[4096]{0:T(1024)S(1)}, f32[4096]{0:T(1024)}, u32[]{:S(2)}) copy-start(f32[4096]{0:T(1024)} %param.18) | copy-start | bytes 49156
Sparse Core Ops, SparseCore 0:
  10.1 31.7 all-gather.4
  85.1 28.0 all-gather.6

commit v4 on v3

--- a/solution.py
+++ b/solution.py
@@ -125,29 +125,26 @@
         [partial_value.reshape(seq_count * total_len, col_width), route_row.reshape(extra_rows, col_width)],
         axis=0,
     )
-    summed = lax.psum(extended, "expert").astype(jnp.bfloat16)
+    summed = lax.psum(extended.astype(jnp.bfloat16), "expert")
     gathered = lax.all_gather(summed[None], ("dp", "ctx"), axis=0, tiled=True)
     gathered = gathered.reshape(dp_count, ctx_count, seq_count * total_len + extra_rows, col_width)
     routes = gathered[:, :, seq_count * total_len :, :].reshape(dp_count, ctx_count, -1)
     routes = routes[:, :, : group_count * route_len].astype(jnp.int32)
     routes = routes.reshape(dp_count, ctx_count, group_count, seq_count, per_block, pick_count, 2)
     routes = jnp.transpose(routes, (0, 3, 1, 2, 4, 5, 6))
-    tokens = gathered[:, :, : seq_count * total_len, :].reshape(
-        dp_count, ctx_count, seq_count, total_len, col_width
-    )
-    tokens = jnp.transpose(tokens, (0, 2, 3, 1, 4))
-    tok_blocks = tokens.reshape(dp_count, seq_count, ctx_count * group_count, per_block, model_width)
+    row_total = seq_count * total_len
+    tokens = gathered[:, :, :row_total, :]
+    mine_rows = lax.dynamic_index_in_dim(tokens, lax.axis_index("dp"), axis=0, keepdims=False)
+    mine_rows = mine_rows.reshape(ctx_count, seq_count, ctx_count * group_count, per_block, col_width)
     mine_block = lax.axis_index("ctx") * group_count + lax.axis_index("expert")
-    mamba_out = lax.dynamic_index_in_dim(
-        lax.dynamic_index_in_dim(tok_blocks, lax.axis_index("dp"), axis=0, keepdims=False),
-        mine_block,
-        axis=1,
-        keepdims=False,
-    )
-    token_count = dp_count * seq_count * total_len
-    flat = tokens.reshape(token_count, model_width).astype(jnp.float32)
-    scale = lax.rsqrt(jnp.mean(flat * flat, axis=1, keepdims=True) + 1e-05)
-    normed = (flat * scale * moe_gain[None, :]).astype(jnp.bfloat16)
+    mine_rows = lax.dynamic_index_in_dim(mine_rows, mine_block, axis=2, keepdims=False)
+    mamba_out = jnp.transpose(mine_rows, (1, 2, 0, 3)).reshape(seq_count, per_block, model_width)
+    token_count = dp_count * row_total
+    flat = tokens.astype(jnp.float32)
+    square_sum = jnp.sum(flat * flat, axis=(1, 3), keepdims=True)
+    scale = lax.rsqrt(square_sum / model_width + 1e-05)
+    gain = moe_gain.reshape(1, ctx_count, 1, col_width)
+    normed = (flat * scale * gain).astype(jnp.bfloat16)
 
     group = (
         (jnp.arange(dp_count)[:, None, None, None, None] * ctx_count
@@ -159,11 +156,11 @@
     mine = routes[..., 0].reshape(token_count, pick_count) == lax.axis_index("expert")
     slot_count = device_count * capacity
     hit = mine[..., None] & (target[..., None] == jnp.arange(slot_count))
-    selector = jnp.any(hit, axis=1)
+    selector = jnp.any(hit, axis=1).reshape(dp_count, row_total, slot_count)
     dispatched = jnp.einsum(
-        "rq,rd->qd", selector.astype(jnp.bfloat16), normed, preferred_element_type=jnp.float32
+        "drq,dcrk->qck", selector.astype(jnp.bfloat16), normed, preferred_element_type=jnp.float32
     ).astype(jnp.bfloat16)
-    hidden = expert_ffn(gate_up, dispatched)
+    hidden = expert_ffn(gate_up, dispatched.reshape(slot_count, model_width))
     return (mamba_out, hidden[None])
 
 

time: 149 us -> 161 us (1.081)
  waiting for transfers between devices: 44.5 us -> 91.2 us
  blocking collectives: 43.9 us -> 15.2 us
  local copies, waits for them, and re-layouts: 21.3 us -> 14.6 us
  other arithmetic: 5.85 us -> 8.01 us
    psum x0 -> x1, waiting for transfers between devices: none -> 42.9 us  [local(): summed = lax.psum(extended.astype(jnp.bfloat16), 'expert')]
    psum x1 -> x0, blocking collectives: 28.7 us -> none  [local(): summed = lax.psum(extended, 'expert').astype(jnp.bfloat16)]
    slice x2 -> x1, local copies, waits for them, and re-layouts: 6.29 us -> 1.56 us  [local(): tokens = gathered[:, :, :row_total, :]]
    all_gather x1, waiting for transfers between devices: 27.9 us -> 31.6 us  [local(): gathered = lax.all_gather(summed[None], ('dp', 'ctx'), axis=0, tiled=True)]
    convert_element_type x0 -> x1, local copies, waits for them, and re-layouts: none -> 2.85 us  [local(): dispatched = jnp.einsum('drq,dcrk->qck', selector.astype(jnp.bfloat16), n...]
    dot_general x1, matrix products: 10.3 us -> 7.89 us  [expert_ffn(): jnp.einsum('gfd,qd->gfq', gate_up[0], slot_rows, preferred_element_type=j...]
    unnamed x9 -> x12, local copies, waits for them, and re-layouts: 3.89 us -> 1.5 us
    dot_general x0 -> x1, matrix products: none -> 2.18 us  [local(): jnp.einsum('drq,dcrk->qck', selector.astype(jnp.bfloat16), normed, prefer...]
  transfers between devices with their start and end apart: 2 -> 3, of which waited for: 2 -> 3; matrix products, arithmetic and copies ran while one was open for 1% -> 1% of each run, Pallas kernels for 0% -> 0%
where the time goes in v4:
time: 161 us; the launch traced here: 160 us
  waiting for transfers between devices  91.2 us (57%)
  matrix products  17.4 us (11%)
  blocking collectives  15.2 us (9%)
  local copies, waits for them, and re-layouts  14.6 us (9%)
  between operations  14 us (9%)
  other arithmetic  8.01 us (5%)
    psum x1, waiting for transfers between devices, local(): summed = lax.psum(extended.astype(jnp.bfloat16), 'expert')  42.9 us
    all_gather x1, waiting for transfers between devices, local(): gathered = lax.all_gather(summed[None], ('dp', 'ctx'), axis=0, tiled=True)  31.6 us
    all_gather x1, waiting for transfers between devices, local(): packed = lax.all_gather(packed, 'ctx', axis=1, tiled=True)  16.6 us
    all_gather x1, blocking collectives, local(): decay_all = lax.all_gather(decay_log, 'ctx', axis=1, tiled=True)  15.2 us
    dot_general x1, matrix products, expert_ffn(): jnp.einsum('gfd,qd->gfq', gate_up[0], slot_rows, preferred_element_type=j...  7.89 us
    dot_general x1, matrix products, mixer(): ssd = jnp.einsum('sktuh,skuhp->skthp', kernel, x_float, precision=highest)  3.42 us
  transfers between devices with their start and end apart: 3, of which 3 were waited for; matrix products, arithmetic and copies ran while one was open for 1% of the time, Pallas kernels for 0%

profile of v4, /device:TPU:0, one launch (start us, length us, event | category | flops | bytes accessed | tf_op | source)
XLA Modules:
  0.0 160.4 jit_solution(13772776508938057340)
XLA Ops:
  7.2 1.7 %pad_maximum_fusion = bf16[2,16,4352]{2,1,0:T(8,128)(2,1)} fusion(bf16[2,16,128]{2,1,0:T(8,128)(2,1)} %param.14, bf16[2,16,128]{2,1,0:T(8,128)(2,1)} %param.13, bf16[2,16,2048]{2,1,0:T(8,128)(2,1)} %param.12, bf16[2,16,2048]{2,1,0:T(8,128)(2,1)} %param.11), kind=kLoop, calls=%fused_computation.40 | loop fusion | flops 1114112 | bytes 557056 | tf_op jit(solution)/shard_map/concatenate | solution.py:102
  9.0 0.7 add_convert_fusion
  10.1 15.2 %all_gather.10 = f32[2,64,32]{2,1,0:T(8,128)S(1)} all-gather(f32[2,16,32]{2,1,0:T(8,128)} %param.15), channel_id=1, replica_groups=mesh['dp'=2,'ctx'=4,'expert'=4] {'ctx'}, dimensions={1}, use_global_device_ids=true | all-gather | bytes 20480 | tf_op jit(solution)/shard_map/all_gather | solution.py:104
  25.3 16.6 %all-gather.3.cloned.1.call-done = bf16[2,64,4352]{2,1,0:T(8,128)(2,1)} async-done(((bf16[2,16,4352]{2,1,0:T(8,128)(2,1)}), bf16[2,64,4352]{2,1,0:T(8,128)(2,1)}) %all-gather.3.cloned.1.call-update) | async-done | bytes 1114128 | tf_op jit(solution)/shard_map/all_gather | solution.py:103
  41.9 2.0 %fusion.46 = (bf16[2,64,2048]{2,1,0:T(8,128)(2,1)}, f32[2,64,2048]{2,1,0:T(8,128)S(1)}) fusion(bf16[2,64,4352]{2,1,0:T(8,128)(2,1)} %all-gather.3.cloned.1.call-done), kind=kLoop, calls=%fused_computation.61 | loop fusion | flops 262144 | bytes 2097152 | tf_op jit(solution)/shard_map/slice | solution.py:107
  43.9 0.9 fusion.40
  44.8 0.6 copy.89
  45.4 1.5 copy.88
  47.1 3.4 %bitcast_add_fusion = f32[2,1,64,32,64]{2,4,3,0,1:T(8,128)} fusion(f32[2,1,64,32,64]{2,4,3,0,1:T(8,128)S(1)} %bitcast.59, bf16[2,64,32,64]{1,3,2,0:T(8,128)(2,1)S(1)} %bitcast.63, f32[32]{0:T(128)S(1)} %copy-done.4, f32[2,64,64]{2,1,0:T(8,128)S(1)} %fusion.40, f32[2,64,32]{1,2,0:T(8,128)S(1)} %copy.69, pred[64,64]{1,0:T(8,128)(4,1)S(1)} %iota_compare_fusion.1), kind=kOutput, calls=%fused_computation.10 | convolution fusion | flops 202899456 | bytes 2674816 | tf_op jit(solution)/shard_map/sktuh,skuhp->skthp/dot_general | solution.py:25
  50.5 2.3 %copy.90 = f32[2,64,2048]{2,1,0:T(8,128)S(1)} copy(f32[2,64,2048]{1,2,0:T(8,128)} %bitcast.60) | data formatting | bytes 2097152 | tf_op jit(solution)/shard_map/reshape | solution.py:45
  52.8 3.0 %fusion.21 = bf16[2,64,1024]{2,1,0:T(8,128)(2,1)S(1)} fusion(bf16[2048,1024]{1,0:T(8,128)(2,1)} %param.17, f32[2,64,2048]{2,1,0:T(8,128)S(1)} %copy.90, bf16[2,64,4352]{2,1,0:T(8,128)(2,1)S(1)} %copy-done.2), kind=kOutput, calls=%fused_computation.22 | convolution fusion | flops 538836992 | bytes 6029312 | tf_op jit(solution)/shard_map/stk,kd->std/dot_general | solution.py:113
  55.9 0.7 maximum_bitcast_fusion
  56.7 42.9 %all-reduce.2.cloned.1.call-done = bf16[1,129,1024]{2,1,0:T(8,128)(2,1)} async-done(((bf16[1,129,1024]{2,1,0:T(8,128)(2,1)}), bf16[1,129,1024]{2,1,0:T(8,128)(2,1)}) %all-reduce.2.cloned.1.call-update) | async-done | bytes 264208 | tf_op jit(solution)/shard_map/psum | solution.py:128
  100.0 31.6 %all-gather.5.cloned.1.call-done = bf16[8,129,1024]{2,1,0:T(8,128)(2,1)} async-done(((bf16[1,129,1024]{2,1,0:T(8,128)(2,1)}), bf16[8,129,1024]{2,1,0:T(8,128)(2,1)}) %all-gather.5.cloned.1.call-update) | async-done | bytes 2113552 | tf_op jit(solution)/shard_map/all_gather | solution.py:129
  131.6 1.1 slice.45
  132.8 0.5 copy.77
  133.4 2.1 %fusion.2 = f32[2,128]{1,0:T(2,128)S(1)} fusion(bf16[2,4,129,1024]{3,2,1,0:T(8,128)(2,1)} %bitcast.56), kind=kLoop, calls=%fused_computation.4 | loop fusion | flops 3145472 | bytes 2098176 | tf_op jit(solution)/shard_map/reduce_sum | solution.py:144
  135.5 1.6 slice.44
  137.6 2.2 %bitcast_convert_fusion = bf16[256,4,1024]{2,0,1:T(8,128)(2,1)} fusion(pred[2,128,256,1]{2,1,3,0:T(8,128)(4,1)S(1)} %bitcast.68, f32[4,1024]{1,0:T(4,128)S(1)} %mul.117, f32[2,128]{1,0:T(2,128)S(1)} %add_rsqrt_fusion, bf16[2,4,129,1024]{3,2,1,0:T(8,128)(2,1)S(1)} %bitcast.58), kind=kOutput, calls=%fused_computation.7 | convolution fusion | flops 542113792 | bytes 4277248 | tf_op jit(solution)/shard_map/drq,dcrk->qck/dot_general | solution.py:160
  139.8 2.8 %copy.82 = bf16[256,4,1024]{0,2,1:T(8,128)(2,1)S(1)} copy(bf16[256,4,1024]{2,0,1:T(8,128)(2,1)} %bitcast_convert_fusion) | data formatting | bytes 4194304 | tf_op jit(solution)/shard_map/convert_element_type | solution.py:162
  142.6 7.9 %fusion.18 = f32[2,896,256]{1,2,0:T(8,128)S(1)} fusion(bf16[256,4096,1]{0,1,2:T(8,128)(2,1)S(1)} %bitcast.61, bf16[1,2,896,4096]{3,2,1,0:T(8,128)(2,1)} %param.19), kind=kOutput, calls=%fused_computation.19 | convolution fusion | flops 3758096384 | bytes 18612224 | tf_op jit(solution)/shard_map/gfd,qd->gfq/dot_general | solution.py:49
  150.8 1.0 copy.84
  152.3 0.8 copy.75
  153.2 0.7 reshape.209
  (44 shorter events, 2.6 us)
Async XLA Ops:
  7.2 34.8 %all-gather.3.cloned.1.call-start = ((), (), s32[]{:S(2)}) async-start(), calls=%async_computation | async-start | bytes 1392640 | tf_op jit(solution)/shard_map/all_gather | solution.py:103
  9.0 90.6 %all-reduce.2.cloned.1.call-start = ((), (), s32[]{:S(2)}) async-start(), calls=%async_computation.1 | async-start | bytes 557056 | tf_op jit(solution)/shard_map/psum | solution.py:128
  44.8 2.3 %copy-start.4 = (f32[32]{0:T(128)S(1)}, f32[32]{0:T(128)}, u32[]{:S(2)}) copy-start(f32[32]{0:T(128)} %param.16) | copy-start | bytes 388
  50.5 2.3 %copy-start.2 = (bf16[2,64,4352]{2,1,0:T(8,128)(2,1)S(1)}, bf16[2,64,4352]{2,1,0:T(8,128)(2,1)}, u32[]{:S(2)}) copy-start(bf16[2,64,4352]{2,1,0:T(8,128)(2,1)} %all-gather.3.cloned.1.call-done) | copy-start | bytes 3342340
  52.8 47.1 %copy-start.3 = (f32[4096]{0:T(1024)S(1)}, f32[4096]{0:T(1024)}, u32[]{:S(2)}) copy-start(f32[4096]{0:T(1024)} %param.18) | copy-start | bytes 49156
  56.6 75.0 %all-gather.5.cloned.1.call-start = ((), (), s32[]{:S(2)}) async-start(), calls=%async_computation.2 | async-start | bytes 2506752 | tf_op jit(solution)/shard_map/all_gather | solution.py:129
  131.6 3.9 %copy-start = (bf16[8,129,1024]{2,1,0:T(8,128)(2,1)S(1)}, bf16[8,129,1024]{2,1,0:T(8,128)(2,1)}, u32[]{:S(2)}) copy-start(bf16[8,129,1024]{2,1,0:T(8,128)(2,1)} %all-gather.5.cloned.1.call-done) | copy-start | bytes 6340612
  150.5 1.8 %copy-start.1 = (bf16[2,4,128,1024]{3,2,1,0:T(8,128)(2,1)S(1)}, bf16[2,4,128,1024]{3,2,1,0:T(8,128)(2,1)}, u32[]{:S(2)}) copy-start(bf16[2,4,128,1024]{3,2,1,0:T(8,128)(2,1)} %slice.44) | copy-start | bytes 6291460
Sparse Core Ops, SparseCore 0:
  10.1 31.7 all-gather.2
  56.7 42.8 all-reduce.1
  101.2 30.3 all-gather.4

commit v5 on v4

--- a/solution.py
+++ b/solution.py
@@ -125,7 +125,7 @@
         [partial_value.reshape(seq_count * total_len, col_width), route_row.reshape(extra_rows, col_width)],
         axis=0,
     )
-    summed = lax.psum(extended.astype(jnp.bfloat16), "expert")
+    summed = lax.psum(extended, "expert").astype(jnp.bfloat16)
     gathered = lax.all_gather(summed[None], ("dp", "ctx"), axis=0, tiled=True)
     gathered = gathered.reshape(dp_count, ctx_count, seq_count * total_len + extra_rows, col_width)
     routes = gathered[:, :, seq_count * total_len :, :].reshape(dp_count, ctx_count, -1)

time: 161 us -> 142 us (0.88)
  waiting for transfers between devices: 91.2 us -> 44.5 us
  blocking collectives: 15.2 us -> 43.7 us
    psum x1 -> x0, waiting for transfers between devices: 42.9 us -> none  [local(): summed = lax.psum(extended.astype(jnp.bfloat16), 'expert')]
    psum x0 -> x1, blocking collectives: none -> 28.5 us  [local(): summed = lax.psum(extended, 'expert').astype(jnp.bfloat16)]
    all_gather x1, waiting for transfers between devices: 31.6 us -> 27.9 us  [local(): gathered = lax.all_gather(summed[None], ('dp', 'ctx'), axis=0, tiled=True)]
  transfers between devices with their start and end apart: 3 -> 2, of which waited for: 3 -> 2; matrix products, arithmetic and copies ran while one was open for 1% -> 1% of each run, Pallas kernels for 0% -> 0%
where the time goes in v5:
time: 142 us
  waiting for transfers between devices  44.5 us (31%)
  blocking collectives  43.7 us (31%)
  matrix products  17.4 us (12%)
  local copies, waits for them, and re-layouts  14.6 us (10%)
  between operations  14.3 us (10%)
  other arithmetic  7.31 us (5%)
    psum x1, blocking collectives, local(): summed = lax.psum(extended, 'expert').astype(jnp.bfloat16)  28.5 us
    all_gather x1, waiting for transfers between devices, local(): gathered = lax.all_gather(summed[None], ('dp', 'ctx'), axis=0, tiled=True)  27.9 us
    all_gather x1, waiting for transfers between devices, local(): packed = lax.all_gather(packed, 'ctx', axis=1, tiled=True)  16.6 us
    all_gather x1, blocking collectives, local(): decay_all = lax.all_gather(decay_log, 'ctx', axis=1, tiled=True)  15.2 us
    dot_general x1, matrix products, expert_ffn(): jnp.einsum('gfd,qd->gfq', gate_up[0], slot_rows, preferred_element_type=j...  7.89 us
    dot_general x1, matrix products, mixer(): ssd = jnp.einsum('sktuh,skuhp->skthp', kernel, x_float, precision=highest)  3.45 us
    dot_general x1, matrix products, local(): jnp.einsum('stk,kd->std', gated, out_weight, preferred_element_type=jnp.f...  2.99 us
    convert_element_type x1, local copies, waits for them, and re-layouts, local(): dispatched = jnp.einsum('drq,dcrk->qck', selector.astype(jnp.bfloat16), n...  2.85 us
  transfers between devices with their start and end apart: 2, of which 2 were waited for; matrix products, arithmetic and copies ran while one was open for 1% of the time, Pallas kernels for 0%

profile of v5, /device:TPU:0, one launch (start us, length us, event | category | flops | bytes accessed | tf_op | source)
XLA Modules:
  0.0 141.9 jit_solution(8669466119416332907)
XLA Ops:
  7.2 1.7 %pad_maximum_fusion.1 = bf16[2,16,4352]{2,1,0:T(8,128)(2,1)} fusion(bf16[2,16,128]{2,1,0:T(8,128)(2,1)} %param.14, bf16[2,16,128]{2,1,0:T(8,128)(2,1)} %param.13, bf16[2,16,2048]{2,1,0:T(8,128)(2,1)} %param.12, bf16[2,16,2048]{2,1,0:T(8,128)(2,1)} %param.11), kind=kLoop, calls=%fused_computation.40 | loop fusion | flops 1114112 | bytes 557056 | tf_op jit(solution)/shard_map/concatenate | solution.py:102
  9.0 0.7 add_convert_fusion
  10.1 15.2 %all_gather.10 = f32[2,64,32]{2,1,0:T(8,128)S(1)} all-gather(f32[2,16,32]{2,1,0:T(8,128)} %param.15), channel_id=1, replica_groups=mesh['dp'=2,'ctx'=4,'expert'=4] {'ctx'}, dimensions={1}, use_global_device_ids=true | all-gather | bytes 20480 | tf_op jit(solution)/shard_map/all_gather | solution.py:104
  25.3 16.6 %all-gather.5.cloned.1.call-done = bf16[2,64,4352]{2,1,0:T(8,128)(2,1)} async-done(((bf16[2,16,4352]{2,1,0:T(8,128)(2,1)}), bf16[2,64,4352]{2,1,0:T(8,128)(2,1)}) %all-gather.5.cloned.1.call-update) | async-done | bytes 1114128 | tf_op jit(solution)/shard_map/all_gather | solution.py:103
  41.9 2.0 %fusion.43 = (bf16[2,64,2048]{2,1,0:T(8,128)(2,1)}, f32[2,64,2048]{2,1,0:T(8,128)S(1)}) fusion(bf16[2,64,4352]{2,1,0:T(8,128)(2,1)} %all-gather.5.cloned.1.call-done), kind=kLoop, calls=%fused_computation.61 | loop fusion | flops 262144 | bytes 2097152 | tf_op jit(solution)/shard_map/slice | solution.py:107
  43.9 0.9 fusion.37
  44.8 0.6 copy.89
  45.4 1.5 %copy.88 = bf16[2,64,2048]{1,2,0:T(8,128)(2,1)S(1)} copy(bf16[2,64,2048]{2,1,0:T(8,128)(2,1)} %get-tuple-element.16) | data formatting | bytes 1048576 | tf_op jit(solution)/shard_map/reshape.9
  47.1 3.4 %bitcast_add_fusion = f32[2,1,64,32,64]{2,4,3,0,1:T(8,128)} fusion(f32[2,1,64,32,64]{2,4,3,0,1:T(8,128)S(1)} %bitcast.58, bf16[2,64,32,64]{1,3,2,0:T(8,128)(2,1)S(1)} %bitcast.63, f32[32]{0:T(128)S(1)} %copy-done.4, f32[2,64,64]{2,1,0:T(8,128)S(1)} %fusion.37, f32[2,64,32]{1,2,0:T(8,128)S(1)} %copy.69, pred[64,64]{1,0:T(8,128)(4,1)S(1)} %iota_compare_fusion.1), kind=kOutput, calls=%fused_computation.10 | convolution fusion | flops 202899456 | bytes 2674816 | tf_op jit(solution)/shard_map/sktuh,skuhp->skthp/dot_general | solution.py:25
  50.6 2.3 %copy.90 = f32[2,64,2048]{2,1,0:T(8,128)S(1)} copy(f32[2,64,2048]{1,2,0:T(8,128)} %bitcast.59) | data formatting | bytes 2097152 | tf_op jit(solution)/shard_map/reshape | solution.py:45
  52.9 3.0 %fusion.5 = f32[2,64,1024]{2,1,0:T(8,128)S(1)} fusion(bf16[2048,1024]{1,0:T(8,128)(2,1)} %param.17, f32[2,64,2048]{2,1,0:T(8,128)S(1)} %copy.90, bf16[2,64,4352]{2,1,0:T(8,128)(2,1)S(1)} %copy-done.2), kind=kOutput, calls=%fused_computation.8 | convolution fusion | flops 538705920 | bytes 6291456 | tf_op jit(solution)/shard_map/stk,kd->std/dot_general | solution.py:113
  55.9 28.5 %all-reduce.1 = bf16[129,1024]{1,0:T(8,128)(2,1)} all-reduce(f32[129,1024]{1,0:T(8,128)S(1)} %pad_maximum_fusion), channel_id=1, replica_groups=mesh['dp'=2,'ctx'=4,'expert'=4] {'expert'}, use_global_device_ids=true, to_apply=%region_1.2 | all-reduce | flops 132096 | bytes 792576 | tf_op jit(solution)/shard_map/psum | solution.py:128
  84.8 27.9 %all-gather.7.cloned.1.call-done = bf16[8,129,1024]{2,1,0:T(8,128)(2,1)} async-done(((bf16[1,129,1024]{2,1,0:T(8,128)(2,1)}), bf16[8,129,1024]{2,1,0:T(8,128)(2,1)}) %all-gather.7.cloned.1.call-update) | async-done | bytes 2113552 | tf_op jit(solution)/shard_map/all_gather | solution.py:129
  112.7 1.1 slice.45
  113.9 0.5 copy.77
  114.5 2.1 %fusion.2 = f32[2,128]{1,0:T(2,128)S(1)} fusion(bf16[2,4,129,1024]{3,2,1,0:T(8,128)(2,1)} %bitcast.55), kind=kLoop, calls=%fused_computation.4 | loop fusion | flops 3145472 | bytes 2098176 | tf_op jit(solution)/shard_map/reduce_sum | solution.py:144
  116.6 1.6 %slice.44 = bf16[2,4,128,1024]{3,2,1,0:T(8,128)(2,1)} slice(bf16[2,4,129,1024]{3,2,1,0:T(8,128)(2,1)S(1)} %bitcast.56), slice={[0:2], [0:4], [0:128], [0:1024]} | slice | bytes 4194304 | tf_op jit(solution)/shard_map/slice | solution.py:136
  118.7 2.2 %bitcast_convert_fusion = bf16[256,4,1024]{2,0,1:T(8,128)(2,1)} fusion(pred[2,128,256,1]{2,1,3,0:T(8,128)(4,1)S(1)} %bitcast.68, f32[4,1024]{1,0:T(4,128)S(1)} %mul.117, f32[2,128]{1,0:T(2,128)S(1)} %add_rsqrt_fusion, bf16[2,4,129,1024]{3,2,1,0:T(8,128)(2,1)S(1)} %bitcast.57), kind=kOutput, calls=%fused_computation.7 | convolution fusion | flops 542113792 | bytes 4277248 | tf_op jit(solution)/shard_map/drq,dcrk->qck/dot_general | solution.py:160
  120.9 2.8 %copy.82 = bf16[256,4,1024]{0,2,1:T(8,128)(2,1)S(1)} copy(bf16[256,4,1024]{2,0,1:T(8,128)(2,1)} %bitcast_convert_fusion) | data formatting | bytes 4194304 | tf_op jit(solution)/shard_map/convert_element_type | solution.py:162
  123.7 7.9 %fusion.18 = f32[2,896,256]{1,2,0:T(8,128)S(1)} fusion(bf16[256,4096,1]{0,1,2:T(8,128)(2,1)S(1)} %bitcast.60, bf16[1,2,896,4096]{3,2,1,0:T(8,128)(2,1)} %param.19), kind=kOutput, calls=%fused_computation.19 | convolution fusion | flops 3758096384 | bytes 18612224 | tf_op jit(solution)/shard_map/gfd,qd->gfq/dot_general | solution.py:49
  131.9 1.0 copy.84
  132.9 0.5 copy-done.1
  133.5 0.8 copy.75
  134.3 0.7 reshape.208
  (42 shorter events, 2.1 us)
Async XLA Ops:
  7.2 34.8 %all-gather.5.cloned.1.call-start = ((), (), s32[]{:S(2)}) async-start(), calls=%async_computation | async-start | bytes 1392640 | tf_op jit(solution)/shard_map/all_gather | solution.py:103
  9.0 103.7 %all-gather.7.cloned.1.call-start = ((), (), s32[]{:S(2)}) async-start(), calls=%async_computation.1 | async-start | bytes 2506752 | tf_op jit(solution)/shard_map/all_gather | solution.py:129
  44.8 2.3 %copy-start.4 = (f32[32]{0:T(128)S(1)}, f32[32]{0:T(128)}, u32[]{:S(2)}) copy-start(f32[32]{0:T(128)} %param.16) | copy-start | bytes 388
  50.6 2.3 %copy-start.2 = (bf16[2,64,4352]{2,1,0:T(8,128)(2,1)S(1)}, bf16[2,64,4352]{2,1,0:T(8,128)(2,1)}, u32[]{:S(2)}) copy-start(bf16[2,64,4352]{2,1,0:T(8,128)(2,1)} %all-gather.5.cloned.1.call-done) | copy-start | bytes 3342340
  55.9 28.9 %copy-start.3 = (f32[4096]{0:T(1024)S(1)}, f32[4096]{0:T(1024)}, u32[]{:S(2)}) copy-start(f32[4096]{0:T(1024)} %param.18) | copy-start | bytes 49156
  112.7 3.9 %copy-start = (bf16[8,129,1024]{2,1,0:T(8,128)(2,1)S(1)}, bf16[8,129,1024]{2,1,0:T(8,128)(2,1)}, u32[]{:S(2)}) copy-start(bf16[8,129,1024]{2,1,0:T(8,128)(2,1)} %all-gather.7.cloned.1.call-done) | copy-start | bytes 6340612
  131.6 1.8 %copy-start.1 = (bf16[2,4,128,1024]{3,2,1,0:T(8,128)(2,1)S(1)}, bf16[2,4,128,1024]{3,2,1,0:T(8,128)(2,1)}, u32[]{:S(2)}) copy-start(bf16[2,4,128,1024]{3,2,1,0:T(8,128)(2,1)} %slice.44) | copy-start | bytes 6291460
Sparse Core Ops, SparseCore 0:
  10.1 31.7 all-gather.4
  84.6 28.0 all-gather.6

commit v6 on v5

--- a/solution.py
+++ b/solution.py
@@ -5,6 +5,44 @@
 
 P_SIZE = 64
 ALL_AXES = ("dp", "ctx", "expert")
+
+
+def gather_blocks(value, axis_name, count):
+    me = lax.axis_index(axis_name)
+    received = [value]
+    for shift in range(1, count):
+        perm = [(i, (i + shift) % count) for i in range(count)]
+        received.append(lax.ppermute(value, axis_name, perm))
+    order = (me - jnp.arange(count)) % count
+    return jnp.take(jnp.stack(received), order, axis=0)
+
+
+def sum_over(value, axis_name, count):
+    if count & (count - 1) or value.shape[-1] % count:
+        return lax.psum(value, axis_name).astype(jnp.bfloat16)
+    me = lax.axis_index(axis_name)
+    masks = []
+    mask = 1
+    while mask < count:
+        masks.append(mask)
+        mask *= 2
+    data = value
+    for mask in masks:
+        bit = (me // mask) % 2
+        halves = data.reshape(data.shape[:-1] + (2, data.shape[-1] // 2))
+        keep = lax.dynamic_index_in_dim(halves, bit, axis=-2, keepdims=False)
+        send = lax.dynamic_index_in_dim(halves, 1 - bit, axis=-2, keepdims=False)
+        perm = [(i, i ^ mask) for i in range(count)]
+        data = keep + lax.ppermute(send, axis_name, perm)
+    data = data.astype(jnp.bfloat16)
+    for mask in reversed(masks):
+        bit = (me // mask) % 2
+        perm = [(i, i ^ mask) for i in range(count)]
+        other = lax.ppermute(data, axis_name, perm)
+        low = jnp.where(bit == 0, data, other)
+        high = jnp.where(bit == 0, other, data)
+        data = jnp.concatenate([low, high], axis=-1)
+    return data
 
 
 def mixer(x_in, b_in, c_in, decay_log, skip):
@@ -100,8 +138,12 @@
     capacity = max(2, 4 * row_count // group_count)
 
     packed = jnp.concatenate([x_in, z_in, b_in, c_in], axis=2)
-    packed = lax.all_gather(packed, "ctx", axis=1, tiled=True)
-    decay_all = lax.all_gather(decay_log, "ctx", axis=1, tiled=True)
+    packed = jnp.moveaxis(gather_blocks(packed, "ctx", ctx_count), 0, 1).reshape(
+        seq_count, ctx_count * block_len, packed.shape[2]
+    )
+    decay_all = jnp.moveaxis(gather_blocks(decay_log, "ctx", ctx_count), 0, 1).reshape(
+        seq_count, ctx_count * block_len, decay_log.shape[2]
+    )
     packed, decay_all = lax.optimization_barrier((packed, decay_all))
 
     x_all = packed[:, :, :width_in]
@@ -125,8 +167,8 @@
         [partial_value.reshape(seq_count * total_len, col_width), route_row.reshape(extra_rows, col_width)],
         axis=0,
     )
-    summed = lax.psum(extended, "expert").astype(jnp.bfloat16)
-    gathered = lax.all_gather(summed[None], ("dp", "ctx"), axis=0, tiled=True)
+    summed = sum_over(extended, "expert", group_count)
+    gathered = gather_blocks(gather_blocks(summed, "ctx", ctx_count), "dp", dp_count)
     gathered = gathered.reshape(dp_count, ctx_count, seq_count * total_len + extra_rows, col_width)
     routes = gathered[:, :, seq_count * total_len :, :].reshape(dp_count, ctx_count, -1)
     routes = routes[:, :, : group_count * route_len].astype(jnp.int32)

time: 142 us -> 133 us (0.937)
  blocking collectives: 43.7 us -> 0 us
  starting transfers between devices: 0.08 us -> 33.8 us
  between operations: 14.3 us -> 1.1 us
  local copies, waits for them, and re-layouts: 14.6 us -> 26.5 us
  other arithmetic: 7.31 us -> 10.1 us
    all_gather x2 -> x0, waiting for transfers between devices: 44.5 us -> none  [the longest x1 27.9 us: local(): gathered = lax.all_gather(summed[None], ('dp', 'ctx'), axis=0, tiled=True)]
    ppermute x0 -> x14, waiting for transfers between devices: none -> 43.1 us  [the longest x10 27.9 us: gather_blocks(): received.append(lax.ppermute(value, axis_name, perm))]
    ppermute x0 -> x14, starting transfers between devices: none -> 33.8 us  [the longest x10 27.5 us: gather_blocks(): received.append(lax.ppermute(value, axis_name, perm))]
    psum x1 -> x0, blocking collectives: 28.5 us -> none  [local(): summed = lax.psum(extended, 'expert').astype(jnp.bfloat16)]
    all_gather x1 -> x0, blocking collectives: 15.2 us -> none  [local(): decay_all = lax.all_gather(decay_log, 'ctx', axis=1, tiled=True)]
    gather x0 -> x4, local copies, waits for them, and re-layouts: none -> 5.37 us  [gather_blocks(): return jnp.take(jnp.stack(received), order, axis=0)]
    select_n x0 -> x9, other arithmetic: none -> 3.26 us  [the longest x7 3.19 us: gather_blocks(): return jnp.take(jnp.stack(received), order, axis=0)]
    unnamed x12 -> x13, local copies, waits for them, and re-layouts: 1.5 us -> 3.6 us
  transfers between devices with their start and end apart: 2 -> 14, of which waited for: 2 -> 9; matrix products, arithmetic and copies ran while one was open for 1% -> 3% of each run, Pallas kernels for 0% -> 0%
where the time goes in v6:
time: 133 us; the launch traced here: 132 us
  waiting for transfers between devices  43.1 us (32%)
  starting transfers between devices  33.8 us (25%)
  local copies, waits for them, and re-layouts  26.5 us (20%)
  matrix products  17.7 us (13%)
  other arithmetic  10.1 us (8%)
    ppermute x10, waiting for transfers between devices, gather_blocks(): received.append(lax.ppermute(value, axis_name, perm))  27.9 us
    ppermute x10, starting transfers between devices, gather_blocks(): received.append(lax.ppermute(value, axis_name, perm))  27.5 us
    ppermute x2, waiting for transfers between devices, sum_over(): data = keep + lax.ppermute(send, axis_name, perm)  8.87 us
    dot_general x1, matrix products, expert_ffn(): jnp.einsum('gfd,qd->gfq', gate_up[0], slot_rows, preferred_element_type=j...  8.49 us
    ppermute x2, waiting for transfers between devices, sum_over(): other = lax.ppermute(data, axis_name, perm)  6.36 us
    gather x4, local copies, waits for them, and re-layouts, gather_blocks(): return jnp.take(jnp.stack(received), order, axis=0)  5.37 us
    dot_general x1, matrix products, mixer(): ssd = jnp.einsum('sktuh,skuhp->skthp', kernel, x_float, precision=highest)  4.14 us
    unnamed x13, local copies, waits for them, and re-layouts  3.6 us
  transfers between devices with their start and end apart: 14, of which 9 were waited for; matrix products, arithmetic and copies ran while one was open for 3% of the time, Pallas kernels for 0%

profile of v6, /device:TPU:0, one launch (start us, length us, event | category | flops | bytes accessed | tf_op | source)
XLA Modules:
  0.0 132.3 jit_solution(12527718457180119638)
XLA Ops:
  3.9 5.1 %collective-permute-start.2 = (bf16[2,16,4352]{2,1,0:T(8,128)(2,1)S(1)}, bf16[2,16,4352]{2,1,0:T(8,128)(2,1)S(1)}, u32[]{:S(2)}, u32[]{:S(2)}) collective-permute-start(bf16[2,16,4352]{2,1,0:T(8,128)(2,1)S(1)} %constant_dynamic-update-slice_fusion), channel_id=1, source_target_pairs={{0,12},{4,0},{8,4},{12,8},{1,13},{5,1},{9,5},{13,9},{2,14},{6,2},{... | collective-permute-start | bytes 835592 | tf_op jit(solution)/shard_map/ppermute | solution.py:15
  9.4 2.5 %collective-permute-start.4 = (f32[2,16,32]{2,1,0:T(8,128)}, f32[2,16,32]{2,1,0:T(8,128)S(1)}, u32[]{:S(2)}, u32[]{:S(2)}) collective-permute-start(f32[2,16,32]{2,1,0:T(8,128)} %param.15), channel_id=1, source_target_pairs={{0,8},{4,12},{8,0},{12,4},{1,9},{5,13},{9,1},{13,5},{2,10},{6,14},... | collective-permute-start | bytes 12296 | tf_op jit(solution)/shard_map/ppermute | solution.py:15
  11.9 2.0 %collective-permute-start.3 = (f32[2,16,32]{2,1,0:T(8,128)}, f32[2,16,32]{2,1,0:T(8,128)S(1)}, u32[]{:S(2)}, u32[]{:S(2)}) collective-permute-start(f32[2,16,32]{2,1,0:T(8,128)} %param.15), channel_id=1, source_target_pairs={{0,4},{4,8},{8,12},{12,0},{1,5},{5,9},{9,13},{13,1},{2,6},{6,10},{... | collective-permute-start | bytes 12296 | tf_op jit(solution)/shard_map/ppermute | solution.py:15
  16.3 5.3 %collective-permute-done.5 = f32[2,16,32]{2,1,0:T(8,128)S(1)} collective-permute-done((f32[2,16,32]{2,1,0:T(8,128)}, f32[2,16,32]{2,1,0:T(8,128)S(1)}, u32[]{:S(2)}, u32[]{:S(2)}) %collective-permute-start.5) | collective-permute-done | bytes 4128 | tf_op jit(solution)/shard_map/ppermute | solution.py:15
  21.6 12.8 %collective-permute-start = (bf16[2,16,4352]{2,1,0:T(8,128)(2,1)S(1)}, bf16[2,16,4352]{2,1,0:T(8,128)(2,1)S(1)}, u32[]{:S(2)}, u32[]{:S(2)}) collective-permute-start(bf16[2,16,4352]{2,1,0:T(8,128)(2,1)S(1)} %constant_dynamic-update-slice_fusion), channel_id=1, source_target_pairs={{0,4},{4,8},{8,12},{12,0},{1,5},{5,9},{9,13},{13,1},{2,6},{6,10},{... | collective-permute-start | bytes 835592 | tf_op jit(solution)/shard_map/ppermute | solution.py:15
  35.9 3.2 %collective-permute-done = bf16[2,16,4352]{2,1,0:T(8,128)(2,1)S(1)} collective-permute-done((bf16[2,16,4352]{2,1,0:T(8,128)(2,1)S(1)}, bf16[2,16,4352]{2,1,0:T(8,128)(2,1)S(1)}, u32[]{:S(2)}, u32[]{:S(2)}) %collective-permute-start) | collective-permute-done | bytes 278560 | tf_op jit(solution)/shard_map/ppermute | solution.py:15
  40.3 2.0 %copy.120 = f32[2,64,2048]{1,2,0:T(8,128)} copy(f32[2,64,2048]{2,1,0:T(8,128)S(1)} %get-tuple-element.21) | data formatting | bytes 2097152 | tf_op jit(solution)/shard_map/reshape | solution.py:55
  43.8 4.1 %bitcast_add_fusion = f32[2,1,64,32,64]{2,4,3,0,1:T(8,128)S(1)} fusion(f32[2,1,64,32,64]{2,4,3,0,1:T(8,128)} %bitcast.88, bf16[2,64,32,64]{1,3,2,0:T(8,128)(2,1)} %bitcast.92, f32[32]{0:T(128)S(1)} %copy-done.2, f32[2,64,64]{2,1,0:T(8,128)S(1)} %fusion.36, f32[2,64,32]{1,2,0:T(8,128)S(1)} %copy.118, pred[64,64]{1,0:T(8,128)(4,1)S(1)} %iota_compare_fusion.1), kind=kOutput, calls=%fused_computation.16 | convolution fusion | flops 202899456 | bytes 2674816 | tf_op jit(solution)/shard_map/sktuh,skuhp->skthp/dot_general | solution.py:63
  49.5 3.3 %fusion.5 = f32[2,64,1024]{2,1,0:T(8,128)S(1)} fusion(bf16[2048,1024]{1,0:T(8,128)(2,1)} %param.17, f32[2,64,2048]{2,1,0:T(8,128)} %copy.121, bf16[2,64,4352]{2,1,0:T(8,128)(2,1)S(1)} %bitcast.87), kind=kOutput, calls=%fused_computation.12 | convolution fusion | flops 538705920 | bytes 6291456 | tf_op jit(solution)/shard_map/stk,kd->std/dot_general | solution.py:155
  55.4 5.1 %collective-permute-done.6 = f32[129,512]{1,0:T(8,128)S(1)} collective-permute-done((f32[129,512]{1,0:T(8,128)S(1)}, f32[129,512]{1,0:T(8,128)S(1)}, u32[]{:S(2)}, u32[]{:S(2)}) %collective-permute-start.6) | collective-permute-done | bytes 264224 | tf_op jit(solution)/shard_map/ppermute | solution.py:36
  62.5 3.8 %collective-permute-done.7 = f32[129,256]{1,0:T(8,128)S(1)} collective-permute-done((f32[129,256]{1,0:T(8,128)S(1)}, f32[129,256]{1,0:T(8,128)S(1)}, u32[]{:S(2)}, u32[]{:S(2)}) %collective-permute-start.7) | collective-permute-done | bytes 132128 | tf_op jit(solution)/shard_map/ppermute | solution.py:36
  67.9 2.8 %collective-permute-done.8 = bf16[129,256]{1,0:T(8,128)(2,1)S(1)} collective-permute-done((bf16[129,256]{1,0:T(8,128)(2,1)S(1)}, bf16[129,256]{1,0:T(8,128)(2,1)S(1)}, u32[]{:S(2)}, u32[]{:S(2)}) %collective-permute-start.8) | collective-permute-done | bytes 66080 | tf_op jit(solution)/shard_map/ppermute | solution.py:41
  72.3 3.6 %collective-permute-done.9 = bf16[129,512]{1,0:T(8,128)(2,1)S(1)} collective-permute-done((bf16[129,512]{1,0:T(8,128)(2,1)S(1)}, bf16[129,512]{1,0:T(8,128)(2,1)S(1)}, u32[]{:S(2)}, u32[]{:S(2)}) %collective-permute-start.9) | collective-permute-done | bytes 132128 | tf_op jit(solution)/shard_map/ppermute | solution.py:41
  76.0 2.2 %collective-permute-start.12 = (bf16[129,1024]{1,0:T(8,128)(2,1)S(1)}, bf16[129,1024]{1,0:T(8,128)(2,1)S(1)}, u32[]{:S(2)}, u32[]{:S(2)}) collective-permute-start(bf16[129,1024]{1,0:T(8,128)(2,1)S(1)} %get-tuple-element.25), channel_id=1, source_target_pairs={{0,12},{4,0},{8,4},{12,8},{1,13},{5,1},{9,5},{13,9},{2,14},{6,2},{... | collective-permute-start | bytes 792584 | tf_op jit(solution)/shard_map/ppermute | solution.py:15
  78.3 1.7 %collective-permute-start.11 = (bf16[129,1024]{1,0:T(8,128)(2,1)S(1)}, bf16[129,1024]{1,0:T(8,128)(2,1)S(1)}, u32[]{:S(2)}, u32[]{:S(2)}) collective-permute-start(bf16[129,1024]{1,0:T(8,128)(2,1)S(1)} %get-tuple-element.25), channel_id=1, source_target_pairs={{0,8},{4,12},{8,0},{12,4},{1,9},{5,13},{9,1},{13,5},{2,10},{6,14},... | collective-permute-start | bytes 792584 | tf_op jit(solution)/shard_map/ppermute | solution.py:15
  80.6 7.0 %collective-permute-done.12 = bf16[129,1024]{1,0:T(8,128)(2,1)S(1)} collective-permute-done((bf16[129,1024]{1,0:T(8,128)(2,1)S(1)}, bf16[129,1024]{1,0:T(8,128)(2,1)S(1)}, u32[]{:S(2)}, u32[]{:S(2)}) %collective-permute-start.12) | collective-permute-done | bytes 264224 | tf_op jit(solution)/shard_map/ppermute | solution.py:15
  87.5 10.3 %collective-permute-done.11 = bf16[129,1024]{1,0:T(8,128)(2,1)S(1)} collective-permute-done((bf16[129,1024]{1,0:T(8,128)(2,1)S(1)}, bf16[129,1024]{1,0:T(8,128)(2,1)S(1)}, u32[]{:S(2)}, u32[]{:S(2)}) %collective-permute-start.11) | collective-permute-done | bytes 264224 | tf_op jit(solution)/shard_map/ppermute | solution.py:15
  100.3 2.1 %collective-permute-done.13 = bf16[4,129,1024]{2,0,1:T(4,128)(2,1)S(1)} collective-permute-done((bf16[4,129,1024]{2,0,1:T(4,128)(2,1)S(1)}, bf16[4,129,1024]{2,0,1:T(4,128)(2,1)S(1)}, u32[]{:S(2)}, u32[]{:S(2)}) %collective-permute-start.13) | collective-permute-done | bytes 1056800 | tf_op jit(solution)/shard_map/ppermute | solution.py:15
  104.6 3.6 %gather_fusion.3 = bf16[2,4,129,1024]{3,1,2,0:T(4,128)(2,1)} fusion(bf16[2,4,129,1024]{3,1,2,0:T(4,128)(2,1)S(1)} %copy.125, s32[1024]{0:T(1024)S(1)} %pad_clamp_fusion), kind=kCustom, calls=%fused_computation.3 | custom fusion | bytes 4227080 | tf_op jit(solution)/shard_map/jit(_take)/gather | solution.py:17
  108.1 2.6 %broadcast_select_fusion = bf16[2,4,129,1024]{3,1,2,0:T(4,128)(2,1)S(1)} fusion(bf16[2,4,129,1024]{3,1,2,0:T(4,128)(2,1)} %gather_fusion.3, pred[2]{0:T(512)(128)(4,1)S(1)} %compare_and_fusion.1), kind=kLoop, calls=%fused_computation.15 | loop fusion | flops 1056768 | bytes 4227074 | tf_op jit(solution)/shard_map/jit(_take)/select_n | solution.py:17
  110.7 2.1 %slice.52 = bf16[2,4,128,1024]{3,1,2,0:T(4,128)(2,1)} slice(bf16[2,4,129,1024]{3,1,2,0:T(4,128)(2,1)S(1)} %broadcast_select_fusion), slice={[0:2], [0:4], [0:128], [0:1024]} | slice | bytes 4194304 | tf_op jit(solution)/shard_map/slice | solution.py:178
  113.5 1.7 %fusion.2 = f32[2,128]{1,0:T(2,128)S(1)} fusion(bf16[2,4,129,1024]{3,1,2,0:T(4,128)(2,1)S(1)} %broadcast_select_fusion), kind=kLoop, calls=%fused_computation.8 | loop fusion | flops 3145472 | bytes 2098176 | tf_op jit(solution)/shard_map/reduce_sum | solution.py:186
  120.0 2.6 %copy.132 = bf16[256,4,1024]{0,2,1:T(8,128)(2,1)} copy(bf16[256,4,1024]{2,0,1:T(8,128)(2,1)S(1)} %bitcast_convert_fusion) | data formatting | bytes 4194304 | tf_op jit(solution)/shard_map/convert_element_type | solution.py:204
  122.5 8.5 %fusion.16 = f32[2,896,256]{1,2,0:T(8,128)S(1)} fusion(bf16[256,4096,1]{0,1,2:T(8,128)(2,1)} %bitcast.90, bf16[1,2,896,4096]{3,2,1,0:T(8,128)(2,1)} %param.19), kind=kOutput, calls=%fused_computation.24 | convolution fusion | flops 3758096384 | bytes 18612224 | tf_op jit(solution)/shard_map/gfd,qd->gfq/dot_general | solution.py:87
  (100 shorter events, 31.3 us)
Async XLA Ops:
  3.9 32.0 %collective-permute-start.2 = (bf16[2,16,4352]{2,1,0:T(8,128)(2,1)S(1)}, bf16[2,16,4352]{2,1,0:T(8,128)(2,1)S(1)}, u32[]{:S(2)}, u32[]{:S(2)}) collective-permute-start(bf16[2,16,4352]{2,1,0:T(8,128)(2,1)S(1)} %constant_dynamic-update-slice_fusion), channel_id=1, source_target_pairs={{0,12},{4,0},{8,4},{12,8},{1,13},{5,1},{9,5},{13,9},{2,14},{6,2},{... | collective-permute-start | bytes 835592 | tf_op jit(solution)/shard_map/ppermute | solution.py:15
  9.0 26.9 %collective-permute-start.1 = (bf16[2,16,4352]{2,1,0:T(8,128)(2,1)S(1)}, bf16[2,16,4352]{2,1,0:T(8,128)(2,1)S(1)}, u32[]{:S(2)}, u32[]{:S(2)}) collective-permute-start(bf16[2,16,4352]{2,1,0:T(8,128)(2,1)S(1)} %constant_dynamic-update-slice_fusion), channel_id=1, source_target_pairs={{0,8},{4,12},{8,0},{12,4},{1,9},{5,13},{9,1},{13,5},{2,10},{6,14},... | collective-permute-start | bytes 835592 | tf_op jit(solution)/shard_map/ppermute | solution.py:15
  9.0 12.7 %collective-permute-start.5 = (f32[2,16,32]{2,1,0:T(8,128)}, f32[2,16,32]{2,1,0:T(8,128)S(1)}, u32[]{:S(2)}, u32[]{:S(2)}) collective-permute-start(f32[2,16,32]{2,1,0:T(8,128)} %param.15), channel_id=1, source_target_pairs={{0,12},{4,0},{8,4},{12,8},{1,13},{5,1},{9,5},{13,9},{2,14},{6,2},{... | collective-permute-start | bytes 12296 | tf_op jit(solution)/shard_map/ppermute | solution.py:15
  9.4 25.1 %collective-permute-start.4 = (f32[2,16,32]{2,1,0:T(8,128)}, f32[2,16,32]{2,1,0:T(8,128)S(1)}, u32[]{:S(2)}, u32[]{:S(2)}) collective-permute-start(f32[2,16,32]{2,1,0:T(8,128)} %param.15), channel_id=1, source_target_pairs={{0,8},{4,12},{8,0},{12,4},{1,9},{5,13},{9,1},{13,5},{2,10},{6,14},... | collective-permute-start | bytes 12296 | tf_op jit(solution)/shard_map/ppermute | solution.py:15
  11.9 22.6 %collective-permute-start.3 = (f32[2,16,32]{2,1,0:T(8,128)}, f32[2,16,32]{2,1,0:T(8,128)S(1)}, u32[]{:S(2)}, u32[]{:S(2)}) collective-permute-start(f32[2,16,32]{2,1,0:T(8,128)} %param.15), channel_id=1, source_target_pairs={{0,4},{4,8},{8,12},{12,0},{1,5},{5,9},{9,13},{13,1},{2,6},{6,10},{... | collective-permute-start | bytes 12296 | tf_op jit(solution)/shard_map/ppermute | solution.py:15
  21.6 17.4 %collective-permute-start = (bf16[2,16,4352]{2,1,0:T(8,128)(2,1)S(1)}, bf16[2,16,4352]{2,1,0:T(8,128)(2,1)S(1)}, u32[]{:S(2)}, u32[]{:S(2)}) collective-permute-start(bf16[2,16,4352]{2,1,0:T(8,128)(2,1)S(1)} %constant_dynamic-update-slice_fusion), channel_id=1, source_target_pairs={{0,4},{4,8},{8,12},{12,0},{1,5},{5,9},{9,13},{13,1},{2,6},{6,10},{... | collective-permute-start | bytes 835592 | tf_op jit(solution)/shard_map/ppermute | solution.py:15
  40.3 3.5 %copy-start.2 = (f32[32]{0:T(128)S(1)}, f32[32]{0:T(128)}, u32[]{:S(2)}) copy-start(f32[32]{0:T(128)} %param.16) | copy-start | bytes 388
  53.8 6.6 %collective-permute-start.6 = (f32[129,512]{1,0:T(8,128)S(1)}, f32[129,512]{1,0:T(8,128)S(1)}, u32[]{:S(2)}, u32[]{:S(2)}) collective-permute-start(f32[129,512]{1,0:T(8,128)S(1)} %bitcast.103), channel_id=1, source_target_pairs={{0,1},{1,0},{2,3},{3,2},{4,5},{5,4},{6,7},{7,6},{8,9},{9,8},{10,11... | collective-permute-start | bytes 792584 | tf_op jit(solution)/shard_map/ppermute | solution.py:36
  60.9 5.4 %collective-permute-start.7 = (f32[129,256]{1,0:T(8,128)S(1)}, f32[129,256]{1,0:T(8,128)S(1)}, u32[]{:S(2)}, u32[]{:S(2)}) collective-permute-start(f32[129,256]{1,0:T(8,128)S(1)} %bitcast.106), channel_id=1, source_target_pairs={{0,2},{1,3},{2,0},{3,1},{4,6},{5,7},{6,4},{7,5},{8,10},{9,11},{10,... | collective-permute-start | bytes 396296 | tf_op jit(solution)/shard_map/ppermute | solution.py:36
  66.3 4.4 %collective-permute-start.8 = (bf16[129,256]{1,0:T(8,128)(2,1)S(1)}, bf16[129,256]{1,0:T(8,128)(2,1)S(1)}, u32[]{:S(2)}, u32[]{:S(2)}) collective-permute-start(bf16[129,256]{1,0:T(8,128)(2,1)S(1)} %fusion.35), channel_id=1, source_target_pairs={{0,2},{1,3},{2,0},{3,1},{4,6},{5,7},{6,4},{7,5},{8,10},{9,11},{10,... | collective-permute-start | bytes 198152 | tf_op jit(solution)/shard_map/ppermute | solution.py:41
  70.8 5.1 %collective-permute-start.9 = (bf16[129,512]{1,0:T(8,128)(2,1)S(1)}, bf16[129,512]{1,0:T(8,128)(2,1)S(1)}, u32[]{:S(2)}, u32[]{:S(2)}) collective-permute-start(bf16[129,512]{1,0:T(8,128)(2,1)S(1)} %pad_maximum_fusion.4), channel_id=1, source_target_pairs={{0,1},{1,0},{2,3},{3,2},{4,5},{5,4},{6,7},{7,6},{8,9},{9,8},{10,11... | collective-permute-start | bytes 396296 | tf_op jit(solution)/shard_map/ppermute | solution.py:41
  76.0 11.5 %collective-permute-start.12 = (bf16[129,1024]{1,0:T(8,128)(2,1)S(1)}, bf16[129,1024]{1,0:T(8,128)(2,1)S(1)}, u32[]{:S(2)}, u32[]{:S(2)}) collective-permute-start(bf16[129,1024]{1,0:T(8,128)(2,1)S(1)} %get-tuple-element.25), channel_id=1, source_target_pairs={{0,12},{4,0},{8,4},{12,8},{1,13},{5,1},{9,5},{13,9},{2,14},{6,2},{... | collective-permute-start | bytes 792584 | tf_op jit(solution)/shard_map/ppermute | solution.py:15
  78.3 19.6 %collective-permute-start.11 = (bf16[129,1024]{1,0:T(8,128)(2,1)S(1)}, bf16[129,1024]{1,0:T(8,128)(2,1)S(1)}, u32[]{:S(2)}, u32[]{:S(2)}) collective-permute-start(bf16[129,1024]{1,0:T(8,128)(2,1)S(1)} %get-tuple-element.25), channel_id=1, source_target_pairs={{0,8},{4,12},{8,0},{12,4},{1,9},{5,13},{9,1},{13,5},{2,10},{6,14},... | collective-permute-start | bytes 792584 | tf_op jit(solution)/shard_map/ppermute | solution.py:15
  80.0 17.8 %collective-permute-start.10 = (bf16[129,1024]{1,0:T(8,128)(2,1)S(1)}, bf16[129,1024]{1,0:T(8,128)(2,1)S(1)}, u32[]{:S(2)}, u32[]{:S(2)}) collective-permute-start(bf16[129,1024]{1,0:T(8,128)(2,1)S(1)} %get-tuple-element.25), channel_id=1, source_target_pairs={{0,4},{4,8},{8,12},{12,0},{1,5},{5,9},{9,13},{13,1},{2,6},{6,10},{... | collective-permute-start | bytes 792584 | tf_op jit(solution)/shard_map/ppermute | solution.py:15
  98.6 1.4 %copy-start.1 = (f32[4096]{0:T(1024)S(1)}, f32[4096]{0:T(1024)}, u32[]{:S(2)}) copy-start(f32[4096]{0:T(1024)} %param.18) | copy-start | bytes 49156
  99.6 2.7 %collective-permute-start.13 = (bf16[4,129,1024]{2,0,1:T(4,128)(2,1)S(1)}, bf16[4,129,1024]{2,0,1:T(4,128)(2,1)S(1)}, u32[]{:S(2)}, u32[]{:S(2)}) collective-permute-start(bf16[4,129,1024]{2,0,1:T(4,128)(2,1)S(1)} %copy.123), channel_id=1, source_target_pairs={{0,16},{16,0},{1,17},{17,1},{2,18},{18,2},{3,19},{19,3},{4,20},{20... | collective-permute-start | bytes 3170312 | tf_op jit(solution)/shard_map/ppermute | solution.py:15
  113.4 1.8 %copy-start = (bf16[2,4,128,1024]{3,1,2,0:T(4,128)(2,1)S(1)}, bf16[2,4,128,1024]{3,1,2,0:T(4,128)(2,1)}, u32[]{:S(2)}) copy-start(bf16[2,4,128,1024]{3,1,2,0:T(4,128)(2,1)} %slice.52) | copy-start | bytes 6291460

commit v7 on v5

--- a/solution.py
+++ b/solution.py
@@ -5,6 +5,48 @@
 
 P_SIZE = 64
 ALL_AXES = ("dp", "ctx", "expert")
+
+
+def gather_blocks(value, axis_name, count):
+    me = lax.axis_index(axis_name)
+    received = [value]
+    for shift in range(1, count):
+        perm = [(i, (i + shift) % count) for i in range(count)]
+        received.append(lax.ppermute(value, axis_name, perm))
+    order = (me - jnp.arange(count)) % count
+    return jnp.take(jnp.stack(received), order, axis=0)
+
+
+def sum_over(value, axis_name, count):
+    if count & (count - 1) or value.shape[-1] % count:
+        return lax.psum(value, axis_name).astype(jnp.bfloat16)
+    me = lax.axis_index(axis_name)
+    pieces = value.reshape(value.shape[:-1] + (count, value.shape[-1] // count))
+    total = lax.dynamic_index_in_dim(pieces, me, axis=-2, keepdims=False)
+    for shift in range(1, count):
+        perm = [(i, i ^ shift) for i in range(count)]
+        send = lax.dynamic_index_in_dim(pieces, me ^ shift, axis=-2, keepdims=False)
+        total = total + lax.ppermute(send, axis_name, perm)
+    total = total.astype(jnp.bfloat16)
+    received = [total]
+    for shift in range(1, count):
+        perm = [(i, i ^ shift) for i in range(count)]
+        received.append(lax.ppermute(total, axis_name, perm))
+    ordered = jnp.take(jnp.stack(received, axis=-2), me ^ jnp.arange(count), axis=-2)
+    return ordered.reshape(value.shape)
+
+
+def split_exact(value):
+    high = value.astype(jnp.bfloat16)
+    rest = value - lax.optimization_barrier(high).astype(jnp.float32)
+    middle = rest.astype(jnp.bfloat16)
+    low = (rest - lax.optimization_barrier(middle).astype(jnp.float32)).astype(jnp.bfloat16)
+    return [high, middle, low]
+
+
+def join_exact(parts):
+    high, middle, low = (part.astype(jnp.float32) for part in parts)
+    return (high + middle) + low
 
 
 def mixer(x_in, b_in, c_in, decay_log, skip):
@@ -99,15 +141,20 @@
     row_count = seq_count * per_block
     capacity = max(2, 4 * row_count // group_count)
 
-    packed = jnp.concatenate([x_in, z_in, b_in, c_in], axis=2)
-    packed = lax.all_gather(packed, "ctx", axis=1, tiled=True)
-    decay_all = lax.all_gather(decay_log, "ctx", axis=1, tiled=True)
-    packed, decay_all = lax.optimization_barrier((packed, decay_all))
+    head_count = decay_log.shape[2]
+    packed = jnp.concatenate([x_in, z_in, b_in, c_in] + split_exact(decay_log), axis=2)
+    packed = jnp.moveaxis(gather_blocks(packed, "ctx", ctx_count), 0, 1).reshape(
+        seq_count, ctx_count * block_len, packed.shape[2]
+    )
+    decay_base = 2 * width_in + 2 * state_size
+    decay_all = join_exact(
+        [packed[:, :, decay_base + i * head_count : decay_base + (i + 1) * head_count] for i in range(3)]
+    )
 
     x_all = packed[:, :, :width_in]
     z_all = packed[:, :, width_in : 2 * width_in]
     b_all = packed[:, :, 2 * width_in : 2 * width_in + state_size]
-    c_all = packed[:, :, 2 * width_in + state_size :]
+    c_all = packed[:, :, 2 * width_in + state_size : decay_base]
     ssd = mixer(x_all, b_all, c_all, decay_all, skip)
     gated = (ssd * jax.nn.silu(z_all.astype(jnp.float32))).astype(jnp.bfloat16)
     partial_value = jnp.einsum(
@@ -125,8 +172,8 @@
         [partial_value.reshape(seq_count * total_len, col_width), route_row.reshape(extra_rows, col_width)],
         axis=0,
     )
-    summed = lax.psum(extended, "expert").astype(jnp.bfloat16)
-    gathered = lax.all_gather(summed[None], ("dp", "ctx"), axis=0, tiled=True)
+    summed = sum_over(extended, "expert", group_count)
+    gathered = gather_blocks(gather_blocks(summed, "ctx", ctx_count), "dp", dp_count)
     gathered = gathered.reshape(dp_count, ctx_count, seq_count * total_len + extra_rows, col_width)
     routes = gathered[:, :, seq_count * total_len :, :].reshape(dp_count, ctx_count, -1)
     routes = routes[:, :, : group_count * route_len].astype(jnp.int32)

time: 142 us -> 121 us (0.85)
  the two profiles are of different devices: /device:TPU:0 before, /device:TPU:27 now
where the time goes in v7:
time: 121 us
  waiting for transfers between devices  51.7 us (43%)
  local copies, waits for them, and re-layouts  22.7 us (19%)
  matrix products  17.9 us (15%)
  starting transfers between devices  16 us (13%)
  other arithmetic  11.6 us (10%)
    ppermute x7, waiting for transfers between devices, gather_blocks(): received.append(lax.ppermute(value, axis_name, perm))  44.2 us
    ppermute x7, starting transfers between devices, gather_blocks(): received.append(lax.ppermute(value, axis_name, perm))  10.5 us
    dot_general x1, matrix products, expert_ffn(): jnp.einsum('gfd,qd->gfq', gate_up[0], slot_rows, preferred_element_type=j...  8.48 us
    gather x3, local copies, waits for them, and re-layouts, gather_blocks(): return jnp.take(jnp.stack(received), order, axis=0)  4.9 us
    dot_general x1, matrix products, mixer(): ssd = jnp.einsum('sktuh,skuhp->skthp', kernel, x_float, precision=highest)  4.66 us
    ppermute x3, waiting for transfers between devices, sum_over(): total = total + lax.ppermute(send, axis_name, perm)  4.65 us
    select_n x6, other arithmetic, gather_blocks(): return jnp.take(jnp.stack(received), order, axis=0)  3.13 us
    dot_general x1, matrix products, local(): jnp.einsum('stk,kd->std', gated, out_weight, preferred_element_type=jnp.f...  2.99 us
  transfers between devices with their start and end apart: 13, of which 11 were waited for; matrix products, arithmetic and copies ran while one was open for 3% of the time, Pallas kernels for 0%

profile of v7, /device:TPU:27, one launch (start us, length us, event | category | flops | bytes accessed | tf_op | source)
XLA Modules:
  0.0 120.9 jit_solution(13198045294922043248)
XLA Ops:
  3.9 1.3 %collective-permute-start.1 = (bf16[2,16,4448]{2,1,0:T(8,128)(2,1)S(1)}, bf16[2,16,4448]{2,1,0:T(8,128)(2,1)S(1)}, u32[]{:S(2)}, u32[]{:S(2)}) collective-permute-start(bf16[2,16,4448]{2,1,0:T(8,128)(2,1)S(1)} %concatenate.11), channel_id=1, source_target_pairs={{0,8},{4,12},{8,0},{12,4},{1,9},{5,13},{9,1},{13,5},{2,10},{6,14},... | collective-permute-start | bytes 854024 | tf_op jit(solution)/shard_map/ppermute | solution.py:15
  7.9 3.7 %collective-permute-done = bf16[2,16,4448]{2,1,0:T(8,128)(2,1)S(1)} collective-permute-done((bf16[2,16,4448]{2,1,0:T(8,128)(2,1)S(1)}, bf16[2,16,4448]{2,1,0:T(8,128)(2,1)S(1)}, u32[]{:S(2)}, u32[]{:S(2)}) %collective-permute-start) | collective-permute-done | bytes 284704 | tf_op jit(solution)/shard_map/ppermute | solution.py:15
  11.6 18.3 %collective-permute-done.1 = bf16[2,16,4448]{2,1,0:T(8,128)(2,1)S(1)} collective-permute-done((bf16[2,16,4448]{2,1,0:T(8,128)(2,1)S(1)}, bf16[2,16,4448]{2,1,0:T(8,128)(2,1)S(1)}, u32[]{:S(2)}, u32[]{:S(2)}) %collective-permute-start.1) | collective-permute-done | bytes 284704 | tf_op jit(solution)/shard_map/ppermute | solution.py:15
  31.5 2.0 %copy.102 = f32[2,64,2048]{1,2,0:T(8,128)} copy(f32[2,64,2048]{2,1,0:T(8,128)S(1)} %get-tuple-element.15) | data formatting | bytes 2097152 | tf_op jit(solution)/shard_map/reshape | solution.py:59
  34.1 4.7 %bitcast_add_fusion = f32[2,1,64,32,64]{2,4,3,0,1:T(8,128)} fusion(f32[2,1,64,32,64]{2,4,3,0,1:T(8,128)} %bitcast.95, bf16[2,64,32,64]{1,3,2,0:T(8,128)(2,1)S(1)} %bitcast.103, f32[32]{0:T(128)S(1)} %copy-done.2, f32[2,64,64]{2,1,0:T(8,128)S(1)} %fusion.38, f32[2,64,32]{1,2,0:T(8,128)S(1)} %copy.100, pred[64,64]{1,0:T(8,128)(4,1)S(1)} %iota_compare_fusion.1), kind=kOutput, calls=%fused_computation.16 | convolution fusion | flops 202899456 | bytes 2674816 | tf_op jit(solution)/shard_map/sktuh,skuhp->skthp/dot_general | solution.py:67
  38.8 2.2 %copy.103 = f32[2,64,2048]{2,1,0:T(8,128)S(1)} copy(f32[2,64,2048]{1,2,0:T(8,128)} %bitcast.96) | data formatting | bytes 2097152 | tf_op jit(solution)/shard_map/reshape | solution.py:87
  40.9 3.0 %fusion.5 = f32[2,64,1024]{2,1,0:T(8,128)S(1)} fusion(bf16[2048,1024]{1,0:T(8,128)(2,1)} %param.17, f32[2,64,2048]{2,1,0:T(8,128)S(1)} %copy.103, bf16[2,64,4448]{2,1,0:T(8,128)(2,1)S(1)} %bitcast.94), kind=kOutput, calls=%fused_computation.12 | convolution fusion | flops 538705920 | bytes 6291456 | tf_op jit(solution)/shard_map/stk,kd->std/dot_general | solution.py:160
  45.1 1.3 %collective-permute-start.4 = (f32[129,256]{1,0:T(8,128)S(1)}, f32[129,256]{1,0:T(8,128)S(1)}, u32[]{:S(2)}, u32[]{:S(2)}) collective-permute-start(f32[129,256]{1,0:T(8,128)S(1)} %bitcast.116), channel_id=1, source_target_pairs={{0,2},{1,3},{2,0},{3,1},{4,6},{5,7},{6,4},{7,5},{8,10},{9,11},{10,... | collective-permute-start | bytes 396296 | tf_op jit(solution)/shard_map/ppermute | solution.py:29
  46.4 1.2 %collective-permute-start.5 = (f32[129,256]{1,0:T(8,128)S(1)}, f32[129,256]{1,0:T(8,128)S(1)}, u32[]{:S(2)}, u32[]{:S(2)}) collective-permute-start(f32[129,256]{1,0:T(8,128)S(1)} %bitcast.117), channel_id=1, source_target_pairs={{0,3},{1,2},{2,1},{3,0},{4,7},{5,6},{6,5},{7,4},{8,11},{9,10},{10,... | collective-permute-start | bytes 396296 | tf_op jit(solution)/shard_map/ppermute | solution.py:29
  49.0 3.3 %collective-permute-done.5 = f32[129,256]{1,0:T(8,128)S(1)} collective-permute-done((f32[129,256]{1,0:T(8,128)S(1)}, f32[129,256]{1,0:T(8,128)S(1)}, u32[]{:S(2)}, u32[]{:S(2)}) %collective-permute-start.5) | collective-permute-done | bytes 132128 | tf_op jit(solution)/shard_map/ppermute | solution.py:29
  53.8 1.3 %collective-permute-start.8 = (bf16[129,256]{1,0:T(8,128)(2,1)S(1)}, bf16[129,256]{1,0:T(8,128)(2,1)S(1)}, u32[]{:S(2)}, u32[]{:S(2)}) collective-permute-start(bf16[129,256]{1,0:T(8,128)(2,1)S(1)} %fusion.37), channel_id=1, source_target_pairs={{0,3},{1,2},{2,1},{3,0},{4,7},{5,6},{6,5},{7,4},{8,11},{9,10},{10,... | collective-permute-start | bytes 198152 | tf_op jit(solution)/shard_map/ppermute | solution.py:34
  58.9 4.0 %collective-permute-start.10 = (bf16[129,1024]{1,0:T(8,128)(2,1)S(1)}, bf16[129,1024]{1,0:T(8,128)(2,1)S(1)}, u32[]{:S(2)}, u32[]{:S(2)}) collective-permute-start(bf16[129,1024]{1,0:T(8,128)(2,1)S(1)} %broadcast_select_fusion.2), channel_id=1, source_target_pairs={{0,8},{4,12},{8,0},{12,4},{1,9},{5,13},{9,1},{13,5},{2,10},{6,14},... | collective-permute-start | bytes 792584 | tf_op jit(solution)/shard_map/ppermute | solution.py:15
  62.9 1.4 %collective-permute-start.11 = (bf16[129,1024]{1,0:T(8,128)(2,1)S(1)}, bf16[129,1024]{1,0:T(8,128)(2,1)S(1)}, u32[]{:S(2)}, u32[]{:S(2)}) collective-permute-start(bf16[129,1024]{1,0:T(8,128)(2,1)S(1)} %broadcast_select_fusion.2), channel_id=1, source_target_pairs={{0,12},{4,0},{8,4},{12,8},{1,13},{5,1},{9,5},{13,9},{2,14},{6,2},{... | collective-permute-start | bytes 792584 | tf_op jit(solution)/shard_map/ppermute | solution.py:15
  64.8 20.1 %collective-permute-done.10 = bf16[129,1024]{1,0:T(8,128)(2,1)S(1)} collective-permute-done((bf16[129,1024]{1,0:T(8,128)(2,1)S(1)}, bf16[129,1024]{1,0:T(8,128)(2,1)S(1)}, u32[]{:S(2)}, u32[]{:S(2)}) %collective-permute-start.10) | collective-permute-done | bytes 264224 | tf_op jit(solution)/shard_map/ppermute | solution.py:15
  86.7 3.4 %collective-permute-start.12 = (bf16[4,129,1024]{2,0,1:T(4,128)(2,1)S(1)}, bf16[4,129,1024]{2,0,1:T(4,128)(2,1)S(1)}, u32[]{:S(2)}, u32[]{:S(2)}) collective-permute-start(bf16[4,129,1024]{2,0,1:T(4,128)(2,1)S(1)} %copy.107), channel_id=1, source_target_pairs={{0,16},{16,0},{1,17},{17,1},{2,18},{18,2},{3,19},{19,3},{4,20},{20... | collective-permute-start | bytes 3170312 | tf_op jit(solution)/shard_map/ppermute | solution.py:15
  90.8 1.7 %collective-permute-done.12 = bf16[4,129,1024]{2,0,1:T(4,128)(2,1)S(1)} collective-permute-done((bf16[4,129,1024]{2,0,1:T(4,128)(2,1)S(1)}, bf16[4,129,1024]{2,0,1:T(4,128)(2,1)S(1)}, u32[]{:S(2)}, u32[]{:S(2)}) %collective-permute-start.12) | collective-permute-done | bytes 1056800 | tf_op jit(solution)/shard_map/ppermute | solution.py:15
  93.0 1.6 %copy.109 = bf16[2,4,129,1024]{3,1,2,0:T(4,128)(2,1)S(1)} copy(bf16[2,4,129,1024]{3,2,1,0:T(8,128)(2,1)S(1)} %pad_maximum_fusion) | data formatting | bytes 4227072 | tf_op jit(solution)/shard_map/stack | solution.py:17
  94.7 3.6 %gather_fusion.3 = bf16[2,4,129,1024]{3,1,2,0:T(4,128)(2,1)} fusion(bf16[2,4,129,1024]{3,1,2,0:T(4,128)(2,1)S(1)} %copy.109, s32[1024]{0:T(1024)S(1)} %pad_clamp_fusion), kind=kCustom, calls=%fused_computation.3 | custom fusion | bytes 4227080 | tf_op jit(solution)/shard_map/jit(_take)/gather | solution.py:17
  98.3 2.6 %broadcast_select_fusion = bf16[2,4,129,1024]{3,1,2,0:T(4,128)(2,1)S(1)} fusion(bf16[2,4,129,1024]{3,1,2,0:T(4,128)(2,1)} %gather_fusion.3, pred[2]{0:T(512)(128)(4,1)S(1)} %compare_and_fusion.2), kind=kLoop, calls=%fused_computation.15 | loop fusion | flops 1056768 | bytes 4227074 | tf_op jit(solution)/shard_map/jit(_take)/select_n | solution.py:17
  100.8 1.7 %fusion.2 = f32[2,128]{1,0:T(2,128)S(1)} fusion(bf16[2,4,129,1024]{3,1,2,0:T(4,128)(2,1)S(1)} %broadcast_select_fusion), kind=kLoop, calls=%fused_computation.8 | loop fusion | flops 3145472 | bytes 2098176 | tf_op jit(solution)/shard_map/reduce_sum | solution.py:191
  103.6 1.5 %fusion.4 = bf16[2,4,128,1024]{3,1,2,0:T(4,128)(2,1)S(1)} fusion(f32[4,1024]{1,0:T(4,128)S(1)} %mul.117, f32[2,128]{1,0:T(2,128)S(1)} %add_rsqrt_fusion, bf16[2,4,129,1024]{3,1,2,0:T(4,128)(2,1)S(1)} %broadcast_select_fusion), kind=kLoop, calls=%fused_computation.10 | loop fusion | flops 4194304 | bytes 4211712 | tf_op jit(solution)/shard_map/convert_element_type | solution.py:194
  105.3 1.6 %bitcast_convert_fusion = bf16[256,4,1024]{2,0,1:T(8,128)(2,1)S(1)} fusion(pred[2,128,256,1]{2,1,0,3:T(8,128)(4,1)S(1)} %bitcast.114, bf16[2,4,128,1024]{3,1,2,0:T(4,128)(2,1)S(1)} %fusion.4), kind=kOutput, calls=%fused_computation.11 | convolution fusion | flops 537919488 | bytes 4259840 | tf_op jit(solution)/shard_map/drq,dcrk->qck/dot_general | solution.py:207
  106.9 2.6 %copy.116 = bf16[256,4,1024]{0,2,1:T(8,128)(2,1)} copy(bf16[256,4,1024]{2,0,1:T(8,128)(2,1)S(1)} %bitcast_convert_fusion) | data formatting | bytes 4194304 | tf_op jit(solution)/shard_map/convert_element_type | solution.py:209
  109.5 8.5 %fusion.16 = f32[2,896,256]{1,2,0:T(8,128)S(1)} fusion(bf16[256,4096,1]{0,1,2:T(8,128)(2,1)} %bitcast.97, bf16[1,2,896,4096]{3,2,1,0:T(8,128)(2,1)} %param.19), kind=kOutput, calls=%fused_computation.24 | convolution fusion | flops 3758096384 | bytes 18612224 | tf_op jit(solution)/shard_map/gfd,qd->gfq/dot_general | solution.py:91
  (102 shorter events, 23.1 us)
Async XLA Ops:
  3.9 7.8 %collective-permute-start = (bf16[2,16,4448]{2,1,0:T(8,128)(2,1)S(1)}, bf16[2,16,4448]{2,1,0:T(8,128)(2,1)S(1)}, u32[]{:S(2)}, u32[]{:S(2)}) collective-permute-start(bf16[2,16,4448]{2,1,0:T(8,128)(2,1)S(1)} %concatenate.11), channel_id=1, source_target_pairs={{0,4},{4,8},{8,12},{12,0},{1,5},{5,9},{9,13},{13,1},{2,6},{6,10},{... | collective-permute-start | bytes 854024 | tf_op jit(solution)/shard_map/ppermute | solution.py:15
  3.9 26.0 %collective-permute-start.1 = (bf16[2,16,4448]{2,1,0:T(8,128)(2,1)S(1)}, bf16[2,16,4448]{2,1,0:T(8,128)(2,1)S(1)}, u32[]{:S(2)}, u32[]{:S(2)}) collective-permute-start(bf16[2,16,4448]{2,1,0:T(8,128)(2,1)S(1)} %concatenate.11), channel_id=1, source_target_pairs={{0,8},{4,12},{8,0},{12,4},{1,9},{5,13},{9,1},{13,5},{2,10},{6,14},... | collective-permute-start | bytes 854024 | tf_op jit(solution)/shard_map/ppermute | solution.py:15
  5.3 24.7 %collective-permute-start.2 = (bf16[2,16,4448]{2,1,0:T(8,128)(2,1)S(1)}, bf16[2,16,4448]{2,1,0:T(8,128)(2,1)S(1)}, u32[]{:S(2)}, u32[]{:S(2)}) collective-permute-start(bf16[2,16,4448]{2,1,0:T(8,128)(2,1)S(1)} %concatenate.11), channel_id=1, source_target_pairs={{0,12},{4,0},{8,4},{12,8},{1,13},{5,1},{9,5},{13,9},{2,14},{6,2},{... | collective-permute-start | bytes 854024 | tf_op jit(solution)/shard_map/ppermute | solution.py:15
  31.5 2.6 %copy-start.2 = (f32[32]{0:T(128)S(1)}, f32[32]{0:T(128)}, u32[]{:S(2)}) copy-start(f32[32]{0:T(128)} %param.16) | copy-start | bytes 388
  44.7 4.0 %collective-permute-start.3 = (f32[129,256]{1,0:T(8,128)S(1)}, f32[129,256]{1,0:T(8,128)S(1)}, u32[]{:S(2)}, u32[]{:S(2)}) collective-permute-start(f32[129,256]{1,0:T(8,128)S(1)} %bitcast.115), channel_id=1, source_target_pairs={{0,1},{1,0},{2,3},{3,2},{4,5},{5,4},{6,7},{7,6},{8,9},{9,8},{10,11... | collective-permute-start | bytes 396296 | tf_op jit(solution)/shard_map/ppermute | solution.py:29
  45.1 4.0 %collective-permute-start.4 = (f32[129,256]{1,0:T(8,128)S(1)}, f32[129,256]{1,0:T(8,128)S(1)}, u32[]{:S(2)}, u32[]{:S(2)}) collective-permute-start(f32[129,256]{1,0:T(8,128)S(1)} %bitcast.116), channel_id=1, source_target_pairs={{0,2},{1,3},{2,0},{3,1},{4,6},{5,7},{6,4},{7,5},{8,10},{9,11},{10,... | collective-permute-start | bytes 396296 | tf_op jit(solution)/shard_map/ppermute | solution.py:29
  46.4 17.9 %copy-start.1 = (f32[4096]{0:T(1024)S(1)}, f32[4096]{0:T(1024)}, u32[]{:S(2)}) copy-start(f32[4096]{0:T(1024)} %param.18) | copy-start | bytes 49156
  46.4 6.0 %collective-permute-start.5 = (f32[129,256]{1,0:T(8,128)S(1)}, f32[129,256]{1,0:T(8,128)S(1)}, u32[]{:S(2)}, u32[]{:S(2)}) collective-permute-start(f32[129,256]{1,0:T(8,128)S(1)} %bitcast.117), channel_id=1, source_target_pairs={{0,3},{1,2},{2,1},{3,0},{4,7},{5,6},{6,5},{7,4},{8,11},{9,10},{10,... | collective-permute-start | bytes 396296 | tf_op jit(solution)/shard_map/ppermute | solution.py:29
  52.4 3.2 %collective-permute-start.6 = (bf16[129,256]{1,0:T(8,128)(2,1)S(1)}, bf16[129,256]{1,0:T(8,128)(2,1)S(1)}, u32[]{:S(2)}, u32[]{:S(2)}) collective-permute-start(bf16[129,256]{1,0:T(8,128)(2,1)S(1)} %fusion.37), channel_id=1, source_target_pairs={{0,1},{1,0},{2,3},{3,2},{4,5},{5,4},{6,7},{7,6},{8,9},{9,8},{10,11... | collective-permute-start | bytes 198152 | tf_op jit(solution)/shard_map/ppermute | solution.py:34
  53.6 3.2 %collective-permute-start.7 = (bf16[129,256]{1,0:T(8,128)(2,1)S(1)}, bf16[129,256]{1,0:T(8,128)(2,1)S(1)}, u32[]{:S(2)}, u32[]{:S(2)}) collective-permute-start(bf16[129,256]{1,0:T(8,128)(2,1)S(1)} %fusion.37), channel_id=1, source_target_pairs={{0,2},{1,3},{2,0},{3,1},{4,6},{5,7},{6,4},{7,5},{8,10},{9,11},{10,... | collective-permute-start | bytes 198152 | tf_op jit(solution)/shard_map/ppermute | solution.py:34
  53.8 4.1 %collective-permute-start.8 = (bf16[129,256]{1,0:T(8,128)(2,1)S(1)}, bf16[129,256]{1,0:T(8,128)(2,1)S(1)}, u32[]{:S(2)}, u32[]{:S(2)}) collective-permute-start(bf16[129,256]{1,0:T(8,128)(2,1)S(1)} %fusion.37), channel_id=1, source_target_pairs={{0,3},{1,2},{2,1},{3,0},{4,7},{5,6},{6,5},{7,4},{8,11},{9,10},{10,... | collective-permute-start | bytes 198152 | tf_op jit(solution)/shard_map/ppermute | solution.py:34
  58.8 6.0 %collective-permute-start.9 = (bf16[129,1024]{1,0:T(8,128)(2,1)S(1)}, bf16[129,1024]{1,0:T(8,128)(2,1)S(1)}, u32[]{:S(2)}, u32[]{:S(2)}) collective-permute-start(bf16[129,1024]{1,0:T(8,128)(2,1)S(1)} %broadcast_select_fusion.2), channel_id=1, source_target_pairs={{0,4},{4,8},{8,12},{12,0},{1,5},{5,9},{9,13},{13,1},{2,6},{6,10},{... | collective-permute-start | bytes 792584 | tf_op jit(solution)/shard_map/ppermute | solution.py:15
  58.9 26.1 %collective-permute-start.10 = (bf16[129,1024]{1,0:T(8,128)(2,1)S(1)}, bf16[129,1024]{1,0:T(8,128)(2,1)S(1)}, u32[]{:S(2)}, u32[]{:S(2)}) collective-permute-start(bf16[129,1024]{1,0:T(8,128)(2,1)S(1)} %broadcast_select_fusion.2), channel_id=1, source_target_pairs={{0,8},{4,12},{8,0},{12,4},{1,9},{5,13},{9,1},{13,5},{2,10},{6,14},... | collective-permute-start | bytes 792584 | tf_op jit(solution)/shard_map/ppermute | solution.py:15
  62.9 22.1 %collective-permute-start.11 = (bf16[129,1024]{1,0:T(8,128)(2,1)S(1)}, bf16[129,1024]{1,0:T(8,128)(2,1)S(1)}, u32[]{:S(2)}, u32[]{:S(2)}) collective-permute-start(bf16[129,1024]{1,0:T(8,128)(2,1)S(1)} %broadcast_select_fusion.2), channel_id=1, source_target_pairs={{0,12},{4,0},{8,4},{12,8},{1,13},{5,1},{9,5},{13,9},{2,14},{6,2},{... | collective-permute-start | bytes 792584 | tf_op jit(solution)/shard_map/ppermute | solution.py:15
  86.7 5.7 %collective-permute-start.12 = (bf16[4,129,1024]{2,0,1:T(4,128)(2,1)S(1)}, bf16[4,129,1024]{2,0,1:T(4,128)(2,1)S(1)}, u32[]{:S(2)}, u32[]{:S(2)}) collective-permute-start(bf16[4,129,1024]{2,0,1:T(4,128)(2,1)S(1)} %copy.107), channel_id=1, source_target_pairs={{0,16},{16,0},{1,17},{17,1},{2,18},{18,2},{3,19},{19,3},{4,20},{20... | collective-permute-start | bytes 3170312 | tf_op jit(solution)/shard_map/ppermute | solution.py:15
  100.8 2.8 %copy-start = (bf16[2,4,129,1024]{3,1,2,0:T(4,128)(2,1)}, bf16[2,4,129,1024]{3,1,2,0:T(4,128)(2,1)S(1)}, u32[]{:S(2)}) copy-start(bf16[2,4,129,1024]{3,1,2,0:T(4,128)(2,1)S(1)} %broadcast_select_fusion) | copy-start | bytes 6340612
  118.0 1.8 %slice-start = ((bf16[2,4,129,1024]{3,1,2,0:T(4,128)(2,1)}), bf16[2,4,128,1024]{3,1,2,0:T(4,128)(2,1)S(1)}, s32[]{:S(2)}) async-start(bf16[2,4,129,1024]{3,1,2,0:T(4,128)(2,1)} %copy-done), calls=%async_computation | async-start | bytes 4194304 | tf_op jit(solution)/shard_map/slice | solution.py:183

commit v8 on v7

--- a/solution.py
+++ b/solution.py
@@ -7,19 +7,36 @@
 ALL_AXES = ("dp", "ctx", "expert")
 
 
+def place(received, sources, count):
+    out = jnp.zeros((count,) + received[0].shape, received[0].dtype)
+    for block, source in zip(received, sources):
+        out = lax.dynamic_update_index_in_dim(out, block, source, axis=0)
+    return out
+
+
 def gather_blocks(value, axis_name, count):
     me = lax.axis_index(axis_name)
     received = [value]
+    sources = [me]
     for shift in range(1, count):
         perm = [(i, (i + shift) % count) for i in range(count)]
         received.append(lax.ppermute(value, axis_name, perm))
-    order = (me - jnp.arange(count)) % count
-    return jnp.take(jnp.stack(received), order, axis=0)
-
-
-def sum_over(value, axis_name, count):
-    if count & (count - 1) or value.shape[-1] % count:
-        return lax.psum(value, axis_name).astype(jnp.bfloat16)
+        sources.append((me - shift) % count)
+    return place(received, sources, count)
+
+
+def gather_xor(value, axis_name, count):
+    me = lax.axis_index(axis_name)
+    received = [value]
+    sources = [me]
+    for shift in range(1, count):
+        perm = [(i, i ^ shift) for i in range(count)]
+        received.append(lax.ppermute(value, axis_name, perm))
+        sources.append(me ^ shift)
+    return place(received, sources, count)
+
+
+def sum_scatter(value, axis_name, count):
     me = lax.axis_index(axis_name)
     pieces = value.reshape(value.shape[:-1] + (count, value.shape[-1] // count))
     total = lax.dynamic_index_in_dim(pieces, me, axis=-2, keepdims=False)
@@ -27,13 +44,7 @@
         perm = [(i, i ^ shift) for i in range(count)]
         send = lax.dynamic_index_in_dim(pieces, me ^ shift, axis=-2, keepdims=False)
         total = total + lax.ppermute(send, axis_name, perm)
-    total = total.astype(jnp.bfloat16)
-    received = [total]
-    for shift in range(1, count):
-        perm = [(i, i ^ shift) for i in range(count)]
-        received.append(lax.ppermute(total, axis_name, perm))
-    ordered = jnp.take(jnp.stack(received, axis=-2), me ^ jnp.arange(count), axis=-2)
-    return ordered.reshape(value.shape)
+    return total.astype(jnp.bfloat16)
 
 
 def split_exact(value):
@@ -172,26 +183,31 @@
         [partial_value.reshape(seq_count * total_len, col_width), route_row.reshape(extra_rows, col_width)],
         axis=0,
     )
-    summed = sum_over(extended, "expert", group_count)
-    gathered = gather_blocks(gather_blocks(summed, "ctx", ctx_count), "dp", dp_count)
-    gathered = gathered.reshape(dp_count, ctx_count, seq_count * total_len + extra_rows, col_width)
-    routes = gathered[:, :, seq_count * total_len :, :].reshape(dp_count, ctx_count, -1)
-    routes = routes[:, :, : group_count * route_len].astype(jnp.int32)
+    piece_width = col_width // group_count
+    piece = sum_scatter(extended, "expert", group_count)
+    gathered = gather_blocks(piece, "ctx", ctx_count)
+    gathered = gather_xor(gathered, "expert", group_count)
+    gathered = gather_blocks(gathered, "dp", dp_count)
+    row_total = seq_count * total_len
+    extra = jnp.transpose(gathered[:, :, :, row_total:, :], (0, 2, 3, 1, 4))
+    routes = extra.reshape(dp_count, ctx_count, -1)[:, :, : group_count * route_len]
+    routes = routes.astype(jnp.int32)
     routes = routes.reshape(dp_count, ctx_count, group_count, seq_count, per_block, pick_count, 2)
     routes = jnp.transpose(routes, (0, 3, 1, 2, 4, 5, 6))
-    row_total = seq_count * total_len
-    tokens = gathered[:, :, :row_total, :]
+    tokens = gathered[:, :, :, :row_total, :]
     mine_rows = lax.dynamic_index_in_dim(tokens, lax.axis_index("dp"), axis=0, keepdims=False)
-    mine_rows = mine_rows.reshape(ctx_count, seq_count, ctx_count * group_count, per_block, col_width)
+    mine_rows = mine_rows.reshape(
+        group_count, ctx_count, seq_count, ctx_count * group_count, per_block, piece_width
+    )
     mine_block = lax.axis_index("ctx") * group_count + lax.axis_index("expert")
-    mine_rows = lax.dynamic_index_in_dim(mine_rows, mine_block, axis=2, keepdims=False)
-    mamba_out = jnp.transpose(mine_rows, (1, 2, 0, 3)).reshape(seq_count, per_block, model_width)
+    mine_rows = lax.dynamic_index_in_dim(mine_rows, mine_block, axis=3, keepdims=False)
+    mamba_out = jnp.transpose(mine_rows, (2, 3, 1, 0, 4)).reshape(seq_count, per_block, model_width)
     token_count = dp_count * row_total
     flat = tokens.astype(jnp.float32)
-    square_sum = jnp.sum(flat * flat, axis=(1, 3), keepdims=True)
+    square_sum = jnp.sum(flat * flat, axis=(1, 2, 4), keepdims=True)
     scale = lax.rsqrt(square_sum / model_width + 1e-05)
-    gain = moe_gain.reshape(1, ctx_count, 1, col_width)
-    normed = (flat * scale * gain).astype(jnp.bfloat16)
+    gain = jnp.transpose(moe_gain.reshape(ctx_count, group_count, piece_width), (1, 0, 2))
+    normed = (flat * scale * gain[None, :, :, None, :]).astype(jnp.bfloat16)
 
     group = (
         (jnp.arange(dp_count)[:, None, None, None, None] * ctx_count
@@ -205,7 +221,7 @@
     hit = mine[..., None] & (target[..., None] == jnp.arange(slot_count))
     selector = jnp.any(hit, axis=1).reshape(dp_count, row_total, slot_count)
     dispatched = jnp.einsum(
-        "drq,dcrk->qck", selector.astype(jnp.bfloat16), normed, preferred_element_type=jnp.float32
+        "drq,decrk->qcek", selector.astype(jnp.bfloat16), normed, preferred_element_type=jnp.float32
     ).astype(jnp.bfloat16)
     hidden = expert_ffn(gate_up, dispatched.reshape(slot_count, model_width))
     return (mamba_out, hidden[None])

time: 121 us -> 127 us (1.050)
  the two profiles are of different devices: /device:TPU:27 before, /device:TPU:0 now
where the time goes in v8:
time: 127 us
  local copies, waits for them, and re-layouts  50.3 us (40%)
  waiting for transfers between devices  26.6 us (21%)
  starting transfers between devices  23.5 us (19%)
  matrix products  18.6 us (15%)
  other arithmetic  6.68 us (5%)
  between operations  1.27 us (1%)
    dynamic_update_slice x13, local copies, waits for them, and re-layouts, place(): out = lax.dynamic_update_index_in_dim(out, block, source, axis=0)  32.8 us
    ppermute x7, waiting for transfers between devices, gather_blocks(): received.append(lax.ppermute(value, axis_name, perm))  20.2 us
    ppermute x7, starting transfers between devices, gather_blocks(): received.append(lax.ppermute(value, axis_name, perm))  16.3 us
    dot_general x1, matrix products, expert_ffn(): jnp.einsum('gfd,qd->gfq', gate_up[0], slot_rows, preferred_element_type=j...  8.37 us
    ppermute x3, waiting for transfers between devices, sum_scatter(): total = total + lax.ppermute(send, axis_name, perm)  6.13 us
    dot_general x1, matrix products, mixer(): ssd = jnp.einsum('sktuh,skuhp->skthp', kernel, x_float, precision=highest)  4.14 us
    ppermute x3, starting transfers between devices, sum_scatter(): total = total + lax.ppermute(send, axis_name, perm)  3.68 us
    ppermute x3, starting transfers between devices, gather_xor(): received.append(lax.ppermute(value, axis_name, perm))  3.55 us
  transfers between devices with their start and end apart: 13, of which 8 were waited for; matrix products, arithmetic and copies ran while one was open for 10% of the time, Pallas kernels for 0%

profile of v8, /device:TPU:0, one launch (start us, length us, event | category | flops | bytes accessed | tf_op | source)
XLA Modules:
  0.0 127.0 jit_solution(7699459062751565219)
XLA Ops:
  3.9 3.1 %collective-permute-start = (bf16[2,16,4448]{2,1,0:T(8,128)(2,1)S(1)}, bf16[2,16,4448]{2,1,0:T(8,128)(2,1)S(1)}, u32[]{:S(2)}, u32[]{:S(2)}) collective-permute-start(bf16[2,16,4448]{2,1,0:T(8,128)(2,1)S(1)} %concatenate.11), channel_id=1, source_target_pairs={{0,4},{4,8},{8,12},{12,0},{1,5},{5,9},{9,13},{13,1},{2,6},{6,10},{... | collective-permute-start | bytes 854024 | tf_op jit(solution)/shard_map/ppermute | solution.py:23
  7.0 2.6 %collective-permute-start.1 = (bf16[2,16,4448]{2,1,0:T(8,128)(2,1)S(1)}, bf16[2,16,4448]{2,1,0:T(8,128)(2,1)S(1)}, u32[]{:S(2)}, u32[]{:S(2)}) collective-permute-start(bf16[2,16,4448]{2,1,0:T(8,128)(2,1)S(1)} %concatenate.11), channel_id=1, source_target_pairs={{0,8},{4,12},{8,0},{12,4},{1,9},{5,13},{9,1},{13,5},{2,10},{6,14},... | collective-permute-start | bytes 854024 | tf_op jit(solution)/shard_map/ppermute | solution.py:23
  12.8 4.1 %collective-permute-done = bf16[2,16,4448]{2,1,0:T(8,128)(2,1)S(1)} collective-permute-done((bf16[2,16,4448]{2,1,0:T(8,128)(2,1)S(1)}, bf16[2,16,4448]{2,1,0:T(8,128)(2,1)S(1)}, u32[]{:S(2)}, u32[]{:S(2)}) %collective-permute-start) | collective-permute-done | bytes 284704 | tf_op jit(solution)/shard_map/ppermute | solution.py:23
  16.9 11.4 %collective-permute-done.1 = bf16[2,16,4448]{2,1,0:T(8,128)(2,1)S(1)} collective-permute-done((bf16[2,16,4448]{2,1,0:T(8,128)(2,1)S(1)}, bf16[2,16,4448]{2,1,0:T(8,128)(2,1)S(1)}, u32[]{:S(2)}, u32[]{:S(2)}) %collective-permute-start.1) | collective-permute-done | bytes 284704 | tf_op jit(solution)/shard_map/ppermute | solution.py:23
  28.7 2.0 %copy.189 = f32[2,64,2048]{1,2,0:T(8,128)} copy(f32[2,64,2048]{2,1,0:T(8,128)S(1)} %get-tuple-element.19) | data formatting | bytes 2097152 | tf_op jit(solution)/shard_map/reshape | solution.py:70
  32.2 4.1 %bitcast_add_fusion = f32[2,1,64,32,64]{2,4,3,0,1:T(8,128)S(1)} fusion(f32[2,1,64,32,64]{2,4,3,0,1:T(8,128)} %bitcast.112, bf16[2,64,32,64]{1,3,2,0:T(8,128)(2,1)} %bitcast.117, f32[32]{0:T(128)S(1)} %copy-done.4, f32[2,64,64]{2,1,0:T(8,128)S(1)} %fusion.41, f32[2,64,32]{1,2,0:T(8,128)S(1)} %copy.161, pred[64,64]{1,0:T(8,128)(4,1)S(1)} %iota_compare_fusion.1), kind=kOutput, calls=%fused_computation.10 | convolution fusion | flops 202899456 | bytes 2674816 | tf_op jit(solution)/shard_map/sktuh,skuhp->skthp/dot_general | solution.py:78
  36.3 1.6 %copy.190 = f32[2,64,2048]{2,1,0:T(8,128)} copy(f32[2,64,2048]{1,2,0:T(8,128)S(1)} %bitcast.113) | data formatting | bytes 2097152 | tf_op jit(solution)/shard_map/reshape | solution.py:98
  37.9 3.3 %fusion.5 = f32[2,64,1024]{2,1,0:T(8,128)S(1)} fusion(bf16[2048,1024]{1,0:T(8,128)(2,1)} %param.17, f32[2,64,2048]{2,1,0:T(8,128)} %copy.190, bf16[2,64,4448]{2,1,0:T(8,128)(2,1)S(1)} %bitcast.111), kind=kOutput, calls=%fused_computation.8 | convolution fusion | flops 538705920 | bytes 6291456 | tf_op jit(solution)/shard_map/stk,kd->std/dot_general | solution.py:171
  42.0 1.6 %collective-permute-start.3 = (f32[129,256]{1,0:T(8,128)S(1)}, f32[129,256]{1,0:T(8,128)S(1)}, u32[]{:S(2)}, u32[]{:S(2)}) collective-permute-start(f32[129,256]{1,0:T(8,128)S(1)} %bitcast.124), channel_id=1, source_target_pairs={{0,1},{1,0},{2,3},{3,2},{4,5},{5,4},{6,7},{7,6},{8,9},{9,8},{10,11... | collective-permute-start | bytes 396296 | tf_op jit(solution)/shard_map/ppermute | solution.py:46
  43.6 1.6 %collective-permute-start.4 = (f32[129,256]{1,0:T(8,128)S(1)}, f32[129,256]{1,0:T(8,128)S(1)}, u32[]{:S(2)}, u32[]{:S(2)}) collective-permute-start(f32[129,256]{1,0:T(8,128)S(1)} %bitcast.125), channel_id=1, source_target_pairs={{0,2},{1,3},{2,0},{3,1},{4,6},{5,7},{6,4},{7,5},{8,10},{9,11},{10,... | collective-permute-start | bytes 396296 | tf_op jit(solution)/shard_map/ppermute | solution.py:46
  45.7 2.3 %collective-permute-done.3 = f32[129,256]{1,0:T(8,128)S(1)} collective-permute-done((f32[129,256]{1,0:T(8,128)S(1)}, f32[129,256]{1,0:T(8,128)S(1)}, u32[]{:S(2)}, u32[]{:S(2)}) %collective-permute-start.3) | collective-permute-done | bytes 132128 | tf_op jit(solution)/shard_map/ppermute | solution.py:46
  48.0 3.8 %collective-permute-done.4 = f32[129,256]{1,0:T(8,128)S(1)} collective-permute-done((f32[129,256]{1,0:T(8,128)S(1)}, f32[129,256]{1,0:T(8,128)S(1)}, u32[]{:S(2)}, u32[]{:S(2)}) %collective-permute-start.4) | collective-permute-done | bytes 132128 | tf_op jit(solution)/shard_map/ppermute | solution.py:46
  51.9 6.7 %collective-permute-start.6 = (bf16[129,256]{1,0:T(8,128)(2,1)S(1)}, bf16[129,256]{1,0:T(8,128)(2,1)S(1)}, u32[]{:S(2)}, u32[]{:S(2)}) collective-permute-start(bf16[129,256]{1,0:T(8,128)(2,1)S(1)} %get-tuple-element.17), channel_id=1, source_target_pairs={{0,4},{4,8},{8,12},{12,0},{1,5},{5,9},{9,13},{13,1},{2,6},{6,10},{... | collective-permute-start | bytes 198152 | tf_op jit(solution)/shard_map/ppermute | solution.py:23
  62.0 3.0 %collective-permute-done.7 = bf16[129,256]{1,0:T(8,128)(2,1)S(1)} collective-permute-done((bf16[129,256]{1,0:T(8,128)(2,1)S(1)}, bf16[129,256]{1,0:T(8,128)(2,1)S(1)}, u32[]{:S(2)}, u32[]{:S(2)}) %collective-permute-start.7) | collective-permute-done | bytes 66080 | tf_op jit(solution)/shard_map/ppermute | solution.py:23
  66.9 1.7 %collective-permute-start.11 = (bf16[4,129,256]{2,1,0:T(8,128)(2,1)S(1)}, bf16[4,129,256]{2,1,0:T(8,128)(2,1)S(1)}, u32[]{:S(2)}, u32[]{:S(2)}) collective-permute-start(bf16[4,129,256]{2,1,0:T(8,128)(2,1)S(1)} %bitcast_dynamic-update-slice_fusion.6), channel_id=1, source_target_pairs={{0,3},{1,2},{2,1},{3,0},{4,7},{5,6},{6,5},{7,4},{8,11},{9,10},{10,... | collective-permute-start | bytes 792584 | tf_op jit(solution)/shard_map/ppermute | solution.py:34
  69.2 7.8 %dynamic_update_slice.59 = bf16[4,4,129,256]{3,0,1,2:T(4,128)(2,1)S(1)} dynamic-update-slice(bf16[4,4,129,256]{3,0,1,2:T(4,128)(2,1)S(1)} %broadcast_in_dim.101, bf16[1,4,129,256]{3,0,1,2:T(2,128)(2,1)S(1)} %copy.167, s32[]{:T(128)S(6)} %select_n.100, s32[]{:T(128)} %constant.128.clone.1, s32[]{:T(128)} %constant.128.clone.1, s32[]{:T(128)} %constant.128.clone.1) | dynamic-update-slice | bytes 528388 | tf_op jit(solution)/shard_map/jit(dynamic_update_index_in_dim)/dynamic_update_slice | solution.py:13
  78.6 7.6 %dynamic_update_slice.60 = bf16[4,4,129,256]{3,0,1,2:T(4,128)(2,1)S(1)} dynamic-update-slice(bf16[4,4,129,256]{3,0,1,2:T(4,128)(2,1)S(1)} %dynamic_update_slice.59, bf16[1,4,129,256]{3,0,1,2:T(2,128)(2,1)S(1)} %copy.168, s32[]{:T(128)S(6)} %select_n.101, s32[]{:T(128)} %constant.128.clone.1, s32[]{:T(128)} %constant.128.clone.1, s32[]{:T(128)} %constant.128.clone.1) | dynamic-update-slice | bytes 528388 | tf_op jit(solution)/shard_map/jit(dynamic_update_index_in_dim)/dynamic_update_slice | solution.py:13
  86.2 7.6 %dynamic_update_slice.61 = bf16[4,4,129,256]{3,0,1,2:T(4,128)(2,1)S(1)} dynamic-update-slice(bf16[4,4,129,256]{3,0,1,2:T(4,128)(2,1)S(1)} %dynamic_update_slice.60, bf16[1,4,129,256]{3,0,1,2:T(2,128)(2,1)S(1)} %copy.169, s32[]{:T(128)S(6)} %select_n.102, s32[]{:T(128)} %constant.128.clone.1, s32[]{:T(128)} %constant.128.clone.1, s32[]{:T(128)} %constant.128.clone.1) | dynamic-update-slice | bytes 528388 | tf_op jit(solution)/shard_map/jit(dynamic_update_index_in_dim)/dynamic_update_slice | solution.py:13
  93.8 7.6 %dynamic_update_slice.62 = bf16[4,4,129,256]{3,0,1,2:T(4,128)(2,1)S(1)} dynamic-update-slice(bf16[4,4,129,256]{3,0,1,2:T(4,128)(2,1)S(1)} %dynamic_update_slice.61, bf16[1,4,129,256]{3,0,1,2:T(2,128)(2,1)S(1)} %copy.170, s32[]{:T(128)S(6)} %select_n.103, s32[]{:T(128)} %constant.128.clone.1, s32[]{:T(128)} %constant.128.clone.1, s32[]{:T(128)} %constant.128.clone.1) | dynamic-update-slice | bytes 528388 | tf_op jit(solution)/shard_map/jit(dynamic_update_index_in_dim)/dynamic_update_slice | solution.py:13
  104.2 1.7 %bitcast_dynamic-update-slice_fusion.1 = bf16[2,4,4,129,256]{4,1,2,0,3:T(4,128)(2,1)S(1)} fusion(bf16[2,4,4,129,256]{4,1,2,0,3:T(4,128)(2,1)S(1)} %bitcast_dynamic-update-slice_fusion, s32[]{:T(128)S(6)} %select_n.106, bf16[4,4,129,256]{3,0,1,2:T(4,128)(2,1)} %collective-permute-done.12), kind=kLoop, calls=%fused_computation.23 | loop fusion | bytes 2113540 | tf_op jit(solution)/shard_map/jit(dynamic_update_index_in_dim)/dynamic_update_slice | solution.py:13
  106.0 1.5 %fusion.2 = f32[2,128]{0,1:T(8,128)S(1)} fusion(bf16[2,4,4,129,256]{4,1,2,0,3:T(4,128)(2,1)S(1)} %bitcast_dynamic-update-slice_fusion.1), kind=kLoop, calls=%fused_computation.4 | loop fusion | flops 3145472 | bytes 2098176 | tf_op jit(solution)/shard_map/reduce_sum | solution.py:207
  108.3 2.3 %slice.63 = bf16[2,4,4,128,256]{4,1,2,0,3:T(4,128)(2,1)} slice(bf16[2,4,4,129,256]{4,1,2,0,3:T(4,128)(2,1)S(1)} %bitcast_dynamic-update-slice_fusion.1), slice={[0:2], [0:4], [0:4], [0:128], [0:256]} | slice | bytes 4194304 | tf_op jit(solution)/shard_map/slice | solution.py:197
  112.4 2.6 %fusion.14 = bf16[256,4,4,256]{0,3,1,2:T(8,128)(2,1)S(1)} fusion(pred[2,128,256,1,1]{2,1,0,4,3:T(8,128)(4,1)S(1)} %bitcast.128, bf16[2,4,4,128,256]{4,1,2,0,3:T(4,128)(2,1)S(1)} %fusion.4), kind=kOutput, calls=%fused_computation.18 | convolution fusion | flops 537919488 | bytes 4259840 | tf_op jit(solution)/shard_map/drq,decrk->qcek/dot_general | solution.py:223
  115.2 8.4 %fusion.19 = f32[2,896,256]{1,2,0:T(8,128)S(1)} fusion(bf16[256,4096,1]{0,1,2:T(8,128)(2,1)S(1)} %bitcast.114, bf16[1,2,896,4096]{3,2,1,0:T(8,128)(2,1)} %param.19), kind=kOutput, calls=%fused_computation.19 | convolution fusion | flops 3758096384 | bytes 18612224 | tf_op jit(solution)/shard_map/gfd,qd->gfq/dot_general | solution.py:102
  (97 shorter events, 25.9 us)
Async XLA Ops:
  0.6 10.5 %copy-start.3 = (s32[2,4,2]{1,2,0:T(2,128)S(1)}, s32[2,4,2]{1,2,0:T(2,128)}, u32[]{:S(2)}) copy-start(s32[2,4,2]{1,2,0:T(2,128)} %param.20) | copy-start | bytes 196
  0.6 10.5 %copy-start.2 = (s32[2,4,2]{1,2,0:T(2,128)S(1)}, s32[2,4,2]{1,2,0:T(2,128)}, u32[]{:S(2)}) copy-start(s32[2,4,2]{1,2,0:T(2,128)} %param.21) | copy-start | bytes 196
  3.9 13.0 %collective-permute-start = (bf16[2,16,4448]{2,1,0:T(8,128)(2,1)S(1)}, bf16[2,16,4448]{2,1,0:T(8,128)(2,1)S(1)}, u32[]{:S(2)}, u32[]{:S(2)}) collective-permute-start(bf16[2,16,4448]{2,1,0:T(8,128)(2,1)S(1)} %concatenate.11), channel_id=1, source_target_pairs={{0,4},{4,8},{8,12},{12,0},{1,5},{5,9},{9,13},{13,1},{2,6},{6,10},{... | collective-permute-start | bytes 854024 | tf_op jit(solution)/shard_map/ppermute | solution.py:23
  7.0 21.3 %collective-permute-start.1 = (bf16[2,16,4448]{2,1,0:T(8,128)(2,1)S(1)}, bf16[2,16,4448]{2,1,0:T(8,128)(2,1)S(1)}, u32[]{:S(2)}, u32[]{:S(2)}) collective-permute-start(bf16[2,16,4448]{2,1,0:T(8,128)(2,1)S(1)} %concatenate.11), channel_id=1, source_target_pairs={{0,8},{4,12},{8,0},{12,4},{1,9},{5,13},{9,1},{13,5},{2,10},{6,14},... | collective-permute-start | bytes 854024 | tf_op jit(solution)/shard_map/ppermute | solution.py:23
  9.6 18.7 %collective-permute-start.2 = (bf16[2,16,4448]{2,1,0:T(8,128)(2,1)S(1)}, bf16[2,16,4448]{2,1,0:T(8,128)(2,1)S(1)}, u32[]{:S(2)}, u32[]{:S(2)}) collective-permute-start(bf16[2,16,4448]{2,1,0:T(8,128)(2,1)S(1)} %concatenate.11), channel_id=1, source_target_pairs={{0,12},{4,0},{8,4},{12,8},{1,13},{5,1},{9,5},{13,9},{2,14},{6,2},{... | collective-permute-start | bytes 854024 | tf_op jit(solution)/shard_map/ppermute | solution.py:23
  28.7 3.5 %copy-start.4 = (f32[32]{0:T(128)S(1)}, f32[32]{0:T(128)}, u32[]{:S(2)}) copy-start(f32[32]{0:T(128)} %param.16) | copy-start | bytes 388
  42.0 6.0 %collective-permute-start.3 = (f32[129,256]{1,0:T(8,128)S(1)}, f32[129,256]{1,0:T(8,128)S(1)}, u32[]{:S(2)}, u32[]{:S(2)}) collective-permute-start(f32[129,256]{1,0:T(8,128)S(1)} %bitcast.124), channel_id=1, source_target_pairs={{0,1},{1,0},{2,3},{3,2},{4,5},{5,4},{6,7},{7,6},{8,9},{9,8},{10,11... | collective-permute-start | bytes 396296 | tf_op jit(solution)/shard_map/ppermute | solution.py:46
  43.6 8.3 %collective-permute-start.4 = (f32[129,256]{1,0:T(8,128)S(1)}, f32[129,256]{1,0:T(8,128)S(1)}, u32[]{:S(2)}, u32[]{:S(2)}) collective-permute-start(f32[129,256]{1,0:T(8,128)S(1)} %bitcast.125), channel_id=1, source_target_pairs={{0,2},{1,3},{2,0},{3,1},{4,6},{5,7},{6,4},{7,5},{8,10},{9,11},{10,... | collective-permute-start | bytes 396296 | tf_op jit(solution)/shard_map/ppermute | solution.py:46
  45.2 6.7 %collective-permute-start.5 = (f32[129,256]{1,0:T(8,128)S(1)}, f32[129,256]{1,0:T(8,128)S(1)}, u32[]{:S(2)}, u32[]{:S(2)}) collective-permute-start(f32[129,256]{1,0:T(8,128)S(1)} %bitcast.126), channel_id=1, source_target_pairs={{0,3},{1,2},{2,1},{3,0},{4,7},{5,6},{6,5},{7,4},{8,11},{9,10},{10,... | collective-permute-start | bytes 396296 | tf_op jit(solution)/shard_map/ppermute | solution.py:46
  51.9 10.1 %collective-permute-start.6 = (bf16[129,256]{1,0:T(8,128)(2,1)S(1)}, bf16[129,256]{1,0:T(8,128)(2,1)S(1)}, u32[]{:S(2)}, u32[]{:S(2)}) collective-permute-start(bf16[129,256]{1,0:T(8,128)(2,1)S(1)} %get-tuple-element.17), channel_id=1, source_target_pairs={{0,4},{4,8},{8,12},{12,0},{1,5},{5,9},{9,13},{13,1},{2,6},{6,10},{... | collective-permute-start | bytes 198152 | tf_op jit(solution)/shard_map/ppermute | solution.py:23
  58.6 6.3 %collective-permute-start.7 = (bf16[129,256]{1,0:T(8,128)(2,1)S(1)}, bf16[129,256]{1,0:T(8,128)(2,1)S(1)}, u32[]{:S(2)}, u32[]{:S(2)}) collective-permute-start(bf16[129,256]{1,0:T(8,128)(2,1)S(1)} %get-tuple-element.17), channel_id=1, source_target_pairs={{0,8},{4,12},{8,0},{12,4},{1,9},{5,13},{9,1},{13,5},{2,10},{6,14},... | collective-permute-start | bytes 198152 | tf_op jit(solution)/shard_map/ppermute | solution.py:23
  60.0 5.0 %collective-permute-start.8 = (bf16[129,256]{1,0:T(8,128)(2,1)S(1)}, bf16[129,256]{1,0:T(8,128)(2,1)S(1)}, u32[]{:S(2)}, u32[]{:S(2)}) collective-permute-start(bf16[129,256]{1,0:T(8,128)(2,1)S(1)} %get-tuple-element.17), channel_id=1, source_target_pairs={{0,12},{4,0},{8,4},{12,8},{1,13},{5,1},{9,5},{13,9},{2,14},{6,2},{... | collective-permute-start | bytes 198152 | tf_op jit(solution)/shard_map/ppermute | solution.py:23
  65.0 12.0 %collective-permute-start.9 = (bf16[4,129,256]{2,1,0:T(8,128)(2,1)S(1)}, bf16[4,129,256]{2,1,0:T(8,128)(2,1)S(1)}, u32[]{:S(2)}, u32[]{:S(2)}) collective-permute-start(bf16[4,129,256]{2,1,0:T(8,128)(2,1)S(1)} %bitcast_dynamic-update-slice_fusion.6), channel_id=1, source_target_pairs={{0,1},{1,0},{2,3},{3,2},{4,5},{5,4},{6,7},{7,6},{8,9},{9,8},{10,11... | collective-permute-start | bytes 792584 | tf_op jit(solution)/shard_map/ppermute | solution.py:34
  66.0 11.4 %collective-permute-start.10 = (bf16[4,129,256]{2,1,0:T(8,128)(2,1)S(1)}, bf16[4,129,256]{2,1,0:T(8,128)(2,1)S(1)}, u32[]{:S(2)}, u32[]{:S(2)}) collective-permute-start(bf16[4,129,256]{2,1,0:T(8,128)(2,1)S(1)} %bitcast_dynamic-update-slice_fusion.6), channel_id=1, source_target_pairs={{0,2},{1,3},{2,0},{3,1},{4,6},{5,7},{6,4},{7,5},{8,10},{9,11},{10,... | collective-permute-start | bytes 792584 | tf_op jit(solution)/shard_map/ppermute | solution.py:34
  66.9 11.3 %collective-permute-start.11 = (bf16[4,129,256]{2,1,0:T(8,128)(2,1)S(1)}, bf16[4,129,256]{2,1,0:T(8,128)(2,1)S(1)}, u32[]{:S(2)}, u32[]{:S(2)}) collective-permute-start(bf16[4,129,256]{2,1,0:T(8,128)(2,1)S(1)} %bitcast_dynamic-update-slice_fusion.6), channel_id=1, source_target_pairs={{0,3},{1,2},{2,1},{3,0},{4,7},{5,6},{6,5},{7,4},{8,11},{9,10},{10,... | collective-permute-start | bytes 792584 | tf_op jit(solution)/shard_map/ppermute | solution.py:34
  77.9 23.6 %copy-start.1 = (f32[4096]{0:T(1024)S(1)}, f32[4096]{0:T(1024)}, u32[]{:S(2)}) copy-start(f32[4096]{0:T(1024)} %param.18) | copy-start | bytes 49156
  101.4 2.9 %collective-permute-start.12 = (bf16[4,4,129,256]{3,0,1,2:T(4,128)(2,1)S(1)}, bf16[4,4,129,256]{3,0,1,2:T(4,128)(2,1)}, u32[]{:S(2)}, u32[]{:S(2)}) collective-permute-start(bf16[4,4,129,256]{3,0,1,2:T(4,128)(2,1)S(1)} %dynamic_update_slice.62), channel_id=1, source_target_pairs={{0,16},{16,0},{1,17},{17,1},{2,18},{18,2},{3,19},{19,3},{4,20},{20... | collective-permute-start | bytes 3170312 | tf_op jit(solution)/shard_map/ppermute | solution.py:23
  123.5 1.8 %copy-start = (bf16[2,4,4,128,256]{4,1,2,0,3:T(4,128)(2,1)S(1)}, bf16[2,4,4,128,256]{4,1,2,0,3:T(4,128)(2,1)}, u32[]{:S(2)}) copy-start(bf16[2,4,4,128,256]{4,1,2,0,3:T(4,128)(2,1)} %slice.63) | copy-start | bytes 6291460

commit v9 on v8

--- a/solution.py
+++ b/solution.py
@@ -8,10 +8,13 @@
 
 
 def place(received, sources, count):
-    out = jnp.zeros((count,) + received[0].shape, received[0].dtype)
-    for block, source in zip(received, sources):
-        out = lax.dynamic_update_index_in_dim(out, block, source, axis=0)
-    return out
+    slots = []
+    for slot in range(count):
+        block = received[0]
+        for other, source in zip(received[1:], sources[1:]):
+            block = jnp.where(source == slot, other, block)
+        slots.append(block)
+    return jnp.stack(slots)
 
 
 def gather_blocks(value, axis_name, count):

time: 127 us -> 102 us (0.80)
  local copies, waits for them, and re-layouts: 50.3 us -> 12.7 us
  waiting for transfers between devices: 26.6 us -> 42.3 us
  starting transfers between devices: 23.5 us -> 18.3 us
  other arithmetic: 6.68 us -> 8.86 us
    dynamic_update_slice x13 -> x0, local copies, waits for them, and re-layouts: 32.8 us -> none  [place(): out = lax.dynamic_update_index_in_dim(out, block, source, axis=0)]
    ppermute x3, waiting for transfers between devices: 0.33 us -> 8.71 us  [gather_xor(): received.append(lax.ppermute(value, axis_name, perm))]
    ppermute x7, waiting for transfers between devices: 20.2 us -> 27.6 us  [gather_blocks(): received.append(lax.ppermute(value, axis_name, perm))]
    ppermute x7, starting transfers between devices: 16.3 us -> 11.1 us  [gather_blocks(): received.append(lax.ppermute(value, axis_name, perm))]
    broadcast_in_dim x8 -> x0, local copies, waits for them, and re-layouts: 3.06 us -> none  [the longest x4 1.64 us: place(): out = lax.dynamic_update_index_in_dim(out, block, source, axis=0)]
    another operation x0 -> x8, other arithmetic: none -> 2.29 us  [place(): return jnp.stack(slots)]
  transfers between devices with their start and end apart: 13 -> 13, of which waited for: 8 -> 9; matrix products, arithmetic and copies ran while one was open for 10% -> 3% of each run, Pallas kernels for 0% -> 0%
where the time goes in v9:
time: 102 us; the launch traced here: 101 us
  waiting for transfers between devices  42.3 us (41%)
  starting transfers between devices  18.3 us (18%)
  matrix products  18.2 us (18%)
  local copies, waits for them, and re-layouts  12.7 us (12%)
  other arithmetic  8.86 us (9%)
  between operations  1.07 us (1%)
    ppermute x7, waiting for transfers between devices, gather_blocks(): received.append(lax.ppermute(value, axis_name, perm))  27.6 us
    ppermute x7, starting transfers between devices, gather_blocks(): received.append(lax.ppermute(value, axis_name, perm))  11.1 us
    ppermute x3, waiting for transfers between devices, gather_xor(): received.append(lax.ppermute(value, axis_name, perm))  8.71 us
    dot_general x1, matrix products, expert_ffn(): jnp.einsum('gfd,qd->gfq', gate_up[0], slot_rows, preferred_element_type=j...  8.15 us
    ppermute x3, waiting for transfers between devices, sum_scatter(): total = total + lax.ppermute(send, axis_name, perm)  5.94 us
    dot_general x1, matrix products, mixer(): ssd = jnp.einsum('sktuh,skuhp->skthp', kernel, x_float, precision=highest)  4.14 us
    ppermute x3, starting transfers between devices, sum_scatter(): total = total + lax.ppermute(send, axis_name, perm)  3.68 us
    ppermute x3, starting transfers between devices, gather_xor(): received.append(lax.ppermute(value, axis_name, perm))  3.55 us
  transfers between devices with their start and end apart: 13, of which 9 were waited for; matrix products, arithmetic and copies ran while one was open for 3% of the time, Pallas kernels for 0%

profile of v9, /device:TPU:0, one launch (start us, length us, event | category | flops | bytes accessed | tf_op | source)
XLA Modules:
  0.0 101.4 jit_solution(10696824183283842923)
XLA Ops:
  3.9 5.1 %collective-permute-start = (bf16[2,16,4448]{2,1,0:T(8,128)(2,1)S(1)}, bf16[2,16,4448]{2,1,0:T(8,128)(2,1)S(1)}, u32[]{:S(2)}, u32[]{:S(2)}) collective-permute-start(bf16[2,16,4448]{2,1,0:T(8,128)(2,1)S(1)} %concatenate.11), channel_id=1, source_target_pairs={{0,12},{4,0},{8,4},{12,8},{1,13},{5,1},{9,5},{13,9},{2,14},{6,2},{... | collective-permute-start | bytes 854024 | tf_op jit(solution)/shard_map/ppermute | solution.py:26
  12.3 3.9 %collective-permute-done = bf16[2,16,4448]{2,1,0:T(8,128)(2,1)S(1)} collective-permute-done((bf16[2,16,4448]{2,1,0:T(8,128)(2,1)S(1)}, bf16[2,16,4448]{2,1,0:T(8,128)(2,1)S(1)}, u32[]{:S(2)}, u32[]{:S(2)}) %collective-permute-start) | collective-permute-done | bytes 284704 | tf_op jit(solution)/shard_map/ppermute | solution.py:26
  16.2 17.2 %collective-permute-done.1 = bf16[2,16,4448]{2,1,0:T(8,128)(2,1)S(1)} collective-permute-done((bf16[2,16,4448]{2,1,0:T(8,128)(2,1)S(1)}, bf16[2,16,4448]{2,1,0:T(8,128)(2,1)S(1)}, u32[]{:S(2)}, u32[]{:S(2)}) %collective-permute-start.1) | collective-permute-done | bytes 284704 | tf_op jit(solution)/shard_map/ppermute | solution.py:26
  34.1 2.0 %copy.150 = f32[2,64,2048]{1,2,0:T(8,128)} copy(f32[2,64,2048]{2,1,0:T(8,128)S(1)} %get-tuple-element.21) | data formatting | bytes 2097152 | tf_op jit(solution)/shard_map/reshape | solution.py:73
  36.1 1.3 %copy.147 = bf16[2,64,2048]{1,2,0:T(8,128)(2,1)} copy(bf16[2,64,2048]{2,1,0:T(8,128)(2,1)S(1)} %get-tuple-element.20) | data formatting | bytes 1048576 | tf_op jit(solution)/shard_map/slice | solution.py:168
  37.6 4.1 %bitcast_add_fusion = f32[2,1,64,32,64]{2,4,3,0,1:T(8,128)S(1)} fusion(f32[2,1,64,32,64]{2,4,3,0,1:T(8,128)} %bitcast.113, bf16[2,64,32,64]{1,3,2,0:T(8,128)(2,1)} %bitcast.117, f32[32]{0:T(128)S(1)} %copy-done.2, f32[2,64,64]{2,1,0:T(8,128)S(1)} %fusion.42, f32[2,64,32]{1,2,0:T(8,128)S(1)} %copy.148, pred[64,64]{1,0:T(8,128)(4,1)S(1)} %iota_compare_fusion.1), kind=kOutput, calls=%fused_computation.14 | convolution fusion | flops 202899456 | bytes 2674816 | tf_op jit(solution)/shard_map/sktuh,skuhp->skthp/dot_general | solution.py:81
  41.7 1.6 %copy.151 = f32[2,64,2048]{2,1,0:T(8,128)} copy(f32[2,64,2048]{1,2,0:T(8,128)S(1)} %bitcast.114) | data formatting | bytes 2097152 | tf_op jit(solution)/shard_map/reshape | solution.py:101
  43.3 3.3 %fusion.5 = f32[2,64,1024]{2,1,0:T(8,128)S(1)} fusion(bf16[2048,1024]{1,0:T(8,128)(2,1)} %param.17, f32[2,64,2048]{2,1,0:T(8,128)} %copy.151, bf16[2,64,4448]{2,1,0:T(8,128)(2,1)S(1)} %bitcast.112), kind=kOutput, calls=%fused_computation.8 | convolution fusion | flops 538705920 | bytes 6291456 | tf_op jit(solution)/shard_map/stk,kd->std/dot_general | solution.py:174
  47.4 1.6 %collective-permute-start.3 = (f32[129,256]{1,0:T(8,128)S(1)}, f32[129,256]{1,0:T(8,128)S(1)}, u32[]{:S(2)}, u32[]{:S(2)}) collective-permute-start(f32[129,256]{1,0:T(8,128)S(1)} %bitcast.121), channel_id=1, source_target_pairs={{0,1},{1,0},{2,3},{3,2},{4,5},{5,4},{6,7},{7,6},{8,9},{9,8},{10,11... | collective-permute-start | bytes 396296 | tf_op jit(solution)/shard_map/ppermute | solution.py:49
  49.0 1.6 %collective-permute-start.4 = (f32[129,256]{1,0:T(8,128)S(1)}, f32[129,256]{1,0:T(8,128)S(1)}, u32[]{:S(2)}, u32[]{:S(2)}) collective-permute-start(f32[129,256]{1,0:T(8,128)S(1)} %bitcast.122), channel_id=1, source_target_pairs={{0,2},{1,3},{2,0},{3,1},{4,6},{5,7},{6,4},{7,5},{8,10},{9,11},{10,... | collective-permute-start | bytes 396296 | tf_op jit(solution)/shard_map/ppermute | solution.py:49
  51.1 2.3 %collective-permute-done.3 = f32[129,256]{1,0:T(8,128)S(1)} collective-permute-done((f32[129,256]{1,0:T(8,128)S(1)}, f32[129,256]{1,0:T(8,128)S(1)}, u32[]{:S(2)}, u32[]{:S(2)}) %collective-permute-start.3) | collective-permute-done | bytes 132128 | tf_op jit(solution)/shard_map/ppermute | solution.py:49
  53.5 3.6 %collective-permute-done.4 = f32[129,256]{1,0:T(8,128)S(1)} collective-permute-done((f32[129,256]{1,0:T(8,128)S(1)}, f32[129,256]{1,0:T(8,128)S(1)}, u32[]{:S(2)}, u32[]{:S(2)}) %collective-permute-start.4) | collective-permute-done | bytes 132128 | tf_op jit(solution)/shard_map/ppermute | solution.py:49
  57.2 2.9 %collective-permute-start.7 = (bf16[129,256]{1,0:T(8,128)(2,1)S(1)}, bf16[129,256]{1,0:T(8,128)(2,1)S(1)}, u32[]{:S(2)}, u32[]{:S(2)}) collective-permute-start(bf16[129,256]{1,0:T(8,128)(2,1)S(1)} %fusion.40), channel_id=1, source_target_pairs={{0,8},{4,12},{8,0},{12,4},{1,9},{5,13},{9,1},{13,5},{2,10},{6,14},... | collective-permute-start | bytes 198152 | tf_op jit(solution)/shard_map/ppermute | solution.py:26
  60.1 1.9 %collective-permute-start.8 = (bf16[129,256]{1,0:T(8,128)(2,1)S(1)}, bf16[129,256]{1,0:T(8,128)(2,1)S(1)}, u32[]{:S(2)}, u32[]{:S(2)}) collective-permute-start(bf16[129,256]{1,0:T(8,128)(2,1)S(1)} %fusion.40), channel_id=1, source_target_pairs={{0,4},{4,8},{8,12},{12,0},{1,5},{5,9},{9,13},{13,1},{2,6},{6,10},{... | collective-permute-start | bytes 198152 | tf_op jit(solution)/shard_map/ppermute | solution.py:26
  62.0 1.8 %collective-permute-done.7 = bf16[129,256]{1,0:T(8,128)(2,1)S(1)} collective-permute-done((bf16[129,256]{1,0:T(8,128)(2,1)S(1)}, bf16[129,256]{1,0:T(8,128)(2,1)S(1)}, u32[]{:S(2)}, u32[]{:S(2)}) %collective-permute-start.7) | collective-permute-done | bytes 66080 | tf_op jit(solution)/shard_map/ppermute | solution.py:26
  63.8 2.4 %collective-permute-done.8 = bf16[129,256]{1,0:T(8,128)(2,1)S(1)} collective-permute-done((bf16[129,256]{1,0:T(8,128)(2,1)S(1)}, bf16[129,256]{1,0:T(8,128)(2,1)S(1)}, u32[]{:S(2)}, u32[]{:S(2)}) %collective-permute-start.8) | collective-permute-done | bytes 66080 | tf_op jit(solution)/shard_map/ppermute | solution.py:26
  68.0 1.9 %collective-permute-start.9 = (bf16[4,129,256]{2,1,0:T(8,128)(2,1)S(1)}, bf16[4,129,256]{2,1,0:T(8,128)(2,1)S(1)}, u32[]{:S(2)}, u32[]{:S(2)}) collective-permute-start(bf16[4,129,256]{2,1,0:T(8,128)(2,1)S(1)} %pad_maximum_fusion.2), channel_id=1, source_target_pairs={{0,3},{1,2},{2,1},{3,0},{4,7},{5,6},{6,5},{7,4},{8,11},{9,10},{10,... | collective-permute-start | bytes 792584 | tf_op jit(solution)/shard_map/ppermute | solution.py:37
  69.8 5.7 %collective-permute-done.10 = bf16[4,129,256]{2,1,0:T(8,128)(2,1)S(1)} collective-permute-done((bf16[4,129,256]{2,1,0:T(8,128)(2,1)S(1)}, bf16[4,129,256]{2,1,0:T(8,128)(2,1)S(1)}, u32[]{:S(2)}, u32[]{:S(2)}) %collective-permute-start.10) | collective-permute-done | bytes 264224 | tf_op jit(solution)/shard_map/ppermute | solution.py:37
  75.6 3.0 %collective-permute-done.9 = bf16[4,129,256]{2,1,0:T(8,128)(2,1)S(1)} collective-permute-done((bf16[4,129,256]{2,1,0:T(8,128)(2,1)S(1)}, bf16[4,129,256]{2,1,0:T(8,128)(2,1)S(1)}, u32[]{:S(2)}, u32[]{:S(2)}) %collective-permute-start.9) | collective-permute-done | bytes 264224 | tf_op jit(solution)/shard_map/ppermute | solution.py:37
  79.8 2.4 %collective-permute-done.12 = bf16[4,4,129,256]{3,1,2,0:T(4,128)(2,1)} collective-permute-done((bf16[4,4,129,256]{3,1,2,0:T(4,128)(2,1)S(1)}, bf16[4,4,129,256]{3,1,2,0:T(4,128)(2,1)}, u32[]{:S(2)}, u32[]{:S(2)}) %collective-permute-start.12) | collective-permute-done | bytes 1056800 | tf_op jit(solution)/shard_map/ppermute | solution.py:26
  82.2 1.5 %select_bitcast_fusion.1 = (bf16[1,4,4,129,256]{4,3,2,1,0:T(8,128)(2,1)S(1)}, bf16[1,4,4,129,256]{4,3,2,1,0:T(8,128)(2,1)S(1)}) fusion(pred[]{:T(512)S(6)} %eq.124, bf16[4,4,129,256]{3,1,2,0:T(4,128)(2,1)} %collective-permute-done.12, bf16[1,4,129,256]{3,2,1,0:T(8,128)(2,1)S(1)} %get-tuple-element.27, bf16[1,4,129,256]{3,2,1,0:T(8,128)(2,1)S(1)} %get-tuple-element.29, ...), kind=kLoop, calls=%fused_computation.29 | loop fusion | flops 2641920 | bytes 4227074 | tf_op jit(solution)/shard_map/stack | solution.py:17
  84.5 2.0 %fusion.2 = (f32[2,128]{1,0:T(2,128)S(1)}, bf16[2,4,4,128,256]{4,3,2,1,0:T(8,128)(2,1)}) fusion(bf16[1,4,4,129,256]{4,3,2,1,0:T(8,128)(2,1)S(1)} %get-tuple-element.19, bf16[1,4,4,129,256]{4,3,2,1,0:T(8,128)(2,1)S(1)} %get-tuple-element.18), kind=kLoop, calls=%fused_computation.4 | loop fusion | flops 4194048 | bytes 4211712 | tf_op jit(solution)/shard_map/reduce_sum | solution.py:210
  87.0 2.5 %fusion.9 = bf16[4,4,256,256,1]{3,2,0,1,4:T(8,128)(2,1)S(1)} fusion(pred[2,128,256,1,1]{2,1,3,4,0:T(8,128)(4,1)S(1)} %bitcast.124, bf16[2,4,4,128,256]{4,3,2,1,0:T(8,128)(2,1)} %get-tuple-element.17, f32[4,4,256]{2,1,0:T(4,128)S(1)} %copy.159, f32[2,128]{1,0:T(2,128)S(1)} %add_rsqrt_fusion), kind=kOutput, calls=%fused_computation.15 | convolution fusion | flops 541065216 | bytes 4277248 | tf_op jit(solution)/shard_map/drq,decrk->qcek/dot_general | solution.py:226
  89.9 8.2 %fusion.19 = f32[2,896,256]{1,2,0:T(8,128)S(1)} fusion(bf16[256,4096,1]{0,1,2:T(8,128)(2,1)S(1)} %bitcast.115, bf16[1,2,896,4096]{3,2,1,0:T(8,128)(2,1)} %param.19), kind=kOutput, calls=%fused_computation.23 | convolution fusion | flops 3758096384 | bytes 18612224 | tf_op jit(solution)/shard_map/gfd,qd->gfq/dot_general | solution.py:105
  (82 shorter events, 16.8 us)
Async XLA Ops:
  3.9 12.4 %collective-permute-start = (bf16[2,16,4448]{2,1,0:T(8,128)(2,1)S(1)}, bf16[2,16,4448]{2,1,0:T(8,128)(2,1)S(1)}, u32[]{:S(2)}, u32[]{:S(2)}) collective-permute-start(bf16[2,16,4448]{2,1,0:T(8,128)(2,1)S(1)} %concatenate.11), channel_id=1, source_target_pairs={{0,12},{4,0},{8,4},{12,8},{1,13},{5,1},{9,5},{13,9},{2,14},{6,2},{... | collective-permute-start | bytes 854024 | tf_op jit(solution)/shard_map/ppermute | solution.py:26
  9.0 24.4 %collective-permute-start.1 = (bf16[2,16,4448]{2,1,0:T(8,128)(2,1)S(1)}, bf16[2,16,4448]{2,1,0:T(8,128)(2,1)S(1)}, u32[]{:S(2)}, u32[]{:S(2)}) collective-permute-start(bf16[2,16,4448]{2,1,0:T(8,128)(2,1)S(1)} %concatenate.11), channel_id=1, source_target_pairs={{0,8},{4,12},{8,0},{12,4},{1,9},{5,13},{9,1},{13,5},{2,10},{6,14},... | collective-permute-start | bytes 854024 | tf_op jit(solution)/shard_map/ppermute | solution.py:26
  9.0 24.4 %collective-permute-start.2 = (bf16[2,16,4448]{2,1,0:T(8,128)(2,1)S(1)}, bf16[2,16,4448]{2,1,0:T(8,128)(2,1)S(1)}, u32[]{:S(2)}, u32[]{:S(2)}) collective-permute-start(bf16[2,16,4448]{2,1,0:T(8,128)(2,1)S(1)} %concatenate.11), channel_id=1, source_target_pairs={{0,4},{4,8},{8,12},{12,0},{1,5},{5,9},{9,13},{13,1},{2,6},{6,10},{... | collective-permute-start | bytes 854024 | tf_op jit(solution)/shard_map/ppermute | solution.py:26
  34.1 3.4 %copy-start.2 = (f32[32]{0:T(128)S(1)}, f32[32]{0:T(128)}, u32[]{:S(2)}) copy-start(f32[32]{0:T(128)} %param.16) | copy-start | bytes 388
  47.4 6.0 %collective-permute-start.3 = (f32[129,256]{1,0:T(8,128)S(1)}, f32[129,256]{1,0:T(8,128)S(1)}, u32[]{:S(2)}, u32[]{:S(2)}) collective-permute-start(f32[129,256]{1,0:T(8,128)S(1)} %bitcast.121), channel_id=1, source_target_pairs={{0,1},{1,0},{2,3},{3,2},{4,5},{5,4},{6,7},{7,6},{8,9},{9,8},{10,11... | collective-permute-start | bytes 396296 | tf_op jit(solution)/shard_map/ppermute | solution.py:49
  49.0 8.1 %collective-permute-start.4 = (f32[129,256]{1,0:T(8,128)S(1)}, f32[129,256]{1,0:T(8,128)S(1)}, u32[]{:S(2)}, u32[]{:S(2)}) collective-permute-start(f32[129,256]{1,0:T(8,128)S(1)} %bitcast.122), channel_id=1, source_target_pairs={{0,2},{1,3},{2,0},{3,1},{4,6},{5,7},{6,4},{7,5},{8,10},{9,11},{10,... | collective-permute-start | bytes 396296 | tf_op jit(solution)/shard_map/ppermute | solution.py:49
  50.6 6.5 %collective-permute-start.5 = (f32[129,256]{1,0:T(8,128)S(1)}, f32[129,256]{1,0:T(8,128)S(1)}, u32[]{:S(2)}, u32[]{:S(2)}) collective-permute-start(f32[129,256]{1,0:T(8,128)S(1)} %bitcast.123), channel_id=1, source_target_pairs={{0,3},{1,2},{2,1},{3,0},{4,7},{5,6},{6,5},{7,4},{8,11},{9,10},{10,... | collective-permute-start | bytes 396296 | tf_op jit(solution)/shard_map/ppermute | solution.py:49
  57.1 4.9 %collective-permute-start.6 = (bf16[129,256]{1,0:T(8,128)(2,1)S(1)}, bf16[129,256]{1,0:T(8,128)(2,1)S(1)}, u32[]{:S(2)}, u32[]{:S(2)}) collective-permute-start(bf16[129,256]{1,0:T(8,128)(2,1)S(1)} %fusion.40), channel_id=1, source_target_pairs={{0,12},{4,0},{8,4},{12,8},{1,13},{5,1},{9,5},{13,9},{2,14},{6,2},{... | collective-permute-start | bytes 198152 | tf_op jit(solution)/shard_map/ppermute | solution.py:26
  57.2 6.6 %collective-permute-start.7 = (bf16[129,256]{1,0:T(8,128)(2,1)S(1)}, bf16[129,256]{1,0:T(8,128)(2,1)S(1)}, u32[]{:S(2)}, u32[]{:S(2)}) collective-permute-start(bf16[129,256]{1,0:T(8,128)(2,1)S(1)} %fusion.40), channel_id=1, source_target_pairs={{0,8},{4,12},{8,0},{12,4},{1,9},{5,13},{9,1},{13,5},{2,10},{6,14},... | collective-permute-start | bytes 198152 | tf_op jit(solution)/shard_map/ppermute | solution.py:26
  60.1 6.1 %collective-permute-start.8 = (bf16[129,256]{1,0:T(8,128)(2,1)S(1)}, bf16[129,256]{1,0:T(8,128)(2,1)S(1)}, u32[]{:S(2)}, u32[]{:S(2)}) collective-permute-start(bf16[129,256]{1,0:T(8,128)(2,1)S(1)} %fusion.40), channel_id=1, source_target_pairs={{0,4},{4,8},{8,12},{12,0},{1,5},{5,9},{9,13},{13,1},{2,6},{6,10},{... | collective-permute-start | bytes 198152 | tf_op jit(solution)/shard_map/ppermute | solution.py:26
  66.3 9.3 %collective-permute-start.10 = (bf16[4,129,256]{2,1,0:T(8,128)(2,1)S(1)}, bf16[4,129,256]{2,1,0:T(8,128)(2,1)S(1)}, u32[]{:S(2)}, u32[]{:S(2)}) collective-permute-start(bf16[4,129,256]{2,1,0:T(8,128)(2,1)S(1)} %pad_maximum_fusion.2), channel_id=1, source_target_pairs={{0,2},{1,3},{2,0},{3,1},{4,6},{5,7},{6,4},{7,5},{8,10},{9,11},{10,... | collective-permute-start | bytes 792584 | tf_op jit(solution)/shard_map/ppermute | solution.py:37
  67.5 8.1 %collective-permute-start.11 = (bf16[4,129,256]{2,1,0:T(8,128)(2,1)S(1)}, bf16[4,129,256]{2,1,0:T(8,128)(2,1)S(1)}, u32[]{:S(2)}, u32[]{:S(2)}) collective-permute-start(bf16[4,129,256]{2,1,0:T(8,128)(2,1)S(1)} %pad_maximum_fusion.2), channel_id=1, source_target_pairs={{0,1},{1,0},{2,3},{3,2},{4,5},{5,4},{6,7},{7,6},{8,9},{9,8},{10,11... | collective-permute-start | bytes 792584 | tf_op jit(solution)/shard_map/ppermute | solution.py:37
  68.0 10.6 %collective-permute-start.9 = (bf16[4,129,256]{2,1,0:T(8,128)(2,1)S(1)}, bf16[4,129,256]{2,1,0:T(8,128)(2,1)S(1)}, u32[]{:S(2)}, u32[]{:S(2)}) collective-permute-start(bf16[4,129,256]{2,1,0:T(8,128)(2,1)S(1)} %pad_maximum_fusion.2), channel_id=1, source_target_pairs={{0,3},{1,2},{2,1},{3,0},{4,7},{5,6},{6,5},{7,4},{8,11},{9,10},{10,... | collective-permute-start | bytes 792584 | tf_op jit(solution)/shard_map/ppermute | solution.py:37
  78.7 1.0 %copy-start.1 = (f32[4096]{0:T(1024)S(1)}, f32[4096]{0:T(1024)}, u32[]{:S(2)}) copy-start(f32[4096]{0:T(1024)} %param.18) | copy-start | bytes 49156
  79.3 2.9 %collective-permute-start.12 = (bf16[4,4,129,256]{3,1,2,0:T(4,128)(2,1)S(1)}, bf16[4,4,129,256]{3,1,2,0:T(4,128)(2,1)}, u32[]{:S(2)}, u32[]{:S(2)}) collective-permute-start(bf16[4,4,129,256]{3,1,2,0:T(4,128)(2,1)S(1)} %copy.153), channel_id=1, source_target_pairs={{0,16},{16,0},{1,17},{17,1},{2,18},{18,2},{3,19},{19,3},{4,20},{20... | collective-permute-start | bytes 3170312 | tf_op jit(solution)/shard_map/ppermute | solution.py:26
  98.0 1.8 %copy-start = (bf16[2,4,4,128,256]{4,3,2,1,0:T(8,128)(2,1)S(1)}, bf16[2,4,4,128,256]{4,3,2,1,0:T(8,128)(2,1)}, u32[]{:S(2)}) copy-start(bf16[2,4,4,128,256]{4,3,2,1,0:T(8,128)(2,1)} %get-tuple-element.17) | copy-start | bytes 6291460

commit v10 on v9

--- a/solution.py
+++ b/solution.py
@@ -156,41 +156,55 @@
     capacity = max(2, 4 * row_count // group_count)
 
     head_count = decay_log.shape[2]
-    packed = jnp.concatenate([x_in, z_in, b_in, c_in] + split_exact(decay_log), axis=2)
-    packed = jnp.moveaxis(gather_blocks(packed, "ctx", ctx_count), 0, 1).reshape(
-        seq_count, ctx_count * block_len, packed.shape[2]
-    )
     decay_base = 2 * width_in + 2 * state_size
-    decay_all = join_exact(
-        [packed[:, :, decay_base + i * head_count : decay_base + (i + 1) * head_count] for i in range(3)]
-    )
-
-    x_all = packed[:, :, :width_in]
-    z_all = packed[:, :, width_in : 2 * width_in]
-    b_all = packed[:, :, 2 * width_in : 2 * width_in + state_size]
-    c_all = packed[:, :, 2 * width_in + state_size : decay_base]
-    ssd = mixer(x_all, b_all, c_all, decay_all, skip)
-    gated = (ssd * jax.nn.silu(z_all.astype(jnp.float32))).astype(jnp.bfloat16)
-    partial_value = jnp.einsum(
-        "stk,kd->std", gated, out_weight, preferred_element_type=jnp.float32
-    )
+
+    def front(x_part, z_part, b_part, c_part, decay_part):
+        part_count = x_part.shape[0]
+        packed = jnp.concatenate([x_part, z_part, b_part, c_part] + split_exact(decay_part), axis=2)
+        packed = jnp.moveaxis(gather_blocks(packed, "ctx", ctx_count), 0, 1).reshape(
+            part_count, ctx_count * block_len, packed.shape[2]
+        )
+        decay_all = join_exact(
+            [packed[:, :, decay_base + i * head_count : decay_base + (i + 1) * head_count] for i in range(3)]
+        )
+        x_all = packed[:, :, :width_in]
+        z_all = packed[:, :, width_in : 2 * width_in]
+        b_all = packed[:, :, 2 * width_in : 2 * width_in + state_size]
+        c_all = packed[:, :, 2 * width_in + state_size : decay_base]
+        ssd = mixer(x_all, b_all, c_all, decay_all, skip)
+        gated = (ssd * jax.nn.silu(z_all.astype(jnp.float32))).astype(jnp.bfloat16)
+        return jnp.einsum("stk,kd->std", gated, out_weight, preferred_element_type=jnp.float32)
+
     if device_count * row_count * model_width * 2 > (8 << 20):
+        partial_value = front(x_in, z_in, b_in, c_in, decay_log)
         return dispatch_routed(partial_value, moe_gain, gate_up, expert_ids, slot_ids, capacity)
-    total_len = partial_value.shape[1]
+    total_len = ctx_count * block_len
     route = jnp.stack([expert_ids, slot_ids], axis=-1).astype(jnp.float32).reshape(-1)
     route_len = route.shape[0]
     extra_rows = -(-(group_count * route_len) // col_width)
     route_row = jnp.zeros((extra_rows * col_width,), jnp.float32)
     route_row = lax.dynamic_update_slice(route_row, route, (lax.axis_index("expert") * route_len,))
-    extended = jnp.concatenate(
-        [partial_value.reshape(seq_count * total_len, col_width), route_row.reshape(extra_rows, col_width)],
-        axis=0,
-    )
     piece_width = col_width // group_count
-    piece = sum_scatter(extended, "expert", group_count)
-    gathered = gather_blocks(piece, "ctx", ctx_count)
-    gathered = gather_xor(gathered, "expert", group_count)
-    gathered = gather_blocks(gathered, "dp", dp_count)
+    split = 2 if seq_count % 2 == 0 else 1
+    part_len = seq_count // split
+    token_parts = []
+    for part in range(split):
+        streams = slice(part * part_len, (part + 1) * part_len)
+        partial_value = front(
+            x_in[streams], z_in[streams], b_in[streams], c_in[streams], decay_log[streams]
+        )
+        rows = partial_value.reshape(part_len * total_len, col_width)
+        if part == 0:
+            rows = jnp.concatenate([rows, route_row.reshape(extra_rows, col_width)], axis=0)
+        piece = sum_scatter(rows, "expert", group_count)
+        gathered = gather_blocks(piece, "ctx", ctx_count)
+        gathered = gather_xor(gathered, "expert", group_count)
+        gathered = gather_blocks(gathered, "dp", dp_count)
+        token_parts.append(gathered)
+    part_rows = part_len * total_len
+    extra = token_parts[0][:, :, :, part_rows:, :]
+    token_parts[0] = token_parts[0][:, :, :, :part_rows, :]
+    gathered = jnp.concatenate(token_parts + [extra], axis=3)
     row_total = seq_count * total_len
     extra = jnp.transpose(gathered[:, :, :, row_total:, :], (0, 2, 3, 1, 4))
     routes = extra.reshape(dp_count, ctx_count, -1)[:, :, : group_count * route_len]

time: 102 us -> 102 us (level)
  waiting for transfers between devices: 42.3 us -> 14.1 us
  starting transfers between devices: 18.3 us -> 36.6 us
  local copies, waits for them, and re-layouts: 12.7 us -> 20.5 us
  matrix products: 18.2 us -> 20.3 us
    ppermute x7 -> x14, waiting for transfers between devices: 27.6 us -> 8.36 us  [gather_blocks(): received.append(lax.ppermute(value, axis_name, perm))]
    ppermute x7 -> x14, starting transfers between devices: 11.1 us -> 20.9 us  [gather_blocks(): received.append(lax.ppermute(value, axis_name, perm))]
    dot_general x0 -> x1, local copies, waits for them, and re-layouts: none -> 6.5 us  [front(): jnp.einsum('stk,kd->std', gated, out_weight, preferred_element_type=jnp.f...]
    ppermute x3 -> x6, starting transfers between devices: 3.55 us -> 8.63 us  [gather_xor(): received.append(lax.ppermute(value, axis_name, perm))]
    ppermute x3 -> x6, waiting for transfers between devices: 5.94 us -> 1.17 us  [sum_scatter(): total = total + lax.ppermute(send, axis_name, perm)]
    ppermute x3 -> x6, waiting for transfers between devices: 8.71 us -> 4.56 us  [gather_xor(): received.append(lax.ppermute(value, axis_name, perm))]
    ppermute x3 -> x6, starting transfers between devices: 3.68 us -> 7.11 us  [sum_scatter(): total = total + lax.ppermute(send, axis_name, perm)]
    slice x1 -> x5, local copies, waits for them, and re-layouts: 1.32 us -> 4.65 us  [the longest x2 2.24 us: front(): x_all = packed[:, :, :width_in]]
  transfers between devices with their start and end apart: 13 -> 26, of which waited for: 9 -> 7; matrix products, arithmetic and copies ran while one was open for 3% -> 11% of each run, Pallas kernels for 0% -> 0%
where the time goes in v10:
time: 102 us; the launch traced here: 101 us
  starting transfers between devices  36.6 us (36%)
  local copies, waits for them, and re-layouts  20.5 us (20%)
  matrix products  20.3 us (20%)
  waiting for transfers between devices  14.1 us (14%)
  other arithmetic  8.59 us (8%)
  between operations  1.12 us (1%)
    ppermute x14, starting transfers between devices, gather_blocks(): received.append(lax.ppermute(value, axis_name, perm))  20.9 us
    ppermute x6, starting transfers between devices, gather_xor(): received.append(lax.ppermute(value, axis_name, perm))  8.63 us
    ppermute x14, waiting for transfers between devices, gather_blocks(): received.append(lax.ppermute(value, axis_name, perm))  8.36 us
    dot_general x1, matrix products, expert_ffn(): jnp.einsum('gfd,qd->gfq', gate_up[0], slot_rows, preferred_element_type=j...  8.15 us
    ppermute x6, starting transfers between devices, sum_scatter(): total = total + lax.ppermute(send, axis_name, perm)  7.11 us
    dot_general x1, local copies, waits for them, and re-layouts, front(): jnp.einsum('stk,kd->std', gated, out_weight, preferred_element_type=jnp.f...  6.5 us
    dot_general x2, matrix products, mixer(): ssd = jnp.einsum('sktuh,skuhp->skthp', kernel, x_float, precision=highest)  5.29 us
    dot_general x2, matrix products, front(): jnp.einsum('stk,kd->std', gated, out_weight, preferred_element_type=jnp.f...  5.14 us
  transfers between devices with their start and end apart: 26, of which 7 were waited for; matrix products, arithmetic and copies ran while one was open for 11% of the time, Pallas kernels for 0%

profile of v10, /device:TPU:0, one launch (start us, length us, event | category | flops | bytes accessed | tf_op | source)
XLA Modules:
  0.0 101.3 jit_solution(9096966446627057496)
XLA Ops:
  4.6 3.1 %collective-permute-start.15 = (bf16[1,16,4448]{2,1,0:T(8,128)(2,1)S(1)}, bf16[1,16,4448]{2,1,0:T(8,128)(2,1)S(1)}, u32[]{:S(2)}, u32[]{:S(2)}) collective-permute-start(bf16[1,16,4448]{2,1,0:T(8,128)(2,1)S(1)} %concatenate.18), channel_id=1, source_target_pairs={{0,4},{4,8},{8,12},{12,0},{1,5},{5,9},{9,13},{13,1},{2,6},{6,10},{... | collective-permute-start | bytes 427016 | tf_op jit(solution)/shard_map/ppermute | solution.py:26
  7.6 2.6 %collective-permute-start.14 = (bf16[1,16,4448]{2,1,0:T(8,128)(2,1)S(1)}, bf16[1,16,4448]{2,1,0:T(8,128)(2,1)S(1)}, u32[]{:S(2)}, u32[]{:S(2)}) collective-permute-start(bf16[1,16,4448]{2,1,0:T(8,128)(2,1)S(1)} %concatenate.18), channel_id=1, source_target_pairs={{0,8},{4,12},{8,0},{12,4},{1,9},{5,13},{9,1},{13,5},{2,10},{6,14},... | collective-permute-start | bytes 427016 | tf_op jit(solution)/shard_map/ppermute | solution.py:26
  10.2 1.3 %collective-permute-start.13 = (bf16[1,16,4448]{2,1,0:T(8,128)(2,1)S(1)}, bf16[1,16,4448]{2,1,0:T(8,128)(2,1)S(1)}, u32[]{:S(2)}, u32[]{:S(2)}) collective-permute-start(bf16[1,16,4448]{2,1,0:T(8,128)(2,1)S(1)} %concatenate.18), channel_id=1, source_target_pairs={{0,12},{4,0},{8,4},{12,8},{1,13},{5,1},{9,5},{13,9},{2,14},{6,2},{... | collective-permute-start | bytes 427016 | tf_op jit(solution)/shard_map/ppermute | solution.py:26
  14.1 6.5 %copy.197 = bf16[1024,2048]{1,0:T(8,128)(2,1)} copy(bf16[1024,2048]{0,1:T(8,128)(2,1)} %bitcast.177) | data formatting | bytes 8388608 | tf_op jit(solution)/shard_map/stk,kd->std/dot_general | solution.py:176
  20.7 2.9 %collective-permute-start = (bf16[1,16,4448]{2,1,0:T(8,128)(2,1)S(1)}, bf16[1,16,4448]{2,1,0:T(8,128)(2,1)S(1)}, u32[]{:S(2)}, u32[]{:S(2)}) collective-permute-start(bf16[1,16,4448]{2,1,0:T(8,128)(2,1)S(1)} %concatenate.15), channel_id=1, source_target_pairs={{0,12},{4,0},{8,4},{12,8},{1,13},{5,1},{9,5},{13,9},{2,14},{6,2},{... | collective-permute-start | bytes 427016 | tf_op jit(solution)/shard_map/ppermute | solution.py:26
  24.0 7.9 %collective-permute-done.1 = bf16[1,16,4448]{2,1,0:T(8,128)(2,1)S(1)} collective-permute-done((bf16[1,16,4448]{2,1,0:T(8,128)(2,1)S(1)}, bf16[1,16,4448]{2,1,0:T(8,128)(2,1)S(1)}, u32[]{:S(2)}, u32[]{:S(2)}) %collective-permute-start.1) | collective-permute-done | bytes 142368 | tf_op jit(solution)/shard_map/ppermute | solution.py:26
  36.9 3.0 %fusion.12 = f32[1,1,64,32,64]{2,4,3,1,0:T(8,128)} fusion(bf16[64,32,64]{0,2,1:T(8,128)(2,1)S(1)} %bitcast.195, f32[1,1,64,32,64]{2,4,3,1,0:T(8,128)S(1)} %bitcast.191, f32[32]{0:T(128)S(1)} %copy-done.3, f32[64,64]{1,0:T(8,128)} %fusion.71, f32[64,32]{0,1:T(8,128)} %copy.164, pred[64,64]{1,0:T(8,128)(4,1)S(1)} %iota_compare_fusion.1), kind=kOutput, calls=%fused_computation.15 | convolution fusion | flops 101449728 | bytes 1339520 | tf_op jit(solution)/shard_map/sktuh,skuhp->skthp/dot_general | solution.py:81
  39.9 2.3 %copy.167 = f32[1,64,2048]{2,1,0:T(8,128)} copy(f32[1,64,2048]{1,2,0:T(8,128)} %bitcast.193) | data formatting | bytes 1048576 | tf_op jit(solution)/shard_map/reshape | solution.py:101
  43.6 2.3 %fusion.13 = f32[1,1,64,32,64]{2,4,3,1,0:T(8,128)S(1)} fusion(bf16[64,32,64]{0,2,1:T(8,128)(2,1)} %bitcast.194, f32[1,1,64,32,64]{2,4,3,1,0:T(8,128)S(1)} %bitcast.190, f32[64,64]{1,0:T(8,128)S(1)} %fusion.70, f32[64,32]{0,1:T(8,128)} %copy.174, f32[32]{0:T(128)S(1)} %copy-done.3, pred[64,64]{1,0:T(8,128)(4,1)S(1)} %iota_compare_fusion.1), kind=kOutput, calls=%fused_computation.16 | convolution fusion | flops 101449728 | bytes 1339520 | tf_op jit(solution)/shard_map/sktuh,skuhp->skthp/dot_general | solution.py:81
  46.2 3.7 %fusion.48 = f32[64,4,256]{2,0,1:T(8,128)S(1)} fusion(bf16[4,256,2048]{2,1,0:T(8,128)(2,1)} %bitcast.178, f32[1,64,2048]{2,1,0:T(8,128)S(1)} %copy.177, bf16[1,64,4448]{2,1,0:T(8,128)(2,1)S(1)} %bitcast.184), kind=kOutput, calls=%fused_computation.75 | convolution fusion | flops 269352960 | bytes 5242880 | tf_op jit(solution)/shard_map/stk,kd->std/dot_general | solution.py:176
  50.0 1.4 %fusion.50 = f32[64,4,256]{2,0,1:T(8,128)S(1)} fusion(bf16[4,256,2048]{2,1,0:T(8,128)(2,1)S(1)} %bitcast.179, f32[1,64,2048]{2,1,0:T(8,128)S(1)} %copy-done.1, bf16[1,64,4448]{2,1,0:T(8,128)(2,1)S(1)} %bitcast.188), kind=kOutput, calls=%fused_computation.77 | convolution fusion | flops 269352960 | bytes 5242880 | tf_op jit(solution)/shard_map/stk,kd->std/dot_general | solution.py:176
  51.4 1.6 %collective-permute-start.16 = (f32[64,256]{1,0:T(8,128)S(1)}, f32[64,256]{1,0:T(8,128)S(1)}, u32[]{:S(2)}, u32[]{:S(2)}) collective-permute-start(f32[64,256]{1,0:T(8,128)S(1)} %get-tuple-element.45), channel_id=1, source_target_pairs={{0,1},{1,0},{2,3},{3,2},{4,5},{5,4},{6,7},{7,6},{8,9},{9,8},{10,11... | collective-permute-start | bytes 196616 | tf_op jit(solution)/shard_map/ppermute | solution.py:49
  53.0 1.5 %collective-permute-start.18 = (f32[64,256]{1,0:T(8,128)S(1)}, f32[64,256]{1,0:T(8,128)S(1)}, u32[]{:S(2)}, u32[]{:S(2)}) collective-permute-start(f32[64,256]{1,0:T(8,128)S(1)} %get-tuple-element.46), channel_id=1, source_target_pairs={{0,3},{1,2},{2,1},{3,0},{4,7},{5,6},{6,5},{7,4},{8,11},{9,10},{10,... | collective-permute-start | bytes 196616 | tf_op jit(solution)/shard_map/ppermute | solution.py:49
  55.0 1.6 %collective-permute-start.3 = (f32[65,256]{1,0:T(8,128)S(1)}, f32[65,256]{1,0:T(8,128)S(1)}, u32[]{:S(2)}, u32[]{:S(2)}) collective-permute-start(f32[65,256]{1,0:T(8,128)S(1)} %get-tuple-element.42), channel_id=1, source_target_pairs={{0,1},{1,0},{2,3},{3,2},{4,5},{5,4},{6,7},{7,6},{8,9},{9,8},{10,11... | collective-permute-start | bytes 199688 | tf_op jit(solution)/shard_map/ppermute | solution.py:49
  56.6 1.5 %collective-permute-start.4 = (f32[65,256]{1,0:T(8,128)S(1)}, f32[65,256]{1,0:T(8,128)S(1)}, u32[]{:S(2)}, u32[]{:S(2)}) collective-permute-start(f32[65,256]{1,0:T(8,128)S(1)} %get-tuple-element.43), channel_id=1, source_target_pairs={{0,2},{1,3},{2,0},{3,1},{4,6},{5,7},{6,4},{7,5},{8,10},{9,11},{10,... | collective-permute-start | bytes 199688 | tf_op jit(solution)/shard_map/ppermute | solution.py:49
  59.8 3.5 %collective-permute-start.21 = (bf16[64,256]{1,0:T(8,128)(2,1)S(1)}, bf16[64,256]{1,0:T(8,128)(2,1)S(1)}, u32[]{:S(2)}, u32[]{:S(2)}) collective-permute-start(bf16[64,256]{1,0:T(8,128)(2,1)S(1)} %fusion.68), channel_id=1, source_target_pairs={{0,4},{4,8},{8,12},{12,0},{1,5},{5,9},{9,13},{13,1},{2,6},{6,10},{... | collective-permute-start | bytes 98312 | tf_op jit(solution)/shard_map/ppermute | solution.py:26
  67.0 1.7 %collective-permute-start.7 = (bf16[65,256]{1,0:T(8,128)(2,1)S(1)}, bf16[65,256]{1,0:T(8,128)(2,1)S(1)}, u32[]{:S(2)}, u32[]{:S(2)}) collective-permute-start(bf16[65,256]{1,0:T(8,128)(2,1)S(1)} %fusion.61), channel_id=1, source_target_pairs={{0,8},{4,12},{8,0},{12,4},{1,9},{5,13},{9,1},{13,5},{2,10},{6,14},... | collective-permute-start | bytes 99848 | tf_op jit(solution)/shard_map/ppermute | solution.py:26
  69.7 1.9 %collective-permute-start.24 = (bf16[4,64,256]{2,1,0:T(8,128)(2,1)S(1)}, bf16[4,64,256]{2,1,0:T(8,128)(2,1)S(1)}, u32[]{:S(2)}, u32[]{:S(2)}) collective-permute-start(bf16[4,64,256]{2,1,0:T(8,128)(2,1)S(1)} %pad_maximum_fusion.5), channel_id=1, source_target_pairs={{0,1},{1,0},{2,3},{3,2},{4,5},{5,4},{6,7},{7,6},{8,9},{9,8},{10,11... | collective-permute-start | bytes 393224 | tf_op jit(solution)/shard_map/ppermute | solution.py:37
  72.6 1.3 %collective-permute-start.22 = (bf16[4,64,256]{2,1,0:T(8,128)(2,1)S(1)}, bf16[4,64,256]{2,1,0:T(8,128)(2,1)S(1)}, u32[]{:S(2)}, u32[]{:S(2)}) collective-permute-start(bf16[4,64,256]{2,1,0:T(8,128)(2,1)S(1)} %pad_maximum_fusion.5), channel_id=1, source_target_pairs={{0,3},{1,2},{2,1},{3,0},{4,7},{5,6},{6,5},{7,4},{8,11},{9,10},{10,... | collective-permute-start | bytes 393224 | tf_op jit(solution)/shard_map/ppermute | solution.py:37
  76.3 2.2 %collective-permute-start.9 = (bf16[4,65,256]{2,1,0:T(8,128)(2,1)S(1)}, bf16[4,65,256]{2,1,0:T(8,128)(2,1)S(1)}, u32[]{:S(2)}, u32[]{:S(2)}) collective-permute-start(bf16[4,65,256]{2,1,0:T(8,128)(2,1)S(1)} %pad_maximum_fusion.4), channel_id=1, source_target_pairs={{0,3},{1,2},{2,1},{3,0},{4,7},{5,6},{6,5},{7,4},{8,11},{9,10},{10,... | collective-permute-start | bytes 399368 | tf_op jit(solution)/shard_map/ppermute | solution.py:37
  78.4 1.7 %collective-permute-done.22 = bf16[4,64,256]{2,1,0:T(8,128)(2,1)S(1)} collective-permute-done((bf16[4,64,256]{2,1,0:T(8,128)(2,1)S(1)}, bf16[4,64,256]{2,1,0:T(8,128)(2,1)S(1)}, u32[]{:S(2)}, u32[]{:S(2)}) %collective-permute-start.22) | collective-permute-done | bytes 131104 | tf_op jit(solution)/shard_map/ppermute | solution.py:37
  81.7 1.6 %collective-permute-done.9 = bf16[4,65,256]{2,1,0:T(8,128)(2,1)S(1)} collective-permute-done((bf16[4,65,256]{2,1,0:T(8,128)(2,1)S(1)}, bf16[4,65,256]{2,1,0:T(8,128)(2,1)S(1)}, u32[]{:S(2)}, u32[]{:S(2)}) %collective-permute-start.9) | collective-permute-done | bytes 133152 | tf_op jit(solution)/shard_map/ppermute | solution.py:37
  86.8 1.8 %fusion.2 = (f32[2,128]{1,0:T(2,128)S(1)}, bf16[2,4,4,128,256]{4,3,2,1,0:T(8,128)(2,1)S(1)}) fusion(bf16[1,4,4,64,256]{4,3,2,1,0:T(8,128)(2,1)} %get-tuple-element.21, bf16[1,4,4,64,256]{4,3,2,1,0:T(8,128)(2,1)} %get-tuple-element.20, bf16[2,4,4,64,256]{4,3,2,1,0:T(8,128)(2,1)S(1)} %fusion.14), kind=kLoop, calls=%fused_computation.4 | loop fusion | flops 9436928 | bytes 4195328 | tf_op jit(solution)/shard_map/reduce_sum | solution.py:224
  90.3 8.2 %fusion.9 = f32[2,896,256]{1,2,0:T(8,128)S(1)} fusion(bf16[256,4096,1]{0,1,2:T(8,128)(2,1)S(1)} %bitcast.180, bf16[1,2,896,4096]{3,2,1,0:T(8,128)(2,1)} %param.19), kind=kOutput, calls=%fused_computation.12 | convolution fusion | flops 3758096384 | bytes 18612224 | tf_op jit(solution)/shard_map/gfd,qd->gfq/dot_general | solution.py:105
  (127 shorter events, 33.2 us)
Async XLA Ops:
  4.6 16.2 %collective-permute-start.15 = (bf16[1,16,4448]{2,1,0:T(8,128)(2,1)S(1)}, bf16[1,16,4448]{2,1,0:T(8,128)(2,1)S(1)}, u32[]{:S(2)}, u32[]{:S(2)}) collective-permute-start(bf16[1,16,4448]{2,1,0:T(8,128)(2,1)S(1)} %concatenate.18), channel_id=1, source_target_pairs={{0,4},{4,8},{8,12},{12,0},{1,5},{5,9},{9,13},{13,1},{2,6},{6,10},{... | collective-permute-start | bytes 427016 | tf_op jit(solution)/shard_map/ppermute | solution.py:26
  7.6 16.0 %collective-permute-start.14 = (bf16[1,16,4448]{2,1,0:T(8,128)(2,1)S(1)}, bf16[1,16,4448]{2,1,0:T(8,128)(2,1)S(1)}, u32[]{:S(2)}, u32[]{:S(2)}) collective-permute-start(bf16[1,16,4448]{2,1,0:T(8,128)(2,1)S(1)} %concatenate.18), channel_id=1, source_target_pairs={{0,8},{4,12},{8,0},{12,4},{1,9},{5,13},{9,1},{13,5},{2,10},{6,14},... | collective-permute-start | bytes 427016 | tf_op jit(solution)/shard_map/ppermute | solution.py:26
  10.2 13.4 %collective-permute-start.13 = (bf16[1,16,4448]{2,1,0:T(8,128)(2,1)S(1)}, bf16[1,16,4448]{2,1,0:T(8,128)(2,1)S(1)}, u32[]{:S(2)}, u32[]{:S(2)}) collective-permute-start(bf16[1,16,4448]{2,1,0:T(8,128)(2,1)S(1)} %concatenate.18), channel_id=1, source_target_pairs={{0,12},{4,0},{8,4},{12,8},{1,13},{5,1},{9,5},{13,9},{2,14},{6,2},{... | collective-permute-start | bytes 427016 | tf_op jit(solution)/shard_map/ppermute | solution.py:26
  11.7 12.4 %collective-permute-start.2 = (bf16[1,16,4448]{2,1,0:T(8,128)(2,1)S(1)}, bf16[1,16,4448]{2,1,0:T(8,128)(2,1)S(1)}, u32[]{:S(2)}, u32[]{:S(2)}) collective-permute-start(bf16[1,16,4448]{2,1,0:T(8,128)(2,1)S(1)} %concatenate.15), channel_id=1, source_target_pairs={{0,4},{4,8},{8,12},{12,0},{1,5},{5,9},{9,13},{13,1},{2,6},{6,10},{... | collective-permute-start | bytes 427016 | tf_op jit(solution)/shard_map/ppermute | solution.py:26
  12.3 19.6 %collective-permute-start.1 = (bf16[1,16,4448]{2,1,0:T(8,128)(2,1)S(1)}, bf16[1,16,4448]{2,1,0:T(8,128)(2,1)S(1)}, u32[]{:S(2)}, u32[]{:S(2)}) collective-permute-start(bf16[1,16,4448]{2,1,0:T(8,128)(2,1)S(1)} %concatenate.15), channel_id=1, source_target_pairs={{0,8},{4,12},{8,0},{12,4},{1,9},{5,13},{9,1},{13,5},{2,10},{6,14},... | collective-permute-start | bytes 427016 | tf_op jit(solution)/shard_map/ppermute | solution.py:26
  20.7 11.2 %collective-permute-start = (bf16[1,16,4448]{2,1,0:T(8,128)(2,1)S(1)}, bf16[1,16,4448]{2,1,0:T(8,128)(2,1)S(1)}, u32[]{:S(2)}, u32[]{:S(2)}) collective-permute-start(bf16[1,16,4448]{2,1,0:T(8,128)(2,1)S(1)} %concatenate.15), channel_id=1, source_target_pairs={{0,12},{4,0},{8,4},{12,8},{1,13},{5,1},{9,5},{13,9},{2,14},{6,2},{... | collective-permute-start | bytes 427016 | tf_op jit(solution)/shard_map/ppermute | solution.py:26
  51.4 6.7 %collective-permute-start.16 = (f32[64,256]{1,0:T(8,128)S(1)}, f32[64,256]{1,0:T(8,128)S(1)}, u32[]{:S(2)}, u32[]{:S(2)}) collective-permute-start(f32[64,256]{1,0:T(8,128)S(1)} %get-tuple-element.45), channel_id=1, source_target_pairs={{0,1},{1,0},{2,3},{3,2},{4,5},{5,4},{6,7},{7,6},{8,9},{9,8},{10,11... | collective-permute-start | bytes 196616 | tf_op jit(solution)/shard_map/ppermute | solution.py:49
  53.0 5.6 %collective-permute-start.18 = (f32[64,256]{1,0:T(8,128)S(1)}, f32[64,256]{1,0:T(8,128)S(1)}, u32[]{:S(2)}, u32[]{:S(2)}) collective-permute-start(f32[64,256]{1,0:T(8,128)S(1)} %get-tuple-element.46), channel_id=1, source_target_pairs={{0,3},{1,2},{2,1},{3,0},{4,7},{5,6},{6,5},{7,4},{8,11},{9,10},{10,... | collective-permute-start | bytes 196616 | tf_op jit(solution)/shard_map/ppermute | solution.py:49
  54.5 5.2 %collective-permute-start.17 = (f32[64,256]{1,0:T(8,128)S(1)}, f32[64,256]{1,0:T(8,128)S(1)}, u32[]{:S(2)}, u32[]{:S(2)}) collective-permute-start(f32[64,256]{1,0:T(8,128)S(1)} %get-tuple-element.47), channel_id=1, source_target_pairs={{0,2},{1,3},{2,0},{3,1},{4,6},{5,7},{6,4},{7,5},{8,10},{9,11},{10,... | collective-permute-start | bytes 196616 | tf_op jit(solution)/shard_map/ppermute | solution.py:49
  55.0 9.5 %collective-permute-start.3 = (f32[65,256]{1,0:T(8,128)S(1)}, f32[65,256]{1,0:T(8,128)S(1)}, u32[]{:S(2)}, u32[]{:S(2)}) collective-permute-start(f32[65,256]{1,0:T(8,128)S(1)} %get-tuple-element.42), channel_id=1, source_target_pairs={{0,1},{1,0},{2,3},{3,2},{4,5},{5,4},{6,7},{7,6},{8,9},{9,8},{10,11... | collective-permute-start | bytes 199688 | tf_op jit(solution)/shard_map/ppermute | solution.py:49
  56.6 9.2 %collective-permute-start.4 = (f32[65,256]{1,0:T(8,128)S(1)}, f32[65,256]{1,0:T(8,128)S(1)}, u32[]{:S(2)}, u32[]{:S(2)}) collective-permute-start(f32[65,256]{1,0:T(8,128)S(1)} %get-tuple-element.43), channel_id=1, source_target_pairs={{0,2},{1,3},{2,0},{3,1},{4,6},{5,7},{6,4},{7,5},{8,10},{9,11},{10,... | collective-permute-start | bytes 199688 | tf_op jit(solution)/shard_map/ppermute | solution.py:49
  58.1 7.7 %collective-permute-start.5 = (f32[65,256]{1,0:T(8,128)S(1)}, f32[65,256]{1,0:T(8,128)S(1)}, u32[]{:S(2)}, u32[]{:S(2)}) collective-permute-start(f32[65,256]{1,0:T(8,128)S(1)} %get-tuple-element.44), channel_id=1, source_target_pairs={{0,3},{1,2},{2,1},{3,0},{4,7},{5,6},{6,5},{7,4},{8,11},{9,10},{10,... | collective-permute-start | bytes 199688 | tf_op jit(solution)/shard_map/ppermute | solution.py:49
  59.8 8.9 %collective-permute-start.21 = (bf16[64,256]{1,0:T(8,128)(2,1)S(1)}, bf16[64,256]{1,0:T(8,128)(2,1)S(1)}, u32[]{:S(2)}, u32[]{:S(2)}) collective-permute-start(bf16[64,256]{1,0:T(8,128)(2,1)S(1)} %fusion.68), channel_id=1, source_target_pairs={{0,4},{4,8},{8,12},{12,0},{1,5},{5,9},{9,13},{13,1},{2,6},{6,10},{... | collective-permute-start | bytes 98312 | tf_op jit(solution)/shard_map/ppermute | solution.py:26
  63.3 6.4 %collective-permute-start.20 = (bf16[64,256]{1,0:T(8,128)(2,1)S(1)}, bf16[64,256]{1,0:T(8,128)(2,1)S(1)}, u32[]{:S(2)}, u32[]{:S(2)}) collective-permute-start(bf16[64,256]{1,0:T(8,128)(2,1)S(1)} %fusion.68), channel_id=1, source_target_pairs={{0,8},{4,12},{8,0},{12,4},{1,9},{5,13},{9,1},{13,5},{2,10},{6,14},... | collective-permute-start | bytes 98312 | tf_op jit(solution)/shard_map/ppermute | solution.py:26
  64.5 5.1 %collective-permute-start.19 = (bf16[64,256]{1,0:T(8,128)(2,1)S(1)}, bf16[64,256]{1,0:T(8,128)(2,1)S(1)}, u32[]{:S(2)}, u32[]{:S(2)}) collective-permute-start(bf16[64,256]{1,0:T(8,128)(2,1)S(1)} %fusion.68), channel_id=1, source_target_pairs={{0,12},{4,0},{8,4},{12,8},{1,13},{5,1},{9,5},{13,9},{2,14},{6,2},{... | collective-permute-start | bytes 98312 | tf_op jit(solution)/shard_map/ppermute | solution.py:26
  65.8 6.9 %collective-permute-start.8 = (bf16[65,256]{1,0:T(8,128)(2,1)S(1)}, bf16[65,256]{1,0:T(8,128)(2,1)S(1)}, u32[]{:S(2)}, u32[]{:S(2)}) collective-permute-start(bf16[65,256]{1,0:T(8,128)(2,1)S(1)} %fusion.61), channel_id=1, source_target_pairs={{0,4},{4,8},{8,12},{12,0},{1,5},{5,9},{9,13},{13,1},{2,6},{6,10},{... | collective-permute-start | bytes 99848 | tf_op jit(solution)/shard_map/ppermute | solution.py:26
  67.0 7.0 %collective-permute-start.7 = (bf16[65,256]{1,0:T(8,128)(2,1)S(1)}, bf16[65,256]{1,0:T(8,128)(2,1)S(1)}, u32[]{:S(2)}, u32[]{:S(2)}) collective-permute-start(bf16[65,256]{1,0:T(8,128)(2,1)S(1)} %fusion.61), channel_id=1, source_target_pairs={{0,8},{4,12},{8,0},{12,4},{1,9},{5,13},{9,1},{13,5},{2,10},{6,14},... | collective-permute-start | bytes 99848 | tf_op jit(solution)/shard_map/ppermute | solution.py:26
  68.6 5.3 %collective-permute-start.6 = (bf16[65,256]{1,0:T(8,128)(2,1)S(1)}, bf16[65,256]{1,0:T(8,128)(2,1)S(1)}, u32[]{:S(2)}, u32[]{:S(2)}) collective-permute-start(bf16[65,256]{1,0:T(8,128)(2,1)S(1)} %fusion.61), channel_id=1, source_target_pairs={{0,12},{4,0},{8,4},{12,8},{1,13},{5,1},{9,5},{13,9},{2,14},{6,2},{... | collective-permute-start | bytes 99848 | tf_op jit(solution)/shard_map/ppermute | solution.py:26
  69.7 6.5 %collective-permute-start.24 = (bf16[4,64,256]{2,1,0:T(8,128)(2,1)S(1)}, bf16[4,64,256]{2,1,0:T(8,128)(2,1)S(1)}, u32[]{:S(2)}, u32[]{:S(2)}) collective-permute-start(bf16[4,64,256]{2,1,0:T(8,128)(2,1)S(1)} %pad_maximum_fusion.5), channel_id=1, source_target_pairs={{0,1},{1,0},{2,3},{3,2},{4,5},{5,4},{6,7},{7,6},{8,9},{9,8},{10,11... | collective-permute-start | bytes 393224 | tf_op jit(solution)/shard_map/ppermute | solution.py:37
  71.6 6.8 %collective-permute-start.23 = (bf16[4,64,256]{2,1,0:T(8,128)(2,1)S(1)}, bf16[4,64,256]{2,1,0:T(8,128)(2,1)S(1)}, u32[]{:S(2)}, u32[]{:S(2)}) collective-permute-start(bf16[4,64,256]{2,1,0:T(8,128)(2,1)S(1)} %pad_maximum_fusion.5), channel_id=1, source_target_pairs={{0,2},{1,3},{2,0},{3,1},{4,6},{5,7},{6,4},{7,5},{8,10},{9,11},{10,... | collective-permute-start | bytes 393224 | tf_op jit(solution)/shard_map/ppermute | solution.py:37
  72.6 7.5 %collective-permute-start.22 = (bf16[4,64,256]{2,1,0:T(8,128)(2,1)S(1)}, bf16[4,64,256]{2,1,0:T(8,128)(2,1)S(1)}, u32[]{:S(2)}, u32[]{:S(2)}) collective-permute-start(bf16[4,64,256]{2,1,0:T(8,128)(2,1)S(1)} %pad_maximum_fusion.5), channel_id=1, source_target_pairs={{0,3},{1,2},{2,1},{3,0},{4,7},{5,6},{6,5},{7,4},{8,11},{9,10},{10,... | collective-permute-start | bytes 393224 | tf_op jit(solution)/shard_map/ppermute | solution.py:37
  74.0 7.2 %collective-permute-start.11 = (bf16[4,65,256]{2,1,0:T(8,128)(2,1)S(1)}, bf16[4,65,256]{2,1,0:T(8,128)(2,1)S(1)}, u32[]{:S(2)}, u32[]{:S(2)}) collective-permute-start(bf16[4,65,256]{2,1,0:T(8,128)(2,1)S(1)} %pad_maximum_fusion.4), channel_id=1, source_target_pairs={{0,1},{1,0},{2,3},{3,2},{4,5},{5,4},{6,7},{7,6},{8,9},{9,8},{10,11... | collective-permute-start | bytes 399368 | tf_op jit(solution)/shard_map/ppermute | solution.py:37
  75.2 6.5 %collective-permute-start.10 = (bf16[4,65,256]{2,1,0:T(8,128)(2,1)S(1)}, bf16[4,65,256]{2,1,0:T(8,128)(2,1)S(1)}, u32[]{:S(2)}, u32[]{:S(2)}) collective-permute-start(bf16[4,65,256]{2,1,0:T(8,128)(2,1)S(1)} %pad_maximum_fusion.4), channel_id=1, source_target_pairs={{0,2},{1,3},{2,0},{3,1},{4,6},{5,7},{6,4},{7,5},{8,10},{9,11},{10,... | collective-permute-start | bytes 399368 | tf_op jit(solution)/shard_map/ppermute | solution.py:37
  76.3 7.0 %collective-permute-start.9 = (bf16[4,65,256]{2,1,0:T(8,128)(2,1)S(1)}, bf16[4,65,256]{2,1,0:T(8,128)(2,1)S(1)}, u32[]{:S(2)}, u32[]{:S(2)}) collective-permute-start(bf16[4,65,256]{2,1,0:T(8,128)(2,1)S(1)} %pad_maximum_fusion.4), channel_id=1, source_target_pairs={{0,3},{1,2},{2,1},{3,0},{4,7},{5,6},{6,5},{7,4},{8,11},{9,10},{10,... | collective-permute-start | bytes 399368 | tf_op jit(solution)/shard_map/ppermute | solution.py:37
  (7 other events, 75.0 us)

commit v11 on v9

--- a/solution.py
+++ b/solution.py
@@ -74,11 +74,22 @@
     b_float = b_in.astype(jnp.float32).reshape(seq_count, chunks, chunk, state_size)
     c_float = c_in.astype(jnp.float32).reshape(seq_count, chunks, chunk, state_size)
     cum_decay = jnp.cumsum(decay_log.reshape(seq_count, chunks, chunk, head_count), axis=2)
-    scores = jnp.einsum("sktn,skun->sktu", c_float, b_float, precision=highest)
+    scores = jnp.einsum(
+        "sktn,skun->sktu",
+        c_in.reshape(seq_count, chunks, chunk, state_size),
+        b_in.reshape(seq_count, chunks, chunk, state_size),
+        preferred_element_type=jnp.float32,
+    )
     causal = (jnp.arange(chunk)[:, None] >= jnp.arange(chunk)[None, :])[None, None, :, :, None]
     spans = cum_decay[:, :, :, None, :] - cum_decay[:, :, None, :, :]
     kernel = jnp.where(causal, jnp.exp(jnp.where(causal, spans, 0.0)), 0.0) * scores[..., None]
-    ssd = jnp.einsum("sktuh,skuhp->skthp", kernel, x_float, precision=highest)
+    x_parts = x_in.reshape(seq_count, chunks, chunk, head_count, P_SIZE)
+    ssd = jnp.einsum(
+        "sktuh,skuhp->skthp",
+        jnp.concatenate(split_exact(kernel), axis=3),
+        jnp.concatenate([x_parts] * 3, axis=2),
+        preferred_element_type=jnp.float32,
+    )
     if chunks > 1:
         final_decay = cum_decay[:, :, -1, :]
         tails = jnp.exp(final_decay[:, :, None, :] - cum_decay)

time: 102 us -> 108 us (1.059)
  other arithmetic: 8.86 us -> 12 us
  matrix products: 18.2 us -> 20 us
    dot_general x2, matrix products: 4.26 us -> 6.41 us  [the longest x1 6.28 us: mixer(): jnp.einsum('sktuh,skuhp->skthp', jnp.concatenate(split_exact(kernel), axi...]
    convert_element_type x1 -> x2, other arithmetic: 0.72 us -> 2.46 us  [split_exact(): (rest - lax.optimization_barrier(middle).astype(jnp.float32)).astype(jnp....]
    another operation x8 -> x7, other arithmetic: 2.29 us -> 2.12 us  [place(): return jnp.stack(slots)]
  transfers between devices with their start and end apart: 13 -> 13, of which waited for: 9 -> 9; matrix products, arithmetic and copies ran while one was open for 3% -> 2% of each run, Pallas kernels for 0% -> 0%
where the time goes in v11:
time: 108 us; the launch traced here: 107 us
  waiting for transfers between devices  42.3 us (39%)
  matrix products  20 us (19%)
  starting transfers between devices  18.3 us (17%)
  local copies, waits for them, and re-layouts  13.4 us (12%)
  other arithmetic  12 us (11%)
  between operations  1.09 us (1%)
    ppermute x7, waiting for transfers between devices, gather_blocks(): received.append(lax.ppermute(value, axis_name, perm))  27.6 us
    ppermute x7, starting transfers between devices, gather_blocks(): received.append(lax.ppermute(value, axis_name, perm))  11.1 us
    ppermute x3, waiting for transfers between devices, gather_xor(): received.append(lax.ppermute(value, axis_name, perm))  8.71 us
    dot_general x1, matrix products, expert_ffn(): jnp.einsum('gfd,qd->gfq', gate_up[0], slot_rows, preferred_element_type=j...  8.15 us
    dot_general x1, matrix products, mixer(): jnp.einsum('sktuh,skuhp->skthp', jnp.concatenate(split_exact(kernel), axi...  6.28 us
    ppermute x3, waiting for transfers between devices, sum_scatter(): total = total + lax.ppermute(send, axis_name, perm)  5.94 us
    ppermute x3, starting transfers between devices, sum_scatter(): total = total + lax.ppermute(send, axis_name, perm)  3.68 us
    ppermute x3, starting transfers between devices, gather_xor(): received.append(lax.ppermute(value, axis_name, perm))  3.55 us
  transfers between devices with their start and end apart: 13, of which 9 were waited for; matrix products, arithmetic and copies ran while one was open for 2% of the time, Pallas kernels for 0%

profile of v11, /device:TPU:0, one launch (start us, length us, event | category | flops | bytes accessed | tf_op | source)
XLA Modules:
  0.0 107.1 jit_solution(17762989099850324066)
XLA Ops:
  3.9 5.1 %collective-permute-start = (bf16[2,16,4448]{2,1,0:T(8,128)(2,1)S(1)}, bf16[2,16,4448]{2,1,0:T(8,128)(2,1)S(1)}, u32[]{:S(2)}, u32[]{:S(2)}) collective-permute-start(bf16[2,16,4448]{2,1,0:T(8,128)(2,1)S(1)} %concatenate.17), channel_id=1, source_target_pairs={{0,12},{4,0},{8,4},{12,8},{1,13},{5,1},{9,5},{13,9},{2,14},{6,2},{... | collective-permute-start | bytes 854024 | tf_op jit(solution)/shard_map/ppermute | solution.py:26
  12.3 3.9 %collective-permute-done = bf16[2,16,4448]{2,1,0:T(8,128)(2,1)S(1)} collective-permute-done((bf16[2,16,4448]{2,1,0:T(8,128)(2,1)S(1)}, bf16[2,16,4448]{2,1,0:T(8,128)(2,1)S(1)}, u32[]{:S(2)}, u32[]{:S(2)}) %collective-permute-start) | collective-permute-done | bytes 284704 | tf_op jit(solution)/shard_map/ppermute | solution.py:26
  16.2 17.2 %collective-permute-done.1 = bf16[2,16,4448]{2,1,0:T(8,128)(2,1)S(1)} collective-permute-done((bf16[2,16,4448]{2,1,0:T(8,128)(2,1)S(1)}, bf16[2,16,4448]{2,1,0:T(8,128)(2,1)S(1)}, u32[]{:S(2)}, u32[]{:S(2)}) %collective-permute-start.1) | collective-permute-done | bytes 284704 | tf_op jit(solution)/shard_map/ppermute | solution.py:26
  36.7 1.7 %subtract_convert_fusion = bf16[2,1,64,64,32]{3,2,4,0,1:T(8,128)(2,1)} fusion(bf16[2,1,64,64,32]{3,2,4,0,1:T(8,128)(2,1)S(1)} %fusion.21, bf16[2,1,64,64,32]{3,2,4,0,1:T(8,128)(2,1)S(1)} %fusion.20, f32[2,64,64]{2,1,0:T(8,128)S(1)} %fusion.40, f32[2,64,32]{1,2,0:T(8,128)S(1)} %copy.151, pred[64,64]{1,0:T(8,128)(4,1)S(1)} %iota_compare_fusion.1), kind=kLoop, calls=%fused_computation.28 | loop fusion | flops 2359296 | bytes 1626112 | tf_op jit(solution)/shard_map/convert_element_type | solution.py:57
  38.4 2.4 %copy.180 = bf16[2,64,2048]{1,2,0:T(8,128)(2,1)} copy(bf16[2,64,2048]{2,1,0:T(8,128)(2,1)} %slice.56) | data formatting | bytes 1048576 | tf_op jit(solution)/shard_map/reshape | solution.py:86
  40.8 6.3 %bitcast_add_fusion = f32[2,1,64,32,64]{2,4,3,0,1:T(8,128)} fusion(bf16[2,1,64,32,64]{2,4,3,0,1:T(8,128)(2,1)} %bitcast.118, bf16[2,1,64,64,32]{3,2,4,0,1:T(8,128)(2,1)} %subtract_convert_fusion, bf16[2,1,64,64,32]{3,2,4,0,1:T(8,128)(2,1)S(1)} %fusion.21, bf16[2,1,64,64,32]{3,2,4,0,1:T(8,128)(2,1)S(1)} %fusion.20, f32[32]{0:T(128)S(1)} %copy-done.2), kind=kOutput, calls=%fused_computation.25 | convolution fusion | flops 110886912 | bytes 3145856 | tf_op jit(solution)/shard_map/sktuh,skuhp->skthp/dot_general | solution.py:87
  47.1 2.2 %copy.176 = f32[2,64,2048]{2,1,0:T(8,128)S(1)} copy(f32[2,64,2048]{1,2,0:T(8,128)} %bitcast.115) | data formatting | bytes 2097152 | tf_op jit(solution)/shard_map/reshape | solution.py:112
  49.3 3.0 %fusion.5 = f32[2,64,1024]{2,1,0:T(8,128)S(1)} fusion(bf16[2048,1024]{1,0:T(8,128)(2,1)} %param.17, f32[2,64,2048]{2,1,0:T(8,128)S(1)} %copy.176, bf16[2,64,4448]{2,1,0:T(8,128)(2,1)S(1)} %bitcast.114), kind=kOutput, calls=%fused_computation.8 | convolution fusion | flops 538705920 | bytes 6291456 | tf_op jit(solution)/shard_map/stk,kd->std/dot_general | solution.py:185
  53.1 1.6 %collective-permute-start.3 = (f32[129,256]{1,0:T(8,128)S(1)}, f32[129,256]{1,0:T(8,128)S(1)}, u32[]{:S(2)}, u32[]{:S(2)}) collective-permute-start(f32[129,256]{1,0:T(8,128)S(1)} %bitcast.122), channel_id=1, source_target_pairs={{0,1},{1,0},{2,3},{3,2},{4,5},{5,4},{6,7},{7,6},{8,9},{9,8},{10,11... | collective-permute-start | bytes 396296 | tf_op jit(solution)/shard_map/ppermute | solution.py:49
  54.6 1.6 %collective-permute-start.4 = (f32[129,256]{1,0:T(8,128)S(1)}, f32[129,256]{1,0:T(8,128)S(1)}, u32[]{:S(2)}, u32[]{:S(2)}) collective-permute-start(f32[129,256]{1,0:T(8,128)S(1)} %bitcast.123), channel_id=1, source_target_pairs={{0,2},{1,3},{2,0},{3,1},{4,6},{5,7},{6,4},{7,5},{8,10},{9,11},{10,... | collective-permute-start | bytes 396296 | tf_op jit(solution)/shard_map/ppermute | solution.py:49
  56.8 2.3 %collective-permute-done.3 = f32[129,256]{1,0:T(8,128)S(1)} collective-permute-done((f32[129,256]{1,0:T(8,128)S(1)}, f32[129,256]{1,0:T(8,128)S(1)}, u32[]{:S(2)}, u32[]{:S(2)}) %collective-permute-start.3) | collective-permute-done | bytes 132128 | tf_op jit(solution)/shard_map/ppermute | solution.py:49
  59.1 3.6 %collective-permute-done.4 = f32[129,256]{1,0:T(8,128)S(1)} collective-permute-done((f32[129,256]{1,0:T(8,128)S(1)}, f32[129,256]{1,0:T(8,128)S(1)}, u32[]{:S(2)}, u32[]{:S(2)}) %collective-permute-start.4) | collective-permute-done | bytes 132128 | tf_op jit(solution)/shard_map/ppermute | solution.py:49
  62.8 2.9 %collective-permute-start.7 = (bf16[129,256]{1,0:T(8,128)(2,1)S(1)}, bf16[129,256]{1,0:T(8,128)(2,1)S(1)}, u32[]{:S(2)}, u32[]{:S(2)}) collective-permute-start(bf16[129,256]{1,0:T(8,128)(2,1)S(1)} %fusion.38), channel_id=1, source_target_pairs={{0,8},{4,12},{8,0},{12,4},{1,9},{5,13},{9,1},{13,5},{2,10},{6,14},... | collective-permute-start | bytes 198152 | tf_op jit(solution)/shard_map/ppermute | solution.py:26
  65.7 1.9 %collective-permute-start.8 = (bf16[129,256]{1,0:T(8,128)(2,1)S(1)}, bf16[129,256]{1,0:T(8,128)(2,1)S(1)}, u32[]{:S(2)}, u32[]{:S(2)}) collective-permute-start(bf16[129,256]{1,0:T(8,128)(2,1)S(1)} %fusion.38), channel_id=1, source_target_pairs={{0,4},{4,8},{8,12},{12,0},{1,5},{5,9},{9,13},{13,1},{2,6},{6,10},{... | collective-permute-start | bytes 198152 | tf_op jit(solution)/shard_map/ppermute | solution.py:26
  67.7 1.8 %collective-permute-done.7 = bf16[129,256]{1,0:T(8,128)(2,1)S(1)} collective-permute-done((bf16[129,256]{1,0:T(8,128)(2,1)S(1)}, bf16[129,256]{1,0:T(8,128)(2,1)S(1)}, u32[]{:S(2)}, u32[]{:S(2)}) %collective-permute-start.7) | collective-permute-done | bytes 66080 | tf_op jit(solution)/shard_map/ppermute | solution.py:26
  69.4 2.4 %collective-permute-done.8 = bf16[129,256]{1,0:T(8,128)(2,1)S(1)} collective-permute-done((bf16[129,256]{1,0:T(8,128)(2,1)S(1)}, bf16[129,256]{1,0:T(8,128)(2,1)S(1)}, u32[]{:S(2)}, u32[]{:S(2)}) %collective-permute-start.8) | collective-permute-done | bytes 66080 | tf_op jit(solution)/shard_map/ppermute | solution.py:26
  73.6 1.9 %collective-permute-start.9 = (bf16[4,129,256]{2,1,0:T(8,128)(2,1)S(1)}, bf16[4,129,256]{2,1,0:T(8,128)(2,1)S(1)}, u32[]{:S(2)}, u32[]{:S(2)}) collective-permute-start(bf16[4,129,256]{2,1,0:T(8,128)(2,1)S(1)} %pad_maximum_fusion.1), channel_id=1, source_target_pairs={{0,3},{1,2},{2,1},{3,0},{4,7},{5,6},{6,5},{7,4},{8,11},{9,10},{10,... | collective-permute-start | bytes 792584 | tf_op jit(solution)/shard_map/ppermute | solution.py:37
  75.5 5.7 %collective-permute-done.10 = bf16[4,129,256]{2,1,0:T(8,128)(2,1)S(1)} collective-permute-done((bf16[4,129,256]{2,1,0:T(8,128)(2,1)S(1)}, bf16[4,129,256]{2,1,0:T(8,128)(2,1)S(1)}, u32[]{:S(2)}, u32[]{:S(2)}) %collective-permute-start.10) | collective-permute-done | bytes 264224 | tf_op jit(solution)/shard_map/ppermute | solution.py:37
  81.2 3.0 %collective-permute-done.9 = bf16[4,129,256]{2,1,0:T(8,128)(2,1)S(1)} collective-permute-done((bf16[4,129,256]{2,1,0:T(8,128)(2,1)S(1)}, bf16[4,129,256]{2,1,0:T(8,128)(2,1)S(1)}, u32[]{:S(2)}, u32[]{:S(2)}) %collective-permute-start.9) | collective-permute-done | bytes 264224 | tf_op jit(solution)/shard_map/ppermute | solution.py:37
  85.5 2.4 %collective-permute-done.12 = bf16[4,4,129,256]{3,1,2,0:T(4,128)(2,1)} collective-permute-done((bf16[4,4,129,256]{3,1,2,0:T(4,128)(2,1)S(1)}, bf16[4,4,129,256]{3,1,2,0:T(4,128)(2,1)}, u32[]{:S(2)}, u32[]{:S(2)}) %collective-permute-start.12) | collective-permute-done | bytes 1056800 | tf_op jit(solution)/shard_map/ppermute | solution.py:26
  87.8 1.5 %select_bitcast_fusion.1 = (bf16[1,4,4,129,256]{4,3,2,1,0:T(8,128)(2,1)S(1)}, bf16[1,4,4,129,256]{4,3,2,1,0:T(8,128)(2,1)S(1)}) fusion(pred[]{:T(512)S(6)} %eq.124, bf16[4,4,129,256]{3,1,2,0:T(4,128)(2,1)} %collective-permute-done.12, bf16[1,4,129,256]{3,2,1,0:T(8,128)(2,1)S(1)} %get-tuple-element.25, bf16[1,4,129,256]{3,2,1,0:T(8,128)(2,1)S(1)} %get-tuple-element.27, ...), kind=kLoop, calls=%fused_computation.39 | loop fusion | flops 2641920 | bytes 4227074 | tf_op jit(solution)/shard_map/stack | solution.py:17
  90.2 2.0 %fusion.2 = (f32[2,128]{1,0:T(2,128)S(1)}, bf16[2,4,4,128,256]{4,3,2,1,0:T(8,128)(2,1)}) fusion(bf16[1,4,4,129,256]{4,3,2,1,0:T(8,128)(2,1)S(1)} %get-tuple-element.19, bf16[1,4,4,129,256]{4,3,2,1,0:T(8,128)(2,1)S(1)} %get-tuple-element.18), kind=kLoop, calls=%fused_computation.4 | loop fusion | flops 4194048 | bytes 4211712 | tf_op jit(solution)/shard_map/reduce_sum | solution.py:221
  92.6 2.5 %fusion.18 = bf16[4,4,256,256,1]{3,2,0,1,4:T(8,128)(2,1)S(1)} fusion(pred[2,128,256,1,1]{2,1,3,4,0:T(8,128)(4,1)S(1)} %bitcast.125, bf16[2,4,4,128,256]{4,3,2,1,0:T(8,128)(2,1)} %get-tuple-element.17, f32[4,4,256]{2,1,0:T(4,128)S(1)} %copy.162, f32[2,128]{1,0:T(2,128)S(1)} %add_rsqrt_fusion), kind=kOutput, calls=%fused_computation.26 | convolution fusion | flops 541065216 | bytes 4277248 | tf_op jit(solution)/shard_map/drq,decrk->qcek/dot_general | solution.py:237
  95.5 8.2 %fusion.22 = f32[2,896,256]{1,2,0:T(8,128)S(1)} fusion(bf16[256,4096,1]{0,1,2:T(8,128)(2,1)S(1)} %bitcast.116, bf16[1,2,896,4096]{3,2,1,0:T(8,128)(2,1)} %param.19), kind=kOutput, calls=%fused_computation.33 | convolution fusion | flops 3758096384 | bytes 18612224 | tf_op jit(solution)/shard_map/gfd,qd->gfq/dot_general | solution.py:116
  (85 shorter events, 19.1 us)
Async XLA Ops:
  3.9 12.4 %collective-permute-start = (bf16[2,16,4448]{2,1,0:T(8,128)(2,1)S(1)}, bf16[2,16,4448]{2,1,0:T(8,128)(2,1)S(1)}, u32[]{:S(2)}, u32[]{:S(2)}) collective-permute-start(bf16[2,16,4448]{2,1,0:T(8,128)(2,1)S(1)} %concatenate.17), channel_id=1, source_target_pairs={{0,12},{4,0},{8,4},{12,8},{1,13},{5,1},{9,5},{13,9},{2,14},{6,2},{... | collective-permute-start | bytes 854024 | tf_op jit(solution)/shard_map/ppermute | solution.py:26
  9.0 24.4 %collective-permute-start.1 = (bf16[2,16,4448]{2,1,0:T(8,128)(2,1)S(1)}, bf16[2,16,4448]{2,1,0:T(8,128)(2,1)S(1)}, u32[]{:S(2)}, u32[]{:S(2)}) collective-permute-start(bf16[2,16,4448]{2,1,0:T(8,128)(2,1)S(1)} %concatenate.17), channel_id=1, source_target_pairs={{0,8},{4,12},{8,0},{12,4},{1,9},{5,13},{9,1},{13,5},{2,10},{6,14},... | collective-permute-start | bytes 854024 | tf_op jit(solution)/shard_map/ppermute | solution.py:26
  9.0 24.4 %collective-permute-start.2 = (bf16[2,16,4448]{2,1,0:T(8,128)(2,1)S(1)}, bf16[2,16,4448]{2,1,0:T(8,128)(2,1)S(1)}, u32[]{:S(2)}, u32[]{:S(2)}) collective-permute-start(bf16[2,16,4448]{2,1,0:T(8,128)(2,1)S(1)} %concatenate.17), channel_id=1, source_target_pairs={{0,4},{4,8},{8,12},{12,0},{1,5},{5,9},{9,13},{13,1},{2,6},{6,10},{... | collective-permute-start | bytes 854024 | tf_op jit(solution)/shard_map/ppermute | solution.py:26
  36.7 4.1 %copy-start.2 = (f32[32]{0:T(128)S(1)}, f32[32]{0:T(128)}, u32[]{:S(2)}) copy-start(f32[32]{0:T(128)} %param.16) | copy-start | bytes 388
  53.1 6.0 %collective-permute-start.3 = (f32[129,256]{1,0:T(8,128)S(1)}, f32[129,256]{1,0:T(8,128)S(1)}, u32[]{:S(2)}, u32[]{:S(2)}) collective-permute-start(f32[129,256]{1,0:T(8,128)S(1)} %bitcast.122), channel_id=1, source_target_pairs={{0,1},{1,0},{2,3},{3,2},{4,5},{5,4},{6,7},{7,6},{8,9},{9,8},{10,11... | collective-permute-start | bytes 396296 | tf_op jit(solution)/shard_map/ppermute | solution.py:49
  54.6 8.1 %collective-permute-start.4 = (f32[129,256]{1,0:T(8,128)S(1)}, f32[129,256]{1,0:T(8,128)S(1)}, u32[]{:S(2)}, u32[]{:S(2)}) collective-permute-start(f32[129,256]{1,0:T(8,128)S(1)} %bitcast.123), channel_id=1, source_target_pairs={{0,2},{1,3},{2,0},{3,1},{4,6},{5,7},{6,4},{7,5},{8,10},{9,11},{10,... | collective-permute-start | bytes 396296 | tf_op jit(solution)/shard_map/ppermute | solution.py:49
  56.2 6.5 %collective-permute-start.5 = (f32[129,256]{1,0:T(8,128)S(1)}, f32[129,256]{1,0:T(8,128)S(1)}, u32[]{:S(2)}, u32[]{:S(2)}) collective-permute-start(f32[129,256]{1,0:T(8,128)S(1)} %bitcast.124), channel_id=1, source_target_pairs={{0,3},{1,2},{2,1},{3,0},{4,7},{5,6},{6,5},{7,4},{8,11},{9,10},{10,... | collective-permute-start | bytes 396296 | tf_op jit(solution)/shard_map/ppermute | solution.py:49
  62.8 4.9 %collective-permute-start.6 = (bf16[129,256]{1,0:T(8,128)(2,1)S(1)}, bf16[129,256]{1,0:T(8,128)(2,1)S(1)}, u32[]{:S(2)}, u32[]{:S(2)}) collective-permute-start(bf16[129,256]{1,0:T(8,128)(2,1)S(1)} %fusion.38), channel_id=1, source_target_pairs={{0,12},{4,0},{8,4},{12,8},{1,13},{5,1},{9,5},{13,9},{2,14},{6,2},{... | collective-permute-start | bytes 198152 | tf_op jit(solution)/shard_map/ppermute | solution.py:26
  62.8 6.6 %collective-permute-start.7 = (bf16[129,256]{1,0:T(8,128)(2,1)S(1)}, bf16[129,256]{1,0:T(8,128)(2,1)S(1)}, u32[]{:S(2)}, u32[]{:S(2)}) collective-permute-start(bf16[129,256]{1,0:T(8,128)(2,1)S(1)} %fusion.38), channel_id=1, source_target_pairs={{0,8},{4,12},{8,0},{12,4},{1,9},{5,13},{9,1},{13,5},{2,10},{6,14},... | collective-permute-start | bytes 198152 | tf_op jit(solution)/shard_map/ppermute | solution.py:26
  65.7 6.1 %collective-permute-start.8 = (bf16[129,256]{1,0:T(8,128)(2,1)S(1)}, bf16[129,256]{1,0:T(8,128)(2,1)S(1)}, u32[]{:S(2)}, u32[]{:S(2)}) collective-permute-start(bf16[129,256]{1,0:T(8,128)(2,1)S(1)} %fusion.38), channel_id=1, source_target_pairs={{0,4},{4,8},{8,12},{12,0},{1,5},{5,9},{9,13},{13,1},{2,6},{6,10},{... | collective-permute-start | bytes 198152 | tf_op jit(solution)/shard_map/ppermute | solution.py:26
  71.9 9.3 %collective-permute-start.10 = (bf16[4,129,256]{2,1,0:T(8,128)(2,1)S(1)}, bf16[4,129,256]{2,1,0:T(8,128)(2,1)S(1)}, u32[]{:S(2)}, u32[]{:S(2)}) collective-permute-start(bf16[4,129,256]{2,1,0:T(8,128)(2,1)S(1)} %pad_maximum_fusion.1), channel_id=1, source_target_pairs={{0,2},{1,3},{2,0},{3,1},{4,6},{5,7},{6,4},{7,5},{8,10},{9,11},{10,... | collective-permute-start | bytes 792584 | tf_op jit(solution)/shard_map/ppermute | solution.py:37
  73.1 8.1 %collective-permute-start.11 = (bf16[4,129,256]{2,1,0:T(8,128)(2,1)S(1)}, bf16[4,129,256]{2,1,0:T(8,128)(2,1)S(1)}, u32[]{:S(2)}, u32[]{:S(2)}) collective-permute-start(bf16[4,129,256]{2,1,0:T(8,128)(2,1)S(1)} %pad_maximum_fusion.1), channel_id=1, source_target_pairs={{0,1},{1,0},{2,3},{3,2},{4,5},{5,4},{6,7},{7,6},{8,9},{9,8},{10,11... | collective-permute-start | bytes 792584 | tf_op jit(solution)/shard_map/ppermute | solution.py:37
  73.6 10.6 %collective-permute-start.9 = (bf16[4,129,256]{2,1,0:T(8,128)(2,1)S(1)}, bf16[4,129,256]{2,1,0:T(8,128)(2,1)S(1)}, u32[]{:S(2)}, u32[]{:S(2)}) collective-permute-start(bf16[4,129,256]{2,1,0:T(8,128)(2,1)S(1)} %pad_maximum_fusion.1), channel_id=1, source_target_pairs={{0,3},{1,2},{2,1},{3,0},{4,7},{5,6},{6,5},{7,4},{8,11},{9,10},{10,... | collective-permute-start | bytes 792584 | tf_op jit(solution)/shard_map/ppermute | solution.py:37
  84.4 1.0 copy-start.1
  85.0 2.9 %collective-permute-start.12 = (bf16[4,4,129,256]{3,1,2,0:T(4,128)(2,1)S(1)}, bf16[4,4,129,256]{3,1,2,0:T(4,128)(2,1)}, u32[]{:S(2)}, u32[]{:S(2)}) collective-permute-start(bf16[4,4,129,256]{3,1,2,0:T(4,128)(2,1)S(1)} %copy.156), channel_id=1, source_target_pairs={{0,16},{16,0},{1,17},{17,1},{2,18},{18,2},{3,19},{19,3},{4,20},{20... | collective-permute-start | bytes 3170312 | tf_op jit(solution)/shard_map/ppermute | solution.py:26
  103.7 1.8 %copy-start = (bf16[2,4,4,128,256]{4,3,2,1,0:T(8,128)(2,1)S(1)}, bf16[2,4,4,128,256]{4,3,2,1,0:T(8,128)(2,1)}, u32[]{:S(2)}) copy-start(bf16[2,4,4,128,256]{4,3,2,1,0:T(8,128)(2,1)} %get-tuple-element.17) | copy-start | bytes 6291460

commit v12 on v10

--- a/solution.py
+++ b/solution.py
@@ -158,9 +158,11 @@
     head_count = decay_log.shape[2]
     decay_base = 2 * width_in + 2 * state_size
 
-    def front(x_part, z_part, b_part, c_part, decay_part):
+    def front(x_part, z_part, b_part, c_part, decay_part, after=None):
         part_count = x_part.shape[0]
         packed = jnp.concatenate([x_part, z_part, b_part, c_part] + split_exact(decay_part), axis=2)
+        if after is not None:
+            _, packed = lax.optimization_barrier((after, packed))
         packed = jnp.moveaxis(gather_blocks(packed, "ctx", ctx_count), 0, 1).reshape(
             part_count, ctx_count * block_len, packed.shape[2]
         )
@@ -173,10 +175,10 @@
         c_all = packed[:, :, 2 * width_in + state_size : decay_base]
         ssd = mixer(x_all, b_all, c_all, decay_all, skip)
         gated = (ssd * jax.nn.silu(z_all.astype(jnp.float32))).astype(jnp.bfloat16)
-        return jnp.einsum("stk,kd->std", gated, out_weight, preferred_element_type=jnp.float32)
+        return jnp.einsum("stk,kd->std", gated, out_weight, preferred_element_type=jnp.float32), packed
 
     if device_count * row_count * model_width * 2 > (8 << 20):
-        partial_value = front(x_in, z_in, b_in, c_in, decay_log)
+        partial_value = front(x_in, z_in, b_in, c_in, decay_log)[0]
         return dispatch_routed(partial_value, moe_gain, gate_up, expert_ids, slot_ids, capacity)
     total_len = ctx_count * block_len
     route = jnp.stack([expert_ids, slot_ids], axis=-1).astype(jnp.float32).reshape(-1)
@@ -188,10 +190,11 @@
     split = 2 if seq_count % 2 == 0 else 1
     part_len = seq_count // split
     token_parts = []
+    arrived = None
     for part in range(split):
         streams = slice(part * part_len, (part + 1) * part_len)
-        partial_value = front(
-            x_in[streams], z_in[streams], b_in[streams], c_in[streams], decay_log[streams]
+        partial_value, arrived = front(
+            x_in[streams], z_in[streams], b_in[streams], c_in[streams], decay_log[streams], arrived
         )
         rows = partial_value.reshape(part_len * total_len, col_width)
         if part == 0:

time: 102 us -> 100 us (0.980)
  waiting for transfers between devices: 14.1 us -> 22 us
  local copies, waits for them, and re-layouts: 20.5 us -> 15.7 us
  other arithmetic: 8.59 us -> 5.22 us
  matrix products: 20.3 us -> 18.9 us
    ppermute x6, waiting for transfers between devices: 1.17 us -> 5.92 us  [sum_scatter(): total = total + lax.ppermute(send, axis_name, perm)]
    ppermute x14, waiting for transfers between devices: 8.36 us -> 12 us  [gather_blocks(): received.append(lax.ppermute(value, axis_name, perm))]
    dot_general x2, matrix products: 5.29 us -> 2.43 us  [mixer(): ssd = jnp.einsum('sktuh,skuhp->skthp', kernel, x_float, precision=highest)]
    reshape x2, local copies, waits for them, and re-layouts: 2.65 us -> 0.63 us  [mixer(): return ssd.reshape(seq_count, total_len, width_in)]
    dot_general x2, matrix products: 5.14 us -> 7.16 us  [front(): jnp.einsum('stk,kd->std', gated, out_weight, preferred_element_type=jnp.f...]
    slice x2, local copies, waits for them, and re-layouts: 2.24 us -> 0.56 us  [front(): x_all = packed[:, :, :width_in]]
    ppermute x6, starting transfers between devices: 8.63 us -> 7.01 us  [gather_xor(): received.append(lax.ppermute(value, axis_name, perm))]
    ppermute x14, starting transfers between devices: 20.9 us -> 22.4 us  [gather_blocks(): received.append(lax.ppermute(value, axis_name, perm))]
  transfers between devices with their start and end apart: 26 -> 26, of which waited for: 7 -> 15; matrix products, arithmetic and copies ran while one was open for 11% -> 10% of each run, Pallas kernels for 0% -> 0%
where the time goes in v12:
time: 100 us; the launch traced here: 99.4 us
  starting transfers between devices  36.5 us (36%)
  waiting for transfers between devices  22 us (22%)
  matrix products  18.9 us (19%)
  local copies, waits for them, and re-layouts  15.7 us (16%)
  other arithmetic  5.22 us (5%)
  between operations  1.1 us (1%)
    ppermute x14, starting transfers between devices, gather_blocks(): received.append(lax.ppermute(value, axis_name, perm))  22.4 us
    ppermute x14, waiting for transfers between devices, gather_blocks(): received.append(lax.ppermute(value, axis_name, perm))  12 us
    dot_general x1, matrix products, expert_ffn(): jnp.einsum('gfd,qd->gfq', gate_up[0], slot_rows, preferred_element_type=j...  8.15 us
    dot_general x2, matrix products, front(): jnp.einsum('stk,kd->std', gated, out_weight, preferred_element_type=jnp.f...  7.16 us
    ppermute x6, starting transfers between devices, sum_scatter(): total = total + lax.ppermute(send, axis_name, perm)  7.11 us
    ppermute x6, starting transfers between devices, gather_xor(): received.append(lax.ppermute(value, axis_name, perm))  7.01 us
    dot_general x1, local copies, waits for them, and re-layouts, front(): jnp.einsum('stk,kd->std', gated, out_weight, preferred_element_type=jnp.f...  6.56 us
    ppermute x6, waiting for transfers between devices, sum_scatter(): total = total + lax.ppermute(send, axis_name, perm)  5.92 us
  transfers between devices with their start and end apart: 26, of which 15 were waited for; matrix products, arithmetic and copies ran while one was open for 10% of the time, Pallas kernels for 0%

profile of v12, /device:TPU:0, one launch (start us, length us, event | category | flops | bytes accessed | tf_op | source)
XLA Modules:
  0.0 99.4 jit_solution(11122779946346313510)
XLA Ops:
  4.6 3.1 %collective-permute-start.2 = (bf16[1,16,4448]{2,1,0:T(8,128)(2,1)S(1)}, bf16[1,16,4448]{2,1,0:T(8,128)(2,1)S(1)}, u32[]{:S(2)}, u32[]{:S(2)}) collective-permute-start(bf16[1,16,4448]{2,1,0:T(8,128)(2,1)S(1)} %concatenate.15), channel_id=1, source_target_pairs={{0,4},{4,8},{8,12},{12,0},{1,5},{5,9},{9,13},{13,1},{2,6},{6,10},{... | collective-permute-start | bytes 427016 | tf_op jit(solution)/shard_map/ppermute | solution.py:26
  7.6 2.6 %collective-permute-start.1 = (bf16[1,16,4448]{2,1,0:T(8,128)(2,1)S(1)}, bf16[1,16,4448]{2,1,0:T(8,128)(2,1)S(1)}, u32[]{:S(2)}, u32[]{:S(2)}) collective-permute-start(bf16[1,16,4448]{2,1,0:T(8,128)(2,1)S(1)} %concatenate.15), channel_id=1, source_target_pairs={{0,8},{4,12},{8,0},{12,4},{1,9},{5,13},{9,1},{13,5},{2,10},{6,14},... | collective-permute-start | bytes 427016 | tf_op jit(solution)/shard_map/ppermute | solution.py:26
  10.2 1.3 %collective-permute-start = (bf16[1,16,4448]{2,1,0:T(8,128)(2,1)S(1)}, bf16[1,16,4448]{2,1,0:T(8,128)(2,1)S(1)}, u32[]{:S(2)}, u32[]{:S(2)}) collective-permute-start(bf16[1,16,4448]{2,1,0:T(8,128)(2,1)S(1)} %concatenate.15), channel_id=1, source_target_pairs={{0,12},{4,0},{8,4},{12,8},{1,13},{5,1},{9,5},{13,9},{2,14},{6,2},{... | collective-permute-start | bytes 427016 | tf_op jit(solution)/shard_map/ppermute | solution.py:26
  12.5 6.6 %copy.197 = bf16[1024,2048]{1,0:T(8,128)(2,1)} copy(bf16[1024,2048]{0,1:T(8,128)(2,1)} %bitcast.177) | data formatting | bytes 8388608 | tf_op jit(solution)/shard_map/stk,kd->std/dot_general | solution.py:178
  22.5 3.6 %fusion.50 = f32[64,4,256]{2,0,1:T(8,128)S(1)} fusion(bf16[4,256,2048]{2,1,0:T(8,128)(2,1)} %bitcast.178, f32[1,64,2048]{2,1,0:T(8,128)S(1)} %copy.167, bf16[1,64,4448]{2,1,0:T(8,128)(2,1)S(1)} %bitcast.188), kind=kOutput, calls=%fused_computation.77 | convolution fusion | flops 269352960 | bytes 5242880 | tf_op jit(solution)/shard_map/stk,kd->std/dot_general | solution.py:178
  26.1 1.6 %collective-permute-start.3 = (f32[65,256]{1,0:T(8,128)S(1)}, f32[65,256]{1,0:T(8,128)S(1)}, u32[]{:S(2)}, u32[]{:S(2)}) collective-permute-start(f32[65,256]{1,0:T(8,128)S(1)} %get-tuple-element.44), channel_id=1, source_target_pairs={{0,1},{1,0},{2,3},{3,2},{4,5},{5,4},{6,7},{7,6},{8,9},{9,8},{10,11... | collective-permute-start | bytes 199688 | tf_op jit(solution)/shard_map/ppermute | solution.py:49
  27.7 1.5 %collective-permute-start.4 = (f32[65,256]{1,0:T(8,128)S(1)}, f32[65,256]{1,0:T(8,128)S(1)}, u32[]{:S(2)}, u32[]{:S(2)}) collective-permute-start(f32[65,256]{1,0:T(8,128)S(1)} %get-tuple-element.45), channel_id=1, source_target_pairs={{0,2},{1,3},{2,0},{3,1},{4,6},{5,7},{6,4},{7,5},{8,10},{9,11},{10,... | collective-permute-start | bytes 199688 | tf_op jit(solution)/shard_map/ppermute | solution.py:49
  30.5 1.5 %collective-permute-done.4 = f32[65,256]{1,0:T(8,128)S(1)} collective-permute-done((f32[65,256]{1,0:T(8,128)S(1)}, f32[65,256]{1,0:T(8,128)S(1)}, u32[]{:S(2)}, u32[]{:S(2)}) %collective-permute-start.4) | collective-permute-done | bytes 66592 | tf_op jit(solution)/shard_map/ppermute | solution.py:49
  32.0 2.4 %collective-permute-done.5 = f32[65,256]{1,0:T(8,128)S(1)} collective-permute-done((f32[65,256]{1,0:T(8,128)S(1)}, f32[65,256]{1,0:T(8,128)S(1)}, u32[]{:S(2)}, u32[]{:S(2)}) %collective-permute-start.5) | collective-permute-done | bytes 66592 | tf_op jit(solution)/shard_map/ppermute | solution.py:49
  34.5 3.6 %collective-permute-start.8 = (bf16[65,256]{1,0:T(8,128)(2,1)S(1)}, bf16[65,256]{1,0:T(8,128)(2,1)S(1)}, u32[]{:S(2)}, u32[]{:S(2)}) collective-permute-start(bf16[65,256]{1,0:T(8,128)(2,1)S(1)} %fusion.61), channel_id=1, source_target_pairs={{0,4},{4,8},{8,12},{12,0},{1,5},{5,9},{9,13},{13,1},{2,6},{6,10},{... | collective-permute-start | bytes 99848 | tf_op jit(solution)/shard_map/ppermute | solution.py:26
  38.1 1.6 %collective-permute-start.7 = (bf16[65,256]{1,0:T(8,128)(2,1)S(1)}, bf16[65,256]{1,0:T(8,128)(2,1)S(1)}, u32[]{:S(2)}, u32[]{:S(2)}) collective-permute-start(bf16[65,256]{1,0:T(8,128)(2,1)S(1)} %fusion.61), channel_id=1, source_target_pairs={{0,8},{4,12},{8,0},{12,4},{1,9},{5,13},{9,1},{13,5},{2,10},{6,14},... | collective-permute-start | bytes 99848 | tf_op jit(solution)/shard_map/ppermute | solution.py:26
  43.4 1.3 %collective-permute-start.13 = (bf16[1,16,4448]{2,1,0:T(8,128)(2,1)S(1)}, bf16[1,16,4448]{2,1,0:T(8,128)(2,1)S(1)}, u32[]{:S(2)}, u32[]{:S(2)}) collective-permute-start(bf16[1,16,4448]{2,1,0:T(8,128)(2,1)S(1)} %concatenate.18), channel_id=1, source_target_pairs={{0,12},{4,0},{8,4},{12,8},{1,13},{5,1},{9,5},{13,9},{2,14},{6,2},{... | collective-permute-start | bytes 427016 | tf_op jit(solution)/shard_map/ppermute | solution.py:26
  45.7 3.6 %collective-permute-done.15 = bf16[1,16,4448]{2,1,0:T(8,128)(2,1)S(1)} collective-permute-done((bf16[1,16,4448]{2,1,0:T(8,128)(2,1)S(1)}, bf16[1,16,4448]{2,1,0:T(8,128)(2,1)S(1)}, u32[]{:S(2)}, u32[]{:S(2)}) %collective-permute-start.15) | collective-permute-done | bytes 142368 | tf_op jit(solution)/shard_map/ppermute | solution.py:26
  49.3 4.0 %collective-permute-done.14 = bf16[1,16,4448]{2,1,0:T(8,128)(2,1)S(1)} collective-permute-done((bf16[1,16,4448]{2,1,0:T(8,128)(2,1)S(1)}, bf16[1,16,4448]{2,1,0:T(8,128)(2,1)S(1)}, u32[]{:S(2)}, u32[]{:S(2)}) %collective-permute-start.14) | collective-permute-done | bytes 142368 | tf_op jit(solution)/shard_map/ppermute | solution.py:26
  56.1 3.6 %fusion.48 = f32[64,4,256]{2,0,1:T(8,128)S(1)} fusion(bf16[4,256,2048]{2,1,0:T(8,128)(2,1)} %bitcast.179, f32[1,64,2048]{2,1,0:T(8,128)S(1)} %copy.177, bf16[1,64,4448]{2,1,0:T(8,128)(2,1)S(1)} %bitcast.184), kind=kOutput, calls=%fused_computation.75 | convolution fusion | flops 269352960 | bytes 5242880 | tf_op jit(solution)/shard_map/stk,kd->std/dot_general | solution.py:178
  60.3 1.5 %collective-permute-start.18 = (f32[64,256]{1,0:T(8,128)S(1)}, f32[64,256]{1,0:T(8,128)S(1)}, u32[]{:S(2)}, u32[]{:S(2)}) collective-permute-start(f32[64,256]{1,0:T(8,128)S(1)} %get-tuple-element.48), channel_id=1, source_target_pairs={{0,3},{1,2},{2,1},{3,0},{4,7},{5,6},{6,5},{7,4},{8,11},{9,10},{10,... | collective-permute-start | bytes 196616 | tf_op jit(solution)/shard_map/ppermute | solution.py:49
  61.8 1.5 %collective-permute-start.17 = (f32[64,256]{1,0:T(8,128)S(1)}, f32[64,256]{1,0:T(8,128)S(1)}, u32[]{:S(2)}, u32[]{:S(2)}) collective-permute-start(f32[64,256]{1,0:T(8,128)S(1)} %get-tuple-element.49), channel_id=1, source_target_pairs={{0,2},{1,3},{2,0},{3,1},{4,6},{5,7},{6,4},{7,5},{8,10},{9,11},{10,... | collective-permute-start | bytes 196616 | tf_op jit(solution)/shard_map/ppermute | solution.py:49
  64.6 2.2 %collective-permute-start.9 = (bf16[4,65,256]{2,1,0:T(8,128)(2,1)S(1)}, bf16[4,65,256]{2,1,0:T(8,128)(2,1)S(1)}, u32[]{:S(2)}, u32[]{:S(2)}) collective-permute-start(bf16[4,65,256]{2,1,0:T(8,128)(2,1)S(1)} %pad_maximum_fusion.4), channel_id=1, source_target_pairs={{0,3},{1,2},{2,1},{3,0},{4,7},{5,6},{6,5},{7,4},{8,11},{9,10},{10,... | collective-permute-start | bytes 399368 | tf_op jit(solution)/shard_map/ppermute | solution.py:37
  68.0 2.9 %collective-permute-start.21 = (bf16[64,256]{1,0:T(8,128)(2,1)S(1)}, bf16[64,256]{1,0:T(8,128)(2,1)S(1)}, u32[]{:S(2)}, u32[]{:S(2)}) collective-permute-start(bf16[64,256]{1,0:T(8,128)(2,1)S(1)} %fusion.68), channel_id=1, source_target_pairs={{0,4},{4,8},{8,12},{12,0},{1,5},{5,9},{9,13},{13,1},{2,6},{6,10},{... | collective-permute-start | bytes 98312 | tf_op jit(solution)/shard_map/ppermute | solution.py:26
  73.8 2.0 %collective-permute-done.20 = bf16[64,256]{1,0:T(8,128)(2,1)S(1)} collective-permute-done((bf16[64,256]{1,0:T(8,128)(2,1)S(1)}, bf16[64,256]{1,0:T(8,128)(2,1)S(1)}, u32[]{:S(2)}, u32[]{:S(2)}) %collective-permute-start.20) | collective-permute-done | bytes 32800 | tf_op jit(solution)/shard_map/ppermute | solution.py:26
  76.2 1.7 %collective-permute-start.24 = (bf16[4,64,256]{2,1,0:T(8,128)(2,1)S(1)}, bf16[4,64,256]{2,1,0:T(8,128)(2,1)S(1)}, u32[]{:S(2)}, u32[]{:S(2)}) collective-permute-start(bf16[4,64,256]{2,1,0:T(8,128)(2,1)S(1)} %pad_maximum_fusion.5), channel_id=1, source_target_pairs={{0,1},{1,0},{2,3},{3,2},{4,5},{5,4},{6,7},{7,6},{8,9},{9,8},{10,11... | collective-permute-start | bytes 393224 | tf_op jit(solution)/shard_map/ppermute | solution.py:37
  78.0 1.7 %collective-permute-start.22 = (bf16[4,64,256]{2,1,0:T(8,128)(2,1)S(1)}, bf16[4,64,256]{2,1,0:T(8,128)(2,1)S(1)}, u32[]{:S(2)}, u32[]{:S(2)}) collective-permute-start(bf16[4,64,256]{2,1,0:T(8,128)(2,1)S(1)} %pad_maximum_fusion.5), channel_id=1, source_target_pairs={{0,3},{1,2},{2,1},{3,0},{4,7},{5,6},{6,5},{7,4},{8,11},{9,10},{10,... | collective-permute-start | bytes 393224 | tf_op jit(solution)/shard_map/ppermute | solution.py:37
  81.2 3.1 %collective-permute-done.23 = bf16[4,64,256]{2,1,0:T(8,128)(2,1)S(1)} collective-permute-done((bf16[4,64,256]{2,1,0:T(8,128)(2,1)S(1)}, bf16[4,64,256]{2,1,0:T(8,128)(2,1)S(1)}, u32[]{:S(2)}, u32[]{:S(2)}) %collective-permute-start.23) | collective-permute-done | bytes 131104 | tf_op jit(solution)/shard_map/ppermute | solution.py:37
  88.4 8.2 %fusion.9 = f32[2,896,256]{1,2,0:T(8,128)S(1)} fusion(bf16[256,4096,1]{0,1,2:T(8,128)(2,1)S(1)} %bitcast.180, bf16[1,2,896,4096]{3,2,1,0:T(8,128)(2,1)} %param.19), kind=kOutput, calls=%fused_computation.12 | convolution fusion | flops 3758096384 | bytes 18612224 | tf_op jit(solution)/shard_map/gfd,qd->gfq/dot_general | solution.py:105
  (121 shorter events, 31.7 us)
Async XLA Ops:
  4.6 14.6 %collective-permute-start.2 = (bf16[1,16,4448]{2,1,0:T(8,128)(2,1)S(1)}, bf16[1,16,4448]{2,1,0:T(8,128)(2,1)S(1)}, u32[]{:S(2)}, u32[]{:S(2)}) collective-permute-start(bf16[1,16,4448]{2,1,0:T(8,128)(2,1)S(1)} %concatenate.15), channel_id=1, source_target_pairs={{0,4},{4,8},{8,12},{12,0},{1,5},{5,9},{9,13},{13,1},{2,6},{6,10},{... | collective-permute-start | bytes 427016 | tf_op jit(solution)/shard_map/ppermute | solution.py:26
  7.6 12.0 %collective-permute-start.1 = (bf16[1,16,4448]{2,1,0:T(8,128)(2,1)S(1)}, bf16[1,16,4448]{2,1,0:T(8,128)(2,1)S(1)}, u32[]{:S(2)}, u32[]{:S(2)}) collective-permute-start(bf16[1,16,4448]{2,1,0:T(8,128)(2,1)S(1)} %concatenate.15), channel_id=1, source_target_pairs={{0,8},{4,12},{8,0},{12,4},{1,9},{5,13},{9,1},{13,5},{2,10},{6,14},... | collective-permute-start | bytes 427016 | tf_op jit(solution)/shard_map/ppermute | solution.py:26
  10.2 9.4 %collective-permute-start = (bf16[1,16,4448]{2,1,0:T(8,128)(2,1)S(1)}, bf16[1,16,4448]{2,1,0:T(8,128)(2,1)S(1)}, u32[]{:S(2)}, u32[]{:S(2)}) collective-permute-start(bf16[1,16,4448]{2,1,0:T(8,128)(2,1)S(1)} %concatenate.15), channel_id=1, source_target_pairs={{0,12},{4,0},{8,4},{12,8},{1,13},{5,1},{9,5},{13,9},{2,14},{6,2},{... | collective-permute-start | bytes 427016 | tf_op jit(solution)/shard_map/ppermute | solution.py:26
  26.1 4.4 %collective-permute-start.3 = (f32[65,256]{1,0:T(8,128)S(1)}, f32[65,256]{1,0:T(8,128)S(1)}, u32[]{:S(2)}, u32[]{:S(2)}) collective-permute-start(f32[65,256]{1,0:T(8,128)S(1)} %get-tuple-element.44), channel_id=1, source_target_pairs={{0,1},{1,0},{2,3},{3,2},{4,5},{5,4},{6,7},{7,6},{8,9},{9,8},{10,11... | collective-permute-start | bytes 199688 | tf_op jit(solution)/shard_map/ppermute | solution.py:49
  27.7 4.4 %collective-permute-start.4 = (f32[65,256]{1,0:T(8,128)S(1)}, f32[65,256]{1,0:T(8,128)S(1)}, u32[]{:S(2)}, u32[]{:S(2)}) collective-permute-start(f32[65,256]{1,0:T(8,128)S(1)} %get-tuple-element.45), channel_id=1, source_target_pairs={{0,2},{1,3},{2,0},{3,1},{4,6},{5,7},{6,4},{7,5},{8,10},{9,11},{10,... | collective-permute-start | bytes 199688 | tf_op jit(solution)/shard_map/ppermute | solution.py:49
  29.2 5.3 %collective-permute-start.5 = (f32[65,256]{1,0:T(8,128)S(1)}, f32[65,256]{1,0:T(8,128)S(1)}, u32[]{:S(2)}, u32[]{:S(2)}) collective-permute-start(f32[65,256]{1,0:T(8,128)S(1)} %get-tuple-element.46), channel_id=1, source_target_pairs={{0,3},{1,2},{2,1},{3,0},{4,7},{5,6},{6,5},{7,4},{8,11},{9,10},{10,... | collective-permute-start | bytes 199688 | tf_op jit(solution)/shard_map/ppermute | solution.py:49
  34.5 8.9 %collective-permute-start.8 = (bf16[65,256]{1,0:T(8,128)(2,1)S(1)}, bf16[65,256]{1,0:T(8,128)(2,1)S(1)}, u32[]{:S(2)}, u32[]{:S(2)}) collective-permute-start(bf16[65,256]{1,0:T(8,128)(2,1)S(1)} %fusion.61), channel_id=1, source_target_pairs={{0,4},{4,8},{8,12},{12,0},{1,5},{5,9},{9,13},{13,1},{2,6},{6,10},{... | collective-permute-start | bytes 99848 | tf_op jit(solution)/shard_map/ppermute | solution.py:26
  38.1 6.7 %collective-permute-start.7 = (bf16[65,256]{1,0:T(8,128)(2,1)S(1)}, bf16[65,256]{1,0:T(8,128)(2,1)S(1)}, u32[]{:S(2)}, u32[]{:S(2)}) collective-permute-start(bf16[65,256]{1,0:T(8,128)(2,1)S(1)} %fusion.61), channel_id=1, source_target_pairs={{0,8},{4,12},{8,0},{12,4},{1,9},{5,13},{9,1},{13,5},{2,10},{6,14},... | collective-permute-start | bytes 99848 | tf_op jit(solution)/shard_map/ppermute | solution.py:26
  39.7 6.0 %collective-permute-start.6 = (bf16[65,256]{1,0:T(8,128)(2,1)S(1)}, bf16[65,256]{1,0:T(8,128)(2,1)S(1)}, u32[]{:S(2)}, u32[]{:S(2)}) collective-permute-start(bf16[65,256]{1,0:T(8,128)(2,1)S(1)} %fusion.61), channel_id=1, source_target_pairs={{0,12},{4,0},{8,4},{12,8},{1,13},{5,1},{9,5},{13,9},{2,14},{6,2},{... | collective-permute-start | bytes 99848 | tf_op jit(solution)/shard_map/ppermute | solution.py:26
  40.9 8.4 %collective-permute-start.15 = (bf16[1,16,4448]{2,1,0:T(8,128)(2,1)S(1)}, bf16[1,16,4448]{2,1,0:T(8,128)(2,1)S(1)}, u32[]{:S(2)}, u32[]{:S(2)}) collective-permute-start(bf16[1,16,4448]{2,1,0:T(8,128)(2,1)S(1)} %concatenate.18), channel_id=1, source_target_pairs={{0,4},{4,8},{8,12},{12,0},{1,5},{5,9},{9,13},{13,1},{2,6},{6,10},{... | collective-permute-start | bytes 427016 | tf_op jit(solution)/shard_map/ppermute | solution.py:26
  42.1 11.2 %collective-permute-start.14 = (bf16[1,16,4448]{2,1,0:T(8,128)(2,1)S(1)}, bf16[1,16,4448]{2,1,0:T(8,128)(2,1)S(1)}, u32[]{:S(2)}, u32[]{:S(2)}) collective-permute-start(bf16[1,16,4448]{2,1,0:T(8,128)(2,1)S(1)} %concatenate.18), channel_id=1, source_target_pairs={{0,8},{4,12},{8,0},{12,4},{1,9},{5,13},{9,1},{13,5},{2,10},{6,14},... | collective-permute-start | bytes 427016 | tf_op jit(solution)/shard_map/ppermute | solution.py:26
  43.4 9.9 %collective-permute-start.13 = (bf16[1,16,4448]{2,1,0:T(8,128)(2,1)S(1)}, bf16[1,16,4448]{2,1,0:T(8,128)(2,1)S(1)}, u32[]{:S(2)}, u32[]{:S(2)}) collective-permute-start(bf16[1,16,4448]{2,1,0:T(8,128)(2,1)S(1)} %concatenate.18), channel_id=1, source_target_pairs={{0,12},{4,0},{8,4},{12,8},{1,13},{5,1},{9,5},{13,9},{2,14},{6,2},{... | collective-permute-start | bytes 427016 | tf_op jit(solution)/shard_map/ppermute | solution.py:26
  59.7 4.9 %collective-permute-start.16 = (f32[64,256]{1,0:T(8,128)S(1)}, f32[64,256]{1,0:T(8,128)S(1)}, u32[]{:S(2)}, u32[]{:S(2)}) collective-permute-start(f32[64,256]{1,0:T(8,128)S(1)} %get-tuple-element.47), channel_id=1, source_target_pairs={{0,1},{1,0},{2,3},{3,2},{4,5},{5,4},{6,7},{7,6},{8,9},{9,8},{10,11... | collective-permute-start | bytes 196616 | tf_op jit(solution)/shard_map/ppermute | solution.py:49
  60.3 6.5 %collective-permute-start.18 = (f32[64,256]{1,0:T(8,128)S(1)}, f32[64,256]{1,0:T(8,128)S(1)}, u32[]{:S(2)}, u32[]{:S(2)}) collective-permute-start(f32[64,256]{1,0:T(8,128)S(1)} %get-tuple-element.48), channel_id=1, source_target_pairs={{0,3},{1,2},{2,1},{3,0},{4,7},{5,6},{6,5},{7,4},{8,11},{9,10},{10,... | collective-permute-start | bytes 196616 | tf_op jit(solution)/shard_map/ppermute | solution.py:49
  61.8 6.2 %collective-permute-start.17 = (f32[64,256]{1,0:T(8,128)S(1)}, f32[64,256]{1,0:T(8,128)S(1)}, u32[]{:S(2)}, u32[]{:S(2)}) collective-permute-start(f32[64,256]{1,0:T(8,128)S(1)} %get-tuple-element.49), channel_id=1, source_target_pairs={{0,2},{1,3},{2,0},{3,1},{4,6},{5,7},{6,4},{7,5},{8,10},{9,11},{10,... | collective-permute-start | bytes 196616 | tf_op jit(solution)/shard_map/ppermute | solution.py:49
  63.3 8.8 %collective-permute-start.11 = (bf16[4,65,256]{2,1,0:T(8,128)(2,1)S(1)}, bf16[4,65,256]{2,1,0:T(8,128)(2,1)S(1)}, u32[]{:S(2)}, u32[]{:S(2)}) collective-permute-start(bf16[4,65,256]{2,1,0:T(8,128)(2,1)S(1)} %pad_maximum_fusion.4), channel_id=1, source_target_pairs={{0,1},{1,0},{2,3},{3,2},{4,5},{5,4},{6,7},{7,6},{8,9},{9,8},{10,11... | collective-permute-start | bytes 399368 | tf_op jit(solution)/shard_map/ppermute | solution.py:37
  63.9 9.5 %collective-permute-start.10 = (bf16[4,65,256]{2,1,0:T(8,128)(2,1)S(1)}, bf16[4,65,256]{2,1,0:T(8,128)(2,1)S(1)}, u32[]{:S(2)}, u32[]{:S(2)}) collective-permute-start(bf16[4,65,256]{2,1,0:T(8,128)(2,1)S(1)} %pad_maximum_fusion.4), channel_id=1, source_target_pairs={{0,2},{1,3},{2,0},{3,1},{4,6},{5,7},{6,4},{7,5},{8,10},{9,11},{10,... | collective-permute-start | bytes 399368 | tf_op jit(solution)/shard_map/ppermute | solution.py:37
  64.6 8.7 %collective-permute-start.9 = (bf16[4,65,256]{2,1,0:T(8,128)(2,1)S(1)}, bf16[4,65,256]{2,1,0:T(8,128)(2,1)S(1)}, u32[]{:S(2)}, u32[]{:S(2)}) collective-permute-start(bf16[4,65,256]{2,1,0:T(8,128)(2,1)S(1)} %pad_maximum_fusion.4), channel_id=1, source_target_pairs={{0,3},{1,2},{2,1},{3,0},{4,7},{5,6},{6,5},{7,4},{8,11},{9,10},{10,... | collective-permute-start | bytes 399368 | tf_op jit(solution)/shard_map/ppermute | solution.py:37
  68.0 5.8 %collective-permute-start.21 = (bf16[64,256]{1,0:T(8,128)(2,1)S(1)}, bf16[64,256]{1,0:T(8,128)(2,1)S(1)}, u32[]{:S(2)}, u32[]{:S(2)}) collective-permute-start(bf16[64,256]{1,0:T(8,128)(2,1)S(1)} %fusion.68), channel_id=1, source_target_pairs={{0,4},{4,8},{8,12},{12,0},{1,5},{5,9},{9,13},{13,1},{2,6},{6,10},{... | collective-permute-start | bytes 98312 | tf_op jit(solution)/shard_map/ppermute | solution.py:26
  70.9 4.8 %collective-permute-start.20 = (bf16[64,256]{1,0:T(8,128)(2,1)S(1)}, bf16[64,256]{1,0:T(8,128)(2,1)S(1)}, u32[]{:S(2)}, u32[]{:S(2)}) collective-permute-start(bf16[64,256]{1,0:T(8,128)(2,1)S(1)} %fusion.68), channel_id=1, source_target_pairs={{0,8},{4,12},{8,0},{12,4},{1,9},{5,13},{9,1},{13,5},{2,10},{6,14},... | collective-permute-start | bytes 98312 | tf_op jit(solution)/shard_map/ppermute | solution.py:26
  76.2 5.0 %collective-permute-start.24 = (bf16[4,64,256]{2,1,0:T(8,128)(2,1)S(1)}, bf16[4,64,256]{2,1,0:T(8,128)(2,1)S(1)}, u32[]{:S(2)}, u32[]{:S(2)}) collective-permute-start(bf16[4,64,256]{2,1,0:T(8,128)(2,1)S(1)} %pad_maximum_fusion.5), channel_id=1, source_target_pairs={{0,1},{1,0},{2,3},{3,2},{4,5},{5,4},{6,7},{7,6},{8,9},{9,8},{10,11... | collective-permute-start | bytes 393224 | tf_op jit(solution)/shard_map/ppermute | solution.py:37
  77.9 6.4 %collective-permute-start.23 = (bf16[4,64,256]{2,1,0:T(8,128)(2,1)S(1)}, bf16[4,64,256]{2,1,0:T(8,128)(2,1)S(1)}, u32[]{:S(2)}, u32[]{:S(2)}) collective-permute-start(bf16[4,64,256]{2,1,0:T(8,128)(2,1)S(1)} %pad_maximum_fusion.5), channel_id=1, source_target_pairs={{0,2},{1,3},{2,0},{3,1},{4,6},{5,7},{6,4},{7,5},{8,10},{9,11},{10,... | collective-permute-start | bytes 393224 | tf_op jit(solution)/shard_map/ppermute | solution.py:37
  78.0 6.2 %collective-permute-start.22 = (bf16[4,64,256]{2,1,0:T(8,128)(2,1)S(1)}, bf16[4,64,256]{2,1,0:T(8,128)(2,1)S(1)}, u32[]{:S(2)}, u32[]{:S(2)}) collective-permute-start(bf16[4,64,256]{2,1,0:T(8,128)(2,1)S(1)} %pad_maximum_fusion.5), channel_id=1, source_target_pairs={{0,3},{1,2},{2,1},{3,0},{4,7},{5,6},{6,5},{7,4},{8,11},{9,10},{10,... | collective-permute-start | bytes 393224 | tf_op jit(solution)/shard_map/ppermute | solution.py:37
  80.1 4.5 %collective-permute-start.12 = (bf16[4,4,65,256]{3,1,2,0:T(4,128)(2,1)S(1)}, bf16[4,4,65,256]{3,1,2,0:T(4,128)(2,1)S(1)}, u32[]{:S(2)}, u32[]{:S(2)}) collective-permute-start(bf16[4,4,65,256]{3,1,2,0:T(4,128)(2,1)S(1)} %copy.170), channel_id=1, source_target_pairs={{0,16},{16,0},{1,17},{17,1},{2,18},{18,2},{3,19},{19,3},{4,20},{20... | collective-permute-start | bytes 1597448 | tf_op jit(solution)/shard_map/ppermute | solution.py:26
  (4 other events, 26.3 us)

commit v13 on v12

--- a/solution.py
+++ b/solution.py
@@ -3,8 +3,8 @@
 from jax import lax
 from jax.sharding import PartitionSpec as P
 
+
 P_SIZE = 64
-ALL_AXES = ("dp", "ctx", "expert")
 
 
 def place(received, sources, count):
@@ -163,8 +163,9 @@
         packed = jnp.concatenate([x_part, z_part, b_part, c_part] + split_exact(decay_part), axis=2)
         if after is not None:
             _, packed = lax.optimization_barrier((after, packed))
-        packed = jnp.moveaxis(gather_blocks(packed, "ctx", ctx_count), 0, 1).reshape(
-            part_count, ctx_count * block_len, packed.shape[2]
+        packed = gather_blocks(packed, "ctx", ctx_count)
+        packed = jnp.moveaxis(packed, 0, 1).reshape(
+            part_count, ctx_count * block_len, packed.shape[3]
         )
         decay_all = join_exact(
             [packed[:, :, decay_base + i * head_count : decay_base + (i + 1) * head_count] for i in range(3)]
@@ -175,7 +176,8 @@
         c_all = packed[:, :, 2 * width_in + state_size : decay_base]
         ssd = mixer(x_all, b_all, c_all, decay_all, skip)
         gated = (ssd * jax.nn.silu(z_all.astype(jnp.float32))).astype(jnp.bfloat16)
-        return jnp.einsum("stk,kd->std", gated, out_weight, preferred_element_type=jnp.float32), packed
+        projected = jnp.einsum("stk,kd->std", gated, out_weight, preferred_element_type=jnp.float32)
+        return projected, packed
 
     if device_count * row_count * model_width * 2 > (8 << 20):
         partial_value = front(x_in, z_in, b_in, c_in, decay_log)[0]
@@ -262,4 +264,5 @@
         P("dp", ("ctx", "expert"), None),
     )
     out_specs = (P("dp", ("ctx", "expert"), None), P("expert", ("dp", "ctx"), None))
+
     return jax.shard_map(local, mesh=mesh, in_specs=in_specs, out_specs=out_specs, check_vma=False)

time: 100 us -> 100 us (level)
  no operation moved by 1% of the time
where the time goes in v13:
time: 100 us; the launch traced here: 99.4 us
  starting transfers between devices  36.5 us (36%)
  waiting for transfers between devices  22 us (22%)
  matrix products  18.9 us (19%)
  local copies, waits for them, and re-layouts  15.7 us (16%)
  other arithmetic  5.22 us (5%)
  between operations  1.1 us (1%)
    ppermute x14, starting transfers between devices, gather_blocks(): received.append(lax.ppermute(value, axis_name, perm))  22.4 us
    ppermute x14, waiting for transfers between devices, gather_blocks(): received.append(lax.ppermute(value, axis_name, perm))  12 us
    dot_general x1, matrix products, expert_ffn(): jnp.einsum('gfd,qd->gfq', gate_up[0], slot_rows, preferred_element_type=j...  8.15 us
    dot_general x2, matrix products, front(): jnp.einsum('stk,kd->std', gated, out_weight, preferred_element_type=jnp.f...  7.16 us
    ppermute x6, starting transfers between devices, sum_scatter(): total = total + lax.ppermute(send, axis_name, perm)  7.11 us
    ppermute x6, starting transfers between devices, gather_xor(): received.append(lax.ppermute(value, axis_name, perm))  7.01 us
    dot_general x1, local copies, waits for them, and re-layouts, front(): jnp.einsum('stk,kd->std', gated, out_weight, preferred_element_type=jnp.f...  6.56 us
    ppermute x6, waiting for transfers between devices, sum_scatter(): total = total + lax.ppermute(send, axis_name, perm)  5.92 us
  transfers between devices with their start and end apart: 26, of which 15 were waited for; matrix products, arithmetic and copies ran while one was open for 10% of the time, Pallas kernels for 0%

profile of v13, /device:TPU:0, one launch (start us, length us, event | category | flops | bytes accessed | tf_op | source)
XLA Modules:
  0.0 99.4 jit_solution(11122779946346313510)
XLA Ops:
  4.6 3.1 %collective-permute-start.2 = (bf16[1,16,4448]{2,1,0:T(8,128)(2,1)S(1)}, bf16[1,16,4448]{2,1,0:T(8,128)(2,1)S(1)}, u32[]{:S(2)}, u32[]{:S(2)}) collective-permute-start(bf16[1,16,4448]{2,1,0:T(8,128)(2,1)S(1)} %concatenate.15), channel_id=1, source_target_pairs={{0,4},{4,8},{8,12},{12,0},{1,5},{5,9},{9,13},{13,1},{2,6},{6,10},{... | collective-permute-start | bytes 427016 | tf_op jit(solution)/shard_map/ppermute | solution.py:26
  7.6 2.6 %collective-permute-start.1 = (bf16[1,16,4448]{2,1,0:T(8,128)(2,1)S(1)}, bf16[1,16,4448]{2,1,0:T(8,128)(2,1)S(1)}, u32[]{:S(2)}, u32[]{:S(2)}) collective-permute-start(bf16[1,16,4448]{2,1,0:T(8,128)(2,1)S(1)} %concatenate.15), channel_id=1, source_target_pairs={{0,8},{4,12},{8,0},{12,4},{1,9},{5,13},{9,1},{13,5},{2,10},{6,14},... | collective-permute-start | bytes 427016 | tf_op jit(solution)/shard_map/ppermute | solution.py:26
  10.2 1.3 %collective-permute-start = (bf16[1,16,4448]{2,1,0:T(8,128)(2,1)S(1)}, bf16[1,16,4448]{2,1,0:T(8,128)(2,1)S(1)}, u32[]{:S(2)}, u32[]{:S(2)}) collective-permute-start(bf16[1,16,4448]{2,1,0:T(8,128)(2,1)S(1)} %concatenate.15), channel_id=1, source_target_pairs={{0,12},{4,0},{8,4},{12,8},{1,13},{5,1},{9,5},{13,9},{2,14},{6,2},{... | collective-permute-start | bytes 427016 | tf_op jit(solution)/shard_map/ppermute | solution.py:26
  12.5 6.6 %copy.197 = bf16[1024,2048]{1,0:T(8,128)(2,1)} copy(bf16[1024,2048]{0,1:T(8,128)(2,1)} %bitcast.177) | data formatting | bytes 8388608 | tf_op jit(solution)/shard_map/stk,kd->std/dot_general | solution.py:179
  22.5 3.6 %fusion.50 = f32[64,4,256]{2,0,1:T(8,128)S(1)} fusion(bf16[4,256,2048]{2,1,0:T(8,128)(2,1)} %bitcast.178, f32[1,64,2048]{2,1,0:T(8,128)S(1)} %copy.167, bf16[1,64,4448]{2,1,0:T(8,128)(2,1)S(1)} %bitcast.188), kind=kOutput, calls=%fused_computation.77 | convolution fusion | flops 269352960 | bytes 5242880 | tf_op jit(solution)/shard_map/stk,kd->std/dot_general | solution.py:179
  26.1 1.6 %collective-permute-start.3 = (f32[65,256]{1,0:T(8,128)S(1)}, f32[65,256]{1,0:T(8,128)S(1)}, u32[]{:S(2)}, u32[]{:S(2)}) collective-permute-start(f32[65,256]{1,0:T(8,128)S(1)} %get-tuple-element.44), channel_id=1, source_target_pairs={{0,1},{1,0},{2,3},{3,2},{4,5},{5,4},{6,7},{7,6},{8,9},{9,8},{10,11... | collective-permute-start | bytes 199688 | tf_op jit(solution)/shard_map/ppermute | solution.py:49
  27.7 1.5 %collective-permute-start.4 = (f32[65,256]{1,0:T(8,128)S(1)}, f32[65,256]{1,0:T(8,128)S(1)}, u32[]{:S(2)}, u32[]{:S(2)}) collective-permute-start(f32[65,256]{1,0:T(8,128)S(1)} %get-tuple-element.45), channel_id=1, source_target_pairs={{0,2},{1,3},{2,0},{3,1},{4,6},{5,7},{6,4},{7,5},{8,10},{9,11},{10,... | collective-permute-start | bytes 199688 | tf_op jit(solution)/shard_map/ppermute | solution.py:49
  30.5 1.5 %collective-permute-done.4 = f32[65,256]{1,0:T(8,128)S(1)} collective-permute-done((f32[65,256]{1,0:T(8,128)S(1)}, f32[65,256]{1,0:T(8,128)S(1)}, u32[]{:S(2)}, u32[]{:S(2)}) %collective-permute-start.4) | collective-permute-done | bytes 66592 | tf_op jit(solution)/shard_map/ppermute | solution.py:49
  32.0 2.4 %collective-permute-done.5 = f32[65,256]{1,0:T(8,128)S(1)} collective-permute-done((f32[65,256]{1,0:T(8,128)S(1)}, f32[65,256]{1,0:T(8,128)S(1)}, u32[]{:S(2)}, u32[]{:S(2)}) %collective-permute-start.5) | collective-permute-done | bytes 66592 | tf_op jit(solution)/shard_map/ppermute | solution.py:49
  34.5 3.6 %collective-permute-start.8 = (bf16[65,256]{1,0:T(8,128)(2,1)S(1)}, bf16[65,256]{1,0:T(8,128)(2,1)S(1)}, u32[]{:S(2)}, u32[]{:S(2)}) collective-permute-start(bf16[65,256]{1,0:T(8,128)(2,1)S(1)} %fusion.61), channel_id=1, source_target_pairs={{0,4},{4,8},{8,12},{12,0},{1,5},{5,9},{9,13},{13,1},{2,6},{6,10},{... | collective-permute-start | bytes 99848 | tf_op jit(solution)/shard_map/ppermute | solution.py:26
  38.1 1.6 %collective-permute-start.7 = (bf16[65,256]{1,0:T(8,128)(2,1)S(1)}, bf16[65,256]{1,0:T(8,128)(2,1)S(1)}, u32[]{:S(2)}, u32[]{:S(2)}) collective-permute-start(bf16[65,256]{1,0:T(8,128)(2,1)S(1)} %fusion.61), channel_id=1, source_target_pairs={{0,8},{4,12},{8,0},{12,4},{1,9},{5,13},{9,1},{13,5},{2,10},{6,14},... | collective-permute-start | bytes 99848 | tf_op jit(solution)/shard_map/ppermute | solution.py:26
  43.4 1.3 %collective-permute-start.13 = (bf16[1,16,4448]{2,1,0:T(8,128)(2,1)S(1)}, bf16[1,16,4448]{2,1,0:T(8,128)(2,1)S(1)}, u32[]{:S(2)}, u32[]{:S(2)}) collective-permute-start(bf16[1,16,4448]{2,1,0:T(8,128)(2,1)S(1)} %concatenate.18), channel_id=1, source_target_pairs={{0,12},{4,0},{8,4},{12,8},{1,13},{5,1},{9,5},{13,9},{2,14},{6,2},{... | collective-permute-start | bytes 427016 | tf_op jit(solution)/shard_map/ppermute | solution.py:26
  45.7 3.6 %collective-permute-done.15 = bf16[1,16,4448]{2,1,0:T(8,128)(2,1)S(1)} collective-permute-done((bf16[1,16,4448]{2,1,0:T(8,128)(2,1)S(1)}, bf16[1,16,4448]{2,1,0:T(8,128)(2,1)S(1)}, u32[]{:S(2)}, u32[]{:S(2)}) %collective-permute-start.15) | collective-permute-done | bytes 142368 | tf_op jit(solution)/shard_map/ppermute | solution.py:26
  49.3 4.0 %collective-permute-done.14 = bf16[1,16,4448]{2,1,0:T(8,128)(2,1)S(1)} collective-permute-done((bf16[1,16,4448]{2,1,0:T(8,128)(2,1)S(1)}, bf16[1,16,4448]{2,1,0:T(8,128)(2,1)S(1)}, u32[]{:S(2)}, u32[]{:S(2)}) %collective-permute-start.14) | collective-permute-done | bytes 142368 | tf_op jit(solution)/shard_map/ppermute | solution.py:26
  56.1 3.6 %fusion.48 = f32[64,4,256]{2,0,1:T(8,128)S(1)} fusion(bf16[4,256,2048]{2,1,0:T(8,128)(2,1)} %bitcast.179, f32[1,64,2048]{2,1,0:T(8,128)S(1)} %copy.177, bf16[1,64,4448]{2,1,0:T(8,128)(2,1)S(1)} %bitcast.184), kind=kOutput, calls=%fused_computation.75 | convolution fusion | flops 269352960 | bytes 5242880 | tf_op jit(solution)/shard_map/stk,kd->std/dot_general | solution.py:179
  60.3 1.5 %collective-permute-start.18 = (f32[64,256]{1,0:T(8,128)S(1)}, f32[64,256]{1,0:T(8,128)S(1)}, u32[]{:S(2)}, u32[]{:S(2)}) collective-permute-start(f32[64,256]{1,0:T(8,128)S(1)} %get-tuple-element.48), channel_id=1, source_target_pairs={{0,3},{1,2},{2,1},{3,0},{4,7},{5,6},{6,5},{7,4},{8,11},{9,10},{10,... | collective-permute-start | bytes 196616 | tf_op jit(solution)/shard_map/ppermute | solution.py:49
  61.8 1.5 %collective-permute-start.17 = (f32[64,256]{1,0:T(8,128)S(1)}, f32[64,256]{1,0:T(8,128)S(1)}, u32[]{:S(2)}, u32[]{:S(2)}) collective-permute-start(f32[64,256]{1,0:T(8,128)S(1)} %get-tuple-element.49), channel_id=1, source_target_pairs={{0,2},{1,3},{2,0},{3,1},{4,6},{5,7},{6,4},{7,5},{8,10},{9,11},{10,... | collective-permute-start | bytes 196616 | tf_op jit(solution)/shard_map/ppermute | solution.py:49
  64.6 2.2 %collective-permute-start.9 = (bf16[4,65,256]{2,1,0:T(8,128)(2,1)S(1)}, bf16[4,65,256]{2,1,0:T(8,128)(2,1)S(1)}, u32[]{:S(2)}, u32[]{:S(2)}) collective-permute-start(bf16[4,65,256]{2,1,0:T(8,128)(2,1)S(1)} %pad_maximum_fusion.4), channel_id=1, source_target_pairs={{0,3},{1,2},{2,1},{3,0},{4,7},{5,6},{6,5},{7,4},{8,11},{9,10},{10,... | collective-permute-start | bytes 399368 | tf_op jit(solution)/shard_map/ppermute | solution.py:37
  68.0 2.9 %collective-permute-start.21 = (bf16[64,256]{1,0:T(8,128)(2,1)S(1)}, bf16[64,256]{1,0:T(8,128)(2,1)S(1)}, u32[]{:S(2)}, u32[]{:S(2)}) collective-permute-start(bf16[64,256]{1,0:T(8,128)(2,1)S(1)} %fusion.68), channel_id=1, source_target_pairs={{0,4},{4,8},{8,12},{12,0},{1,5},{5,9},{9,13},{13,1},{2,6},{6,10},{... | collective-permute-start | bytes 98312 | tf_op jit(solution)/shard_map/ppermute | solution.py:26
  73.8 2.0 %collective-permute-done.20 = bf16[64,256]{1,0:T(8,128)(2,1)S(1)} collective-permute-done((bf16[64,256]{1,0:T(8,128)(2,1)S(1)}, bf16[64,256]{1,0:T(8,128)(2,1)S(1)}, u32[]{:S(2)}, u32[]{:S(2)}) %collective-permute-start.20) | collective-permute-done | bytes 32800 | tf_op jit(solution)/shard_map/ppermute | solution.py:26
  76.2 1.7 %collective-permute-start.24 = (bf16[4,64,256]{2,1,0:T(8,128)(2,1)S(1)}, bf16[4,64,256]{2,1,0:T(8,128)(2,1)S(1)}, u32[]{:S(2)}, u32[]{:S(2)}) collective-permute-start(bf16[4,64,256]{2,1,0:T(8,128)(2,1)S(1)} %pad_maximum_fusion.5), channel_id=1, source_target_pairs={{0,1},{1,0},{2,3},{3,2},{4,5},{5,4},{6,7},{7,6},{8,9},{9,8},{10,11... | collective-permute-start | bytes 393224 | tf_op jit(solution)/shard_map/ppermute | solution.py:37
  78.0 1.7 %collective-permute-start.22 = (bf16[4,64,256]{2,1,0:T(8,128)(2,1)S(1)}, bf16[4,64,256]{2,1,0:T(8,128)(2,1)S(1)}, u32[]{:S(2)}, u32[]{:S(2)}) collective-permute-start(bf16[4,64,256]{2,1,0:T(8,128)(2,1)S(1)} %pad_maximum_fusion.5), channel_id=1, source_target_pairs={{0,3},{1,2},{2,1},{3,0},{4,7},{5,6},{6,5},{7,4},{8,11},{9,10},{10,... | collective-permute-start | bytes 393224 | tf_op jit(solution)/shard_map/ppermute | solution.py:37
  81.2 3.1 %collective-permute-done.23 = bf16[4,64,256]{2,1,0:T(8,128)(2,1)S(1)} collective-permute-done((bf16[4,64,256]{2,1,0:T(8,128)(2,1)S(1)}, bf16[4,64,256]{2,1,0:T(8,128)(2,1)S(1)}, u32[]{:S(2)}, u32[]{:S(2)}) %collective-permute-start.23) | collective-permute-done | bytes 131104 | tf_op jit(solution)/shard_map/ppermute | solution.py:37
  88.4 8.2 %fusion.9 = f32[2,896,256]{1,2,0:T(8,128)S(1)} fusion(bf16[256,4096,1]{0,1,2:T(8,128)(2,1)S(1)} %bitcast.180, bf16[1,2,896,4096]{3,2,1,0:T(8,128)(2,1)} %param.19), kind=kOutput, calls=%fused_computation.12 | convolution fusion | flops 3758096384 | bytes 18612224 | tf_op jit(solution)/shard_map/gfd,qd->gfq/dot_general | solution.py:105
  (121 shorter events, 31.7 us)
Async XLA Ops:
  4.6 14.6 %collective-permute-start.2 = (bf16[1,16,4448]{2,1,0:T(8,128)(2,1)S(1)}, bf16[1,16,4448]{2,1,0:T(8,128)(2,1)S(1)}, u32[]{:S(2)}, u32[]{:S(2)}) collective-permute-start(bf16[1,16,4448]{2,1,0:T(8,128)(2,1)S(1)} %concatenate.15), channel_id=1, source_target_pairs={{0,4},{4,8},{8,12},{12,0},{1,5},{5,9},{9,13},{13,1},{2,6},{6,10},{... | collective-permute-start | bytes 427016 | tf_op jit(solution)/shard_map/ppermute | solution.py:26
  7.6 12.0 %collective-permute-start.1 = (bf16[1,16,4448]{2,1,0:T(8,128)(2,1)S(1)}, bf16[1,16,4448]{2,1,0:T(8,128)(2,1)S(1)}, u32[]{:S(2)}, u32[]{:S(2)}) collective-permute-start(bf16[1,16,4448]{2,1,0:T(8,128)(2,1)S(1)} %concatenate.15), channel_id=1, source_target_pairs={{0,8},{4,12},{8,0},{12,4},{1,9},{5,13},{9,1},{13,5},{2,10},{6,14},... | collective-permute-start | bytes 427016 | tf_op jit(solution)/shard_map/ppermute | solution.py:26
  10.2 9.4 %collective-permute-start = (bf16[1,16,4448]{2,1,0:T(8,128)(2,1)S(1)}, bf16[1,16,4448]{2,1,0:T(8,128)(2,1)S(1)}, u32[]{:S(2)}, u32[]{:S(2)}) collective-permute-start(bf16[1,16,4448]{2,1,0:T(8,128)(2,1)S(1)} %concatenate.15), channel_id=1, source_target_pairs={{0,12},{4,0},{8,4},{12,8},{1,13},{5,1},{9,5},{13,9},{2,14},{6,2},{... | collective-permute-start | bytes 427016 | tf_op jit(solution)/shard_map/ppermute | solution.py:26
  26.1 4.4 %collective-permute-start.3 = (f32[65,256]{1,0:T(8,128)S(1)}, f32[65,256]{1,0:T(8,128)S(1)}, u32[]{:S(2)}, u32[]{:S(2)}) collective-permute-start(f32[65,256]{1,0:T(8,128)S(1)} %get-tuple-element.44), channel_id=1, source_target_pairs={{0,1},{1,0},{2,3},{3,2},{4,5},{5,4},{6,7},{7,6},{8,9},{9,8},{10,11... | collective-permute-start | bytes 199688 | tf_op jit(solution)/shard_map/ppermute | solution.py:49
  27.7 4.4 %collective-permute-start.4 = (f32[65,256]{1,0:T(8,128)S(1)}, f32[65,256]{1,0:T(8,128)S(1)}, u32[]{:S(2)}, u32[]{:S(2)}) collective-permute-start(f32[65,256]{1,0:T(8,128)S(1)} %get-tuple-element.45), channel_id=1, source_target_pairs={{0,2},{1,3},{2,0},{3,1},{4,6},{5,7},{6,4},{7,5},{8,10},{9,11},{10,... | collective-permute-start | bytes 199688 | tf_op jit(solution)/shard_map/ppermute | solution.py:49
  29.2 5.3 %collective-permute-start.5 = (f32[65,256]{1,0:T(8,128)S(1)}, f32[65,256]{1,0:T(8,128)S(1)}, u32[]{:S(2)}, u32[]{:S(2)}) collective-permute-start(f32[65,256]{1,0:T(8,128)S(1)} %get-tuple-element.46), channel_id=1, source_target_pairs={{0,3},{1,2},{2,1},{3,0},{4,7},{5,6},{6,5},{7,4},{8,11},{9,10},{10,... | collective-permute-start | bytes 199688 | tf_op jit(solution)/shard_map/ppermute | solution.py:49
  34.5 8.9 %collective-permute-start.8 = (bf16[65,256]{1,0:T(8,128)(2,1)S(1)}, bf16[65,256]{1,0:T(8,128)(2,1)S(1)}, u32[]{:S(2)}, u32[]{:S(2)}) collective-permute-start(bf16[65,256]{1,0:T(8,128)(2,1)S(1)} %fusion.61), channel_id=1, source_target_pairs={{0,4},{4,8},{8,12},{12,0},{1,5},{5,9},{9,13},{13,1},{2,6},{6,10},{... | collective-permute-start | bytes 99848 | tf_op jit(solution)/shard_map/ppermute | solution.py:26
  38.1 6.7 %collective-permute-start.7 = (bf16[65,256]{1,0:T(8,128)(2,1)S(1)}, bf16[65,256]{1,0:T(8,128)(2,1)S(1)}, u32[]{:S(2)}, u32[]{:S(2)}) collective-permute-start(bf16[65,256]{1,0:T(8,128)(2,1)S(1)} %fusion.61), channel_id=1, source_target_pairs={{0,8},{4,12},{8,0},{12,4},{1,9},{5,13},{9,1},{13,5},{2,10},{6,14},... | collective-permute-start | bytes 99848 | tf_op jit(solution)/shard_map/ppermute | solution.py:26
  39.7 6.0 %collective-permute-start.6 = (bf16[65,256]{1,0:T(8,128)(2,1)S(1)}, bf16[65,256]{1,0:T(8,128)(2,1)S(1)}, u32[]{:S(2)}, u32[]{:S(2)}) collective-permute-start(bf16[65,256]{1,0:T(8,128)(2,1)S(1)} %fusion.61), channel_id=1, source_target_pairs={{0,12},{4,0},{8,4},{12,8},{1,13},{5,1},{9,5},{13,9},{2,14},{6,2},{... | collective-permute-start | bytes 99848 | tf_op jit(solution)/shard_map/ppermute | solution.py:26
  40.9 8.4 %collective-permute-start.15 = (bf16[1,16,4448]{2,1,0:T(8,128)(2,1)S(1)}, bf16[1,16,4448]{2,1,0:T(8,128)(2,1)S(1)}, u32[]{:S(2)}, u32[]{:S(2)}) collective-permute-start(bf16[1,16,4448]{2,1,0:T(8,128)(2,1)S(1)} %concatenate.18), channel_id=1, source_target_pairs={{0,4},{4,8},{8,12},{12,0},{1,5},{5,9},{9,13},{13,1},{2,6},{6,10},{... | collective-permute-start | bytes 427016 | tf_op jit(solution)/shard_map/ppermute | solution.py:26
  42.1 11.2 %collective-permute-start.14 = (bf16[1,16,4448]{2,1,0:T(8,128)(2,1)S(1)}, bf16[1,16,4448]{2,1,0:T(8,128)(2,1)S(1)}, u32[]{:S(2)}, u32[]{:S(2)}) collective-permute-start(bf16[1,16,4448]{2,1,0:T(8,128)(2,1)S(1)} %concatenate.18), channel_id=1, source_target_pairs={{0,8},{4,12},{8,0},{12,4},{1,9},{5,13},{9,1},{13,5},{2,10},{6,14},... | collective-permute-start | bytes 427016 | tf_op jit(solution)/shard_map/ppermute | solution.py:26
  43.4 9.9 %collective-permute-start.13 = (bf16[1,16,4448]{2,1,0:T(8,128)(2,1)S(1)}, bf16[1,16,4448]{2,1,0:T(8,128)(2,1)S(1)}, u32[]{:S(2)}, u32[]{:S(2)}) collective-permute-start(bf16[1,16,4448]{2,1,0:T(8,128)(2,1)S(1)} %concatenate.18), channel_id=1, source_target_pairs={{0,12},{4,0},{8,4},{12,8},{1,13},{5,1},{9,5},{13,9},{2,14},{6,2},{... | collective-permute-start | bytes 427016 | tf_op jit(solution)/shard_map/ppermute | solution.py:26
  59.7 4.9 %collective-permute-start.16 = (f32[64,256]{1,0:T(8,128)S(1)}, f32[64,256]{1,0:T(8,128)S(1)}, u32[]{:S(2)}, u32[]{:S(2)}) collective-permute-start(f32[64,256]{1,0:T(8,128)S(1)} %get-tuple-element.47), channel_id=1, source_target_pairs={{0,1},{1,0},{2,3},{3,2},{4,5},{5,4},{6,7},{7,6},{8,9},{9,8},{10,11... | collective-permute-start | bytes 196616 | tf_op jit(solution)/shard_map/ppermute | solution.py:49
  60.3 6.5 %collective-permute-start.18 = (f32[64,256]{1,0:T(8,128)S(1)}, f32[64,256]{1,0:T(8,128)S(1)}, u32[]{:S(2)}, u32[]{:S(2)}) collective-permute-start(f32[64,256]{1,0:T(8,128)S(1)} %get-tuple-element.48), channel_id=1, source_target_pairs={{0,3},{1,2},{2,1},{3,0},{4,7},{5,6},{6,5},{7,4},{8,11},{9,10},{10,... | collective-permute-start | bytes 196616 | tf_op jit(solution)/shard_map/ppermute | solution.py:49
  61.8 6.2 %collective-permute-start.17 = (f32[64,256]{1,0:T(8,128)S(1)}, f32[64,256]{1,0:T(8,128)S(1)}, u32[]{:S(2)}, u32[]{:S(2)}) collective-permute-start(f32[64,256]{1,0:T(8,128)S(1)} %get-tuple-element.49), channel_id=1, source_target_pairs={{0,2},{1,3},{2,0},{3,1},{4,6},{5,7},{6,4},{7,5},{8,10},{9,11},{10,... | collective-permute-start | bytes 196616 | tf_op jit(solution)/shard_map/ppermute | solution.py:49
  63.3 8.8 %collective-permute-start.11 = (bf16[4,65,256]{2,1,0:T(8,128)(2,1)S(1)}, bf16[4,65,256]{2,1,0:T(8,128)(2,1)S(1)}, u32[]{:S(2)}, u32[]{:S(2)}) collective-permute-start(bf16[4,65,256]{2,1,0:T(8,128)(2,1)S(1)} %pad_maximum_fusion.4), channel_id=1, source_target_pairs={{0,1},{1,0},{2,3},{3,2},{4,5},{5,4},{6,7},{7,6},{8,9},{9,8},{10,11... | collective-permute-start | bytes 399368 | tf_op jit(solution)/shard_map/ppermute | solution.py:37
  63.9 9.5 %collective-permute-start.10 = (bf16[4,65,256]{2,1,0:T(8,128)(2,1)S(1)}, bf16[4,65,256]{2,1,0:T(8,128)(2,1)S(1)}, u32[]{:S(2)}, u32[]{:S(2)}) collective-permute-start(bf16[4,65,256]{2,1,0:T(8,128)(2,1)S(1)} %pad_maximum_fusion.4), channel_id=1, source_target_pairs={{0,2},{1,3},{2,0},{3,1},{4,6},{5,7},{6,4},{7,5},{8,10},{9,11},{10,... | collective-permute-start | bytes 399368 | tf_op jit(solution)/shard_map/ppermute | solution.py:37
  64.6 8.7 %collective-permute-start.9 = (bf16[4,65,256]{2,1,0:T(8,128)(2,1)S(1)}, bf16[4,65,256]{2,1,0:T(8,128)(2,1)S(1)}, u32[]{:S(2)}, u32[]{:S(2)}) collective-permute-start(bf16[4,65,256]{2,1,0:T(8,128)(2,1)S(1)} %pad_maximum_fusion.4), channel_id=1, source_target_pairs={{0,3},{1,2},{2,1},{3,0},{4,7},{5,6},{6,5},{7,4},{8,11},{9,10},{10,... | collective-permute-start | bytes 399368 | tf_op jit(solution)/shard_map/ppermute | solution.py:37
  68.0 5.8 %collective-permute-start.21 = (bf16[64,256]{1,0:T(8,128)(2,1)S(1)}, bf16[64,256]{1,0:T(8,128)(2,1)S(1)}, u32[]{:S(2)}, u32[]{:S(2)}) collective-permute-start(bf16[64,256]{1,0:T(8,128)(2,1)S(1)} %fusion.68), channel_id=1, source_target_pairs={{0,4},{4,8},{8,12},{12,0},{1,5},{5,9},{9,13},{13,1},{2,6},{6,10},{... | collective-permute-start | bytes 98312 | tf_op jit(solution)/shard_map/ppermute | solution.py:26
  70.9 4.8 %collective-permute-start.20 = (bf16[64,256]{1,0:T(8,128)(2,1)S(1)}, bf16[64,256]{1,0:T(8,128)(2,1)S(1)}, u32[]{:S(2)}, u32[]{:S(2)}) collective-permute-start(bf16[64,256]{1,0:T(8,128)(2,1)S(1)} %fusion.68), channel_id=1, source_target_pairs={{0,8},{4,12},{8,0},{12,4},{1,9},{5,13},{9,1},{13,5},{2,10},{6,14},... | collective-permute-start | bytes 98312 | tf_op jit(solution)/shard_map/ppermute | solution.py:26
  76.2 5.0 %collective-permute-start.24 = (bf16[4,64,256]{2,1,0:T(8,128)(2,1)S(1)}, bf16[4,64,256]{2,1,0:T(8,128)(2,1)S(1)}, u32[]{:S(2)}, u32[]{:S(2)}) collective-permute-start(bf16[4,64,256]{2,1,0:T(8,128)(2,1)S(1)} %pad_maximum_fusion.5), channel_id=1, source_target_pairs={{0,1},{1,0},{2,3},{3,2},{4,5},{5,4},{6,7},{7,6},{8,9},{9,8},{10,11... | collective-permute-start | bytes 393224 | tf_op jit(solution)/shard_map/ppermute | solution.py:37
  77.9 6.4 %collective-permute-start.23 = (bf16[4,64,256]{2,1,0:T(8,128)(2,1)S(1)}, bf16[4,64,256]{2,1,0:T(8,128)(2,1)S(1)}, u32[]{:S(2)}, u32[]{:S(2)}) collective-permute-start(bf16[4,64,256]{2,1,0:T(8,128)(2,1)S(1)} %pad_maximum_fusion.5), channel_id=1, source_target_pairs={{0,2},{1,3},{2,0},{3,1},{4,6},{5,7},{6,4},{7,5},{8,10},{9,11},{10,... | collective-permute-start | bytes 393224 | tf_op jit(solution)/shard_map/ppermute | solution.py:37
  78.0 6.2 %collective-permute-start.22 = (bf16[4,64,256]{2,1,0:T(8,128)(2,1)S(1)}, bf16[4,64,256]{2,1,0:T(8,128)(2,1)S(1)}, u32[]{:S(2)}, u32[]{:S(2)}) collective-permute-start(bf16[4,64,256]{2,1,0:T(8,128)(2,1)S(1)} %pad_maximum_fusion.5), channel_id=1, source_target_pairs={{0,3},{1,2},{2,1},{3,0},{4,7},{5,6},{6,5},{7,4},{8,11},{9,10},{10,... | collective-permute-start | bytes 393224 | tf_op jit(solution)/shard_map/ppermute | solution.py:37
  80.1 4.5 %collective-permute-start.12 = (bf16[4,4,65,256]{3,1,2,0:T(4,128)(2,1)S(1)}, bf16[4,4,65,256]{3,1,2,0:T(4,128)(2,1)S(1)}, u32[]{:S(2)}, u32[]{:S(2)}) collective-permute-start(bf16[4,4,65,256]{3,1,2,0:T(4,128)(2,1)S(1)} %copy.170), channel_id=1, source_target_pairs={{0,16},{16,0},{1,17},{17,1},{2,18},{18,2},{3,19},{19,3},{4,20},{20... | collective-permute-start | bytes 1597448 | tf_op jit(solution)/shard_map/ppermute | solution.py:26
  (4 other events, 26.3 us)

commit v14 on v13

--- a/solution.py
+++ b/solution.py
@@ -199,17 +199,13 @@
             x_in[streams], z_in[streams], b_in[streams], c_in[streams], decay_log[streams], arrived
         )
         rows = partial_value.reshape(part_len * total_len, col_width)
-        if part == 0:
+        if part == split - 1:
             rows = jnp.concatenate([rows, route_row.reshape(extra_rows, col_width)], axis=0)
         piece = sum_scatter(rows, "expert", group_count)
-        gathered = gather_blocks(piece, "ctx", ctx_count)
-        gathered = gather_xor(gathered, "expert", group_count)
-        gathered = gather_blocks(gathered, "dp", dp_count)
-        token_parts.append(gathered)
-    part_rows = part_len * total_len
-    extra = token_parts[0][:, :, :, part_rows:, :]
-    token_parts[0] = token_parts[0][:, :, :, :part_rows, :]
-    gathered = jnp.concatenate(token_parts + [extra], axis=3)
+        token_parts.append(gather_blocks(piece, "ctx", ctx_count))
+    gathered = jnp.concatenate(token_parts, axis=1)
+    gathered = gather_xor(gathered, "expert", group_count)
+    gathered = gather_blocks(gathered, "dp", dp_count)
     row_total = seq_count * total_len
     extra = jnp.transpose(gathered[:, :, :, row_total:, :], (0, 2, 3, 1, 4))
     routes = extra.reshape(dp_count, ctx_count, -1)[:, :, : group_count * route_len]

time: 100 us -> 92.5 us (0.925)
  waiting for transfers between devices: 22 us -> 14.5 us
  starting transfers between devices: 36.5 us -> 32.4 us
  other arithmetic: 5.22 us -> 7.41 us
  local copies, waits for them, and re-layouts: 15.7 us -> 17.6 us
    ppermute x14 -> x13, waiting for transfers between devices: 12 us -> 5.39 us  [gather_blocks(): received.append(lax.ppermute(value, axis_name, perm))]
    ppermute x6, waiting for transfers between devices: 5.92 us -> 0.02 us  [sum_scatter(): total = total + lax.ppermute(send, axis_name, perm)]
    ppermute x6 -> x3, waiting for transfers between devices: 4.12 us -> 9.13 us  [gather_xor(): received.append(lax.ppermute(value, axis_name, perm))]
    ppermute x6 -> x3, starting transfers between devices: 7.01 us -> 3.55 us  [gather_xor(): received.append(lax.ppermute(value, axis_name, perm))]
    another operation x17 -> x12, other arithmetic: 1.19 us -> 2.43 us  [place(): return jnp.stack(slots)]
    another operation x1, local copies, waits for them, and re-layouts: 0.21 us -> 1.4 us  [place(): return jnp.stack(slots)]
    ppermute x14 -> x13, starting transfers between devices: 22.4 us -> 21.8 us  [gather_blocks(): received.append(lax.ppermute(value, axis_name, perm))]
  transfers between devices with their start and end apart: 26 -> 22, of which waited for: 15 -> 7; matrix products, arithmetic and copies ran while one was open for 10% -> 25% of each run, Pallas kernels for 0% -> 0%
where the time goes in v14:
time: 92.5 us; the launch traced here: 91.9 us
  starting transfers between devices  32.4 us (35%)
  matrix products  18.9 us (20%)
  local copies, waits for them, and re-layouts  17.6 us (19%)
  waiting for transfers between devices  14.5 us (16%)
  other arithmetic  7.41 us (8%)
  between operations  1.07 us (1%)
    ppermute x13, starting transfers between devices, gather_blocks(): received.append(lax.ppermute(value, axis_name, perm))  21.8 us
    ppermute x3, waiting for transfers between devices, gather_xor(): received.append(lax.ppermute(value, axis_name, perm))  9.13 us
    dot_general x1, matrix products, expert_ffn(): jnp.einsum('gfd,qd->gfq', gate_up[0], slot_rows, preferred_element_type=j...  8.15 us
    dot_general x2, matrix products, front(): jnp.einsum('stk,kd->std', gated, out_weight, preferred_element_type=jnp.f...  7.16 us
    ppermute x6, starting transfers between devices, sum_scatter(): total = total + lax.ppermute(send, axis_name, perm)  7.04 us
    dot_general x1, local copies, waits for them, and re-layouts, front(): jnp.einsum('stk,kd->std', gated, out_weight, preferred_element_type=jnp.f...  6.55 us
    ppermute x13, waiting for transfers between devices, gather_blocks(): received.append(lax.ppermute(value, axis_name, perm))  5.39 us
    ppermute x3, starting transfers between devices, gather_xor(): received.append(lax.ppermute(value, axis_name, perm))  3.55 us
  transfers between devices with their start and end apart: 22, of which 7 were waited for; matrix products, arithmetic and copies ran while one was open for 25% of the time, Pallas kernels for 0%

profile of v14, /device:TPU:0, one launch (start us, length us, event | category | flops | bytes accessed | tf_op | source)
XLA Modules:
  0.0 91.9 jit_solution(18193994196810930129)
XLA Ops:
  4.6 3.1 %collective-permute-start.2 = (bf16[1,16,4448]{2,1,0:T(8,128)(2,1)S(1)}, bf16[1,16,4448]{2,1,0:T(8,128)(2,1)S(1)}, u32[]{:S(2)}, u32[]{:S(2)}) collective-permute-start(bf16[1,16,4448]{2,1,0:T(8,128)(2,1)S(1)} %concatenate.15), channel_id=1, source_target_pairs={{0,4},{4,8},{8,12},{12,0},{1,5},{5,9},{9,13},{13,1},{2,6},{6,10},{... | collective-permute-start | bytes 427016 | tf_op jit(solution)/shard_map/ppermute | solution.py:26
  7.6 2.6 %collective-permute-start.1 = (bf16[1,16,4448]{2,1,0:T(8,128)(2,1)S(1)}, bf16[1,16,4448]{2,1,0:T(8,128)(2,1)S(1)}, u32[]{:S(2)}, u32[]{:S(2)}) collective-permute-start(bf16[1,16,4448]{2,1,0:T(8,128)(2,1)S(1)} %concatenate.15), channel_id=1, source_target_pairs={{0,8},{4,12},{8,0},{12,4},{1,9},{5,13},{9,1},{13,5},{2,10},{6,14},... | collective-permute-start | bytes 427016 | tf_op jit(solution)/shard_map/ppermute | solution.py:26
  10.2 1.3 %collective-permute-start = (bf16[1,16,4448]{2,1,0:T(8,128)(2,1)S(1)}, bf16[1,16,4448]{2,1,0:T(8,128)(2,1)S(1)}, u32[]{:S(2)}, u32[]{:S(2)}) collective-permute-start(bf16[1,16,4448]{2,1,0:T(8,128)(2,1)S(1)} %concatenate.15), channel_id=1, source_target_pairs={{0,12},{4,0},{8,4},{12,8},{1,13},{5,1},{9,5},{13,9},{2,14},{6,2},{... | collective-permute-start | bytes 427016 | tf_op jit(solution)/shard_map/ppermute | solution.py:26
  12.5 6.5 %copy.196 = bf16[1024,2048]{1,0:T(8,128)(2,1)} copy(bf16[1024,2048]{0,1:T(8,128)(2,1)} %bitcast.165) | data formatting | bytes 8388608 | tf_op jit(solution)/shard_map/stk,kd->std/dot_general | solution.py:179
  20.1 3.6 %collective-permute-start.11 = (bf16[1,16,4448]{2,1,0:T(8,128)(2,1)S(1)}, bf16[1,16,4448]{2,1,0:T(8,128)(2,1)S(1)}, u32[]{:S(2)}, u32[]{:S(2)}) collective-permute-start(bf16[1,16,4448]{2,1,0:T(8,128)(2,1)S(1)} %concatenate.16), channel_id=1, source_target_pairs={{0,4},{4,8},{8,12},{12,0},{1,5},{5,9},{9,13},{13,1},{2,6},{6,10},{... | collective-permute-start | bytes 427016 | tf_op jit(solution)/shard_map/ppermute | solution.py:26
  23.6 1.6 %collective-permute-start.10 = (bf16[1,16,4448]{2,1,0:T(8,128)(2,1)S(1)}, bf16[1,16,4448]{2,1,0:T(8,128)(2,1)}, u32[]{:S(2)}, u32[]{:S(2)}) collective-permute-start(bf16[1,16,4448]{2,1,0:T(8,128)(2,1)S(1)} %concatenate.16), channel_id=1, source_target_pairs={{0,8},{4,12},{8,0},{12,4},{1,9},{5,13},{9,1},{13,5},{2,10},{6,14},... | collective-permute-start | bytes 427016 | tf_op jit(solution)/shard_map/ppermute | solution.py:26
  28.4 3.6 %fusion.50 = f32[64,4,256]{2,0,1:T(8,128)S(1)} fusion(bf16[4,256,2048]{2,1,0:T(8,128)(2,1)} %bitcast.166, f32[1,64,2048]{2,1,0:T(8,128)S(1)} %copy.166, bf16[1,64,4448]{2,1,0:T(8,128)(2,1)S(1)} %bitcast.172), kind=kOutput, calls=%fused_computation.78 | convolution fusion | flops 269352960 | bytes 5242880 | tf_op jit(solution)/shard_map/stk,kd->std/dot_general | solution.py:179
  32.7 1.5 %collective-permute-start.3 = (f32[64,256]{1,0:T(8,128)}, f32[64,256]{1,0:T(8,128)S(1)}, u32[]{:S(2)}, u32[]{:S(2)}) collective-permute-start(f32[64,256]{1,0:T(8,128)} %get-tuple-element.37), channel_id=1, source_target_pairs={{0,1},{1,0},{2,3},{3,2},{4,5},{5,4},{6,7},{7,6},{8,9},{9,8},{10,11... | collective-permute-start | bytes 196616 | tf_op jit(solution)/shard_map/ppermute | solution.py:49
  34.2 1.5 %collective-permute-start.5 = (f32[64,256]{1,0:T(8,128)}, f32[64,256]{1,0:T(8,128)}, u32[]{:S(2)}, u32[]{:S(2)}) collective-permute-start(f32[64,256]{1,0:T(8,128)} %get-tuple-element.38), channel_id=1, source_target_pairs={{0,3},{1,2},{2,1},{3,0},{4,7},{5,6},{6,5},{7,4},{8,11},{9,10},{10,... | collective-permute-start | bytes 196616 | tf_op jit(solution)/shard_map/ppermute | solution.py:49
  40.1 3.6 %fusion.48 = f32[64,4,256]{2,0,1:T(8,128)S(1)} fusion(bf16[4,256,2048]{2,1,0:T(8,128)(2,1)} %bitcast.167, f32[1,64,2048]{2,1,0:T(8,128)S(1)} %copy.172, bf16[1,64,4448]{2,1,0:T(8,128)(2,1)S(1)} %bitcast.176), kind=kOutput, calls=%fused_computation.76 | convolution fusion | flops 269352960 | bytes 5242880 | tf_op jit(solution)/shard_map/stk,kd->std/dot_general | solution.py:179
  43.7 1.6 %collective-permute-start.12 = (f32[65,256]{1,0:T(8,128)S(1)}, f32[65,256]{1,0:T(8,128)S(1)}, u32[]{:S(2)}, u32[]{:S(2)}) collective-permute-start(f32[65,256]{1,0:T(8,128)S(1)} %get-tuple-element.34), channel_id=1, source_target_pairs={{0,1},{1,0},{2,3},{3,2},{4,5},{5,4},{6,7},{7,6},{8,9},{9,8},{10,11... | collective-permute-start | bytes 199688 | tf_op jit(solution)/shard_map/ppermute | solution.py:49
  45.2 1.5 %collective-permute-start.13 = (f32[65,256]{1,0:T(8,128)S(1)}, f32[65,256]{1,0:T(8,128)S(1)}, u32[]{:S(2)}, u32[]{:S(2)}) collective-permute-start(f32[65,256]{1,0:T(8,128)S(1)} %get-tuple-element.35), channel_id=1, source_target_pairs={{0,2},{1,3},{2,0},{3,1},{4,6},{5,7},{6,4},{7,5},{8,10},{9,11},{10,... | collective-permute-start | bytes 199688 | tf_op jit(solution)/shard_map/ppermute | solution.py:49
  48.2 1.5 %collective-permute-start.8 = (bf16[64,256]{1,0:T(8,128)(2,1)S(1)}, bf16[64,256]{1,0:T(8,128)(2,1)S(1)}, u32[]{:S(2)}, u32[]{:S(2)}) collective-permute-start(bf16[64,256]{1,0:T(8,128)(2,1)S(1)} %fusion.68), channel_id=1, source_target_pairs={{0,4},{4,8},{8,12},{12,0},{1,5},{5,9},{9,13},{13,1},{2,6},{6,10},{... | collective-permute-start | bytes 98312 | tf_op jit(solution)/shard_map/ppermute | solution.py:26
  49.6 2.2 %collective-permute-start.7 = (bf16[64,256]{1,0:T(8,128)(2,1)S(1)}, bf16[64,256]{1,0:T(8,128)(2,1)S(1)}, u32[]{:S(2)}, u32[]{:S(2)}) collective-permute-start(bf16[64,256]{1,0:T(8,128)(2,1)S(1)} %fusion.68), channel_id=1, source_target_pairs={{0,8},{4,12},{8,0},{12,4},{1,9},{5,13},{9,1},{13,5},{2,10},{6,14},... | collective-permute-start | bytes 98312 | tf_op jit(solution)/shard_map/ppermute | solution.py:26
  52.1 1.8 %collective-permute-start.17 = (bf16[65,256]{1,0:T(8,128)(2,1)S(1)}, bf16[65,256]{1,0:T(8,128)(2,1)S(1)}, u32[]{:S(2)}, u32[]{:S(2)}) collective-permute-start(bf16[65,256]{1,0:T(8,128)(2,1)S(1)} %fusion.61), channel_id=1, source_target_pairs={{0,4},{4,8},{8,12},{12,0},{1,5},{5,9},{9,13},{13,1},{2,6},{6,10},{... | collective-permute-start | bytes 99848 | tf_op jit(solution)/shard_map/ppermute | solution.py:26
  53.9 1.8 %collective-permute-start.16 = (bf16[65,256]{1,0:T(8,128)(2,1)S(1)}, bf16[65,256]{1,0:T(8,128)(2,1)S(1)}, u32[]{:S(2)}, u32[]{:S(2)}) collective-permute-start(bf16[65,256]{1,0:T(8,128)(2,1)S(1)} %fusion.61), channel_id=1, source_target_pairs={{0,8},{4,12},{8,0},{12,4},{1,9},{5,13},{9,1},{13,5},{2,10},{6,14},... | collective-permute-start | bytes 99848 | tf_op jit(solution)/shard_map/ppermute | solution.py:26
  55.7 1.4 %collective-permute-start.15 = (bf16[65,256]{1,0:T(8,128)(2,1)S(1)}, bf16[65,256]{1,0:T(8,128)(2,1)S(1)}, u32[]{:S(2)}, u32[]{:S(2)}) collective-permute-start(bf16[65,256]{1,0:T(8,128)(2,1)S(1)} %fusion.61), channel_id=1, source_target_pairs={{0,12},{4,0},{8,4},{12,8},{1,13},{5,1},{9,5},{13,9},{2,14},{6,2},{... | collective-permute-start | bytes 99848 | tf_op jit(solution)/shard_map/ppermute | solution.py:26
  57.9 1.2 %collective-permute-done.16 = bf16[65,256]{1,0:T(8,128)(2,1)S(1)} collective-permute-done((bf16[65,256]{1,0:T(8,128)(2,1)S(1)}, bf16[65,256]{1,0:T(8,128)(2,1)S(1)}, u32[]{:S(2)}, u32[]{:S(2)}) %collective-permute-start.16) | collective-permute-done | bytes 33312 | tf_op jit(solution)/shard_map/ppermute | solution.py:26
  60.8 1.5 %collective-permute-start.19 = (bf16[4,129,256]{2,1,0:T(8,128)(2,1)S(1)}, bf16[4,129,256]{2,1,0:T(8,128)(2,1)S(1)}, u32[]{:S(2)}, u32[]{:S(2)}) collective-permute-start(bf16[4,129,256]{2,1,0:T(8,128)(2,1)S(1)} %maximum_maximum_fusion), channel_id=1, source_target_pairs={{0,2},{1,3},{2,0},{3,1},{4,6},{5,7},{6,4},{7,5},{8,10},{9,11},{10,... | collective-permute-start | bytes 792584 | tf_op jit(solution)/shard_map/ppermute | solution.py:37
  63.2 5.1 %collective-permute-done.20 = bf16[4,129,256]{2,1,0:T(8,128)(2,1)S(1)} collective-permute-done((bf16[4,129,256]{2,1,0:T(8,128)(2,1)S(1)}, bf16[4,129,256]{2,1,0:T(8,128)(2,1)S(1)}, u32[]{:S(2)}, u32[]{:S(2)}) %collective-permute-start.20) | collective-permute-done | bytes 264224 | tf_op jit(solution)/shard_map/ppermute | solution.py:37
  68.3 4.0 %collective-permute-done.19 = bf16[4,129,256]{2,1,0:T(8,128)(2,1)S(1)} collective-permute-done((bf16[4,129,256]{2,1,0:T(8,128)(2,1)S(1)}, bf16[4,129,256]{2,1,0:T(8,128)(2,1)S(1)}, u32[]{:S(2)}, u32[]{:S(2)}) %collective-permute-start.19) | collective-permute-done | bytes 264224 | tf_op jit(solution)/shard_map/ppermute | solution.py:37
  73.1 1.4 %copy.175 = bf16[4,4,129,256]{3,1,2,0:T(4,128)(2,1)} copy(bf16[4,4,129,256]{3,2,1,0:T(8,128)(2,1)S(1)} %pad_maximum_fusion) | data formatting | bytes 2113536 | tf_op jit(solution)/shard_map/stack | solution.py:17
  74.9 2.5 %collective-permute-done.21 = bf16[4,4,129,256]{3,1,2,0:T(4,128)(2,1)S(1)} collective-permute-done((bf16[4,4,129,256]{3,1,2,0:T(4,128)(2,1)}, bf16[4,4,129,256]{3,1,2,0:T(4,128)(2,1)S(1)}, u32[]{:S(2)}, u32[]{:S(2)}) %collective-permute-start.21) | collective-permute-done | bytes 1056800 | tf_op jit(solution)/shard_map/ppermute | solution.py:26
  80.9 8.2 %fusion.10 = f32[2,896,256]{1,2,0:T(8,128)S(1)} fusion(bf16[256,4096,1]{0,1,2:T(8,128)(2,1)S(1)} %bitcast.168, bf16[1,2,896,4096]{3,2,1,0:T(8,128)(2,1)} %param.19), kind=kOutput, calls=%fused_computation.14 | convolution fusion | flops 3758096384 | bytes 18612224 | tf_op jit(solution)/shard_map/gfd,qd->gfq/dot_general | solution.py:105
  (115 shorter events, 26.3 us)
Async XLA Ops:
  4.6 14.7 %collective-permute-start.2 = (bf16[1,16,4448]{2,1,0:T(8,128)(2,1)S(1)}, bf16[1,16,4448]{2,1,0:T(8,128)(2,1)S(1)}, u32[]{:S(2)}, u32[]{:S(2)}) collective-permute-start(bf16[1,16,4448]{2,1,0:T(8,128)(2,1)S(1)} %concatenate.15), channel_id=1, source_target_pairs={{0,4},{4,8},{8,12},{12,0},{1,5},{5,9},{9,13},{13,1},{2,6},{6,10},{... | collective-permute-start | bytes 427016 | tf_op jit(solution)/shard_map/ppermute | solution.py:26
  7.6 12.0 %collective-permute-start.1 = (bf16[1,16,4448]{2,1,0:T(8,128)(2,1)S(1)}, bf16[1,16,4448]{2,1,0:T(8,128)(2,1)S(1)}, u32[]{:S(2)}, u32[]{:S(2)}) collective-permute-start(bf16[1,16,4448]{2,1,0:T(8,128)(2,1)S(1)} %concatenate.15), channel_id=1, source_target_pairs={{0,8},{4,12},{8,0},{12,4},{1,9},{5,13},{9,1},{13,5},{2,10},{6,14},... | collective-permute-start | bytes 427016 | tf_op jit(solution)/shard_map/ppermute | solution.py:26
  10.2 9.4 %collective-permute-start = (bf16[1,16,4448]{2,1,0:T(8,128)(2,1)S(1)}, bf16[1,16,4448]{2,1,0:T(8,128)(2,1)S(1)}, u32[]{:S(2)}, u32[]{:S(2)}) collective-permute-start(bf16[1,16,4448]{2,1,0:T(8,128)(2,1)S(1)} %concatenate.15), channel_id=1, source_target_pairs={{0,12},{4,0},{8,4},{12,8},{1,13},{5,1},{9,5},{13,9},{2,14},{6,2},{... | collective-permute-start | bytes 427016 | tf_op jit(solution)/shard_map/ppermute | solution.py:26
  19.3 7.6 %copy-start.2 = (pred[64,64]{1,0:T(8,128)(4,1)}, pred[64,64]{1,0:T(8,128)(4,1)S(1)}, u32[]{:S(2)}) copy-start(pred[64,64]{1,0:T(8,128)(4,1)S(1)} %iota_compare_fusion.1) | copy-start | bytes 12292
  19.9 7.0 %copy-start.4 = (f32[32]{0:T(128)S(1)}, f32[32]{0:T(128)}, u32[]{:S(2)}) copy-start(f32[32]{0:T(128)} %param.16) | copy-start | bytes 388
  20.1 15.7 %collective-permute-start.11 = (bf16[1,16,4448]{2,1,0:T(8,128)(2,1)S(1)}, bf16[1,16,4448]{2,1,0:T(8,128)(2,1)S(1)}, u32[]{:S(2)}, u32[]{:S(2)}) collective-permute-start(bf16[1,16,4448]{2,1,0:T(8,128)(2,1)S(1)} %concatenate.16), channel_id=1, source_target_pairs={{0,4},{4,8},{8,12},{12,0},{1,5},{5,9},{9,13},{13,1},{2,6},{6,10},{... | collective-permute-start | bytes 427016 | tf_op jit(solution)/shard_map/ppermute | solution.py:26
  23.6 12.6 %collective-permute-start.10 = (bf16[1,16,4448]{2,1,0:T(8,128)(2,1)S(1)}, bf16[1,16,4448]{2,1,0:T(8,128)(2,1)}, u32[]{:S(2)}, u32[]{:S(2)}) collective-permute-start(bf16[1,16,4448]{2,1,0:T(8,128)(2,1)S(1)} %concatenate.16), channel_id=1, source_target_pairs={{0,8},{4,12},{8,0},{12,4},{1,9},{5,13},{9,1},{13,5},{2,10},{6,14},... | collective-permute-start | bytes 427016 | tf_op jit(solution)/shard_map/ppermute | solution.py:26
  25.3 11.0 %collective-permute-start.9 = (bf16[1,16,4448]{2,1,0:T(8,128)(2,1)S(1)}, bf16[1,16,4448]{2,1,0:T(8,128)(2,1)}, u32[]{:S(2)}, u32[]{:S(2)}) collective-permute-start(bf16[1,16,4448]{2,1,0:T(8,128)(2,1)S(1)} %concatenate.16), channel_id=1, source_target_pairs={{0,12},{4,0},{8,4},{12,8},{1,13},{5,1},{9,5},{13,9},{2,14},{6,2},{... | collective-permute-start | bytes 427016 | tf_op jit(solution)/shard_map/ppermute | solution.py:26
  32.7 14.0 %collective-permute-start.3 = (f32[64,256]{1,0:T(8,128)}, f32[64,256]{1,0:T(8,128)S(1)}, u32[]{:S(2)}, u32[]{:S(2)}) collective-permute-start(f32[64,256]{1,0:T(8,128)} %get-tuple-element.37), channel_id=1, source_target_pairs={{0,1},{1,0},{2,3},{3,2},{4,5},{5,4},{6,7},{7,6},{8,9},{9,8},{10,11... | collective-permute-start | bytes 196616 | tf_op jit(solution)/shard_map/ppermute | solution.py:49
  34.2 13.0 %collective-permute-start.5 = (f32[64,256]{1,0:T(8,128)}, f32[64,256]{1,0:T(8,128)}, u32[]{:S(2)}, u32[]{:S(2)}) collective-permute-start(f32[64,256]{1,0:T(8,128)} %get-tuple-element.38), channel_id=1, source_target_pairs={{0,3},{1,2},{2,1},{3,0},{4,7},{5,6},{6,5},{7,4},{8,11},{9,10},{10,... | collective-permute-start | bytes 196616 | tf_op jit(solution)/shard_map/ppermute | solution.py:49
  35.7 11.5 %collective-permute-start.4 = (f32[64,256]{1,0:T(8,128)}, f32[64,256]{1,0:T(8,128)}, u32[]{:S(2)}, u32[]{:S(2)}) collective-permute-start(f32[64,256]{1,0:T(8,128)} %get-tuple-element.39), channel_id=1, source_target_pairs={{0,2},{1,3},{2,0},{3,1},{4,6},{5,7},{6,4},{7,5},{8,10},{9,11},{10,... | collective-permute-start | bytes 196616 | tf_op jit(solution)/shard_map/ppermute | solution.py:49
  43.7 8.1 %collective-permute-start.12 = (f32[65,256]{1,0:T(8,128)S(1)}, f32[65,256]{1,0:T(8,128)S(1)}, u32[]{:S(2)}, u32[]{:S(2)}) collective-permute-start(f32[65,256]{1,0:T(8,128)S(1)} %get-tuple-element.34), channel_id=1, source_target_pairs={{0,1},{1,0},{2,3},{3,2},{4,5},{5,4},{6,7},{7,6},{8,9},{9,8},{10,11... | collective-permute-start | bytes 199688 | tf_op jit(solution)/shard_map/ppermute | solution.py:49
  45.2 6.8 %collective-permute-start.13 = (f32[65,256]{1,0:T(8,128)S(1)}, f32[65,256]{1,0:T(8,128)S(1)}, u32[]{:S(2)}, u32[]{:S(2)}) collective-permute-start(f32[65,256]{1,0:T(8,128)S(1)} %get-tuple-element.35), channel_id=1, source_target_pairs={{0,2},{1,3},{2,0},{3,1},{4,6},{5,7},{6,4},{7,5},{8,10},{9,11},{10,... | collective-permute-start | bytes 199688 | tf_op jit(solution)/shard_map/ppermute | solution.py:49
  46.8 5.3 %collective-permute-start.14 = (f32[65,256]{1,0:T(8,128)S(1)}, f32[65,256]{1,0:T(8,128)S(1)}, u32[]{:S(2)}, u32[]{:S(2)}) collective-permute-start(f32[65,256]{1,0:T(8,128)S(1)} %get-tuple-element.36), channel_id=1, source_target_pairs={{0,3},{1,2},{2,1},{3,0},{4,7},{5,6},{6,5},{7,4},{8,11},{9,10},{10,... | collective-permute-start | bytes 199688 | tf_op jit(solution)/shard_map/ppermute | solution.py:49
  48.2 7.5 %collective-permute-start.8 = (bf16[64,256]{1,0:T(8,128)(2,1)S(1)}, bf16[64,256]{1,0:T(8,128)(2,1)S(1)}, u32[]{:S(2)}, u32[]{:S(2)}) collective-permute-start(bf16[64,256]{1,0:T(8,128)(2,1)S(1)} %fusion.68), channel_id=1, source_target_pairs={{0,4},{4,8},{8,12},{12,0},{1,5},{5,9},{9,13},{13,1},{2,6},{6,10},{... | collective-permute-start | bytes 98312 | tf_op jit(solution)/shard_map/ppermute | solution.py:26
  49.6 7.5 %collective-permute-start.7 = (bf16[64,256]{1,0:T(8,128)(2,1)S(1)}, bf16[64,256]{1,0:T(8,128)(2,1)S(1)}, u32[]{:S(2)}, u32[]{:S(2)}) collective-permute-start(bf16[64,256]{1,0:T(8,128)(2,1)S(1)} %fusion.68), channel_id=1, source_target_pairs={{0,8},{4,12},{8,0},{12,4},{1,9},{5,13},{9,1},{13,5},{2,10},{6,14},... | collective-permute-start | bytes 98312 | tf_op jit(solution)/shard_map/ppermute | solution.py:26
  51.8 5.3 %collective-permute-start.6 = (bf16[64,256]{1,0:T(8,128)(2,1)S(1)}, bf16[64,256]{1,0:T(8,128)(2,1)S(1)}, u32[]{:S(2)}, u32[]{:S(2)}) collective-permute-start(bf16[64,256]{1,0:T(8,128)(2,1)S(1)} %fusion.68), channel_id=1, source_target_pairs={{0,12},{4,0},{8,4},{12,8},{1,13},{5,1},{9,5},{13,9},{2,14},{6,2},{... | collective-permute-start | bytes 98312 | tf_op jit(solution)/shard_map/ppermute | solution.py:26
  52.1 5.8 %collective-permute-start.17 = (bf16[65,256]{1,0:T(8,128)(2,1)S(1)}, bf16[65,256]{1,0:T(8,128)(2,1)S(1)}, u32[]{:S(2)}, u32[]{:S(2)}) collective-permute-start(bf16[65,256]{1,0:T(8,128)(2,1)S(1)} %fusion.61), channel_id=1, source_target_pairs={{0,4},{4,8},{8,12},{12,0},{1,5},{5,9},{9,13},{13,1},{2,6},{6,10},{... | collective-permute-start | bytes 99848 | tf_op jit(solution)/shard_map/ppermute | solution.py:26
  53.9 5.3 %collective-permute-start.16 = (bf16[65,256]{1,0:T(8,128)(2,1)S(1)}, bf16[65,256]{1,0:T(8,128)(2,1)S(1)}, u32[]{:S(2)}, u32[]{:S(2)}) collective-permute-start(bf16[65,256]{1,0:T(8,128)(2,1)S(1)} %fusion.61), channel_id=1, source_target_pairs={{0,8},{4,12},{8,0},{12,4},{1,9},{5,13},{9,1},{13,5},{2,10},{6,14},... | collective-permute-start | bytes 99848 | tf_op jit(solution)/shard_map/ppermute | solution.py:26
  55.7 4.0 %collective-permute-start.15 = (bf16[65,256]{1,0:T(8,128)(2,1)S(1)}, bf16[65,256]{1,0:T(8,128)(2,1)S(1)}, u32[]{:S(2)}, u32[]{:S(2)}) collective-permute-start(bf16[65,256]{1,0:T(8,128)(2,1)S(1)} %fusion.61), channel_id=1, source_target_pairs={{0,12},{4,0},{8,4},{12,8},{1,13},{5,1},{9,5},{13,9},{2,14},{6,2},{... | collective-permute-start | bytes 99848 | tf_op jit(solution)/shard_map/ppermute | solution.py:26
  59.7 8.6 %collective-permute-start.20 = (bf16[4,129,256]{2,1,0:T(8,128)(2,1)S(1)}, bf16[4,129,256]{2,1,0:T(8,128)(2,1)S(1)}, u32[]{:S(2)}, u32[]{:S(2)}) collective-permute-start(bf16[4,129,256]{2,1,0:T(8,128)(2,1)S(1)} %maximum_maximum_fusion), channel_id=1, source_target_pairs={{0,1},{1,0},{2,3},{3,2},{4,5},{5,4},{6,7},{7,6},{8,9},{9,8},{10,11... | collective-permute-start | bytes 792584 | tf_op jit(solution)/shard_map/ppermute | solution.py:37
  60.8 11.6 %collective-permute-start.19 = (bf16[4,129,256]{2,1,0:T(8,128)(2,1)S(1)}, bf16[4,129,256]{2,1,0:T(8,128)(2,1)S(1)}, u32[]{:S(2)}, u32[]{:S(2)}) collective-permute-start(bf16[4,129,256]{2,1,0:T(8,128)(2,1)S(1)} %maximum_maximum_fusion), channel_id=1, source_target_pairs={{0,2},{1,3},{2,0},{3,1},{4,6},{5,7},{6,4},{7,5},{8,10},{9,11},{10,... | collective-permute-start | bytes 792584 | tf_op jit(solution)/shard_map/ppermute | solution.py:37
  62.3 10.1 %collective-permute-start.18 = (bf16[4,129,256]{2,1,0:T(8,128)(2,1)S(1)}, bf16[4,129,256]{2,1,0:T(8,128)(2,1)S(1)}, u32[]{:S(2)}, u32[]{:S(2)}) collective-permute-start(bf16[4,129,256]{2,1,0:T(8,128)(2,1)S(1)} %maximum_maximum_fusion), channel_id=1, source_target_pairs={{0,3},{1,2},{2,1},{3,0},{4,7},{5,6},{6,5},{7,4},{8,11},{9,10},{10,... | collective-permute-start | bytes 792584 | tf_op jit(solution)/shard_map/ppermute | solution.py:37
  74.5 2.9 %collective-permute-start.21 = (bf16[4,4,129,256]{3,1,2,0:T(4,128)(2,1)}, bf16[4,4,129,256]{3,1,2,0:T(4,128)(2,1)S(1)}, u32[]{:S(2)}, u32[]{:S(2)}) collective-permute-start(bf16[4,4,129,256]{3,1,2,0:T(4,128)(2,1)} %copy.175), channel_id=1, source_target_pairs={{0,16},{16,0},{1,17},{17,1},{2,18},{18,2},{3,19},{19,3},{4,20},{20... | collective-permute-start | bytes 3170312 | tf_op jit(solution)/shard_map/ppermute | solution.py:26
  (3 other events, 8.5 us)

commit v15 on v14

--- a/solution.py
+++ b/solution.py
@@ -158,9 +158,8 @@
     head_count = decay_log.shape[2]
     decay_base = 2 * width_in + 2 * state_size
 
-    def front(x_part, z_part, b_part, c_part, decay_part, after=None):
-        part_count = x_part.shape[0]
-        packed = jnp.concatenate([x_part, z_part, b_part, c_part] + split_exact(decay_part), axis=2)
+    def front(packed, after=None):
+        part_count = packed.shape[0]
         if after is not None:
             _, packed = lax.optimization_barrier((after, packed))
         packed = gather_blocks(packed, "ctx", ctx_count)
@@ -180,7 +179,8 @@
         return projected, packed
 
     if device_count * row_count * model_width * 2 > (8 << 20):
-        partial_value = front(x_in, z_in, b_in, c_in, decay_log)[0]
+        packed = jnp.concatenate([x_in, z_in, b_in, c_in] + split_exact(decay_log), axis=2)
+        partial_value = front(packed)[0]
         return dispatch_routed(partial_value, moe_gain, gate_up, expert_ids, slot_ids, capacity)
     total_len = ctx_count * block_len
     route = jnp.stack([expert_ids, slot_ids], axis=-1).astype(jnp.float32).reshape(-1)
@@ -193,11 +193,10 @@
     part_len = seq_count // split
     token_parts = []
     arrived = None
+    packed_all = jnp.concatenate([x_in, z_in, b_in, c_in] + split_exact(decay_log), axis=2)
     for part in range(split):
         streams = slice(part * part_len, (part + 1) * part_len)
-        partial_value, arrived = front(
-            x_in[streams], z_in[streams], b_in[streams], c_in[streams], decay_log[streams], arrived
-        )
+        partial_value, arrived = front(packed_all[streams], arrived)
         rows = partial_value.reshape(part_len * total_len, col_width)
         if part == split - 1:
             rows = jnp.concatenate([rows, route_row.reshape(extra_rows, col_width)], axis=0)

time: 92.5 us -> 91.8 us (level)
  local copies, waits for them, and re-layouts: 17.6 us -> 16.1 us
    slice x3 -> x1, local copies, waits for them, and re-layouts: 2.41 us -> 0.02 us  [local(): partial_value, arrived = front(packed_all[streams], arrived)]
where the time goes in v15:
time: 91.8 us; the launch traced here: 91.3 us
  starting transfers between devices  32.4 us (35%)
  matrix products  18.9 us (21%)
  local copies, waits for them, and re-layouts  16.1 us (18%)
  waiting for transfers between devices  14.6 us (16%)
  other arithmetic  8.13 us (9%)
  between operations  1.08 us (1%)
    ppermute x13, starting transfers between devices, gather_blocks(): received.append(lax.ppermute(value, axis_name, perm))  21.8 us
    ppermute x3, waiting for transfers between devices, gather_xor(): received.append(lax.ppermute(value, axis_name, perm))  9.13 us
    dot_general x1, matrix products, expert_ffn(): jnp.einsum('gfd,qd->gfq', gate_up[0], slot_rows, preferred_element_type=j...  8.15 us
    dot_general x2, matrix products, front(): jnp.einsum('stk,kd->std', gated, out_weight, preferred_element_type=jnp.f...  7.16 us
    ppermute x6, starting transfers between devices, sum_scatter(): total = total + lax.ppermute(send, axis_name, perm)  7.04 us
    dot_general x1, local copies, waits for them, and re-layouts, front(): jnp.einsum('stk,kd->std', gated, out_weight, preferred_element_type=jnp.f...  6.55 us
    ppermute x13, waiting for transfers between devices, gather_blocks(): received.append(lax.ppermute(value, axis_name, perm))  5.47 us
    ppermute x3, starting transfers between devices, gather_xor(): received.append(lax.ppermute(value, axis_name, perm))  3.55 us
  transfers between devices with their start and end apart: 22, of which 7 were waited for; matrix products, arithmetic and copies ran while one was open for 25% of the time, Pallas kernels for 0%

profile of v15, /device:TPU:0, one launch (start us, length us, event | category | flops | bytes accessed | tf_op | source)
XLA Modules:
  0.0 91.3 jit_solution(931670989762172191)
XLA Ops:
  3.9 3.1 %collective-permute-start.2 = (bf16[1,16,4448]{2,1,0:T(8,128)(2,1)S(1)}, bf16[1,16,4448]{2,1,0:T(8,128)(2,1)S(1)}, u32[]{:S(2)}, u32[]{:S(2)}) collective-permute-start(bf16[1,16,4448]{2,1,0:T(8,128)(2,1)S(1)} %get-tuple-element.35), channel_id=1, source_target_pairs={{0,4},{4,8},{8,12},{12,0},{1,5},{5,9},{9,13},{13,1},{2,6},{6,10},{... | collective-permute-start | bytes 427016 | tf_op jit(solution)/shard_map/ppermute | solution.py:26
  7.0 2.6 %collective-permute-start.1 = (bf16[1,16,4448]{2,1,0:T(8,128)(2,1)S(1)}, bf16[1,16,4448]{2,1,0:T(8,128)(2,1)S(1)}, u32[]{:S(2)}, u32[]{:S(2)}) collective-permute-start(bf16[1,16,4448]{2,1,0:T(8,128)(2,1)S(1)} %get-tuple-element.35), channel_id=1, source_target_pairs={{0,8},{4,12},{8,0},{12,4},{1,9},{5,13},{9,1},{13,5},{2,10},{6,14},... | collective-permute-start | bytes 427016 | tf_op jit(solution)/shard_map/ppermute | solution.py:26
  9.6 1.3 %collective-permute-start = (bf16[1,16,4448]{2,1,0:T(8,128)(2,1)S(1)}, bf16[1,16,4448]{2,1,0:T(8,128)(2,1)S(1)}, u32[]{:S(2)}, u32[]{:S(2)}) collective-permute-start(bf16[1,16,4448]{2,1,0:T(8,128)(2,1)S(1)} %get-tuple-element.35), channel_id=1, source_target_pairs={{0,12},{4,0},{8,4},{12,8},{1,13},{5,1},{9,5},{13,9},{2,14},{6,2},{... | collective-permute-start | bytes 427016 | tf_op jit(solution)/shard_map/ppermute | solution.py:26
  11.8 6.5 %copy.196 = bf16[1024,2048]{1,0:T(8,128)(2,1)} copy(bf16[1024,2048]{0,1:T(8,128)(2,1)} %bitcast.165) | data formatting | bytes 8388608 | tf_op jit(solution)/shard_map/stk,kd->std/dot_general | solution.py:178
  19.4 3.6 %collective-permute-start.11 = (bf16[1,16,4448]{2,1,0:T(8,128)(2,1)S(1)}, bf16[1,16,4448]{2,1,0:T(8,128)(2,1)S(1)}, u32[]{:S(2)}, u32[]{:S(2)}) collective-permute-start(bf16[1,16,4448]{2,1,0:T(8,128)(2,1)S(1)} %get-tuple-element.3), channel_id=1, source_target_pairs={{0,4},{4,8},{8,12},{12,0},{1,5},{5,9},{9,13},{13,1},{2,6},{6,10},{... | collective-permute-start | bytes 427016 | tf_op jit(solution)/shard_map/ppermute | solution.py:26
  23.0 1.6 %collective-permute-start.10 = (bf16[1,16,4448]{2,1,0:T(8,128)(2,1)S(1)}, bf16[1,16,4448]{2,1,0:T(8,128)(2,1)}, u32[]{:S(2)}, u32[]{:S(2)}) collective-permute-start(bf16[1,16,4448]{2,1,0:T(8,128)(2,1)S(1)} %get-tuple-element.3), channel_id=1, source_target_pairs={{0,8},{4,12},{8,0},{12,4},{1,9},{5,13},{9,1},{13,5},{2,10},{6,14},... | collective-permute-start | bytes 427016 | tf_op jit(solution)/shard_map/ppermute | solution.py:26
  27.8 3.6 %fusion.50 = f32[64,4,256]{2,0,1:T(8,128)S(1)} fusion(bf16[4,256,2048]{2,1,0:T(8,128)(2,1)} %bitcast.166, f32[1,64,2048]{2,1,0:T(8,128)S(1)} %copy.166, bf16[1,64,4448]{2,1,0:T(8,128)(2,1)S(1)} %bitcast.172), kind=kOutput, calls=%fused_computation.78 | convolution fusion | flops 269352960 | bytes 5242880 | tf_op jit(solution)/shard_map/stk,kd->std/dot_general | solution.py:178
  32.1 1.5 %collective-permute-start.3 = (f32[64,256]{1,0:T(8,128)}, f32[64,256]{1,0:T(8,128)S(1)}, u32[]{:S(2)}, u32[]{:S(2)}) collective-permute-start(f32[64,256]{1,0:T(8,128)} %get-tuple-element.39), channel_id=1, source_target_pairs={{0,1},{1,0},{2,3},{3,2},{4,5},{5,4},{6,7},{7,6},{8,9},{9,8},{10,11... | collective-permute-start | bytes 196616 | tf_op jit(solution)/shard_map/ppermute | solution.py:49
  33.6 1.5 %collective-permute-start.5 = (f32[64,256]{1,0:T(8,128)}, f32[64,256]{1,0:T(8,128)}, u32[]{:S(2)}, u32[]{:S(2)}) collective-permute-start(f32[64,256]{1,0:T(8,128)} %get-tuple-element.40), channel_id=1, source_target_pairs={{0,3},{1,2},{2,1},{3,0},{4,7},{5,6},{6,5},{7,4},{8,11},{9,10},{10,... | collective-permute-start | bytes 196616 | tf_op jit(solution)/shard_map/ppermute | solution.py:49
  39.4 3.6 %fusion.48 = f32[64,4,256]{2,0,1:T(8,128)S(1)} fusion(bf16[4,256,2048]{2,1,0:T(8,128)(2,1)} %bitcast.167, f32[1,64,2048]{2,1,0:T(8,128)S(1)} %copy.172, bf16[1,64,4448]{2,1,0:T(8,128)(2,1)S(1)} %bitcast.176), kind=kOutput, calls=%fused_computation.76 | convolution fusion | flops 269352960 | bytes 5242880 | tf_op jit(solution)/shard_map/stk,kd->std/dot_general | solution.py:178
  43.0 1.6 %collective-permute-start.12 = (f32[65,256]{1,0:T(8,128)S(1)}, f32[65,256]{1,0:T(8,128)S(1)}, u32[]{:S(2)}, u32[]{:S(2)}) collective-permute-start(f32[65,256]{1,0:T(8,128)S(1)} %get-tuple-element.36), channel_id=1, source_target_pairs={{0,1},{1,0},{2,3},{3,2},{4,5},{5,4},{6,7},{7,6},{8,9},{9,8},{10,11... | collective-permute-start | bytes 199688 | tf_op jit(solution)/shard_map/ppermute | solution.py:49
  44.6 1.5 %collective-permute-start.13 = (f32[65,256]{1,0:T(8,128)S(1)}, f32[65,256]{1,0:T(8,128)S(1)}, u32[]{:S(2)}, u32[]{:S(2)}) collective-permute-start(f32[65,256]{1,0:T(8,128)S(1)} %get-tuple-element.37), channel_id=1, source_target_pairs={{0,2},{1,3},{2,0},{3,1},{4,6},{5,7},{6,4},{7,5},{8,10},{9,11},{10,... | collective-permute-start | bytes 199688 | tf_op jit(solution)/shard_map/ppermute | solution.py:49
  47.5 1.4 %collective-permute-start.8 = (bf16[64,256]{1,0:T(8,128)(2,1)S(1)}, bf16[64,256]{1,0:T(8,128)(2,1)S(1)}, u32[]{:S(2)}, u32[]{:S(2)}) collective-permute-start(bf16[64,256]{1,0:T(8,128)(2,1)S(1)} %fusion.68), channel_id=1, source_target_pairs={{0,4},{4,8},{8,12},{12,0},{1,5},{5,9},{9,13},{13,1},{2,6},{6,10},{... | collective-permute-start | bytes 98312 | tf_op jit(solution)/shard_map/ppermute | solution.py:26
  49.0 2.2 %collective-permute-start.7 = (bf16[64,256]{1,0:T(8,128)(2,1)S(1)}, bf16[64,256]{1,0:T(8,128)(2,1)S(1)}, u32[]{:S(2)}, u32[]{:S(2)}) collective-permute-start(bf16[64,256]{1,0:T(8,128)(2,1)S(1)} %fusion.68), channel_id=1, source_target_pairs={{0,8},{4,12},{8,0},{12,4},{1,9},{5,13},{9,1},{13,5},{2,10},{6,14},... | collective-permute-start | bytes 98312 | tf_op jit(solution)/shard_map/ppermute | solution.py:26
  51.5 1.8 %collective-permute-start.17 = (bf16[65,256]{1,0:T(8,128)(2,1)S(1)}, bf16[65,256]{1,0:T(8,128)(2,1)S(1)}, u32[]{:S(2)}, u32[]{:S(2)}) collective-permute-start(bf16[65,256]{1,0:T(8,128)(2,1)S(1)} %fusion.61), channel_id=1, source_target_pairs={{0,4},{4,8},{8,12},{12,0},{1,5},{5,9},{9,13},{13,1},{2,6},{6,10},{... | collective-permute-start | bytes 99848 | tf_op jit(solution)/shard_map/ppermute | solution.py:26
  53.3 1.8 %collective-permute-start.16 = (bf16[65,256]{1,0:T(8,128)(2,1)S(1)}, bf16[65,256]{1,0:T(8,128)(2,1)S(1)}, u32[]{:S(2)}, u32[]{:S(2)}) collective-permute-start(bf16[65,256]{1,0:T(8,128)(2,1)S(1)} %fusion.61), channel_id=1, source_target_pairs={{0,8},{4,12},{8,0},{12,4},{1,9},{5,13},{9,1},{13,5},{2,10},{6,14},... | collective-permute-start | bytes 99848 | tf_op jit(solution)/shard_map/ppermute | solution.py:26
  55.0 1.4 %collective-permute-start.15 = (bf16[65,256]{1,0:T(8,128)(2,1)S(1)}, bf16[65,256]{1,0:T(8,128)(2,1)S(1)}, u32[]{:S(2)}, u32[]{:S(2)}) collective-permute-start(bf16[65,256]{1,0:T(8,128)(2,1)S(1)} %fusion.61), channel_id=1, source_target_pairs={{0,12},{4,0},{8,4},{12,8},{1,13},{5,1},{9,5},{13,9},{2,14},{6,2},{... | collective-permute-start | bytes 99848 | tf_op jit(solution)/shard_map/ppermute | solution.py:26
  57.3 1.2 %collective-permute-done.16 = bf16[65,256]{1,0:T(8,128)(2,1)S(1)} collective-permute-done((bf16[65,256]{1,0:T(8,128)(2,1)S(1)}, bf16[65,256]{1,0:T(8,128)(2,1)S(1)}, u32[]{:S(2)}, u32[]{:S(2)}) %collective-permute-start.16) | collective-permute-done | bytes 33312 | tf_op jit(solution)/shard_map/ppermute | solution.py:26
  60.1 1.5 %collective-permute-start.19 = (bf16[4,129,256]{2,1,0:T(8,128)(2,1)S(1)}, bf16[4,129,256]{2,1,0:T(8,128)(2,1)S(1)}, u32[]{:S(2)}, u32[]{:S(2)}) collective-permute-start(bf16[4,129,256]{2,1,0:T(8,128)(2,1)S(1)} %maximum_maximum_fusion), channel_id=1, source_target_pairs={{0,2},{1,3},{2,0},{3,1},{4,6},{5,7},{6,4},{7,5},{8,10},{9,11},{10,... | collective-permute-start | bytes 792584 | tf_op jit(solution)/shard_map/ppermute | solution.py:37
  62.6 5.1 %collective-permute-done.20 = bf16[4,129,256]{2,1,0:T(8,128)(2,1)S(1)} collective-permute-done((bf16[4,129,256]{2,1,0:T(8,128)(2,1)S(1)}, bf16[4,129,256]{2,1,0:T(8,128)(2,1)S(1)}, u32[]{:S(2)}, u32[]{:S(2)}) %collective-permute-start.20) | collective-permute-done | bytes 264224 | tf_op jit(solution)/shard_map/ppermute | solution.py:37
  67.7 4.0 %collective-permute-done.19 = bf16[4,129,256]{2,1,0:T(8,128)(2,1)S(1)} collective-permute-done((bf16[4,129,256]{2,1,0:T(8,128)(2,1)S(1)}, bf16[4,129,256]{2,1,0:T(8,128)(2,1)S(1)}, u32[]{:S(2)}, u32[]{:S(2)}) %collective-permute-start.19) | collective-permute-done | bytes 264224 | tf_op jit(solution)/shard_map/ppermute | solution.py:37
  72.5 1.4 %copy.175 = bf16[4,4,129,256]{3,1,2,0:T(4,128)(2,1)} copy(bf16[4,4,129,256]{3,2,1,0:T(8,128)(2,1)S(1)} %pad_maximum_fusion) | data formatting | bytes 2113536 | tf_op jit(solution)/shard_map/stack | solution.py:17
  74.3 2.5 %collective-permute-done.21 = bf16[4,4,129,256]{3,1,2,0:T(4,128)(2,1)S(1)} collective-permute-done((bf16[4,4,129,256]{3,1,2,0:T(4,128)(2,1)}, bf16[4,4,129,256]{3,1,2,0:T(4,128)(2,1)S(1)}, u32[]{:S(2)}, u32[]{:S(2)}) %collective-permute-start.21) | collective-permute-done | bytes 1056800 | tf_op jit(solution)/shard_map/ppermute | solution.py:26
  80.3 8.2 %fusion.10 = f32[2,896,256]{1,2,0:T(8,128)S(1)} fusion(bf16[256,4096,1]{0,1,2:T(8,128)(2,1)S(1)} %bitcast.168, bf16[1,2,896,4096]{3,2,1,0:T(8,128)(2,1)} %param.19), kind=kOutput, calls=%fused_computation.14 | convolution fusion | flops 3758096384 | bytes 18612224 | tf_op jit(solution)/shard_map/gfd,qd->gfq/dot_general | solution.py:105
  (113 shorter events, 25.6 us)
Async XLA Ops:
  3.9 14.6 %collective-permute-start.2 = (bf16[1,16,4448]{2,1,0:T(8,128)(2,1)S(1)}, bf16[1,16,4448]{2,1,0:T(8,128)(2,1)S(1)}, u32[]{:S(2)}, u32[]{:S(2)}) collective-permute-start(bf16[1,16,4448]{2,1,0:T(8,128)(2,1)S(1)} %get-tuple-element.35), channel_id=1, source_target_pairs={{0,4},{4,8},{8,12},{12,0},{1,5},{5,9},{9,13},{13,1},{2,6},{6,10},{... | collective-permute-start | bytes 427016 | tf_op jit(solution)/shard_map/ppermute | solution.py:26
  7.0 12.0 %collective-permute-start.1 = (bf16[1,16,4448]{2,1,0:T(8,128)(2,1)S(1)}, bf16[1,16,4448]{2,1,0:T(8,128)(2,1)S(1)}, u32[]{:S(2)}, u32[]{:S(2)}) collective-permute-start(bf16[1,16,4448]{2,1,0:T(8,128)(2,1)S(1)} %get-tuple-element.35), channel_id=1, source_target_pairs={{0,8},{4,12},{8,0},{12,4},{1,9},{5,13},{9,1},{13,5},{2,10},{6,14},... | collective-permute-start | bytes 427016 | tf_op jit(solution)/shard_map/ppermute | solution.py:26
  9.6 9.4 %collective-permute-start = (bf16[1,16,4448]{2,1,0:T(8,128)(2,1)S(1)}, bf16[1,16,4448]{2,1,0:T(8,128)(2,1)S(1)}, u32[]{:S(2)}, u32[]{:S(2)}) collective-permute-start(bf16[1,16,4448]{2,1,0:T(8,128)(2,1)S(1)} %get-tuple-element.35), channel_id=1, source_target_pairs={{0,12},{4,0},{8,4},{12,8},{1,13},{5,1},{9,5},{13,9},{2,14},{6,2},{... | collective-permute-start | bytes 427016 | tf_op jit(solution)/shard_map/ppermute | solution.py:26
  18.5 7.7 %copy-start.2 = (pred[64,64]{1,0:T(8,128)(4,1)}, pred[64,64]{1,0:T(8,128)(4,1)S(1)}, u32[]{:S(2)}) copy-start(pred[64,64]{1,0:T(8,128)(4,1)S(1)} %iota_compare_fusion.1) | copy-start | bytes 12292
  19.2 7.0 %copy-start.4 = (f32[32]{0:T(128)S(1)}, f32[32]{0:T(128)}, u32[]{:S(2)}) copy-start(f32[32]{0:T(128)} %param.16) | copy-start | bytes 388
  19.4 15.7 %collective-permute-start.11 = (bf16[1,16,4448]{2,1,0:T(8,128)(2,1)S(1)}, bf16[1,16,4448]{2,1,0:T(8,128)(2,1)S(1)}, u32[]{:S(2)}, u32[]{:S(2)}) collective-permute-start(bf16[1,16,4448]{2,1,0:T(8,128)(2,1)S(1)} %get-tuple-element.3), channel_id=1, source_target_pairs={{0,4},{4,8},{8,12},{12,0},{1,5},{5,9},{9,13},{13,1},{2,6},{6,10},{... | collective-permute-start | bytes 427016 | tf_op jit(solution)/shard_map/ppermute | solution.py:26
  23.0 12.6 %collective-permute-start.10 = (bf16[1,16,4448]{2,1,0:T(8,128)(2,1)S(1)}, bf16[1,16,4448]{2,1,0:T(8,128)(2,1)}, u32[]{:S(2)}, u32[]{:S(2)}) collective-permute-start(bf16[1,16,4448]{2,1,0:T(8,128)(2,1)S(1)} %get-tuple-element.3), channel_id=1, source_target_pairs={{0,8},{4,12},{8,0},{12,4},{1,9},{5,13},{9,1},{13,5},{2,10},{6,14},... | collective-permute-start | bytes 427016 | tf_op jit(solution)/shard_map/ppermute | solution.py:26
  24.6 11.0 %collective-permute-start.9 = (bf16[1,16,4448]{2,1,0:T(8,128)(2,1)S(1)}, bf16[1,16,4448]{2,1,0:T(8,128)(2,1)}, u32[]{:S(2)}, u32[]{:S(2)}) collective-permute-start(bf16[1,16,4448]{2,1,0:T(8,128)(2,1)S(1)} %get-tuple-element.3), channel_id=1, source_target_pairs={{0,12},{4,0},{8,4},{12,8},{1,13},{5,1},{9,5},{13,9},{2,14},{6,2},{... | collective-permute-start | bytes 427016 | tf_op jit(solution)/shard_map/ppermute | solution.py:26
  32.1 14.0 %collective-permute-start.3 = (f32[64,256]{1,0:T(8,128)}, f32[64,256]{1,0:T(8,128)S(1)}, u32[]{:S(2)}, u32[]{:S(2)}) collective-permute-start(f32[64,256]{1,0:T(8,128)} %get-tuple-element.39), channel_id=1, source_target_pairs={{0,1},{1,0},{2,3},{3,2},{4,5},{5,4},{6,7},{7,6},{8,9},{9,8},{10,11... | collective-permute-start | bytes 196616 | tf_op jit(solution)/shard_map/ppermute | solution.py:49
  33.6 13.0 %collective-permute-start.5 = (f32[64,256]{1,0:T(8,128)}, f32[64,256]{1,0:T(8,128)}, u32[]{:S(2)}, u32[]{:S(2)}) collective-permute-start(f32[64,256]{1,0:T(8,128)} %get-tuple-element.40), channel_id=1, source_target_pairs={{0,3},{1,2},{2,1},{3,0},{4,7},{5,6},{6,5},{7,4},{8,11},{9,10},{10,... | collective-permute-start | bytes 196616 | tf_op jit(solution)/shard_map/ppermute | solution.py:49
  35.1 11.5 %collective-permute-start.4 = (f32[64,256]{1,0:T(8,128)}, f32[64,256]{1,0:T(8,128)}, u32[]{:S(2)}, u32[]{:S(2)}) collective-permute-start(f32[64,256]{1,0:T(8,128)} %get-tuple-element.41), channel_id=1, source_target_pairs={{0,2},{1,3},{2,0},{3,1},{4,6},{5,7},{6,4},{7,5},{8,10},{9,11},{10,... | collective-permute-start | bytes 196616 | tf_op jit(solution)/shard_map/ppermute | solution.py:49
  43.0 8.1 %collective-permute-start.12 = (f32[65,256]{1,0:T(8,128)S(1)}, f32[65,256]{1,0:T(8,128)S(1)}, u32[]{:S(2)}, u32[]{:S(2)}) collective-permute-start(f32[65,256]{1,0:T(8,128)S(1)} %get-tuple-element.36), channel_id=1, source_target_pairs={{0,1},{1,0},{2,3},{3,2},{4,5},{5,4},{6,7},{7,6},{8,9},{9,8},{10,11... | collective-permute-start | bytes 199688 | tf_op jit(solution)/shard_map/ppermute | solution.py:49
  44.6 6.8 %collective-permute-start.13 = (f32[65,256]{1,0:T(8,128)S(1)}, f32[65,256]{1,0:T(8,128)S(1)}, u32[]{:S(2)}, u32[]{:S(2)}) collective-permute-start(f32[65,256]{1,0:T(8,128)S(1)} %get-tuple-element.37), channel_id=1, source_target_pairs={{0,2},{1,3},{2,0},{3,1},{4,6},{5,7},{6,4},{7,5},{8,10},{9,11},{10,... | collective-permute-start | bytes 199688 | tf_op jit(solution)/shard_map/ppermute | solution.py:49
  46.1 5.3 %collective-permute-start.14 = (f32[65,256]{1,0:T(8,128)S(1)}, f32[65,256]{1,0:T(8,128)S(1)}, u32[]{:S(2)}, u32[]{:S(2)}) collective-permute-start(f32[65,256]{1,0:T(8,128)S(1)} %get-tuple-element.38), channel_id=1, source_target_pairs={{0,3},{1,2},{2,1},{3,0},{4,7},{5,6},{6,5},{7,4},{8,11},{9,10},{10,... | collective-permute-start | bytes 199688 | tf_op jit(solution)/shard_map/ppermute | solution.py:49
  47.5 7.5 %collective-permute-start.8 = (bf16[64,256]{1,0:T(8,128)(2,1)S(1)}, bf16[64,256]{1,0:T(8,128)(2,1)S(1)}, u32[]{:S(2)}, u32[]{:S(2)}) collective-permute-start(bf16[64,256]{1,0:T(8,128)(2,1)S(1)} %fusion.68), channel_id=1, source_target_pairs={{0,4},{4,8},{8,12},{12,0},{1,5},{5,9},{9,13},{13,1},{2,6},{6,10},{... | collective-permute-start | bytes 98312 | tf_op jit(solution)/shard_map/ppermute | solution.py:26
  49.0 7.5 %collective-permute-start.7 = (bf16[64,256]{1,0:T(8,128)(2,1)S(1)}, bf16[64,256]{1,0:T(8,128)(2,1)S(1)}, u32[]{:S(2)}, u32[]{:S(2)}) collective-permute-start(bf16[64,256]{1,0:T(8,128)(2,1)S(1)} %fusion.68), channel_id=1, source_target_pairs={{0,8},{4,12},{8,0},{12,4},{1,9},{5,13},{9,1},{13,5},{2,10},{6,14},... | collective-permute-start | bytes 98312 | tf_op jit(solution)/shard_map/ppermute | solution.py:26
  51.1 5.3 %collective-permute-start.6 = (bf16[64,256]{1,0:T(8,128)(2,1)S(1)}, bf16[64,256]{1,0:T(8,128)(2,1)S(1)}, u32[]{:S(2)}, u32[]{:S(2)}) collective-permute-start(bf16[64,256]{1,0:T(8,128)(2,1)S(1)} %fusion.68), channel_id=1, source_target_pairs={{0,12},{4,0},{8,4},{12,8},{1,13},{5,1},{9,5},{13,9},{2,14},{6,2},{... | collective-permute-start | bytes 98312 | tf_op jit(solution)/shard_map/ppermute | solution.py:26
  51.5 5.8 %collective-permute-start.17 = (bf16[65,256]{1,0:T(8,128)(2,1)S(1)}, bf16[65,256]{1,0:T(8,128)(2,1)S(1)}, u32[]{:S(2)}, u32[]{:S(2)}) collective-permute-start(bf16[65,256]{1,0:T(8,128)(2,1)S(1)} %fusion.61), channel_id=1, source_target_pairs={{0,4},{4,8},{8,12},{12,0},{1,5},{5,9},{9,13},{13,1},{2,6},{6,10},{... | collective-permute-start | bytes 99848 | tf_op jit(solution)/shard_map/ppermute | solution.py:26
  53.3 5.3 %collective-permute-start.16 = (bf16[65,256]{1,0:T(8,128)(2,1)S(1)}, bf16[65,256]{1,0:T(8,128)(2,1)S(1)}, u32[]{:S(2)}, u32[]{:S(2)}) collective-permute-start(bf16[65,256]{1,0:T(8,128)(2,1)S(1)} %fusion.61), channel_id=1, source_target_pairs={{0,8},{4,12},{8,0},{12,4},{1,9},{5,13},{9,1},{13,5},{2,10},{6,14},... | collective-permute-start | bytes 99848 | tf_op jit(solution)/shard_map/ppermute | solution.py:26
  55.0 4.0 %collective-permute-start.15 = (bf16[65,256]{1,0:T(8,128)(2,1)S(1)}, bf16[65,256]{1,0:T(8,128)(2,1)S(1)}, u32[]{:S(2)}, u32[]{:S(2)}) collective-permute-start(bf16[65,256]{1,0:T(8,128)(2,1)S(1)} %fusion.61), channel_id=1, source_target_pairs={{0,12},{4,0},{8,4},{12,8},{1,13},{5,1},{9,5},{13,9},{2,14},{6,2},{... | collective-permute-start | bytes 99848 | tf_op jit(solution)/shard_map/ppermute | solution.py:26
  59.0 8.6 %collective-permute-start.20 = (bf16[4,129,256]{2,1,0:T(8,128)(2,1)S(1)}, bf16[4,129,256]{2,1,0:T(8,128)(2,1)S(1)}, u32[]{:S(2)}, u32[]{:S(2)}) collective-permute-start(bf16[4,129,256]{2,1,0:T(8,128)(2,1)S(1)} %maximum_maximum_fusion), channel_id=1, source_target_pairs={{0,1},{1,0},{2,3},{3,2},{4,5},{5,4},{6,7},{7,6},{8,9},{9,8},{10,11... | collective-permute-start | bytes 792584 | tf_op jit(solution)/shard_map/ppermute | solution.py:37
  60.1 11.6 %collective-permute-start.19 = (bf16[4,129,256]{2,1,0:T(8,128)(2,1)S(1)}, bf16[4,129,256]{2,1,0:T(8,128)(2,1)S(1)}, u32[]{:S(2)}, u32[]{:S(2)}) collective-permute-start(bf16[4,129,256]{2,1,0:T(8,128)(2,1)S(1)} %maximum_maximum_fusion), channel_id=1, source_target_pairs={{0,2},{1,3},{2,0},{3,1},{4,6},{5,7},{6,4},{7,5},{8,10},{9,11},{10,... | collective-permute-start | bytes 792584 | tf_op jit(solution)/shard_map/ppermute | solution.py:37
  61.7 10.1 %collective-permute-start.18 = (bf16[4,129,256]{2,1,0:T(8,128)(2,1)S(1)}, bf16[4,129,256]{2,1,0:T(8,128)(2,1)S(1)}, u32[]{:S(2)}, u32[]{:S(2)}) collective-permute-start(bf16[4,129,256]{2,1,0:T(8,128)(2,1)S(1)} %maximum_maximum_fusion), channel_id=1, source_target_pairs={{0,3},{1,2},{2,1},{3,0},{4,7},{5,6},{6,5},{7,4},{8,11},{9,10},{10,... | collective-permute-start | bytes 792584 | tf_op jit(solution)/shard_map/ppermute | solution.py:37
  73.9 2.9 %collective-permute-start.21 = (bf16[4,4,129,256]{3,1,2,0:T(4,128)(2,1)}, bf16[4,4,129,256]{3,1,2,0:T(4,128)(2,1)S(1)}, u32[]{:S(2)}, u32[]{:S(2)}) collective-permute-start(bf16[4,4,129,256]{3,1,2,0:T(4,128)(2,1)} %copy.175), channel_id=1, source_target_pairs={{0,16},{16,0},{1,17},{17,1},{2,18},{18,2},{3,19},{19,3},{4,20},{20... | collective-permute-start | bytes 3170312 | tf_op jit(solution)/shard_map/ppermute | solution.py:26
  (3 other events, 8.6 us)
